TPU v7x, 1024 devices: a whole 4x4x32 slice. The times are simulated.
1024 devices in a mesh: ctx: 64 (over y, x, z_hi, core), tp: 16 (over z_lo).
Axes of the slice: x: 4, y: 4, z: 32 (z_hi: 2, z_lo: 16; z = z_hi * 16 + z_lo), core: 2. Of those that a mesh axis runs over, the one named last changes fastest.
Arguments:
- query_stream: bfloat16 [16384, 8192], P('ctx', 'tp'), may hold values from -6 to 6
- key_stream: bfloat16 [16384, 8192], P('ctx', 'tp'), may hold values from -6 to 6
- value_stream: bfloat16 [16384, 8192], P('ctx', 'tp'), may hold values from -6 to 6
- feat_taps: float32 [3, 7, 8192], P(None, None, 'tp'), may hold values from -2 to 2
- filt_taps: float32 [128, 8192], P(None, 'tp'), may hold values from -0.5 to 0.5
- skip_bias: float32 [8192], P('tp'), may hold values from -3 to 3
- out_weight: bfloat16 [8192, 8192], P('tp'), may hold values from -0.09375 to 0.09375
Outputs:
- block_out: bfloat16 [16384, 8192], P('ctx', 'tp')
All inputs are finite; a program needn't handle non-finite values.
Results may differ from a plain program's by a relative error of at most 0.02.
Values may be sent and summed in bfloat16 or wider, within the bound.
No kernel may reach another device: no remote copies, remote signals or barrier semaphores. Data moves between devices by JAX's collectives and lax.ppermute only.
A program may use at most 32 MiB of HBM per device.

v0:
```python
import jax
import jax.numpy as jnp
from jax import lax
from jax.sharding import PartitionSpec as P


def shifted(block, axis, distance):
    devices = range(lax.axis_size(axis))
    route = [(i - distance, i) for i in devices if i - distance in devices]
    return lax.ppermute(block, axis, route)


def valid_conv(extended, taps):
    tap_count = taps.shape[0]
    out_rows = extended.shape[0] - tap_count + 1
    running = taps[0][None, :] * extended[tap_count - 1 : tap_count - 1 + out_rows]
    for offset in range(1, tap_count):
        running = (
            running
            + taps[offset][None, :]
            * extended[tap_count - 1 - offset : tap_count - 1 - offset + out_rows]
        )
    return running


def shards(query_stream, key_stream, value_stream, feat_taps, filt_taps, skip_bias, out_weight):
    filt_reach = filt_taps.shape[0] - 1
    feat_reach = feat_taps.shape[1] - 1
    full_reach = filt_reach + feat_reach
    outgoing = jnp.concatenate(
        [key_stream[-full_reach:], value_stream[-full_reach:], query_stream[-feat_reach:]], 0
    )
    incoming = shifted(outgoing, "ctx", 1)
    key_ext = jnp.concatenate([incoming[:full_reach], key_stream], 0)
    value_ext = jnp.concatenate([incoming[full_reach : 2 * full_reach], value_stream], 0)
    query_ext = jnp.concatenate([incoming[2 * full_reach :], query_stream], 0)
    key_feat = valid_conv(key_ext.astype(jnp.float32), feat_taps[1])
    value_feat = valid_conv(value_ext.astype(jnp.float32), feat_taps[2])
    query_feat = valid_conv(query_ext.astype(jnp.float32), feat_taps[0])
    gated = (key_feat * value_feat).astype(jnp.bfloat16)
    own_gated = gated[filt_reach:].astype(jnp.float32)
    mixed = valid_conv(gated.astype(jnp.float32), filt_taps) + skip_bias[None, :] * own_gated
    product = (query_feat * mixed).astype(jnp.bfloat16)
    terms = jnp.dot(product, out_weight, preferred_element_type=jnp.float32)
    block_out = lax.psum_scatter(terms.astype(jnp.bfloat16), "tp", scatter_dimension=1, tiled=True)
    return block_out


def solution(mesh):
    in_specs = (
        P("ctx", "tp"),
        P("ctx", "tp"),
        P("ctx", "tp"),
        P(None, None, "tp"),
        P(None, "tp"),
        P("tp"),
        P("tp", None),
    )
    out_specs = P("ctx", "tp")
    return jax.shard_map(shards, mesh=mesh, in_specs=in_specs, out_specs=out_specs, check_vma=False)
```

profile of v0, /device:TPU:10, one launch (start us, length us, event | category | flops | bytes accessed | tf_op | source)
XLA Modules:
  0.0 307.2 jit_solution(11825674752984003141)
XLA Ops:
  6.5 0.0 reduce-scatter.2.cloned.1.call-start
  6.5 0.7 slice.963
  7.2 0.9 slice.961
  8.2 0.9 slice.962
  9.2 1.9 collective-permute-start
  11.1 1.1 fusion.160
  12.2 1.2 fusion.158
  13.4 1.3 fusion.157
  14.7 1.3 fusion.156
  16.0 1.2 fusion.155
  17.2 1.1 fusion.154
  18.3 0.0 copy-start
  18.3 1.2 fusion.161
  19.5 0.8 fusion.162
  20.3 1.2 fusion.159
  21.5 21.0 %collective-permute-done = bf16[272,512]{1,0:T(8,128)(2,1)S(1)} collective-permute-done((bf16[272,512]{1,0:T(8,128)(2,1)S(1)}, bf16[272,512]{1,0:T(8,128)(2,1)S(1)}, u32[]{:S(2)}, u32[]{:S(2)}) %collective-permute-start) | collective-permute-done | bytes 278560 | tf_op jit(solution)/shard_map/ppermute | solution.py:10
  42.5 1.0 maximum_convert_fusion.2
  43.6 1.2 maximum_convert_fusion
  44.8 1.3 fusion.151
  46.1 0.0 copy-done
  46.1 18.1 %convolution_convert_fusion = bf16[256,8192]{1,0:T(8,128)(2,1)} fusion(bf16[512,8192]{1,0:T(8,128)(2,1)} %param.13, f32[383,512]{1,0:T(8,128)S(1)} %get-tuple-element.5, f32[512]{0:T(512)S(1)} %bitcast.176, f32[512]{0:T(512)S(1)} %bitcast.177, f32[512]{0:T(512)S(1)} %bitcast.255, f32[512]{0:T(512)S(1)} %bitcast.256, f32[512]{0:T(512)S(1)} %bitcast.257, ...), kind=kOutput, calls=%fused_computation | convolution fusion | flops 2185363456 | bytes 83902464 | tf_op jit(solution)/shard_map/dot_general | solution.py:44
  64.2 0.0 reduce-scatter.2.cloned.1.call-update
  64.2 236.1 %reduce-scatter.2.cloned.1.call-done = bf16[256,512]{1,0:T(8,128)(2,1)} async-done(((bf16[256,8192]{1,0:T(8,128)(2,1)}), bf16[256,512]{1,0:T(8,128)(2,1)}) %reduce-scatter.2.cloned.1.call-update) | async-done | bytes 262160 | tf_op jit(solution)/shard_map/reduce_scatter | solution.py:45
  (3 shorter events, 0.1 us)
Async XLA Ops:
  6.5 293.8 %reduce-scatter.2.cloned.1.call-start = ((), (), s32[]{:S(2)}) async-start(), calls=%async_computation.1 | async-start | bytes 4456448 | tf_op jit(solution)/shard_map/reduce_scatter | solution.py:45
  9.2 33.3 %collective-permute-start = (bf16[272,512]{1,0:T(8,128)(2,1)S(1)}, bf16[272,512]{1,0:T(8,128)(2,1)S(1)}, u32[]{:S(2)}, u32[]{:S(2)}) collective-permute-start(bf16[272,512]{1,0:T(8,128)(2,1)S(1)} %pad_maximum_fusion), channel_id=1, source_target_pairs={{0,16},{16,32},{32,48},{48,64},{64,80},{80,96},{96,112},{112,128},... | collective-permute-start | bytes 835592 | tf_op jit(solution)/shard_map/ppermute | solution.py:10
  18.3 27.8 %copy-start = (f32[512]{0:T(512)S(1)}, f32[512]{0:T(512)}, u32[]{:S(2)}) copy-start(f32[512]{0:T(512)} %param.12) | copy-start | bytes 6148
Sparse Core Ops, SparseCore 0:
  64.4 235.9 reduce-scatter.1
where the time goes:
time: 308 us; the launch traced here: 307 us
  waiting for transfers between devices  257 us (83%)
  matrix products  18.1 us (6%)
  between operations  13.5 us (4%)
  local copies, waits for them, and re-layouts  13 us (4%)
  other arithmetic  3.63 us (1%)
    reduce_scatter x1, waiting for transfers between devices, shards(): lax.psum_scatter(terms.astype(jnp.bfloat16), 'tp', scatter_dimension=1, t...  236 us
    ppermute x1, waiting for transfers between devices, shifted(): return lax.ppermute(block, axis, route)  21 us
    dot_general x1, matrix products, shards(): terms = jnp.dot(product, out_weight, preferred_element_type=jnp.float32)  18.1 us
    slice x7, local copies, waits for them, and re-layouts, valid_conv(): taps[offset][None, :]  8.03 us
  transfers between devices with their start and end apart: 2, of which 2 were waited for; matrix products, arithmetic and copies ran while one was open for 3% of the time, Pallas kernels for 0%

commit v1 on v0

--- a/solution.py
+++ b/solution.py
@@ -23,6 +23,26 @@
     return running
 
 
+def line_reduce_scatter(terms, axis):
+    n = lax.axis_size(axis)
+    me = lax.axis_index(axis)
+    width = terms.shape[1] // n
+
+    def block(j):
+        j = jnp.clip(j, 0, n - 1)
+        return lax.dynamic_slice_in_dim(terms, j * width, width, 1).astype(jnp.float32)
+
+    zeros = jnp.zeros((terms.shape[0], width), terms.dtype)
+    from_left, from_right = zeros, zeros
+    for step in range(n - 1):
+        send_right = (from_left.astype(jnp.float32) + block(n - 1 + me - step)).astype(terms.dtype)
+        send_left = (from_right.astype(jnp.float32) + block(step - (n - 1) + me)).astype(terms.dtype)
+        from_left = lax.ppermute(send_right, axis, [(k, k + 1) for k in range(n - 1) if k <= step])
+        from_right = lax.ppermute(send_left, axis, [(k, k - 1) for k in range(1, n) if k >= n - 1 - step])
+    total = from_left.astype(jnp.float32) + block(me) + from_right.astype(jnp.float32)
+    return total.astype(terms.dtype)
+
+
 def shards(query_stream, key_stream, value_stream, feat_taps, filt_taps, skip_bias, out_weight):
     filt_reach = filt_taps.shape[0] - 1
     feat_reach = feat_taps.shape[1] - 1
@@ -42,8 +62,7 @@
     mixed = valid_conv(gated.astype(jnp.float32), filt_taps) + skip_bias[None, :] * own_gated
     product = (query_feat * mixed).astype(jnp.bfloat16)
     terms = jnp.dot(product, out_weight, preferred_element_type=jnp.float32)
-    block_out = lax.psum_scatter(terms.astype(jnp.bfloat16), "tp", scatter_dimension=1, tiled=True)
-    return block_out
+    return line_reduce_scatter(terms.astype(jnp.bfloat16), "tp")
 
 
 def solution(mesh):

time: 308 us -> 267 us (0.87)
  the two profiles are of different devices: /device:TPU:10 before, /device:TPU:112 now
where the time goes in v1:
time: 267 us; the launch traced here: 265 us
  waiting for transfers between devices  144 us (54%)
  starting transfers between devices  66.8 us (25%)
  other arithmetic  21.6 us (8%)
  matrix products  18.1 us (7%)
  local copies, waits for them, and re-layouts  14 us (5%)
    ppermute x15, waiting for transfers between devices, line_reduce_scatter(): lax.ppermute(send_right, axis, [(k, k + 1) for k in range(n - 1) if k <=...  79.1 us
    ppermute x15, starting transfers between devices, line_reduce_scatter(): lax.ppermute(send_right, axis, [(k, k + 1) for k in range(n - 1) if k <=...  47.6 us
    ppermute x1, waiting for transfers between devices, shifted(): return lax.ppermute(block, axis, route)  38.2 us
    ppermute x15, waiting for transfers between devices, line_reduce_scatter(): lax.ppermute(send_left, axis, [(k, k - 1) for k in range(1, n) if k >= n...  26.4 us
    dot_general x1, matrix products, shards(): terms = jnp.dot(product, out_weight, preferred_element_type=jnp.float32)  18.1 us
    ppermute x15, starting transfers between devices, line_reduce_scatter(): lax.ppermute(send_left, axis, [(k, k - 1) for k in range(1, n) if k >= n...  17.3 us
    convert_element_type x14, other arithmetic, line_reduce_scatter(): (from_left.astype(jnp.float32) + block(n - 1 + me - step)).astype(terms.d...  16.2 us
    slice x7, local copies, waits for them, and re-layouts, valid_conv(): taps[offset][None, :]  8.03 us
  transfers between devices with their start and end apart: 31, of which 18 were waited for; matrix products, arithmetic and copies ran while one was open for 4% of the time, Pallas kernels for 0%

profile of v1, /device:TPU:112, one launch (start us, length us, event | category | flops | bytes accessed | tf_op | source)
XLA Modules:
  0.0 264.7 jit_solution(10748368899630607393)
XLA Ops:
  14.9 38.2 %collective-permute-done = bf16[272,512]{1,0:T(8,128)(2,1)S(1)} collective-permute-done((bf16[272,512]{1,0:T(8,128)(2,1)S(1)}, bf16[272,512]{1,0:T(8,128)(2,1)S(1)}, u32[]{:S(2)}, u32[]{:S(2)}) %collective-permute-start) | collective-permute-done | bytes 278560 | tf_op jit(solution)/shard_map/ppermute | solution.py:10
  56.8 18.1 %convolution_convert_fusion = bf16[256,8192]{1,0:T(8,128)(2,1)} fusion(bf16[512,8192]{1,0:T(8,128)(2,1)} %param.13, f32[383,512]{1,0:T(8,128)S(1)} %get-tuple-element.5, f32[512]{0:T(512)S(1)} %bitcast.271, f32[512]{0:T(512)S(1)} %bitcast.272, f32[512]{0:T(512)S(1)} %bitcast.203, f32[512]{0:T(512)S(1)} %bitcast.204, f32[512]{0:T(512)S(1)} %bitcast.205, ...), kind=kOutput, calls=%fused_computation | convolution fusion | flops 2185363456 | bytes 83902464 | tf_op jit(solution)/shard_map/dot_general | solution.py:64
  83.2 21.2 %collective-permute-done.3 = bf16[256,512]{1,0:T(8,128)(2,1)S(1)} collective-permute-done((bf16[256,512]{1,0:T(8,128)(2,1)S(1)}, bf16[256,512]{1,0:T(8,128)(2,1)S(1)}, u32[]{:S(2)}, u32[]{:S(2)}) %collective-permute-start.3) | collective-permute-done | bytes 262176 | tf_op jit(solution)/shard_map/ppermute | solution.py:40
  108.2 6.9 %collective-permute-done.4 = bf16[256,512]{1,0:T(8,128)(2,1)S(1)} collective-permute-done((bf16[256,512]{1,0:T(8,128)(2,1)S(1)}, bf16[256,512]{1,0:T(8,128)(2,1)S(1)}, u32[]{:S(2)}, u32[]{:S(2)}) %collective-permute-start.4) | collective-permute-done | bytes 262176 | tf_op jit(solution)/shard_map/ppermute | solution.py:40
  119.5 7.6 %collective-permute-done.5 = bf16[256,512]{1,0:T(8,128)(2,1)S(1)} collective-permute-done((bf16[256,512]{1,0:T(8,128)(2,1)S(1)}, bf16[256,512]{1,0:T(8,128)(2,1)S(1)}, u32[]{:S(2)}, u32[]{:S(2)}) %collective-permute-start.5) | collective-permute-done | bytes 262176 | tf_op jit(solution)/shard_map/ppermute | solution.py:40
  131.0 9.5 %collective-permute-done.6 = bf16[256,512]{1,0:T(8,128)(2,1)S(1)} collective-permute-done((bf16[256,512]{1,0:T(8,128)(2,1)S(1)}, bf16[256,512]{1,0:T(8,128)(2,1)S(1)}, u32[]{:S(2)}, u32[]{:S(2)}) %collective-permute-start.6) | collective-permute-done | bytes 262176 | tf_op jit(solution)/shard_map/ppermute | solution.py:40
  144.3 8.3 %collective-permute-done.7 = bf16[256,512]{1,0:T(8,128)(2,1)S(1)} collective-permute-done((bf16[256,512]{1,0:T(8,128)(2,1)S(1)}, bf16[256,512]{1,0:T(8,128)(2,1)S(1)}, u32[]{:S(2)}, u32[]{:S(2)}) %collective-permute-start.7) | collective-permute-done | bytes 262176 | tf_op jit(solution)/shard_map/ppermute | solution.py:40
  154.5 3.8 %collective-permute-start.8 = (bf16[256,512]{1,0:T(8,128)(2,1)S(1)}, bf16[256,512]{1,0:T(8,128)(2,1)S(1)}, u32[]{:S(2)}, u32[]{:S(2)}) collective-permute-start(bf16[256,512]{1,0:T(8,128)(2,1)S(1)} %get-tuple-element.21), channel_id=1, source_target_pairs={{0,1},{1,2},{2,3},{3,4},{4,5},{5,6},{6,7},{7,8},{16,17},{17,18},{1... | collective-permute-start | bytes 786440 | tf_op jit(solution)/shard_map/ppermute | solution.py:40
  158.3 5.6 %collective-permute-done.8 = bf16[256,512]{1,0:T(8,128)(2,1)S(1)} collective-permute-done((bf16[256,512]{1,0:T(8,128)(2,1)S(1)}, bf16[256,512]{1,0:T(8,128)(2,1)S(1)}, u32[]{:S(2)}, u32[]{:S(2)}) %collective-permute-start.8) | collective-permute-done | bytes 262176 | tf_op jit(solution)/shard_map/ppermute | solution.py:40
  165.7 5.3 %collective-permute-start.9 = (bf16[256,512]{1,0:T(8,128)(2,1)S(1)}, bf16[256,512]{1,0:T(8,128)(2,1)S(1)}, u32[]{:S(2)}, u32[]{:S(2)}) collective-permute-start(bf16[256,512]{1,0:T(8,128)(2,1)S(1)} %get-tuple-element.19), channel_id=1, source_target_pairs={{0,1},{1,2},{2,3},{3,4},{4,5},{5,6},{6,7},{7,8},{8,9},{16,17},{17,... | collective-permute-start | bytes 786440 | tf_op jit(solution)/shard_map/ppermute | solution.py:40
  171.1 3.9 %collective-permute-done.9 = bf16[256,512]{1,0:T(8,128)(2,1)S(1)} collective-permute-done((bf16[256,512]{1,0:T(8,128)(2,1)S(1)}, bf16[256,512]{1,0:T(8,128)(2,1)S(1)}, u32[]{:S(2)}, u32[]{:S(2)}) %collective-permute-start.9) | collective-permute-done | bytes 262176 | tf_op jit(solution)/shard_map/ppermute | solution.py:40
  176.1 5.6 %collective-permute-start.10 = (bf16[256,512]{1,0:T(8,128)(2,1)S(1)}, bf16[256,512]{1,0:T(8,128)(2,1)S(1)}, u32[]{:S(2)}, u32[]{:S(2)}) collective-permute-start(bf16[256,512]{1,0:T(8,128)(2,1)S(1)} %get-tuple-element.17), channel_id=1, source_target_pairs={{0,1},{1,2},{2,3},{3,4},{4,5},{5,6},{6,7},{7,8},{8,9},{9,10},{16,1... | collective-permute-start | bytes 786440 | tf_op jit(solution)/shard_map/ppermute | solution.py:40
  182.4 3.2 %collective-permute-done.10 = bf16[256,512]{1,0:T(8,128)(2,1)S(1)} collective-permute-done((bf16[256,512]{1,0:T(8,128)(2,1)S(1)}, bf16[256,512]{1,0:T(8,128)(2,1)S(1)}, u32[]{:S(2)}, u32[]{:S(2)}) %collective-permute-start.10) | collective-permute-done | bytes 262176 | tf_op jit(solution)/shard_map/ppermute | solution.py:40
  186.8 5.6 %collective-permute-start.11 = (bf16[256,512]{1,0:T(8,128)(2,1)S(1)}, bf16[256,512]{1,0:T(8,128)(2,1)S(1)}, u32[]{:S(2)}, u32[]{:S(2)}) collective-permute-start(bf16[256,512]{1,0:T(8,128)(2,1)S(1)} %get-tuple-element.15), channel_id=1, source_target_pairs={{0,1},{1,2},{2,3},{3,4},{4,5},{5,6},{6,7},{7,8},{8,9},{9,10},{10,1... | collective-permute-start | bytes 786440 | tf_op jit(solution)/shard_map/ppermute | solution.py:40
  193.1 3.2 %collective-permute-done.11 = bf16[256,512]{1,0:T(8,128)(2,1)S(1)} collective-permute-done((bf16[256,512]{1,0:T(8,128)(2,1)S(1)}, bf16[256,512]{1,0:T(8,128)(2,1)S(1)}, u32[]{:S(2)}, u32[]{:S(2)}) %collective-permute-start.11) | collective-permute-done | bytes 262176 | tf_op jit(solution)/shard_map/ppermute | solution.py:40
  197.4 7.1 %collective-permute-start.12 = (bf16[256,512]{1,0:T(8,128)(2,1)S(1)}, bf16[256,512]{1,0:T(8,128)(2,1)S(1)}, u32[]{:S(2)}, u32[]{:S(2)}) collective-permute-start(bf16[256,512]{1,0:T(8,128)(2,1)S(1)} %get-tuple-element.13), channel_id=1, source_target_pairs={{0,1},{1,2},{2,3},{3,4},{4,5},{5,6},{6,7},{7,8},{8,9},{9,10},{10,1... | collective-permute-start | bytes 786440 | tf_op jit(solution)/shard_map/ppermute | solution.py:40
  208.4 5.6 %collective-permute-done.27 = bf16[256,512]{1,0:T(8,128)(2,1)S(1)} collective-permute-done((bf16[256,512]{1,0:T(8,128)(2,1)S(1)}, bf16[256,512]{1,0:T(8,128)(2,1)S(1)}, u32[]{:S(2)}, u32[]{:S(2)}) %collective-permute-start.27) | collective-permute-done | bytes 262176 | tf_op jit(solution)/shard_map/ppermute | solution.py:41
  217.3 3.7 %collective-permute-start.28 = (bf16[256,512]{1,0:T(8,128)(2,1)S(1)}, bf16[256,512]{1,0:T(8,128)(2,1)S(1)}, u32[]{:S(2)}, u32[]{:S(2)}) collective-permute-start(bf16[256,512]{1,0:T(8,128)(2,1)S(1)} %get-tuple-element.12), channel_id=1, source_target_pairs={{3,2},{4,3},{5,4},{6,5},{7,6},{8,7},{9,8},{10,9},{11,10},{12,11},{... | collective-permute-start | bytes 786440 | tf_op jit(solution)/shard_map/ppermute | solution.py:41
  223.4 3.3 %collective-permute-done.28 = bf16[256,512]{1,0:T(8,128)(2,1)S(1)} collective-permute-done((bf16[256,512]{1,0:T(8,128)(2,1)S(1)}, bf16[256,512]{1,0:T(8,128)(2,1)S(1)}, u32[]{:S(2)}, u32[]{:S(2)}) %collective-permute-start.28) | collective-permute-done | bytes 262176 | tf_op jit(solution)/shard_map/ppermute | solution.py:41
  227.9 2.9 %collective-permute-start.14 = (bf16[256,512]{1,0:T(8,128)(2,1)S(1)}, bf16[256,512]{1,0:T(8,128)(2,1)S(1)}, u32[]{:S(2)}, u32[]{:S(2)}) collective-permute-start(bf16[256,512]{1,0:T(8,128)(2,1)S(1)} %get-tuple-element.9), channel_id=1, source_target_pairs={{0,1},{1,2},{2,3},{3,4},{4,5},{5,6},{6,7},{7,8},{8,9},{9,10},{10,1... | collective-permute-start | bytes 786440 | tf_op jit(solution)/shard_map/ppermute | solution.py:40
  230.8 2.9 %collective-permute-start.29 = (bf16[256,512]{1,0:T(8,128)(2,1)S(1)}, bf16[256,512]{1,0:T(8,128)(2,1)S(1)}, u32[]{:S(2)}, u32[]{:S(2)}) collective-permute-start(bf16[256,512]{1,0:T(8,128)(2,1)S(1)} %get-tuple-element.10), channel_id=1, source_target_pairs={{2,1},{3,2},{4,3},{5,4},{6,5},{7,6},{8,7},{9,8},{10,9},{11,10},{12... | collective-permute-start | bytes 786440 | tf_op jit(solution)/shard_map/ppermute | solution.py:41
  236.2 12.3 %collective-permute-done.29 = bf16[256,512]{1,0:T(8,128)(2,1)S(1)} collective-permute-done((bf16[256,512]{1,0:T(8,128)(2,1)S(1)}, bf16[256,512]{1,0:T(8,128)(2,1)S(1)}, u32[]{:S(2)}, u32[]{:S(2)}) %collective-permute-start.29) | collective-permute-done | bytes 262176 | tf_op jit(solution)/shard_map/ppermute | solution.py:41
  249.6 3.9 %collective-permute-start.15 = (bf16[256,512]{1,0:T(8,128)(2,1)S(1)}, bf16[256,512]{1,0:T(8,128)(2,1)S(1)}, u32[]{:S(2)}, u32[]{:S(2)}) collective-permute-start(bf16[256,512]{1,0:T(8,128)(2,1)S(1)} %get-tuple-element.7), channel_id=1, source_target_pairs={{0,1},{1,2},{2,3},{3,4},{4,5},{5,6},{6,7},{7,8},{8,9},{9,10},{10,1... | collective-permute-start | bytes 786440 | tf_op jit(solution)/shard_map/ppermute | solution.py:40
  257.8 5.1 %collective-permute-done.30 = bf16[256,512]{1,0:T(8,128)(2,1)S(1)} collective-permute-done((bf16[256,512]{1,0:T(8,128)(2,1)S(1)}, bf16[256,512]{1,0:T(8,128)(2,1)S(1)}, u32[]{:S(2)}, u32[]{:S(2)}) %collective-permute-start.30) | collective-permute-done | bytes 262176 | tf_op jit(solution)/shard_map/ppermute | solution.py:41
  (75 shorter events, 71.3 us)
Async XLA Ops:
  2.6 50.5 %collective-permute-start = (bf16[272,512]{1,0:T(8,128)(2,1)S(1)}, bf16[272,512]{1,0:T(8,128)(2,1)S(1)}, u32[]{:S(2)}, u32[]{:S(2)}) collective-permute-start(bf16[272,512]{1,0:T(8,128)(2,1)S(1)} %pad_maximum_fusion), channel_id=1, source_target_pairs={{0,16},{16,32},{32,48},{48,64},{64,80},{80,96},{96,112},{112,128},... | collective-permute-start | bytes 835592 | tf_op jit(solution)/shard_map/ppermute | solution.py:10
  81.8 22.5 %collective-permute-start.3 = (bf16[256,512]{1,0:T(8,128)(2,1)S(1)}, bf16[256,512]{1,0:T(8,128)(2,1)S(1)}, u32[]{:S(2)}, u32[]{:S(2)}) collective-permute-start(bf16[256,512]{1,0:T(8,128)(2,1)S(1)} %get-tuple-element.31), channel_id=1, source_target_pairs={{0,1},{1,2},{2,3},{16,17},{17,18},{18,19},{32,33},{33,34},{34,35},... | collective-permute-start | bytes 786440 | tf_op jit(solution)/shard_map/ppermute | solution.py:40
  106.2 8.8 %collective-permute-start.4 = (bf16[256,512]{1,0:T(8,128)(2,1)S(1)}, bf16[256,512]{1,0:T(8,128)(2,1)S(1)}, u32[]{:S(2)}, u32[]{:S(2)}) collective-permute-start(bf16[256,512]{1,0:T(8,128)(2,1)S(1)} %get-tuple-element.29), channel_id=1, source_target_pairs={{0,1},{1,2},{2,3},{3,4},{16,17},{17,18},{18,19},{19,20},{32,33},{3... | collective-permute-start | bytes 786440 | tf_op jit(solution)/shard_map/ppermute | solution.py:40
  116.2 3.3 %collective-permute-start.20 = (bf16[256,512]{1,0:T(8,128)(2,1)S(1)}, bf16[256,512]{1,0:T(8,128)(2,1)S(1)}, u32[]{:S(2)}, u32[]{:S(2)}) collective-permute-start(bf16[256,512]{1,0:T(8,128)(2,1)S(1)} %get-tuple-element.28), channel_id=1, source_target_pairs={{11,10},{12,11},{13,12},{14,13},{15,14},{27,26},{28,27},{29,28},{3... | collective-permute-start | bytes 786440 | tf_op jit(solution)/shard_map/ppermute | solution.py:41
  116.9 10.2 %collective-permute-start.5 = (bf16[256,512]{1,0:T(8,128)(2,1)S(1)}, bf16[256,512]{1,0:T(8,128)(2,1)S(1)}, u32[]{:S(2)}, u32[]{:S(2)}) collective-permute-start(bf16[256,512]{1,0:T(8,128)(2,1)S(1)} %get-tuple-element.27), channel_id=1, source_target_pairs={{0,1},{1,2},{2,3},{3,4},{4,5},{16,17},{17,18},{18,19},{19,20},{20,... | collective-permute-start | bytes 786440 | tf_op jit(solution)/shard_map/ppermute | solution.py:40
  128.2 2.8 %collective-permute-start.21 = (bf16[256,512]{1,0:T(8,128)(2,1)S(1)}, bf16[256,512]{1,0:T(8,128)(2,1)S(1)}, u32[]{:S(2)}, u32[]{:S(2)}) collective-permute-start(bf16[256,512]{1,0:T(8,128)(2,1)S(1)} %get-tuple-element.26), channel_id=1, source_target_pairs={{10,9},{11,10},{12,11},{13,12},{14,13},{15,14},{26,25},{27,26},{28... | collective-permute-start | bytes 786440 | tf_op jit(solution)/shard_map/ppermute | solution.py:41
  128.9 11.6 %collective-permute-start.6 = (bf16[256,512]{1,0:T(8,128)(2,1)S(1)}, bf16[256,512]{1,0:T(8,128)(2,1)S(1)}, u32[]{:S(2)}, u32[]{:S(2)}) collective-permute-start(bf16[256,512]{1,0:T(8,128)(2,1)S(1)} %get-tuple-element.25), channel_id=1, source_target_pairs={{0,1},{1,2},{2,3},{3,4},{4,5},{5,6},{16,17},{17,18},{18,19},{19,20... | collective-permute-start | bytes 786440 | tf_op jit(solution)/shard_map/ppermute | solution.py:40
  142.4 10.2 %collective-permute-start.7 = (bf16[256,512]{1,0:T(8,128)(2,1)S(1)}, bf16[256,512]{1,0:T(8,128)(2,1)S(1)}, u32[]{:S(2)}, u32[]{:S(2)}) collective-permute-start(bf16[256,512]{1,0:T(8,128)(2,1)S(1)} %get-tuple-element.23), channel_id=1, source_target_pairs={{0,1},{1,2},{2,3},{3,4},{4,5},{5,6},{6,7},{16,17},{17,18},{18,19},... | collective-permute-start | bytes 786440 | tf_op jit(solution)/shard_map/ppermute | solution.py:40
  153.8 4.5 %collective-permute-start.23 = (bf16[256,512]{1,0:T(8,128)(2,1)S(1)}, bf16[256,512]{1,0:T(8,128)(2,1)S(1)}, u32[]{:S(2)}, u32[]{:S(2)}) collective-permute-start(bf16[256,512]{1,0:T(8,128)(2,1)S(1)} %get-tuple-element.22), channel_id=1, source_target_pairs={{8,7},{9,8},{10,9},{11,10},{12,11},{13,12},{14,13},{15,14},{24,23}... | collective-permute-start | bytes 786440 | tf_op jit(solution)/shard_map/ppermute | solution.py:41
  154.5 9.4 %collective-permute-start.8 = (bf16[256,512]{1,0:T(8,128)(2,1)S(1)}, bf16[256,512]{1,0:T(8,128)(2,1)S(1)}, u32[]{:S(2)}, u32[]{:S(2)}) collective-permute-start(bf16[256,512]{1,0:T(8,128)(2,1)S(1)} %get-tuple-element.21), channel_id=1, source_target_pairs={{0,1},{1,2},{2,3},{3,4},{4,5},{5,6},{6,7},{7,8},{16,17},{17,18},{1... | collective-permute-start | bytes 786440 | tf_op jit(solution)/shard_map/ppermute | solution.py:40
  165.0 6.0 %collective-permute-start.24 = (bf16[256,512]{1,0:T(8,128)(2,1)S(1)}, bf16[256,512]{1,0:T(8,128)(2,1)S(1)}, u32[]{:S(2)}, u32[]{:S(2)}) collective-permute-start(bf16[256,512]{1,0:T(8,128)(2,1)S(1)} %get-tuple-element.20), channel_id=1, source_target_pairs={{7,6},{8,7},{9,8},{10,9},{11,10},{12,11},{13,12},{14,13},{15,14},{... | collective-permute-start | bytes 786440 | tf_op jit(solution)/shard_map/ppermute | solution.py:41
  165.7 9.3 %collective-permute-start.9 = (bf16[256,512]{1,0:T(8,128)(2,1)S(1)}, bf16[256,512]{1,0:T(8,128)(2,1)S(1)}, u32[]{:S(2)}, u32[]{:S(2)}) collective-permute-start(bf16[256,512]{1,0:T(8,128)(2,1)S(1)} %get-tuple-element.19), channel_id=1, source_target_pairs={{0,1},{1,2},{2,3},{3,4},{4,5},{5,6},{6,7},{7,8},{8,9},{16,17},{17,... | collective-permute-start | bytes 786440 | tf_op jit(solution)/shard_map/ppermute | solution.py:40
  176.1 9.5 %collective-permute-start.10 = (bf16[256,512]{1,0:T(8,128)(2,1)S(1)}, bf16[256,512]{1,0:T(8,128)(2,1)S(1)}, u32[]{:S(2)}, u32[]{:S(2)}) collective-permute-start(bf16[256,512]{1,0:T(8,128)(2,1)S(1)} %get-tuple-element.17), channel_id=1, source_target_pairs={{0,1},{1,2},{2,3},{3,4},{4,5},{5,6},{6,7},{7,8},{8,9},{9,10},{16,1... | collective-permute-start | bytes 786440 | tf_op jit(solution)/shard_map/ppermute | solution.py:40
  181.7 3.9 %collective-permute-start.25 = (bf16[256,512]{1,0:T(8,128)(2,1)S(1)}, bf16[256,512]{1,0:T(8,128)(2,1)S(1)}, u32[]{:S(2)}, u32[]{:S(2)}) collective-permute-start(bf16[256,512]{1,0:T(8,128)(2,1)S(1)} %get-tuple-element.18), channel_id=1, source_target_pairs={{6,5},{7,6},{8,7},{9,8},{10,9},{11,10},{12,11},{13,12},{14,13},{15... | collective-permute-start | bytes 786440 | tf_op jit(solution)/shard_map/ppermute | solution.py:41
  186.8 9.5 %collective-permute-start.11 = (bf16[256,512]{1,0:T(8,128)(2,1)S(1)}, bf16[256,512]{1,0:T(8,128)(2,1)S(1)}, u32[]{:S(2)}, u32[]{:S(2)}) collective-permute-start(bf16[256,512]{1,0:T(8,128)(2,1)S(1)} %get-tuple-element.15), channel_id=1, source_target_pairs={{0,1},{1,2},{2,3},{3,4},{4,5},{5,6},{6,7},{7,8},{8,9},{9,10},{10,1... | collective-permute-start | bytes 786440 | tf_op jit(solution)/shard_map/ppermute | solution.py:40
  192.4 3.9 %collective-permute-start.26 = (bf16[256,512]{1,0:T(8,128)(2,1)S(1)}, bf16[256,512]{1,0:T(8,128)(2,1)S(1)}, u32[]{:S(2)}, u32[]{:S(2)}) collective-permute-start(bf16[256,512]{1,0:T(8,128)(2,1)S(1)} %get-tuple-element.16), channel_id=1, source_target_pairs={{5,4},{6,5},{7,6},{8,7},{9,8},{10,9},{11,10},{12,11},{13,12},{14,1... | collective-permute-start | bytes 786440 | tf_op jit(solution)/shard_map/ppermute | solution.py:41
  197.4 11.0 %collective-permute-start.12 = (bf16[256,512]{1,0:T(8,128)(2,1)S(1)}, bf16[256,512]{1,0:T(8,128)(2,1)S(1)}, u32[]{:S(2)}, u32[]{:S(2)}) collective-permute-start(bf16[256,512]{1,0:T(8,128)(2,1)S(1)} %get-tuple-element.13), channel_id=1, source_target_pairs={{0,1},{1,2},{2,3},{3,4},{4,5},{5,6},{6,7},{7,8},{8,9},{9,10},{10,1... | collective-permute-start | bytes 786440 | tf_op jit(solution)/shard_map/ppermute | solution.py:40
  204.5 9.5 %collective-permute-start.27 = (bf16[256,512]{1,0:T(8,128)(2,1)S(1)}, bf16[256,512]{1,0:T(8,128)(2,1)S(1)}, u32[]{:S(2)}, u32[]{:S(2)}) collective-permute-start(bf16[256,512]{1,0:T(8,128)(2,1)S(1)} %get-tuple-element.14), channel_id=1, source_target_pairs={{4,3},{5,4},{6,5},{7,6},{8,7},{9,8},{10,9},{11,10},{12,11},{13,12}... | collective-permute-start | bytes 786440 | tf_op jit(solution)/shard_map/ppermute | solution.py:41
  215.1 8.3 %collective-permute-start.13 = (bf16[256,512]{1,0:T(8,128)(2,1)S(1)}, bf16[256,512]{1,0:T(8,128)(2,1)S(1)}, u32[]{:S(2)}, u32[]{:S(2)}) collective-permute-start(bf16[256,512]{1,0:T(8,128)(2,1)S(1)} %get-tuple-element.11), channel_id=1, source_target_pairs={{0,1},{1,2},{2,3},{3,4},{4,5},{5,6},{6,7},{7,8},{8,9},{9,10},{10,1... | collective-permute-start | bytes 786440 | tf_op jit(solution)/shard_map/ppermute | solution.py:40
  217.3 9.5 %collective-permute-start.28 = (bf16[256,512]{1,0:T(8,128)(2,1)S(1)}, bf16[256,512]{1,0:T(8,128)(2,1)S(1)}, u32[]{:S(2)}, u32[]{:S(2)}) collective-permute-start(bf16[256,512]{1,0:T(8,128)(2,1)S(1)} %get-tuple-element.12), channel_id=1, source_target_pairs={{3,2},{4,3},{5,4},{6,5},{7,6},{8,7},{9,8},{10,9},{11,10},{12,11},{... | collective-permute-start | bytes 786440 | tf_op jit(solution)/shard_map/ppermute | solution.py:41
  227.9 8.3 %collective-permute-start.14 = (bf16[256,512]{1,0:T(8,128)(2,1)S(1)}, bf16[256,512]{1,0:T(8,128)(2,1)S(1)}, u32[]{:S(2)}, u32[]{:S(2)}) collective-permute-start(bf16[256,512]{1,0:T(8,128)(2,1)S(1)} %get-tuple-element.9), channel_id=1, source_target_pairs={{0,1},{1,2},{2,3},{3,4},{4,5},{5,6},{6,7},{7,8},{8,9},{9,10},{10,1... | collective-permute-start | bytes 786440 | tf_op jit(solution)/shard_map/ppermute | solution.py:40
  230.8 17.6 %collective-permute-start.29 = (bf16[256,512]{1,0:T(8,128)(2,1)S(1)}, bf16[256,512]{1,0:T(8,128)(2,1)S(1)}, u32[]{:S(2)}, u32[]{:S(2)}) collective-permute-start(bf16[256,512]{1,0:T(8,128)(2,1)S(1)} %get-tuple-element.10), channel_id=1, source_target_pairs={{2,1},{3,2},{4,3},{5,4},{6,5},{7,6},{8,7},{9,8},{10,9},{11,10},{12... | collective-permute-start | bytes 786440 | tf_op jit(solution)/shard_map/ppermute | solution.py:41
  249.6 8.3 %collective-permute-start.15 = (bf16[256,512]{1,0:T(8,128)(2,1)S(1)}, bf16[256,512]{1,0:T(8,128)(2,1)S(1)}, u32[]{:S(2)}, u32[]{:S(2)}) collective-permute-start(bf16[256,512]{1,0:T(8,128)(2,1)S(1)} %get-tuple-element.7), channel_id=1, source_target_pairs={{0,1},{1,2},{2,3},{3,4},{4,5},{5,6},{6,7},{7,8},{8,9},{9,10},{10,1... | collective-permute-start | bytes 786440 | tf_op jit(solution)/shard_map/ppermute | solution.py:40
  253.5 9.5 %collective-permute-start.30 = (bf16[256,512]{1,0:T(8,128)(2,1)S(1)}, bf16[256,512]{1,0:T(8,128)(2,1)S(1)}, u32[]{:S(2)}, u32[]{:S(2)}) collective-permute-start(bf16[256,512]{1,0:T(8,128)(2,1)S(1)} %get-tuple-element.8), channel_id=1, source_target_pairs={{1,0},{2,1},{3,2},{4,3},{5,4},{6,5},{7,6},{8,7},{9,8},{10,9},{11,1... | collective-permute-start | bytes 786440 | tf_op jit(solution)/shard_map/ppermute | solution.py:41
  (8 other events, 12.8 us)

commit v2 on v0

--- a/solution.py
+++ b/solution.py
@@ -23,6 +23,36 @@
     return running
 
 
+def line_reduce_scatter(product, out_weight, axis, chains=2):
+    n = lax.axis_size(axis)
+    me = lax.axis_index(axis)
+    width = out_weight.shape[1] // n
+    piece = width // chains
+
+    def block(j, chain):
+        j = jnp.clip(j, 0, n - 1)
+        columns = lax.dynamic_slice_in_dim(out_weight, j * width + chain * piece, piece, 1)
+        term = jnp.dot(product, columns, preferred_element_type=jnp.float32)
+        return term.astype(jnp.bfloat16).astype(jnp.float32)
+
+    zeros = jnp.zeros((product.shape[0], piece), jnp.bfloat16)
+    from_left = [zeros] * chains
+    from_right = [zeros] * chains
+    for step in range(n - 1):
+        rightward = [(k, k + 1) for k in range(n - 1) if k <= step]
+        leftward = [(k, k - 1) for k in range(1, n) if k >= n - 1 - step]
+        for chain in range(chains):
+            send_right = (from_left[chain].astype(jnp.float32) + block(n - 1 + me - step, chain)).astype(jnp.bfloat16)
+            send_left = (from_right[chain].astype(jnp.float32) + block(step - (n - 1) + me, chain)).astype(jnp.bfloat16)
+            from_left[chain] = lax.ppermute(send_right, axis, rightward)
+            from_right[chain] = lax.ppermute(send_left, axis, leftward)
+    pieces = [
+        from_left[chain].astype(jnp.float32) + block(me, chain) + from_right[chain].astype(jnp.float32)
+        for chain in range(chains)
+    ]
+    return jnp.concatenate(pieces, 1).astype(jnp.bfloat16)
+
+
 def shards(query_stream, key_stream, value_stream, feat_taps, filt_taps, skip_bias, out_weight):
     filt_reach = filt_taps.shape[0] - 1
     feat_reach = feat_taps.shape[1] - 1
@@ -41,9 +71,7 @@
     own_gated = gated[filt_reach:].astype(jnp.float32)
     mixed = valid_conv(gated.astype(jnp.float32), filt_taps) + skip_bias[None, :] * own_gated
     product = (query_feat * mixed).astype(jnp.bfloat16)
-    terms = jnp.dot(product, out_weight, preferred_element_type=jnp.float32)
-    block_out = lax.psum_scatter(terms.astype(jnp.bfloat16), "tp", scatter_dimension=1, tiled=True)
-    return block_out
+    return line_reduce_scatter(product, out_weight, "tp")
 
 
 def solution(mesh):

time: 308 us -> 907 us (2.94)
  the two profiles are of different devices: /device:TPU:10 before, /device:TPU:96 now
where the time goes in v2:
time: 907 us; the launch traced here: 906 us
  starting transfers between devices  837 us (92%)
  waiting for transfers between devices  21.1 us (2%)
  other arithmetic  17.8 us (2%)
  matrix products  15.2 us (2%)
  local copies, waits for them, and re-layouts  13 us (1%)
    ppermute x30, starting transfers between devices, line_reduce_scatter(): from_left[chain] = lax.ppermute(send_right, axis, rightward)  426 us
    ppermute x30, starting transfers between devices, line_reduce_scatter(): from_right[chain] = lax.ppermute(send_left, axis, leftward)  378 us
    ppermute x1, starting transfers between devices, shifted(): return lax.ppermute(block, axis, route)  33.3 us
  transfers between devices with their start and end apart: 61, of which 3 were waited for; matrix products, arithmetic and copies ran while one was open for 3% of the time, Pallas kernels for 0%

profile of v2, /device:TPU:96, one launch (start us, length us, event | category | flops | bytes accessed | tf_op | source)
XLA Modules:
  0.0 905.5 jit_solution(17307161898087294819)
XLA Ops:
  2.6 33.3 %collective-permute-start = (bf16[272,512]{1,0:T(8,128)(2,1)S(1)}, bf16[272,512]{1,0:T(8,128)(2,1)S(1)}, u32[]{:S(2)}, u32[]{:S(2)}) collective-permute-start(bf16[272,512]{1,0:T(8,128)(2,1)S(1)} %pad_maximum_fusion), channel_id=1, source_target_pairs={{0,16},{16,32},{32,48},{48,64},{64,80},{80,96},{96,112},{112,128},... | collective-permute-start | bytes 835592 | tf_op jit(solution)/shard_map/ppermute | solution.py:10
  140.3 50.7 %collective-permute-start.10 = (bf16[256,256]{1,0:T(8,128)(2,1)S(1)}, bf16[256,256]{1,0:T(8,128)(2,1)S(1)}, u32[]{:S(2)}, u32[]{:S(2)}) collective-permute-start(bf16[256,256]{1,0:T(8,128)(2,1)S(1)} %add_convert_fusion.49), channel_id=1, source_target_pairs={{0,1},{1,2},{2,3},{3,4},{4,5},{5,6},{6,7},{7,8},{8,9},{9,10},{16,1... | collective-permute-start | bytes 393224 | tf_op jit(solution)/shard_map/ppermute | solution.py:47
  191.2 30.1 %collective-permute-start.25 = (bf16[256,256]{1,0:T(8,128)(2,1)S(1)}, bf16[256,256]{1,0:T(8,128)(2,1)S(1)}, u32[]{:S(2)}, u32[]{:S(2)}) collective-permute-start(bf16[256,256]{1,0:T(8,128)(2,1)S(1)} %add_convert_fusion.35), channel_id=1, source_target_pairs={{6,5},{7,6},{8,7},{9,8},{10,9},{11,10},{12,11},{13,12},{14,13},{15... | collective-permute-start | bytes 393224 | tf_op jit(solution)/shard_map/ppermute | solution.py:48
  221.6 30.8 %collective-permute-start.40 = (bf16[256,256]{1,0:T(8,128)(2,1)S(1)}, bf16[256,256]{1,0:T(8,128)(2,1)S(1)}, u32[]{:S(2)}, u32[]{:S(2)}) collective-permute-start(bf16[256,256]{1,0:T(8,128)(2,1)S(1)} %add_convert_fusion.20), channel_id=1, source_target_pairs={{0,1},{1,2},{2,3},{3,4},{4,5},{5,6},{6,7},{7,8},{8,9},{9,10},{16,1... | collective-permute-start | bytes 393224 | tf_op jit(solution)/shard_map/ppermute | solution.py:47
  252.7 30.1 %collective-permute-start.55 = (bf16[256,256]{1,0:T(8,128)(2,1)S(1)}, bf16[256,256]{1,0:T(8,128)(2,1)S(1)}, u32[]{:S(2)}, u32[]{:S(2)}) collective-permute-start(bf16[256,256]{1,0:T(8,128)(2,1)S(1)} %add_convert_fusion.6), channel_id=1, source_target_pairs={{6,5},{7,6},{8,7},{9,8},{10,9},{11,10},{12,11},{13,12},{14,13},{15... | collective-permute-start | bytes 393224 | tf_op jit(solution)/shard_map/ppermute | solution.py:48
  283.1 30.8 %collective-permute-start.11 = (bf16[256,256]{1,0:T(8,128)(2,1)S(1)}, bf16[256,256]{1,0:T(8,128)(2,1)S(1)}, u32[]{:S(2)}, u32[]{:S(2)}) collective-permute-start(bf16[256,256]{1,0:T(8,128)(2,1)S(1)} %add_convert_fusion.48), channel_id=1, source_target_pairs={{0,1},{1,2},{2,3},{3,4},{4,5},{5,6},{6,7},{7,8},{8,9},{9,10},{10,1... | collective-permute-start | bytes 393224 | tf_op jit(solution)/shard_map/ppermute | solution.py:47
  314.1 30.1 %collective-permute-start.26 = (bf16[256,256]{1,0:T(8,128)(2,1)S(1)}, bf16[256,256]{1,0:T(8,128)(2,1)S(1)}, u32[]{:S(2)}, u32[]{:S(2)}) collective-permute-start(bf16[256,256]{1,0:T(8,128)(2,1)S(1)} %add_convert_fusion.34), channel_id=1, source_target_pairs={{5,4},{6,5},{7,6},{8,7},{9,8},{10,9},{11,10},{12,11},{13,12},{14,1... | collective-permute-start | bytes 393224 | tf_op jit(solution)/shard_map/ppermute | solution.py:48
  344.5 30.8 %collective-permute-start.41 = (bf16[256,256]{1,0:T(8,128)(2,1)S(1)}, bf16[256,256]{1,0:T(8,128)(2,1)S(1)}, u32[]{:S(2)}, u32[]{:S(2)}) collective-permute-start(bf16[256,256]{1,0:T(8,128)(2,1)S(1)} %add_convert_fusion.19), channel_id=1, source_target_pairs={{0,1},{1,2},{2,3},{3,4},{4,5},{5,6},{6,7},{7,8},{8,9},{9,10},{10,1... | collective-permute-start | bytes 393224 | tf_op jit(solution)/shard_map/ppermute | solution.py:47
  375.6 30.1 %collective-permute-start.56 = (bf16[256,256]{1,0:T(8,128)(2,1)S(1)}, bf16[256,256]{1,0:T(8,128)(2,1)S(1)}, u32[]{:S(2)}, u32[]{:S(2)}) collective-permute-start(bf16[256,256]{1,0:T(8,128)(2,1)S(1)} %add_convert_fusion.5), channel_id=1, source_target_pairs={{5,4},{6,5},{7,6},{8,7},{9,8},{10,9},{11,10},{12,11},{13,12},{14,1... | collective-permute-start | bytes 393224 | tf_op jit(solution)/shard_map/ppermute | solution.py:48
  406.0 30.8 %collective-permute-start.12 = (bf16[256,256]{1,0:T(8,128)(2,1)S(1)}, bf16[256,256]{1,0:T(8,128)(2,1)S(1)}, u32[]{:S(2)}, u32[]{:S(2)}) collective-permute-start(bf16[256,256]{1,0:T(8,128)(2,1)S(1)} %add_convert_fusion.47), channel_id=1, source_target_pairs={{0,1},{1,2},{2,3},{3,4},{4,5},{5,6},{6,7},{7,8},{8,9},{9,10},{10,1... | collective-permute-start | bytes 393224 | tf_op jit(solution)/shard_map/ppermute | solution.py:47
  437.0 30.1 %collective-permute-start.27 = (bf16[256,256]{1,0:T(8,128)(2,1)S(1)}, bf16[256,256]{1,0:T(8,128)(2,1)S(1)}, u32[]{:S(2)}, u32[]{:S(2)}) collective-permute-start(bf16[256,256]{1,0:T(8,128)(2,1)S(1)} %add_convert_fusion.33), channel_id=1, source_target_pairs={{4,3},{5,4},{6,5},{7,6},{8,7},{9,8},{10,9},{11,10},{12,11},{13,12}... | collective-permute-start | bytes 393224 | tf_op jit(solution)/shard_map/ppermute | solution.py:48
  467.4 30.8 %collective-permute-start.42 = (bf16[256,256]{1,0:T(8,128)(2,1)S(1)}, bf16[256,256]{1,0:T(8,128)(2,1)S(1)}, u32[]{:S(2)}, u32[]{:S(2)}) collective-permute-start(bf16[256,256]{1,0:T(8,128)(2,1)S(1)} %add_convert_fusion.18), channel_id=1, source_target_pairs={{0,1},{1,2},{2,3},{3,4},{4,5},{5,6},{6,7},{7,8},{8,9},{9,10},{10,1... | collective-permute-start | bytes 393224 | tf_op jit(solution)/shard_map/ppermute | solution.py:47
  498.5 30.1 %collective-permute-start.57 = (bf16[256,256]{1,0:T(8,128)(2,1)S(1)}, bf16[256,256]{1,0:T(8,128)(2,1)S(1)}, u32[]{:S(2)}, u32[]{:S(2)}) collective-permute-start(bf16[256,256]{1,0:T(8,128)(2,1)S(1)} %add_convert_fusion.4), channel_id=1, source_target_pairs={{4,3},{5,4},{6,5},{7,6},{8,7},{9,8},{10,9},{11,10},{12,11},{13,12}... | collective-permute-start | bytes 393224 | tf_op jit(solution)/shard_map/ppermute | solution.py:48
  528.9 30.8 %collective-permute-start.13 = (bf16[256,256]{1,0:T(8,128)(2,1)S(1)}, bf16[256,256]{1,0:T(8,128)(2,1)S(1)}, u32[]{:S(2)}, u32[]{:S(2)}) collective-permute-start(bf16[256,256]{1,0:T(8,128)(2,1)S(1)} %add_convert_fusion.46), channel_id=1, source_target_pairs={{0,1},{1,2},{2,3},{3,4},{4,5},{5,6},{6,7},{7,8},{8,9},{9,10},{10,1... | collective-permute-start | bytes 393224 | tf_op jit(solution)/shard_map/ppermute | solution.py:47
  559.9 30.8 %collective-permute-start.28 = (bf16[256,256]{1,0:T(8,128)(2,1)S(1)}, bf16[256,256]{1,0:T(8,128)(2,1)S(1)}, u32[]{:S(2)}, u32[]{:S(2)}) collective-permute-start(bf16[256,256]{1,0:T(8,128)(2,1)S(1)} %add_convert_fusion.32), channel_id=1, source_target_pairs={{3,2},{4,3},{5,4},{6,5},{7,6},{8,7},{9,8},{10,9},{11,10},{12,11},{... | collective-permute-start | bytes 393224 | tf_op jit(solution)/shard_map/ppermute | solution.py:48
  591.0 30.1 %collective-permute-start.43 = (bf16[256,256]{1,0:T(8,128)(2,1)S(1)}, bf16[256,256]{1,0:T(8,128)(2,1)S(1)}, u32[]{:S(2)}, u32[]{:S(2)}) collective-permute-start(bf16[256,256]{1,0:T(8,128)(2,1)S(1)} %add_convert_fusion.17), channel_id=1, source_target_pairs={{0,1},{1,2},{2,3},{3,4},{4,5},{5,6},{6,7},{7,8},{8,9},{9,10},{10,1... | collective-permute-start | bytes 393224 | tf_op jit(solution)/shard_map/ppermute | solution.py:47
  621.4 30.8 %collective-permute-start.58 = (bf16[256,256]{1,0:T(8,128)(2,1)S(1)}, bf16[256,256]{1,0:T(8,128)(2,1)S(1)}, u32[]{:S(2)}, u32[]{:S(2)}) collective-permute-start(bf16[256,256]{1,0:T(8,128)(2,1)S(1)} %add_convert_fusion.3), channel_id=1, source_target_pairs={{3,2},{4,3},{5,4},{6,5},{7,6},{8,7},{9,8},{10,9},{11,10},{12,11},{... | collective-permute-start | bytes 393224 | tf_op jit(solution)/shard_map/ppermute | solution.py:48
  652.4 30.1 %collective-permute-start.14 = (bf16[256,256]{1,0:T(8,128)(2,1)S(1)}, bf16[256,256]{1,0:T(8,128)(2,1)S(1)}, u32[]{:S(2)}, u32[]{:S(2)}) collective-permute-start(bf16[256,256]{1,0:T(8,128)(2,1)S(1)} %add_convert_fusion.45), channel_id=1, source_target_pairs={{0,1},{1,2},{2,3},{3,4},{4,5},{5,6},{6,7},{7,8},{8,9},{9,10},{10,1... | collective-permute-start | bytes 393224 | tf_op jit(solution)/shard_map/ppermute | solution.py:47
  682.9 30.8 %collective-permute-start.29 = (bf16[256,256]{1,0:T(8,128)(2,1)S(1)}, bf16[256,256]{1,0:T(8,128)(2,1)S(1)}, u32[]{:S(2)}, u32[]{:S(2)}) collective-permute-start(bf16[256,256]{1,0:T(8,128)(2,1)S(1)} %add_convert_fusion.31), channel_id=1, source_target_pairs={{2,1},{3,2},{4,3},{5,4},{6,5},{7,6},{8,7},{9,8},{10,9},{11,10},{12... | collective-permute-start | bytes 393224 | tf_op jit(solution)/shard_map/ppermute | solution.py:48
  713.9 30.1 %collective-permute-start.44 = (bf16[256,256]{1,0:T(8,128)(2,1)S(1)}, bf16[256,256]{1,0:T(8,128)(2,1)S(1)}, u32[]{:S(2)}, u32[]{:S(2)}) collective-permute-start(bf16[256,256]{1,0:T(8,128)(2,1)S(1)} %add_convert_fusion.16), channel_id=1, source_target_pairs={{0,1},{1,2},{2,3},{3,4},{4,5},{5,6},{6,7},{7,8},{8,9},{9,10},{10,1... | collective-permute-start | bytes 393224 | tf_op jit(solution)/shard_map/ppermute | solution.py:47
  744.3 30.8 %collective-permute-start.59 = (bf16[256,256]{1,0:T(8,128)(2,1)S(1)}, bf16[256,256]{1,0:T(8,128)(2,1)S(1)}, u32[]{:S(2)}, u32[]{:S(2)}) collective-permute-start(bf16[256,256]{1,0:T(8,128)(2,1)S(1)} %add_convert_fusion.2), channel_id=1, source_target_pairs={{2,1},{3,2},{4,3},{5,4},{6,5},{7,6},{8,7},{9,8},{10,9},{11,10},{12... | collective-permute-start | bytes 393224 | tf_op jit(solution)/shard_map/ppermute | solution.py:48
  805.8 30.8 %collective-permute-start.30 = (bf16[256,256]{1,0:T(8,128)(2,1)S(1)}, bf16[256,256]{1,0:T(8,128)(2,1)S(1)}, u32[]{:S(2)}, u32[]{:S(2)}) collective-permute-start(bf16[256,256]{1,0:T(8,128)(2,1)S(1)} %add_convert_fusion.30), channel_id=1, source_target_pairs={{1,0},{2,1},{3,2},{4,3},{5,4},{6,5},{7,6},{8,7},{9,8},{10,9},{11,1... | collective-permute-start | bytes 393224 | tf_op jit(solution)/shard_map/ppermute | solution.py:48
  836.8 30.1 %collective-permute-start.45 = (bf16[256,256]{1,0:T(8,128)(2,1)S(1)}, bf16[256,256]{1,0:T(8,128)(2,1)S(1)}, u32[]{:S(2)}, u32[]{:S(2)}) collective-permute-start(bf16[256,256]{1,0:T(8,128)(2,1)S(1)} %add_convert_fusion.15), channel_id=1, source_target_pairs={{0,1},{1,2},{2,3},{3,4},{4,5},{5,6},{6,7},{7,8},{8,9},{9,10},{10,1... | collective-permute-start | bytes 393224 | tf_op jit(solution)/shard_map/ppermute | solution.py:47
  867.2 30.8 %collective-permute-start.60 = (bf16[256,256]{1,0:T(8,128)(2,1)S(1)}, bf16[256,256]{1,0:T(8,128)(2,1)S(1)}, u32[]{:S(2)}, u32[]{:S(2)}) collective-permute-start(bf16[256,256]{1,0:T(8,128)(2,1)S(1)} %add_convert_fusion.1), channel_id=1, source_target_pairs={{1,0},{2,1},{3,2},{4,3},{5,4},{6,5},{7,6},{8,7},{9,8},{10,9},{11,1... | collective-permute-start | bytes 393224 | tf_op jit(solution)/shard_map/ppermute | solution.py:48
  (189 shorter events, 149.3 us)
Async XLA Ops:
  137.1 84.3 %collective-permute-start.39 = (bf16[256,256]{1,0:T(8,128)(2,1)S(1)}, bf16[256,256]{1,0:T(8,128)(2,1)S(1)}, u32[]{:S(2)}, u32[]{:S(2)}) collective-permute-start(bf16[256,256]{1,0:T(8,128)(2,1)S(1)} %add_convert_fusion.21), channel_id=1, source_target_pairs={{0,1},{1,2},{2,3},{3,4},{4,5},{5,6},{6,7},{7,8},{8,9},{16,17},{17,... | collective-permute-start | bytes 393224 | tf_op jit(solution)/shard_map/ppermute | solution.py:47
  139.3 113.1 %collective-permute-start.54 = (bf16[256,256]{1,0:T(8,128)(2,1)S(1)}, bf16[256,256]{1,0:T(8,128)(2,1)S(1)}, u32[]{:S(2)}, u32[]{:S(2)}) collective-permute-start(bf16[256,256]{1,0:T(8,128)(2,1)S(1)} %add_convert_fusion.7), channel_id=1, source_target_pairs={{7,6},{8,7},{9,8},{10,9},{11,10},{12,11},{13,12},{14,13},{15,14},{... | collective-permute-start | bytes 393224 | tf_op jit(solution)/shard_map/ppermute | solution.py:48
  140.3 142.5 %collective-permute-start.10 = (bf16[256,256]{1,0:T(8,128)(2,1)S(1)}, bf16[256,256]{1,0:T(8,128)(2,1)S(1)}, u32[]{:S(2)}, u32[]{:S(2)}) collective-permute-start(bf16[256,256]{1,0:T(8,128)(2,1)S(1)} %add_convert_fusion.49), channel_id=1, source_target_pairs={{0,1},{1,2},{2,3},{3,4},{4,5},{5,6},{6,7},{7,8},{8,9},{9,10},{16,1... | collective-permute-start | bytes 393224 | tf_op jit(solution)/shard_map/ppermute | solution.py:47
  191.2 122.7 %collective-permute-start.25 = (bf16[256,256]{1,0:T(8,128)(2,1)S(1)}, bf16[256,256]{1,0:T(8,128)(2,1)S(1)}, u32[]{:S(2)}, u32[]{:S(2)}) collective-permute-start(bf16[256,256]{1,0:T(8,128)(2,1)S(1)} %add_convert_fusion.35), channel_id=1, source_target_pairs={{6,5},{7,6},{8,7},{9,8},{10,9},{11,10},{12,11},{13,12},{14,13},{15... | collective-permute-start | bytes 393224 | tf_op jit(solution)/shard_map/ppermute | solution.py:48
  221.6 122.7 %collective-permute-start.40 = (bf16[256,256]{1,0:T(8,128)(2,1)S(1)}, bf16[256,256]{1,0:T(8,128)(2,1)S(1)}, u32[]{:S(2)}, u32[]{:S(2)}) collective-permute-start(bf16[256,256]{1,0:T(8,128)(2,1)S(1)} %add_convert_fusion.20), channel_id=1, source_target_pairs={{0,1},{1,2},{2,3},{3,4},{4,5},{5,6},{6,7},{7,8},{8,9},{9,10},{16,1... | collective-permute-start | bytes 393224 | tf_op jit(solution)/shard_map/ppermute | solution.py:47
  252.7 122.7 %collective-permute-start.55 = (bf16[256,256]{1,0:T(8,128)(2,1)S(1)}, bf16[256,256]{1,0:T(8,128)(2,1)S(1)}, u32[]{:S(2)}, u32[]{:S(2)}) collective-permute-start(bf16[256,256]{1,0:T(8,128)(2,1)S(1)} %add_convert_fusion.6), channel_id=1, source_target_pairs={{6,5},{7,6},{8,7},{9,8},{10,9},{11,10},{12,11},{13,12},{14,13},{15... | collective-permute-start | bytes 393224 | tf_op jit(solution)/shard_map/ppermute | solution.py:48
  283.1 122.7 %collective-permute-start.11 = (bf16[256,256]{1,0:T(8,128)(2,1)S(1)}, bf16[256,256]{1,0:T(8,128)(2,1)S(1)}, u32[]{:S(2)}, u32[]{:S(2)}) collective-permute-start(bf16[256,256]{1,0:T(8,128)(2,1)S(1)} %add_convert_fusion.48), channel_id=1, source_target_pairs={{0,1},{1,2},{2,3},{3,4},{4,5},{5,6},{6,7},{7,8},{8,9},{9,10},{10,1... | collective-permute-start | bytes 393224 | tf_op jit(solution)/shard_map/ppermute | solution.py:47
  314.1 122.7 %collective-permute-start.26 = (bf16[256,256]{1,0:T(8,128)(2,1)S(1)}, bf16[256,256]{1,0:T(8,128)(2,1)S(1)}, u32[]{:S(2)}, u32[]{:S(2)}) collective-permute-start(bf16[256,256]{1,0:T(8,128)(2,1)S(1)} %add_convert_fusion.34), channel_id=1, source_target_pairs={{5,4},{6,5},{7,6},{8,7},{9,8},{10,9},{11,10},{12,11},{13,12},{14,1... | collective-permute-start | bytes 393224 | tf_op jit(solution)/shard_map/ppermute | solution.py:48
  344.5 122.6 %collective-permute-start.41 = (bf16[256,256]{1,0:T(8,128)(2,1)S(1)}, bf16[256,256]{1,0:T(8,128)(2,1)S(1)}, u32[]{:S(2)}, u32[]{:S(2)}) collective-permute-start(bf16[256,256]{1,0:T(8,128)(2,1)S(1)} %add_convert_fusion.19), channel_id=1, source_target_pairs={{0,1},{1,2},{2,3},{3,4},{4,5},{5,6},{6,7},{7,8},{8,9},{9,10},{10,1... | collective-permute-start | bytes 393224 | tf_op jit(solution)/shard_map/ppermute | solution.py:47
  375.6 122.7 %collective-permute-start.56 = (bf16[256,256]{1,0:T(8,128)(2,1)S(1)}, bf16[256,256]{1,0:T(8,128)(2,1)S(1)}, u32[]{:S(2)}, u32[]{:S(2)}) collective-permute-start(bf16[256,256]{1,0:T(8,128)(2,1)S(1)} %add_convert_fusion.5), channel_id=1, source_target_pairs={{5,4},{6,5},{7,6},{8,7},{9,8},{10,9},{11,10},{12,11},{13,12},{14,1... | collective-permute-start | bytes 393224 | tf_op jit(solution)/shard_map/ppermute | solution.py:48
  406.0 122.6 %collective-permute-start.12 = (bf16[256,256]{1,0:T(8,128)(2,1)S(1)}, bf16[256,256]{1,0:T(8,128)(2,1)S(1)}, u32[]{:S(2)}, u32[]{:S(2)}) collective-permute-start(bf16[256,256]{1,0:T(8,128)(2,1)S(1)} %add_convert_fusion.47), channel_id=1, source_target_pairs={{0,1},{1,2},{2,3},{3,4},{4,5},{5,6},{6,7},{7,8},{8,9},{9,10},{10,1... | collective-permute-start | bytes 393224 | tf_op jit(solution)/shard_map/ppermute | solution.py:47
  437.0 122.7 %collective-permute-start.27 = (bf16[256,256]{1,0:T(8,128)(2,1)S(1)}, bf16[256,256]{1,0:T(8,128)(2,1)S(1)}, u32[]{:S(2)}, u32[]{:S(2)}) collective-permute-start(bf16[256,256]{1,0:T(8,128)(2,1)S(1)} %add_convert_fusion.33), channel_id=1, source_target_pairs={{4,3},{5,4},{6,5},{7,6},{8,7},{9,8},{10,9},{11,10},{12,11},{13,12}... | collective-permute-start | bytes 393224 | tf_op jit(solution)/shard_map/ppermute | solution.py:48
  467.4 123.3 %collective-permute-start.42 = (bf16[256,256]{1,0:T(8,128)(2,1)S(1)}, bf16[256,256]{1,0:T(8,128)(2,1)S(1)}, u32[]{:S(2)}, u32[]{:S(2)}) collective-permute-start(bf16[256,256]{1,0:T(8,128)(2,1)S(1)} %add_convert_fusion.18), channel_id=1, source_target_pairs={{0,1},{1,2},{2,3},{3,4},{4,5},{5,6},{6,7},{7,8},{8,9},{9,10},{10,1... | collective-permute-start | bytes 393224 | tf_op jit(solution)/shard_map/ppermute | solution.py:47
  498.5 122.7 %collective-permute-start.57 = (bf16[256,256]{1,0:T(8,128)(2,1)S(1)}, bf16[256,256]{1,0:T(8,128)(2,1)S(1)}, u32[]{:S(2)}, u32[]{:S(2)}) collective-permute-start(bf16[256,256]{1,0:T(8,128)(2,1)S(1)} %add_convert_fusion.4), channel_id=1, source_target_pairs={{4,3},{5,4},{6,5},{7,6},{8,7},{9,8},{10,9},{11,10},{12,11},{13,12}... | collective-permute-start | bytes 393224 | tf_op jit(solution)/shard_map/ppermute | solution.py:48
  528.9 123.3 %collective-permute-start.13 = (bf16[256,256]{1,0:T(8,128)(2,1)S(1)}, bf16[256,256]{1,0:T(8,128)(2,1)S(1)}, u32[]{:S(2)}, u32[]{:S(2)}) collective-permute-start(bf16[256,256]{1,0:T(8,128)(2,1)S(1)} %add_convert_fusion.46), channel_id=1, source_target_pairs={{0,1},{1,2},{2,3},{3,4},{4,5},{5,6},{6,7},{7,8},{8,9},{9,10},{10,1... | collective-permute-start | bytes 393224 | tf_op jit(solution)/shard_map/ppermute | solution.py:47
  559.9 122.7 %collective-permute-start.28 = (bf16[256,256]{1,0:T(8,128)(2,1)S(1)}, bf16[256,256]{1,0:T(8,128)(2,1)S(1)}, u32[]{:S(2)}, u32[]{:S(2)}) collective-permute-start(bf16[256,256]{1,0:T(8,128)(2,1)S(1)} %add_convert_fusion.32), channel_id=1, source_target_pairs={{3,2},{4,3},{5,4},{6,5},{7,6},{8,7},{9,8},{10,9},{11,10},{12,11},{... | collective-permute-start | bytes 393224 | tf_op jit(solution)/shard_map/ppermute | solution.py:48
  591.0 122.7 %collective-permute-start.43 = (bf16[256,256]{1,0:T(8,128)(2,1)S(1)}, bf16[256,256]{1,0:T(8,128)(2,1)S(1)}, u32[]{:S(2)}, u32[]{:S(2)}) collective-permute-start(bf16[256,256]{1,0:T(8,128)(2,1)S(1)} %add_convert_fusion.17), channel_id=1, source_target_pairs={{0,1},{1,2},{2,3},{3,4},{4,5},{5,6},{6,7},{7,8},{8,9},{9,10},{10,1... | collective-permute-start | bytes 393224 | tf_op jit(solution)/shard_map/ppermute | solution.py:47
  621.4 122.7 %collective-permute-start.58 = (bf16[256,256]{1,0:T(8,128)(2,1)S(1)}, bf16[256,256]{1,0:T(8,128)(2,1)S(1)}, u32[]{:S(2)}, u32[]{:S(2)}) collective-permute-start(bf16[256,256]{1,0:T(8,128)(2,1)S(1)} %add_convert_fusion.3), channel_id=1, source_target_pairs={{3,2},{4,3},{5,4},{6,5},{7,6},{8,7},{9,8},{10,9},{11,10},{12,11},{... | collective-permute-start | bytes 393224 | tf_op jit(solution)/shard_map/ppermute | solution.py:48
  652.4 122.7 %collective-permute-start.14 = (bf16[256,256]{1,0:T(8,128)(2,1)S(1)}, bf16[256,256]{1,0:T(8,128)(2,1)S(1)}, u32[]{:S(2)}, u32[]{:S(2)}) collective-permute-start(bf16[256,256]{1,0:T(8,128)(2,1)S(1)} %add_convert_fusion.45), channel_id=1, source_target_pairs={{0,1},{1,2},{2,3},{3,4},{4,5},{5,6},{6,7},{7,8},{8,9},{9,10},{10,1... | collective-permute-start | bytes 393224 | tf_op jit(solution)/shard_map/ppermute | solution.py:47
  682.9 122.7 %collective-permute-start.29 = (bf16[256,256]{1,0:T(8,128)(2,1)S(1)}, bf16[256,256]{1,0:T(8,128)(2,1)S(1)}, u32[]{:S(2)}, u32[]{:S(2)}) collective-permute-start(bf16[256,256]{1,0:T(8,128)(2,1)S(1)} %add_convert_fusion.31), channel_id=1, source_target_pairs={{2,1},{3,2},{4,3},{5,4},{6,5},{7,6},{8,7},{9,8},{10,9},{11,10},{12... | collective-permute-start | bytes 393224 | tf_op jit(solution)/shard_map/ppermute | solution.py:48
  713.9 122.7 %collective-permute-start.44 = (bf16[256,256]{1,0:T(8,128)(2,1)S(1)}, bf16[256,256]{1,0:T(8,128)(2,1)S(1)}, u32[]{:S(2)}, u32[]{:S(2)}) collective-permute-start(bf16[256,256]{1,0:T(8,128)(2,1)S(1)} %add_convert_fusion.16), channel_id=1, source_target_pairs={{0,1},{1,2},{2,3},{3,4},{4,5},{5,6},{6,7},{7,8},{8,9},{9,10},{10,1... | collective-permute-start | bytes 393224 | tf_op jit(solution)/shard_map/ppermute | solution.py:47
  744.3 122.7 %collective-permute-start.59 = (bf16[256,256]{1,0:T(8,128)(2,1)S(1)}, bf16[256,256]{1,0:T(8,128)(2,1)S(1)}, u32[]{:S(2)}, u32[]{:S(2)}) collective-permute-start(bf16[256,256]{1,0:T(8,128)(2,1)S(1)} %add_convert_fusion.2), channel_id=1, source_target_pairs={{2,1},{3,2},{4,3},{5,4},{6,5},{7,6},{8,7},{9,8},{10,9},{11,10},{12... | collective-permute-start | bytes 393224 | tf_op jit(solution)/shard_map/ppermute | solution.py:48
  775.4 122.7 %collective-permute-start.15 = (bf16[256,256]{1,0:T(8,128)(2,1)S(1)}, bf16[256,256]{1,0:T(8,128)(2,1)S(1)}, u32[]{:S(2)}, u32[]{:S(2)}) collective-permute-start(bf16[256,256]{1,0:T(8,128)(2,1)S(1)} %add_convert_fusion.44), channel_id=1, source_target_pairs={{0,1},{1,2},{2,3},{3,4},{4,5},{5,6},{6,7},{7,8},{8,9},{9,10},{10,1... | collective-permute-start | bytes 393224 | tf_op jit(solution)/shard_map/ppermute | solution.py:47
  805.8 92.3 %collective-permute-start.30 = (bf16[256,256]{1,0:T(8,128)(2,1)S(1)}, bf16[256,256]{1,0:T(8,128)(2,1)S(1)}, u32[]{:S(2)}, u32[]{:S(2)}) collective-permute-start(bf16[256,256]{1,0:T(8,128)(2,1)S(1)} %add_convert_fusion.30), channel_id=1, source_target_pairs={{1,0},{2,1},{3,2},{4,3},{5,4},{6,5},{7,6},{8,7},{9,8},{10,9},{11,1... | collective-permute-start | bytes 393224 | tf_op jit(solution)/shard_map/ppermute | solution.py:48
  (40 other events, 513.8 us)

commit v3 on v2

--- a/solution.py
+++ b/solution.py
@@ -23,7 +23,7 @@
     return running
 
 
-def line_reduce_scatter(product, out_weight, axis, chains=2):
+def line_reduce_scatter(product, out_weight, axis, chains=1):
     n = lax.axis_size(axis)
     me = lax.axis_index(axis)
     width = out_weight.shape[1] // n

time: 907 us -> 246 us (0.27)
  the two profiles are of different devices: /device:TPU:96 before, /device:TPU:126 now
where the time goes in v3:
time: 246 us; the launch traced here: 243 us
  waiting for transfers between devices  91.5 us (37%)
  starting transfers between devices  78.1 us (32%)
  matrix products  41.6 us (17%)
  other arithmetic  17.7 us (7%)
  local copies, waits for them, and re-layouts  13 us (5%)
    ppermute x15, starting transfers between devices, line_reduce_scatter(): from_left[chain] = lax.ppermute(send_right, axis, rightward)  61.7 us
    ppermute x15, waiting for transfers between devices, line_reduce_scatter(): from_left[chain] = lax.ppermute(send_right, axis, rightward)  48.6 us
    dot_general x31, matrix products, block(): term = jnp.dot(product, columns, preferred_element_type=jnp.float32)  41.6 us
    ppermute x1, waiting for transfers between devices, shifted(): return lax.ppermute(block, axis, route)  36.7 us
    ppermute x15, starting transfers between devices, line_reduce_scatter(): from_right[chain] = lax.ppermute(send_left, axis, leftward)  14.5 us
    convert_element_type x1, other arithmetic, shards(): product = (query_feat * mixed).astype(jnp.bfloat16)  13.3 us
    slice x7, local copies, waits for them, and re-layouts, valid_conv(): taps[offset][None, :]  8.03 us
    ppermute x15, waiting for transfers between devices, line_reduce_scatter(): from_right[chain] = lax.ppermute(send_left, axis, leftward)  6.24 us
  transfers between devices with their start and end apart: 31, of which 14 were waited for; matrix products, arithmetic and copies ran while one was open for 21% of the time, Pallas kernels for 0%

profile of v3, /device:TPU:126, one launch (start us, length us, event | category | flops | bytes accessed | tf_op | source)
XLA Modules:
  0.0 242.7 jit_solution(401698927254723864)
XLA Ops:
  15.0 36.7 %collective-permute-done = bf16[272,512]{1,0:T(8,128)(2,1)S(1)} collective-permute-done((bf16[272,512]{1,0:T(8,128)(2,1)S(1)}, bf16[272,512]{1,0:T(8,128)(2,1)S(1)}, u32[]{:S(2)}, u32[]{:S(2)}) %collective-permute-start) | collective-permute-done | bytes 278560 | tf_op jit(solution)/shard_map/ppermute | solution.py:10
  55.3 13.3 %fusion.46 = bf16[256,512]{1,0:T(8,128)(2,1)S(1)} fusion(f32[383,512]{1,0:T(8,128)S(1)} %get-tuple-element.5, f32[512]{0:T(512)S(1)} %bitcast.287, f32[512]{0:T(512)S(1)} %bitcast.288, f32[512]{0:T(512)S(1)} %bitcast.219, f32[512]{0:T(512)S(1)} %bitcast.220, f32[512]{0:T(512)S(1)} %bitcast.221, f32[512]{0:T(512)S(1)} %bitcast.222, f32[512]{0:T(512)S(1)} %bitcast.223, ...), kind=kLoop, calls=%fused_computation.92 | loop fusion | flops 35782656 | bytes 71581696 | tf_op jit(solution)/shard_map/convert_element_type | solution.py:73
  81.5 19.2 %collective-permute-done.3 = bf16[256,512]{1,0:T(8,128)(2,1)S(1)} collective-permute-done((bf16[256,512]{1,0:T(8,128)(2,1)S(1)}, bf16[256,512]{1,0:T(8,128)(2,1)S(1)}, u32[]{:S(2)}, u32[]{:S(2)}) %collective-permute-start.3) | collective-permute-done | bytes 262176 | tf_op jit(solution)/shard_map/ppermute | solution.py:47
  102.1 1.9 collective-permute-start.4
  106.0 4.3 %collective-permute-done.4 = bf16[256,512]{1,0:T(8,128)(2,1)S(1)} collective-permute-done((bf16[256,512]{1,0:T(8,128)(2,1)S(1)}, bf16[256,512]{1,0:T(8,128)(2,1)S(1)}, u32[]{:S(2)}, u32[]{:S(2)}) %collective-permute-start.4) | collective-permute-done | bytes 262176 | tf_op jit(solution)/shard_map/ppermute | solution.py:47
  111.7 3.1 %collective-permute-start.5 = (bf16[256,512]{1,0:T(8,128)(2,1)S(1)}, bf16[256,512]{1,0:T(8,128)(2,1)S(1)}, u32[]{:S(2)}, u32[]{:S(2)}) collective-permute-start(bf16[256,512]{1,0:T(8,128)(2,1)S(1)} %add_convert_fusion.25), channel_id=1, source_target_pairs={{0,1},{1,2},{2,3},{3,4},{4,5},{16,17},{17,18},{18,19},{19,20},{20,... | collective-permute-start | bytes 786440 | tf_op jit(solution)/shard_map/ppermute | solution.py:47
  116.9 3.1 %collective-permute-done.5 = bf16[256,512]{1,0:T(8,128)(2,1)S(1)} collective-permute-done((bf16[256,512]{1,0:T(8,128)(2,1)S(1)}, bf16[256,512]{1,0:T(8,128)(2,1)S(1)}, u32[]{:S(2)}, u32[]{:S(2)}) %collective-permute-start.5) | collective-permute-done | bytes 262176 | tf_op jit(solution)/shard_map/ppermute | solution.py:47
  121.3 4.3 %collective-permute-start.6 = (bf16[256,512]{1,0:T(8,128)(2,1)S(1)}, bf16[256,512]{1,0:T(8,128)(2,1)S(1)}, u32[]{:S(2)}, u32[]{:S(2)}) collective-permute-start(bf16[256,512]{1,0:T(8,128)(2,1)S(1)} %add_convert_fusion.24), channel_id=1, source_target_pairs={{0,1},{1,2},{2,3},{3,4},{4,5},{5,6},{16,17},{17,18},{18,19},{19,20... | collective-permute-start | bytes 786440 | tf_op jit(solution)/shard_map/ppermute | solution.py:47
  130.9 5.6 %collective-permute-start.7 = (bf16[256,512]{1,0:T(8,128)(2,1)S(1)}, bf16[256,512]{1,0:T(8,128)(2,1)S(1)}, u32[]{:S(2)}, u32[]{:S(2)}) collective-permute-start(bf16[256,512]{1,0:T(8,128)(2,1)S(1)} %add_convert_fusion.23), channel_id=1, source_target_pairs={{0,1},{1,2},{2,3},{3,4},{4,5},{5,6},{6,7},{16,17},{17,18},{18,19},... | collective-permute-start | bytes 786440 | tf_op jit(solution)/shard_map/ppermute | solution.py:47
  141.7 5.6 %collective-permute-start.8 = (bf16[256,512]{1,0:T(8,128)(2,1)S(1)}, bf16[256,512]{1,0:T(8,128)(2,1)S(1)}, u32[]{:S(2)}, u32[]{:S(2)}) collective-permute-start(bf16[256,512]{1,0:T(8,128)(2,1)S(1)} %add_convert_fusion.22), channel_id=1, source_target_pairs={{0,1},{1,2},{2,3},{3,4},{4,5},{5,6},{6,7},{7,8},{16,17},{17,18},{1... | collective-permute-start | bytes 786440 | tf_op jit(solution)/shard_map/ppermute | solution.py:47
  149.3 2.4 collective-permute-done.8
  153.1 5.6 %collective-permute-start.9 = (bf16[256,512]{1,0:T(8,128)(2,1)S(1)}, bf16[256,512]{1,0:T(8,128)(2,1)S(1)}, u32[]{:S(2)}, u32[]{:S(2)}) collective-permute-start(bf16[256,512]{1,0:T(8,128)(2,1)S(1)} %add_convert_fusion.21), channel_id=1, source_target_pairs={{0,1},{1,2},{2,3},{3,4},{4,5},{5,6},{6,7},{7,8},{8,9},{16,17},{17,... | collective-permute-start | bytes 786440 | tf_op jit(solution)/shard_map/ppermute | solution.py:47
  160.8 4.3 %collective-permute-done.9 = bf16[256,512]{1,0:T(8,128)(2,1)S(1)} collective-permute-done((bf16[256,512]{1,0:T(8,128)(2,1)S(1)}, bf16[256,512]{1,0:T(8,128)(2,1)S(1)}, u32[]{:S(2)}, u32[]{:S(2)}) %collective-permute-start.9) | collective-permute-done | bytes 262176 | tf_op jit(solution)/shard_map/ppermute | solution.py:47
  166.4 4.9 %collective-permute-start.10 = (bf16[256,512]{1,0:T(8,128)(2,1)S(1)}, bf16[256,512]{1,0:T(8,128)(2,1)S(1)}, u32[]{:S(2)}, u32[]{:S(2)}) collective-permute-start(bf16[256,512]{1,0:T(8,128)(2,1)S(1)} %add_convert_fusion.20), channel_id=1, source_target_pairs={{0,1},{1,2},{2,3},{3,4},{4,5},{5,6},{6,7},{7,8},{8,9},{9,10},{16,1... | collective-permute-start | bytes 786440 | tf_op jit(solution)/shard_map/ppermute | solution.py:47
  173.3 4.5 %collective-permute-done.10 = bf16[256,512]{1,0:T(8,128)(2,1)S(1)} collective-permute-done((bf16[256,512]{1,0:T(8,128)(2,1)S(1)}, bf16[256,512]{1,0:T(8,128)(2,1)S(1)}, u32[]{:S(2)}, u32[]{:S(2)}) %collective-permute-start.10) | collective-permute-done | bytes 262176 | tf_op jit(solution)/shard_map/ppermute | solution.py:47
  179.2 5.6 %collective-permute-start.11 = (bf16[256,512]{1,0:T(8,128)(2,1)S(1)}, bf16[256,512]{1,0:T(8,128)(2,1)S(1)}, u32[]{:S(2)}, u32[]{:S(2)}) collective-permute-start(bf16[256,512]{1,0:T(8,128)(2,1)S(1)} %add_convert_fusion.19), channel_id=1, source_target_pairs={{0,1},{1,2},{2,3},{3,4},{4,5},{5,6},{6,7},{7,8},{8,9},{9,10},{10,1... | collective-permute-start | bytes 786440 | tf_op jit(solution)/shard_map/ppermute | solution.py:47
  186.9 3.7 %collective-permute-done.11 = bf16[256,512]{1,0:T(8,128)(2,1)S(1)} collective-permute-done((bf16[256,512]{1,0:T(8,128)(2,1)S(1)}, bf16[256,512]{1,0:T(8,128)(2,1)S(1)}, u32[]{:S(2)}, u32[]{:S(2)}) %collective-permute-start.11) | collective-permute-done | bytes 262176 | tf_op jit(solution)/shard_map/ppermute | solution.py:47
  191.9 5.6 %collective-permute-start.12 = (bf16[256,512]{1,0:T(8,128)(2,1)S(1)}, bf16[256,512]{1,0:T(8,128)(2,1)S(1)}, u32[]{:S(2)}, u32[]{:S(2)}) collective-permute-start(bf16[256,512]{1,0:T(8,128)(2,1)S(1)} %add_convert_fusion.18), channel_id=1, source_target_pairs={{0,1},{1,2},{2,3},{3,4},{4,5},{5,6},{6,7},{7,8},{8,9},{9,10},{10,1... | collective-permute-start | bytes 786440 | tf_op jit(solution)/shard_map/ppermute | solution.py:47
  200.2 2.2 collective-permute-done.12
  203.7 5.6 %collective-permute-start.13 = (bf16[256,512]{1,0:T(8,128)(2,1)S(1)}, bf16[256,512]{1,0:T(8,128)(2,1)S(1)}, u32[]{:S(2)}, u32[]{:S(2)}) collective-permute-start(bf16[256,512]{1,0:T(8,128)(2,1)S(1)} %add_convert_fusion.17), channel_id=1, source_target_pairs={{0,1},{1,2},{2,3},{3,4},{4,5},{5,6},{6,7},{7,8},{8,9},{9,10},{10,1... | collective-permute-start | bytes 786440 | tf_op jit(solution)/shard_map/ppermute | solution.py:47
  214.7 5.6 %collective-permute-start.14 = (bf16[256,512]{1,0:T(8,128)(2,1)S(1)}, bf16[256,512]{1,0:T(8,128)(2,1)S(1)}, u32[]{:S(2)}, u32[]{:S(2)}) collective-permute-start(bf16[256,512]{1,0:T(8,128)(2,1)S(1)} %add_convert_fusion.16), channel_id=1, source_target_pairs={{0,1},{1,2},{2,3},{3,4},{4,5},{5,6},{6,7},{7,8},{8,9},{9,10},{10,1... | collective-permute-start | bytes 786440 | tf_op jit(solution)/shard_map/ppermute | solution.py:47
  225.5 5.6 %collective-permute-start.15 = (bf16[256,512]{1,0:T(8,128)(2,1)S(1)}, bf16[256,512]{1,0:T(8,128)(2,1)S(1)}, u32[]{:S(2)}, u32[]{:S(2)}) collective-permute-start(bf16[256,512]{1,0:T(8,128)(2,1)S(1)} %add_convert_fusion.15), channel_id=1, source_target_pairs={{0,1},{1,2},{2,3},{3,4},{4,5},{5,6},{6,7},{7,8},{8,9},{9,10},{10,1... | collective-permute-start | bytes 786440 | tf_op jit(solution)/shard_map/ppermute | solution.py:47
  232.4 1.9 collective-permute-start.30
  235.7 6.2 %collective-permute-done.30 = bf16[256,512]{1,0:T(8,128)(2,1)S(1)} collective-permute-done((bf16[256,512]{1,0:T(8,128)(2,1)S(1)}, bf16[256,512]{1,0:T(8,128)(2,1)S(1)}, u32[]{:S(2)}, u32[]{:S(2)}) %collective-permute-start.30) | collective-permute-done | bytes 262176 | tf_op jit(solution)/shard_map/ppermute | solution.py:48
  (91 shorter events, 81.2 us)
Async XLA Ops:
  2.6 49.0 %collective-permute-start = (bf16[272,512]{1,0:T(8,128)(2,1)S(1)}, bf16[272,512]{1,0:T(8,128)(2,1)S(1)}, u32[]{:S(2)}, u32[]{:S(2)}) collective-permute-start(bf16[272,512]{1,0:T(8,128)(2,1)S(1)} %pad_maximum_fusion), channel_id=1, source_target_pairs={{0,16},{16,32},{32,48},{48,64},{64,80},{80,96},{96,112},{112,128},... | collective-permute-start | bytes 835592 | tf_op jit(solution)/shard_map/ppermute | solution.py:10
  78.1 22.6 %collective-permute-start.3 = (bf16[256,512]{1,0:T(8,128)(2,1)S(1)}, bf16[256,512]{1,0:T(8,128)(2,1)S(1)}, u32[]{:S(2)}, u32[]{:S(2)}) collective-permute-start(bf16[256,512]{1,0:T(8,128)(2,1)S(1)} %add_convert_fusion.27), channel_id=1, source_target_pairs={{0,1},{1,2},{2,3},{16,17},{17,18},{18,19},{32,33},{33,34},{34,35},... | collective-permute-start | bytes 786440 | tf_op jit(solution)/shard_map/ppermute | solution.py:47
  80.8 23.2 %collective-permute-start.18 = (bf16[256,512]{1,0:T(8,128)(2,1)S(1)}, bf16[256,512]{1,0:T(8,128)(2,1)S(1)}, u32[]{:S(2)}, u32[]{:S(2)}) collective-permute-start(bf16[256,512]{1,0:T(8,128)(2,1)S(1)} %add_convert_fusion.13), channel_id=1, source_target_pairs={{13,12},{14,13},{15,14},{29,28},{30,29},{31,30},{45,44},{46,45},{4... | collective-permute-start | bytes 786440 | tf_op jit(solution)/shard_map/ppermute | solution.py:48
  105.3 9.5 %collective-permute-start.19 = (bf16[256,512]{1,0:T(8,128)(2,1)S(1)}, bf16[256,512]{1,0:T(8,128)(2,1)S(1)}, u32[]{:S(2)}, u32[]{:S(2)}) collective-permute-start(bf16[256,512]{1,0:T(8,128)(2,1)S(1)} %add_convert_fusion.12), channel_id=1, source_target_pairs={{12,11},{13,12},{14,13},{15,14},{28,27},{29,28},{30,29},{31,30},{4... | collective-permute-start | bytes 786440 | tf_op jit(solution)/shard_map/ppermute | solution.py:48
  116.2 9.5 %collective-permute-start.20 = (bf16[256,512]{1,0:T(8,128)(2,1)S(1)}, bf16[256,512]{1,0:T(8,128)(2,1)S(1)}, u32[]{:S(2)}, u32[]{:S(2)}) collective-permute-start(bf16[256,512]{1,0:T(8,128)(2,1)S(1)} %add_convert_fusion.11), channel_id=1, source_target_pairs={{11,10},{12,11},{13,12},{14,13},{15,14},{27,26},{28,27},{29,28},{3... | collective-permute-start | bytes 786440 | tf_op jit(solution)/shard_map/ppermute | solution.py:48
  127.0 9.5 %collective-permute-start.21 = (bf16[256,512]{1,0:T(8,128)(2,1)S(1)}, bf16[256,512]{1,0:T(8,128)(2,1)S(1)}, u32[]{:S(2)}, u32[]{:S(2)}) collective-permute-start(bf16[256,512]{1,0:T(8,128)(2,1)S(1)} %add_convert_fusion.10), channel_id=1, source_target_pairs={{10,9},{11,10},{12,11},{13,12},{14,13},{15,14},{26,25},{27,26},{28... | collective-permute-start | bytes 786440 | tf_op jit(solution)/shard_map/ppermute | solution.py:48
  130.9 9.4 %collective-permute-start.7 = (bf16[256,512]{1,0:T(8,128)(2,1)S(1)}, bf16[256,512]{1,0:T(8,128)(2,1)S(1)}, u32[]{:S(2)}, u32[]{:S(2)}) collective-permute-start(bf16[256,512]{1,0:T(8,128)(2,1)S(1)} %add_convert_fusion.23), channel_id=1, source_target_pairs={{0,1},{1,2},{2,3},{3,4},{4,5},{5,6},{6,7},{16,17},{17,18},{18,19},... | collective-permute-start | bytes 786440 | tf_op jit(solution)/shard_map/ppermute | solution.py:47
  137.8 9.5 %collective-permute-start.22 = (bf16[256,512]{1,0:T(8,128)(2,1)S(1)}, bf16[256,512]{1,0:T(8,128)(2,1)S(1)}, u32[]{:S(2)}, u32[]{:S(2)}) collective-permute-start(bf16[256,512]{1,0:T(8,128)(2,1)S(1)} %add_convert_fusion.9), channel_id=1, source_target_pairs={{9,8},{10,9},{11,10},{12,11},{13,12},{14,13},{15,14},{25,24},{26,2... | collective-permute-start | bytes 786440 | tf_op jit(solution)/shard_map/ppermute | solution.py:48
  141.7 10.1 %collective-permute-start.8 = (bf16[256,512]{1,0:T(8,128)(2,1)S(1)}, bf16[256,512]{1,0:T(8,128)(2,1)S(1)}, u32[]{:S(2)}, u32[]{:S(2)}) collective-permute-start(bf16[256,512]{1,0:T(8,128)(2,1)S(1)} %add_convert_fusion.22), channel_id=1, source_target_pairs={{0,1},{1,2},{2,3},{3,4},{4,5},{5,6},{6,7},{7,8},{16,17},{17,18},{1... | collective-permute-start | bytes 786440 | tf_op jit(solution)/shard_map/ppermute | solution.py:47
  148.6 10.1 %collective-permute-start.23 = (bf16[256,512]{1,0:T(8,128)(2,1)S(1)}, bf16[256,512]{1,0:T(8,128)(2,1)S(1)}, u32[]{:S(2)}, u32[]{:S(2)}) collective-permute-start(bf16[256,512]{1,0:T(8,128)(2,1)S(1)} %add_convert_fusion.8), channel_id=1, source_target_pairs={{8,7},{9,8},{10,9},{11,10},{12,11},{13,12},{14,13},{15,14},{24,23}... | collective-permute-start | bytes 786440 | tf_op jit(solution)/shard_map/ppermute | solution.py:48
  153.1 11.9 %collective-permute-start.9 = (bf16[256,512]{1,0:T(8,128)(2,1)S(1)}, bf16[256,512]{1,0:T(8,128)(2,1)S(1)}, u32[]{:S(2)}, u32[]{:S(2)}) collective-permute-start(bf16[256,512]{1,0:T(8,128)(2,1)S(1)} %add_convert_fusion.21), channel_id=1, source_target_pairs={{0,1},{1,2},{2,3},{3,4},{4,5},{5,6},{6,7},{7,8},{8,9},{16,17},{17,... | collective-permute-start | bytes 786440 | tf_op jit(solution)/shard_map/ppermute | solution.py:47
  160.1 11.2 %collective-permute-start.24 = (bf16[256,512]{1,0:T(8,128)(2,1)S(1)}, bf16[256,512]{1,0:T(8,128)(2,1)S(1)}, u32[]{:S(2)}, u32[]{:S(2)}) collective-permute-start(bf16[256,512]{1,0:T(8,128)(2,1)S(1)} %add_convert_fusion.7), channel_id=1, source_target_pairs={{7,6},{8,7},{9,8},{10,9},{11,10},{12,11},{13,12},{14,13},{15,14},{... | collective-permute-start | bytes 786440 | tf_op jit(solution)/shard_map/ppermute | solution.py:48
  166.4 11.5 %collective-permute-start.10 = (bf16[256,512]{1,0:T(8,128)(2,1)S(1)}, bf16[256,512]{1,0:T(8,128)(2,1)S(1)}, u32[]{:S(2)}, u32[]{:S(2)}) collective-permute-start(bf16[256,512]{1,0:T(8,128)(2,1)S(1)} %add_convert_fusion.20), channel_id=1, source_target_pairs={{0,1},{1,2},{2,3},{3,4},{4,5},{5,6},{6,7},{7,8},{8,9},{9,10},{16,1... | collective-permute-start | bytes 786440 | tf_op jit(solution)/shard_map/ppermute | solution.py:47
  172.6 12.2 %collective-permute-start.25 = (bf16[256,512]{1,0:T(8,128)(2,1)S(1)}, bf16[256,512]{1,0:T(8,128)(2,1)S(1)}, u32[]{:S(2)}, u32[]{:S(2)}) collective-permute-start(bf16[256,512]{1,0:T(8,128)(2,1)S(1)} %add_convert_fusion.6), channel_id=1, source_target_pairs={{6,5},{7,6},{8,7},{9,8},{10,9},{11,10},{12,11},{13,12},{14,13},{15... | collective-permute-start | bytes 786440 | tf_op jit(solution)/shard_map/ppermute | solution.py:48
  179.2 11.3 %collective-permute-start.11 = (bf16[256,512]{1,0:T(8,128)(2,1)S(1)}, bf16[256,512]{1,0:T(8,128)(2,1)S(1)}, u32[]{:S(2)}, u32[]{:S(2)}) collective-permute-start(bf16[256,512]{1,0:T(8,128)(2,1)S(1)} %add_convert_fusion.19), channel_id=1, source_target_pairs={{0,1},{1,2},{2,3},{3,4},{4,5},{5,6},{6,7},{7,8},{8,9},{9,10},{10,1... | collective-permute-start | bytes 786440 | tf_op jit(solution)/shard_map/ppermute | solution.py:47
  186.2 11.3 %collective-permute-start.26 = (bf16[256,512]{1,0:T(8,128)(2,1)S(1)}, bf16[256,512]{1,0:T(8,128)(2,1)S(1)}, u32[]{:S(2)}, u32[]{:S(2)}) collective-permute-start(bf16[256,512]{1,0:T(8,128)(2,1)S(1)} %add_convert_fusion.5), channel_id=1, source_target_pairs={{5,4},{6,5},{7,6},{8,7},{9,8},{10,9},{11,10},{12,11},{13,12},{14,1... | collective-permute-start | bytes 786440 | tf_op jit(solution)/shard_map/ppermute | solution.py:48
  191.9 10.5 %collective-permute-start.12 = (bf16[256,512]{1,0:T(8,128)(2,1)S(1)}, bf16[256,512]{1,0:T(8,128)(2,1)S(1)}, u32[]{:S(2)}, u32[]{:S(2)}) collective-permute-start(bf16[256,512]{1,0:T(8,128)(2,1)S(1)} %add_convert_fusion.18), channel_id=1, source_target_pairs={{0,1},{1,2},{2,3},{3,4},{4,5},{5,6},{6,7},{7,8},{8,9},{9,10},{10,1... | collective-permute-start | bytes 786440 | tf_op jit(solution)/shard_map/ppermute | solution.py:47
  198.9 10.5 %collective-permute-start.27 = (bf16[256,512]{1,0:T(8,128)(2,1)S(1)}, bf16[256,512]{1,0:T(8,128)(2,1)S(1)}, u32[]{:S(2)}, u32[]{:S(2)}) collective-permute-start(bf16[256,512]{1,0:T(8,128)(2,1)S(1)} %add_convert_fusion.4), channel_id=1, source_target_pairs={{4,3},{5,4},{6,5},{7,6},{8,7},{9,8},{10,9},{11,10},{12,11},{13,12}... | collective-permute-start | bytes 786440 | tf_op jit(solution)/shard_map/ppermute | solution.py:48
  203.7 9.6 %collective-permute-start.13 = (bf16[256,512]{1,0:T(8,128)(2,1)S(1)}, bf16[256,512]{1,0:T(8,128)(2,1)S(1)}, u32[]{:S(2)}, u32[]{:S(2)}) collective-permute-start(bf16[256,512]{1,0:T(8,128)(2,1)S(1)} %add_convert_fusion.17), channel_id=1, source_target_pairs={{0,1},{1,2},{2,3},{3,4},{4,5},{5,6},{6,7},{7,8},{8,9},{9,10},{10,1... | collective-permute-start | bytes 786440 | tf_op jit(solution)/shard_map/ppermute | solution.py:47
  210.7 9.6 %collective-permute-start.28 = (bf16[256,512]{1,0:T(8,128)(2,1)S(1)}, bf16[256,512]{1,0:T(8,128)(2,1)S(1)}, u32[]{:S(2)}, u32[]{:S(2)}) collective-permute-start(bf16[256,512]{1,0:T(8,128)(2,1)S(1)} %add_convert_fusion.3), channel_id=1, source_target_pairs={{3,2},{4,3},{5,4},{6,5},{7,6},{8,7},{9,8},{10,9},{11,10},{12,11},{... | collective-permute-start | bytes 786440 | tf_op jit(solution)/shard_map/ppermute | solution.py:48
  214.7 9.5 %collective-permute-start.14 = (bf16[256,512]{1,0:T(8,128)(2,1)S(1)}, bf16[256,512]{1,0:T(8,128)(2,1)S(1)}, u32[]{:S(2)}, u32[]{:S(2)}) collective-permute-start(bf16[256,512]{1,0:T(8,128)(2,1)S(1)} %add_convert_fusion.16), channel_id=1, source_target_pairs={{0,1},{1,2},{2,3},{3,4},{4,5},{5,6},{6,7},{7,8},{8,9},{9,10},{10,1... | collective-permute-start | bytes 786440 | tf_op jit(solution)/shard_map/ppermute | solution.py:47
  221.6 9.5 %collective-permute-start.29 = (bf16[256,512]{1,0:T(8,128)(2,1)S(1)}, bf16[256,512]{1,0:T(8,128)(2,1)S(1)}, u32[]{:S(2)}, u32[]{:S(2)}) collective-permute-start(bf16[256,512]{1,0:T(8,128)(2,1)S(1)} %add_convert_fusion.2), channel_id=1, source_target_pairs={{2,1},{3,2},{4,3},{5,4},{6,5},{7,6},{8,7},{9,8},{10,9},{11,10},{12... | collective-permute-start | bytes 786440 | tf_op jit(solution)/shard_map/ppermute | solution.py:48
  225.5 10.3 %collective-permute-start.15 = (bf16[256,512]{1,0:T(8,128)(2,1)S(1)}, bf16[256,512]{1,0:T(8,128)(2,1)S(1)}, u32[]{:S(2)}, u32[]{:S(2)}) collective-permute-start(bf16[256,512]{1,0:T(8,128)(2,1)S(1)} %add_convert_fusion.15), channel_id=1, source_target_pairs={{0,1},{1,2},{2,3},{3,4},{4,5},{5,6},{6,7},{7,8},{8,9},{9,10},{10,1... | collective-permute-start | bytes 786440 | tf_op jit(solution)/shard_map/ppermute | solution.py:47
  232.4 9.5 %collective-permute-start.30 = (bf16[256,512]{1,0:T(8,128)(2,1)S(1)}, bf16[256,512]{1,0:T(8,128)(2,1)S(1)}, u32[]{:S(2)}, u32[]{:S(2)}) collective-permute-start(bf16[256,512]{1,0:T(8,128)(2,1)S(1)} %add_convert_fusion.1), channel_id=1, source_target_pairs={{1,0},{2,1},{3,2},{4,3},{5,4},{6,5},{7,6},{8,7},{9,8},{10,9},{11,1... | collective-permute-start | bytes 786440 | tf_op jit(solution)/shard_map/ppermute | solution.py:48
  (8 other events, 79.9 us)

commit v4 on v3

--- a/solution.py
+++ b/solution.py
@@ -56,20 +56,25 @@
 def shards(query_stream, key_stream, value_stream, feat_taps, filt_taps, skip_bias, out_weight):
     filt_reach = filt_taps.shape[0] - 1
     feat_reach = feat_taps.shape[1] - 1
-    full_reach = filt_reach + feat_reach
+    wide = lambda x: x.astype(jnp.float32)
+    key_body = valid_conv(wide(key_stream), feat_taps[1])
+    value_body = valid_conv(wide(value_stream), feat_taps[2])
+    gated_body = (key_body * value_body).astype(jnp.bfloat16)
     outgoing = jnp.concatenate(
-        [key_stream[-full_reach:], value_stream[-full_reach:], query_stream[-feat_reach:]], 0
+        [gated_body[-filt_reach:], key_stream[-feat_reach:], value_stream[-feat_reach:], query_stream[-feat_reach:]], 0
     )
     incoming = shifted(outgoing, "ctx", 1)
-    key_ext = jnp.concatenate([incoming[:full_reach], key_stream], 0)
-    value_ext = jnp.concatenate([incoming[full_reach : 2 * full_reach], value_stream], 0)
-    query_ext = jnp.concatenate([incoming[2 * full_reach :], query_stream], 0)
-    key_feat = valid_conv(key_ext.astype(jnp.float32), feat_taps[1])
-    value_feat = valid_conv(value_ext.astype(jnp.float32), feat_taps[2])
-    query_feat = valid_conv(query_ext.astype(jnp.float32), feat_taps[0])
-    gated = (key_feat * value_feat).astype(jnp.bfloat16)
-    own_gated = gated[filt_reach:].astype(jnp.float32)
-    mixed = valid_conv(gated.astype(jnp.float32), filt_taps) + skip_bias[None, :] * own_gated
+    gated_halo = incoming[:filt_reach]
+    key_halo = incoming[filt_reach : filt_reach + feat_reach]
+    value_halo = incoming[filt_reach + feat_reach : filt_reach + 2 * feat_reach]
+    query_halo = incoming[filt_reach + 2 * feat_reach :]
+    key_head = valid_conv(wide(jnp.concatenate([key_halo, key_stream[:feat_reach]], 0)), feat_taps[1])
+    value_head = valid_conv(wide(jnp.concatenate([value_halo, value_stream[:feat_reach]], 0)), feat_taps[2])
+    gated_head = (key_head * value_head).astype(jnp.bfloat16)
+    gated = jnp.concatenate([gated_halo, gated_head, gated_body], 0)
+    query_feat = valid_conv(wide(jnp.concatenate([query_halo, query_stream], 0)), feat_taps[0])
+    own_gated = wide(gated[filt_reach:])
+    mixed = valid_conv(wide(gated), filt_taps) + skip_bias[None, :] * own_gated
     product = (query_feat * mixed).astype(jnp.bfloat16)
     return line_reduce_scatter(product, out_weight, "tp")
 

time: 246 us -> 233 us (0.947)
  local copies, waits for them, and re-layouts: 13 us -> 3.06 us
    ppermute x15, waiting for transfers between devices: 6.24 us -> 15.1 us  [line_reduce_scatter(): from_right[chain] = lax.ppermute(send_left, axis, leftward)]
    ppermute x1, waiting for transfers between devices: 36.7 us -> 27.8 us  [shifted(): return lax.ppermute(block, axis, route)]
    slice x7, local copies, waits for them, and re-layouts: 8.03 us -> 0.99 us  [valid_conv(): taps[offset][None, :]]
  transfers between devices with their start and end apart: 31 -> 31, of which waited for: 14 -> 15; matrix products, arithmetic and copies ran while one was open for 21% -> 18% of each run, Pallas kernels for 0% -> 0%
where the time goes in v4:
time: 233 us; the launch traced here: 230 us
  waiting for transfers between devices  90.3 us (39%)
  starting transfers between devices  77.1 us (33%)
  matrix products  41.6 us (18%)
  other arithmetic  17.2 us (7%)
  local copies, waits for them, and re-layouts  3.06 us (1%)
    ppermute x15, starting transfers between devices, line_reduce_scatter(): from_left[chain] = lax.ppermute(send_right, axis, rightward)  60.6 us
    ppermute x15, waiting for transfers between devices, line_reduce_scatter(): from_left[chain] = lax.ppermute(send_right, axis, rightward)  47.4 us
    dot_general x31, matrix products, block(): term = jnp.dot(product, columns, preferred_element_type=jnp.float32)  41.6 us
    ppermute x1, waiting for transfers between devices, shifted(): return lax.ppermute(block, axis, route)  27.8 us
    ppermute x15, waiting for transfers between devices, line_reduce_scatter(): from_right[chain] = lax.ppermute(send_left, axis, leftward)  15.1 us
    ppermute x15, starting transfers between devices, line_reduce_scatter(): from_right[chain] = lax.ppermute(send_left, axis, leftward)  14.5 us
    convert_element_type x1, other arithmetic, shards(): product = (query_feat * mixed).astype(jnp.bfloat16)  13.2 us
  transfers between devices with their start and end apart: 31, of which 15 were waited for; matrix products, arithmetic and copies ran while one was open for 18% of the time, Pallas kernels for 0%

profile of v4, /device:TPU:126, one launch (start us, length us, event | category | flops | bytes accessed | tf_op | source)
XLA Modules:
  0.0 230.2 jit_solution(4533183990961236494)
XLA Ops:
  8.1 27.8 %collective-permute-done = bf16[145,512]{1,0:T(8,128)(2,1)S(1)} collective-permute-done((bf16[145,512]{1,0:T(8,128)(2,1)S(1)}, bf16[145,512]{1,0:T(8,128)(2,1)S(1)}, u32[]{:S(2)}, u32[]{:S(2)}) %collective-permute-start) | collective-permute-done | bytes 148512 | tf_op jit(solution)/shard_map/ppermute | solution.py:10
  36.2 13.2 %fusion.32 = bf16[256,512]{1,0:T(8,128)(2,1)S(1)} fusion(f32[383,512]{1,0:T(8,128)S(1)} %maximum_convert_fusion, f32[512]{0:T(512)S(1)} %bitcast.339, f32[512]{0:T(512)S(1)} %bitcast.340, f32[512]{0:T(512)S(1)} %bitcast.252, f32[512]{0:T(512)S(1)} %bitcast.253, f32[512]{0:T(512)S(1)} %bitcast.254, f32[512]{0:T(512)S(1)} %bitcast.255, f32[512]{0:T(512)S(1)} %bitcast.256, ...), kind=kLoop, calls=%fused_computation.64 | loop fusion | flops 36175872 | bytes 71581696 | tf_op jit(solution)/shard_map/convert_element_type | solution.py:78
  62.3 17.4 %collective-permute-done.3 = bf16[256,512]{1,0:T(8,128)(2,1)S(1)} collective-permute-done((bf16[256,512]{1,0:T(8,128)(2,1)S(1)}, bf16[256,512]{1,0:T(8,128)(2,1)S(1)}, u32[]{:S(2)}, u32[]{:S(2)}) %collective-permute-start.3) | collective-permute-done | bytes 262176 | tf_op jit(solution)/shard_map/ppermute | solution.py:47
  85.0 4.9 %collective-permute-done.4 = bf16[256,512]{1,0:T(8,128)(2,1)S(1)} collective-permute-done((bf16[256,512]{1,0:T(8,128)(2,1)S(1)}, bf16[256,512]{1,0:T(8,128)(2,1)S(1)}, u32[]{:S(2)}, u32[]{:S(2)}) %collective-permute-start.4) | collective-permute-done | bytes 262176 | tf_op jit(solution)/shard_map/ppermute | solution.py:47
  91.3 2.9 %collective-permute-start.5 = (bf16[256,512]{1,0:T(8,128)(2,1)S(1)}, bf16[256,512]{1,0:T(8,128)(2,1)S(1)}, u32[]{:S(2)}, u32[]{:S(2)}) collective-permute-start(bf16[256,512]{1,0:T(8,128)(2,1)S(1)} %add_convert_fusion.25), channel_id=1, source_target_pairs={{0,1},{1,2},{2,3},{3,4},{4,5},{16,17},{17,18},{18,19},{19,20},{20,... | collective-permute-start | bytes 786440 | tf_op jit(solution)/shard_map/ppermute | solution.py:47
  96.2 5.3 %collective-permute-done.5 = bf16[256,512]{1,0:T(8,128)(2,1)S(1)} collective-permute-done((bf16[256,512]{1,0:T(8,128)(2,1)S(1)}, bf16[256,512]{1,0:T(8,128)(2,1)S(1)}, u32[]{:S(2)}, u32[]{:S(2)}) %collective-permute-start.5) | collective-permute-done | bytes 262176 | tf_op jit(solution)/shard_map/ppermute | solution.py:47
  102.8 3.6 %collective-permute-start.6 = (bf16[256,512]{1,0:T(8,128)(2,1)S(1)}, bf16[256,512]{1,0:T(8,128)(2,1)S(1)}, u32[]{:S(2)}, u32[]{:S(2)}) collective-permute-start(bf16[256,512]{1,0:T(8,128)(2,1)S(1)} %add_convert_fusion.24), channel_id=1, source_target_pairs={{0,1},{1,2},{2,3},{3,4},{4,5},{5,6},{16,17},{17,18},{18,19},{19,20... | collective-permute-start | bytes 786440 | tf_op jit(solution)/shard_map/ppermute | solution.py:47
  108.5 6.0 %collective-permute-done.6 = bf16[256,512]{1,0:T(8,128)(2,1)S(1)} collective-permute-done((bf16[256,512]{1,0:T(8,128)(2,1)S(1)}, bf16[256,512]{1,0:T(8,128)(2,1)S(1)}, u32[]{:S(2)}, u32[]{:S(2)}) %collective-permute-start.6) | collective-permute-done | bytes 262176 | tf_op jit(solution)/shard_map/ppermute | solution.py:47
  115.8 4.1 %collective-permute-start.7 = (bf16[256,512]{1,0:T(8,128)(2,1)S(1)}, bf16[256,512]{1,0:T(8,128)(2,1)S(1)}, u32[]{:S(2)}, u32[]{:S(2)}) collective-permute-start(bf16[256,512]{1,0:T(8,128)(2,1)S(1)} %add_convert_fusion.23), channel_id=1, source_target_pairs={{0,1},{1,2},{2,3},{3,4},{4,5},{5,6},{6,7},{16,17},{17,18},{18,19},... | collective-permute-start | bytes 786440 | tf_op jit(solution)/shard_map/ppermute | solution.py:47
  121.9 4.0 %collective-permute-done.7 = bf16[256,512]{1,0:T(8,128)(2,1)S(1)} collective-permute-done((bf16[256,512]{1,0:T(8,128)(2,1)S(1)}, bf16[256,512]{1,0:T(8,128)(2,1)S(1)}, u32[]{:S(2)}, u32[]{:S(2)}) %collective-permute-start.7) | collective-permute-done | bytes 262176 | tf_op jit(solution)/shard_map/ppermute | solution.py:47
  127.3 5.3 %collective-permute-start.8 = (bf16[256,512]{1,0:T(8,128)(2,1)S(1)}, bf16[256,512]{1,0:T(8,128)(2,1)S(1)}, u32[]{:S(2)}, u32[]{:S(2)}) collective-permute-start(bf16[256,512]{1,0:T(8,128)(2,1)S(1)} %add_convert_fusion.22), channel_id=1, source_target_pairs={{0,1},{1,2},{2,3},{3,4},{4,5},{5,6},{6,7},{7,8},{16,17},{17,18},{1... | collective-permute-start | bytes 786440 | tf_op jit(solution)/shard_map/ppermute | solution.py:47
  134.7 2.9 %collective-permute-done.8 = bf16[256,512]{1,0:T(8,128)(2,1)S(1)} collective-permute-done((bf16[256,512]{1,0:T(8,128)(2,1)S(1)}, bf16[256,512]{1,0:T(8,128)(2,1)S(1)}, u32[]{:S(2)}, u32[]{:S(2)}) %collective-permute-start.8) | collective-permute-done | bytes 262176 | tf_op jit(solution)/shard_map/ppermute | solution.py:47
  139.0 5.6 %collective-permute-start.9 = (bf16[256,512]{1,0:T(8,128)(2,1)S(1)}, bf16[256,512]{1,0:T(8,128)(2,1)S(1)}, u32[]{:S(2)}, u32[]{:S(2)}) collective-permute-start(bf16[256,512]{1,0:T(8,128)(2,1)S(1)} %add_convert_fusion.21), channel_id=1, source_target_pairs={{0,1},{1,2},{2,3},{3,4},{4,5},{5,6},{6,7},{7,8},{8,9},{16,17},{17,... | collective-permute-start | bytes 786440 | tf_op jit(solution)/shard_map/ppermute | solution.py:47
  146.6 2.0 collective-permute-done.9
  150.0 5.6 %collective-permute-start.10 = (bf16[256,512]{1,0:T(8,128)(2,1)S(1)}, bf16[256,512]{1,0:T(8,128)(2,1)S(1)}, u32[]{:S(2)}, u32[]{:S(2)}) collective-permute-start(bf16[256,512]{1,0:T(8,128)(2,1)S(1)} %add_convert_fusion.20), channel_id=1, source_target_pairs={{0,1},{1,2},{2,3},{3,4},{4,5},{5,6},{6,7},{7,8},{8,9},{9,10},{16,1... | collective-permute-start | bytes 786440 | tf_op jit(solution)/shard_map/ppermute | solution.py:47
  160.8 5.6 %collective-permute-start.11 = (bf16[256,512]{1,0:T(8,128)(2,1)S(1)}, bf16[256,512]{1,0:T(8,128)(2,1)S(1)}, u32[]{:S(2)}, u32[]{:S(2)}) collective-permute-start(bf16[256,512]{1,0:T(8,128)(2,1)S(1)} %add_convert_fusion.19), channel_id=1, source_target_pairs={{0,1},{1,2},{2,3},{3,4},{4,5},{5,6},{6,7},{7,8},{8,9},{9,10},{10,1... | collective-permute-start | bytes 786440 | tf_op jit(solution)/shard_map/ppermute | solution.py:47
  171.6 5.6 %collective-permute-start.12 = (bf16[256,512]{1,0:T(8,128)(2,1)S(1)}, bf16[256,512]{1,0:T(8,128)(2,1)S(1)}, u32[]{:S(2)}, u32[]{:S(2)}) collective-permute-start(bf16[256,512]{1,0:T(8,128)(2,1)S(1)} %add_convert_fusion.18), channel_id=1, source_target_pairs={{0,1},{1,2},{2,3},{3,4},{4,5},{5,6},{6,7},{7,8},{8,9},{9,10},{10,1... | collective-permute-start | bytes 786440 | tf_op jit(solution)/shard_map/ppermute | solution.py:47
  182.4 7.6 %collective-permute-start.13 = (bf16[256,512]{1,0:T(8,128)(2,1)S(1)}, bf16[256,512]{1,0:T(8,128)(2,1)S(1)}, u32[]{:S(2)}, u32[]{:S(2)}) collective-permute-start(bf16[256,512]{1,0:T(8,128)(2,1)S(1)} %add_convert_fusion.17), channel_id=1, source_target_pairs={{0,1},{1,2},{2,3},{3,4},{4,5},{5,6},{6,7},{7,8},{8,9},{9,10},{10,1... | collective-permute-start | bytes 786440 | tf_op jit(solution)/shard_map/ppermute | solution.py:47
  190.0 3.4 %collective-permute-done.27 = bf16[256,512]{1,0:T(8,128)(2,1)S(1)} collective-permute-done((bf16[256,512]{1,0:T(8,128)(2,1)S(1)}, bf16[256,512]{1,0:T(8,128)(2,1)S(1)}, u32[]{:S(2)}, u32[]{:S(2)}) %collective-permute-start.27) | collective-permute-done | bytes 262176 | tf_op jit(solution)/shard_map/ppermute | solution.py:48
  198.0 5.1 %collective-permute-start.14 = (bf16[256,512]{1,0:T(8,128)(2,1)S(1)}, bf16[256,512]{1,0:T(8,128)(2,1)S(1)}, u32[]{:S(2)}, u32[]{:S(2)}) collective-permute-start(bf16[256,512]{1,0:T(8,128)(2,1)S(1)} %add_convert_fusion.16), channel_id=1, source_target_pairs={{0,1},{1,2},{2,3},{3,4},{4,5},{5,6},{6,7},{7,8},{8,9},{9,10},{10,1... | collective-permute-start | bytes 786440 | tf_op jit(solution)/shard_map/ppermute | solution.py:47
  203.2 3.2 %collective-permute-done.28 = bf16[256,512]{1,0:T(8,128)(2,1)S(1)} collective-permute-done((bf16[256,512]{1,0:T(8,128)(2,1)S(1)}, bf16[256,512]{1,0:T(8,128)(2,1)S(1)}, u32[]{:S(2)}, u32[]{:S(2)}) %collective-permute-start.28) | collective-permute-done | bytes 262176 | tf_op jit(solution)/shard_map/ppermute | solution.py:48
  211.0 5.1 %collective-permute-start.15 = (bf16[256,512]{1,0:T(8,128)(2,1)S(1)}, bf16[256,512]{1,0:T(8,128)(2,1)S(1)}, u32[]{:S(2)}, u32[]{:S(2)}) collective-permute-start(bf16[256,512]{1,0:T(8,128)(2,1)S(1)} %add_convert_fusion.15), channel_id=1, source_target_pairs={{0,1},{1,2},{2,3},{3,4},{4,5},{5,6},{6,7},{7,8},{8,9},{9,10},{10,1... | collective-permute-start | bytes 786440 | tf_op jit(solution)/shard_map/ppermute | solution.py:47
  216.1 2.4 %collective-permute-done.29 = bf16[256,512]{1,0:T(8,128)(2,1)S(1)} collective-permute-done((bf16[256,512]{1,0:T(8,128)(2,1)S(1)}, bf16[256,512]{1,0:T(8,128)(2,1)S(1)}, u32[]{:S(2)}, u32[]{:S(2)}) %collective-permute-start.29) | collective-permute-done | bytes 262176 | tf_op jit(solution)/shard_map/ppermute | solution.py:48
  223.2 6.2 %collective-permute-done.30 = bf16[256,512]{1,0:T(8,128)(2,1)S(1)} collective-permute-done((bf16[256,512]{1,0:T(8,128)(2,1)S(1)}, bf16[256,512]{1,0:T(8,128)(2,1)S(1)}, u32[]{:S(2)}, u32[]{:S(2)}) %collective-permute-start.30) | collective-permute-done | bytes 262176 | tf_op jit(solution)/shard_map/ppermute | solution.py:48
  (100 shorter events, 74.5 us)
Async XLA Ops:
  5.0 30.8 %collective-permute-start = (bf16[145,512]{1,0:T(8,128)(2,1)S(1)}, bf16[145,512]{1,0:T(8,128)(2,1)S(1)}, u32[]{:S(2)}, u32[]{:S(2)}) collective-permute-start(bf16[145,512]{1,0:T(8,128)(2,1)S(1)} %pad_maximum_fusion), channel_id=1, source_target_pairs={{0,16},{16,32},{32,48},{48,64},{64,80},{80,96},{96,112},{112,128},... | collective-permute-start | bytes 445448 | tf_op jit(solution)/shard_map/ppermute | solution.py:10
  58.9 20.7 %collective-permute-start.3 = (bf16[256,512]{1,0:T(8,128)(2,1)S(1)}, bf16[256,512]{1,0:T(8,128)(2,1)S(1)}, u32[]{:S(2)}, u32[]{:S(2)}) collective-permute-start(bf16[256,512]{1,0:T(8,128)(2,1)S(1)} %add_convert_fusion.27), channel_id=1, source_target_pairs={{0,1},{1,2},{2,3},{16,17},{17,18},{18,19},{32,33},{33,34},{34,35},... | collective-permute-start | bytes 786440 | tf_op jit(solution)/shard_map/ppermute | solution.py:47
  61.6 21.3 %collective-permute-start.18 = (bf16[256,512]{1,0:T(8,128)(2,1)S(1)}, bf16[256,512]{1,0:T(8,128)(2,1)S(1)}, u32[]{:S(2)}, u32[]{:S(2)}) collective-permute-start(bf16[256,512]{1,0:T(8,128)(2,1)S(1)} %add_convert_fusion.13), channel_id=1, source_target_pairs={{13,12},{14,13},{15,14},{29,28},{30,29},{31,30},{45,44},{46,45},{4... | collective-permute-start | bytes 786440 | tf_op jit(solution)/shard_map/ppermute | solution.py:48
  84.3 9.8 %collective-permute-start.19 = (bf16[256,512]{1,0:T(8,128)(2,1)S(1)}, bf16[256,512]{1,0:T(8,128)(2,1)S(1)}, u32[]{:S(2)}, u32[]{:S(2)}) collective-permute-start(bf16[256,512]{1,0:T(8,128)(2,1)S(1)} %add_convert_fusion.12), channel_id=1, source_target_pairs={{12,11},{13,12},{14,13},{15,14},{28,27},{29,28},{30,29},{31,30},{4... | collective-permute-start | bytes 786440 | tf_op jit(solution)/shard_map/ppermute | solution.py:48
  91.3 10.2 %collective-permute-start.5 = (bf16[256,512]{1,0:T(8,128)(2,1)S(1)}, bf16[256,512]{1,0:T(8,128)(2,1)S(1)}, u32[]{:S(2)}, u32[]{:S(2)}) collective-permute-start(bf16[256,512]{1,0:T(8,128)(2,1)S(1)} %add_convert_fusion.25), channel_id=1, source_target_pairs={{0,1},{1,2},{2,3},{3,4},{4,5},{16,17},{17,18},{18,19},{19,20},{20,... | collective-permute-start | bytes 786440 | tf_op jit(solution)/shard_map/ppermute | solution.py:47
  95.5 10.9 %collective-permute-start.20 = (bf16[256,512]{1,0:T(8,128)(2,1)S(1)}, bf16[256,512]{1,0:T(8,128)(2,1)S(1)}, u32[]{:S(2)}, u32[]{:S(2)}) collective-permute-start(bf16[256,512]{1,0:T(8,128)(2,1)S(1)} %add_convert_fusion.11), channel_id=1, source_target_pairs={{11,10},{12,11},{13,12},{14,13},{15,14},{27,26},{28,27},{29,28},{3... | collective-permute-start | bytes 786440 | tf_op jit(solution)/shard_map/ppermute | solution.py:48
  102.8 11.6 %collective-permute-start.6 = (bf16[256,512]{1,0:T(8,128)(2,1)S(1)}, bf16[256,512]{1,0:T(8,128)(2,1)S(1)}, u32[]{:S(2)}, u32[]{:S(2)}) collective-permute-start(bf16[256,512]{1,0:T(8,128)(2,1)S(1)} %add_convert_fusion.24), channel_id=1, source_target_pairs={{0,1},{1,2},{2,3},{3,4},{4,5},{5,6},{16,17},{17,18},{18,19},{19,20... | collective-permute-start | bytes 786440 | tf_op jit(solution)/shard_map/ppermute | solution.py:47
  107.8 12.1 %collective-permute-start.21 = (bf16[256,512]{1,0:T(8,128)(2,1)S(1)}, bf16[256,512]{1,0:T(8,128)(2,1)S(1)}, u32[]{:S(2)}, u32[]{:S(2)}) collective-permute-start(bf16[256,512]{1,0:T(8,128)(2,1)S(1)} %add_convert_fusion.10), channel_id=1, source_target_pairs={{10,9},{11,10},{12,11},{13,12},{14,13},{15,14},{26,25},{27,26},{28... | collective-permute-start | bytes 786440 | tf_op jit(solution)/shard_map/ppermute | solution.py:48
  115.8 10.2 %collective-permute-start.7 = (bf16[256,512]{1,0:T(8,128)(2,1)S(1)}, bf16[256,512]{1,0:T(8,128)(2,1)S(1)}, u32[]{:S(2)}, u32[]{:S(2)}) collective-permute-start(bf16[256,512]{1,0:T(8,128)(2,1)S(1)} %add_convert_fusion.23), channel_id=1, source_target_pairs={{0,1},{1,2},{2,3},{3,4},{4,5},{5,6},{6,7},{16,17},{17,18},{18,19},... | collective-permute-start | bytes 786440 | tf_op jit(solution)/shard_map/ppermute | solution.py:47
  121.2 11.4 %collective-permute-start.22 = (bf16[256,512]{1,0:T(8,128)(2,1)S(1)}, bf16[256,512]{1,0:T(8,128)(2,1)S(1)}, u32[]{:S(2)}, u32[]{:S(2)}) collective-permute-start(bf16[256,512]{1,0:T(8,128)(2,1)S(1)} %add_convert_fusion.9), channel_id=1, source_target_pairs={{9,8},{10,9},{11,10},{12,11},{13,12},{14,13},{15,14},{25,24},{26,2... | collective-permute-start | bytes 786440 | tf_op jit(solution)/shard_map/ppermute | solution.py:48
  127.3 10.3 %collective-permute-start.8 = (bf16[256,512]{1,0:T(8,128)(2,1)S(1)}, bf16[256,512]{1,0:T(8,128)(2,1)S(1)}, u32[]{:S(2)}, u32[]{:S(2)}) collective-permute-start(bf16[256,512]{1,0:T(8,128)(2,1)S(1)} %add_convert_fusion.22), channel_id=1, source_target_pairs={{0,1},{1,2},{2,3},{3,4},{4,5},{5,6},{6,7},{7,8},{16,17},{17,18},{1... | collective-permute-start | bytes 786440 | tf_op jit(solution)/shard_map/ppermute | solution.py:47
  134.0 10.6 %collective-permute-start.23 = (bf16[256,512]{1,0:T(8,128)(2,1)S(1)}, bf16[256,512]{1,0:T(8,128)(2,1)S(1)}, u32[]{:S(2)}, u32[]{:S(2)}) collective-permute-start(bf16[256,512]{1,0:T(8,128)(2,1)S(1)} %add_convert_fusion.8), channel_id=1, source_target_pairs={{8,7},{9,8},{10,9},{11,10},{12,11},{13,12},{14,13},{15,14},{24,23}... | collective-permute-start | bytes 786440 | tf_op jit(solution)/shard_map/ppermute | solution.py:48
  139.0 9.7 %collective-permute-start.9 = (bf16[256,512]{1,0:T(8,128)(2,1)S(1)}, bf16[256,512]{1,0:T(8,128)(2,1)S(1)}, u32[]{:S(2)}, u32[]{:S(2)}) collective-permute-start(bf16[256,512]{1,0:T(8,128)(2,1)S(1)} %add_convert_fusion.21), channel_id=1, source_target_pairs={{0,1},{1,2},{2,3},{3,4},{4,5},{5,6},{6,7},{7,8},{8,9},{16,17},{17,... | collective-permute-start | bytes 786440 | tf_op jit(solution)/shard_map/ppermute | solution.py:47
  145.9 9.7 %collective-permute-start.24 = (bf16[256,512]{1,0:T(8,128)(2,1)S(1)}, bf16[256,512]{1,0:T(8,128)(2,1)S(1)}, u32[]{:S(2)}, u32[]{:S(2)}) collective-permute-start(bf16[256,512]{1,0:T(8,128)(2,1)S(1)} %add_convert_fusion.7), channel_id=1, source_target_pairs={{7,6},{8,7},{9,8},{10,9},{11,10},{12,11},{13,12},{14,13},{15,14},{... | collective-permute-start | bytes 786440 | tf_op jit(solution)/shard_map/ppermute | solution.py:48
  150.0 9.5 %collective-permute-start.10 = (bf16[256,512]{1,0:T(8,128)(2,1)S(1)}, bf16[256,512]{1,0:T(8,128)(2,1)S(1)}, u32[]{:S(2)}, u32[]{:S(2)}) collective-permute-start(bf16[256,512]{1,0:T(8,128)(2,1)S(1)} %add_convert_fusion.20), channel_id=1, source_target_pairs={{0,1},{1,2},{2,3},{3,4},{4,5},{5,6},{6,7},{7,8},{8,9},{9,10},{16,1... | collective-permute-start | bytes 786440 | tf_op jit(solution)/shard_map/ppermute | solution.py:47
  160.8 9.5 %collective-permute-start.11 = (bf16[256,512]{1,0:T(8,128)(2,1)S(1)}, bf16[256,512]{1,0:T(8,128)(2,1)S(1)}, u32[]{:S(2)}, u32[]{:S(2)}) collective-permute-start(bf16[256,512]{1,0:T(8,128)(2,1)S(1)} %add_convert_fusion.19), channel_id=1, source_target_pairs={{0,1},{1,2},{2,3},{3,4},{4,5},{5,6},{6,7},{7,8},{8,9},{9,10},{10,1... | collective-permute-start | bytes 786440 | tf_op jit(solution)/shard_map/ppermute | solution.py:47
  171.6 9.5 %collective-permute-start.12 = (bf16[256,512]{1,0:T(8,128)(2,1)S(1)}, bf16[256,512]{1,0:T(8,128)(2,1)S(1)}, u32[]{:S(2)}, u32[]{:S(2)}) collective-permute-start(bf16[256,512]{1,0:T(8,128)(2,1)S(1)} %add_convert_fusion.18), channel_id=1, source_target_pairs={{0,1},{1,2},{2,3},{3,4},{4,5},{5,6},{6,7},{7,8},{8,9},{9,10},{10,1... | collective-permute-start | bytes 786440 | tf_op jit(solution)/shard_map/ppermute | solution.py:47
  178.6 14.8 %collective-permute-start.27 = (bf16[256,512]{1,0:T(8,128)(2,1)S(1)}, bf16[256,512]{1,0:T(8,128)(2,1)S(1)}, u32[]{:S(2)}, u32[]{:S(2)}) collective-permute-start(bf16[256,512]{1,0:T(8,128)(2,1)S(1)} %add_convert_fusion.4), channel_id=1, source_target_pairs={{4,3},{5,4},{6,5},{7,6},{8,7},{9,8},{10,9},{11,10},{12,11},{13,12}... | collective-permute-start | bytes 786440 | tf_op jit(solution)/shard_map/ppermute | solution.py:48
  182.4 14.2 %collective-permute-start.13 = (bf16[256,512]{1,0:T(8,128)(2,1)S(1)}, bf16[256,512]{1,0:T(8,128)(2,1)S(1)}, u32[]{:S(2)}, u32[]{:S(2)}) collective-permute-start(bf16[256,512]{1,0:T(8,128)(2,1)S(1)} %add_convert_fusion.17), channel_id=1, source_target_pairs={{0,1},{1,2},{2,3},{3,4},{4,5},{5,6},{6,7},{7,8},{8,9},{9,10},{10,1... | collective-permute-start | bytes 786440 | tf_op jit(solution)/shard_map/ppermute | solution.py:47
  194.7 11.6 %collective-permute-start.28 = (bf16[256,512]{1,0:T(8,128)(2,1)S(1)}, bf16[256,512]{1,0:T(8,128)(2,1)S(1)}, u32[]{:S(2)}, u32[]{:S(2)}) collective-permute-start(bf16[256,512]{1,0:T(8,128)(2,1)S(1)} %add_convert_fusion.3), channel_id=1, source_target_pairs={{3,2},{4,3},{5,4},{6,5},{7,6},{8,7},{9,8},{10,9},{11,10},{12,11},{... | collective-permute-start | bytes 786440 | tf_op jit(solution)/shard_map/ppermute | solution.py:48
  198.0 11.6 %collective-permute-start.14 = (bf16[256,512]{1,0:T(8,128)(2,1)S(1)}, bf16[256,512]{1,0:T(8,128)(2,1)S(1)}, u32[]{:S(2)}, u32[]{:S(2)}) collective-permute-start(bf16[256,512]{1,0:T(8,128)(2,1)S(1)} %add_convert_fusion.16), channel_id=1, source_target_pairs={{0,1},{1,2},{2,3},{3,4},{4,5},{5,6},{6,7},{7,8},{8,9},{9,10},{10,1... | collective-permute-start | bytes 786440 | tf_op jit(solution)/shard_map/ppermute | solution.py:47
  207.7 10.8 %collective-permute-start.29 = (bf16[256,512]{1,0:T(8,128)(2,1)S(1)}, bf16[256,512]{1,0:T(8,128)(2,1)S(1)}, u32[]{:S(2)}, u32[]{:S(2)}) collective-permute-start(bf16[256,512]{1,0:T(8,128)(2,1)S(1)} %add_convert_fusion.2), channel_id=1, source_target_pairs={{2,1},{3,2},{4,3},{5,4},{6,5},{7,6},{8,7},{9,8},{10,9},{11,10},{12... | collective-permute-start | bytes 786440 | tf_op jit(solution)/shard_map/ppermute | solution.py:48
  211.0 12.2 %collective-permute-start.15 = (bf16[256,512]{1,0:T(8,128)(2,1)S(1)}, bf16[256,512]{1,0:T(8,128)(2,1)S(1)}, u32[]{:S(2)}, u32[]{:S(2)}) collective-permute-start(bf16[256,512]{1,0:T(8,128)(2,1)S(1)} %add_convert_fusion.15), channel_id=1, source_target_pairs={{0,1},{1,2},{2,3},{3,4},{4,5},{5,6},{6,7},{7,8},{8,9},{9,10},{10,1... | collective-permute-start | bytes 786440 | tf_op jit(solution)/shard_map/ppermute | solution.py:47
  219.9 9.5 %collective-permute-start.30 = (bf16[256,512]{1,0:T(8,128)(2,1)S(1)}, bf16[256,512]{1,0:T(8,128)(2,1)S(1)}, u32[]{:S(2)}, u32[]{:S(2)}) collective-permute-start(bf16[256,512]{1,0:T(8,128)(2,1)S(1)} %add_convert_fusion.1), channel_id=1, source_target_pairs={{1,0},{2,1},{3,2},{4,3},{5,4},{6,5},{7,6},{8,7},{9,8},{10,9},{11,1... | collective-permute-start | bytes 786440 | tf_op jit(solution)/shard_map/ppermute | solution.py:48
  (10 other events, 87.5 us)

commit v5 on v4

--- a/solution.py
+++ b/solution.py
@@ -56,6 +56,7 @@
 def shards(query_stream, key_stream, value_stream, feat_taps, filt_taps, skip_bias, out_weight):
     filt_reach = filt_taps.shape[0] - 1
     feat_reach = feat_taps.shape[1] - 1
+    full_reach = filt_reach + feat_reach
     wide = lambda x: x.astype(jnp.float32)
     key_body = valid_conv(wide(key_stream), feat_taps[1])
     value_body = valid_conv(wide(value_stream), feat_taps[2])
@@ -64,6 +65,9 @@
         [gated_body[-filt_reach:], key_stream[-feat_reach:], value_stream[-feat_reach:], query_stream[-feat_reach:]], 0
     )
     incoming = shifted(outgoing, "ctx", 1)
+    query_body = valid_conv(wide(query_stream), feat_taps[0])
+    mixed_tail = valid_conv(wide(gated_body), filt_taps) + skip_bias[None, :] * wide(gated_body[filt_reach:])
+    product_tail = (query_body[filt_reach:] * mixed_tail).astype(jnp.bfloat16)
     gated_halo = incoming[:filt_reach]
     key_halo = incoming[filt_reach : filt_reach + feat_reach]
     value_halo = incoming[filt_reach + feat_reach : filt_reach + 2 * feat_reach]
@@ -71,11 +75,13 @@
     key_head = valid_conv(wide(jnp.concatenate([key_halo, key_stream[:feat_reach]], 0)), feat_taps[1])
     value_head = valid_conv(wide(jnp.concatenate([value_halo, value_stream[:feat_reach]], 0)), feat_taps[2])
     gated_head = (key_head * value_head).astype(jnp.bfloat16)
-    gated = jnp.concatenate([gated_halo, gated_head, gated_body], 0)
-    query_feat = valid_conv(wide(jnp.concatenate([query_halo, query_stream], 0)), feat_taps[0])
+    query_head = valid_conv(wide(jnp.concatenate([query_halo, query_stream[:feat_reach]], 0)), feat_taps[0])
+    gated = jnp.concatenate([gated_halo, gated_head, gated_body[: full_reach - feat_reach]], 0)
     own_gated = wide(gated[filt_reach:])
-    mixed = valid_conv(wide(gated), filt_taps) + skip_bias[None, :] * own_gated
-    product = (query_feat * mixed).astype(jnp.bfloat16)
+    mixed_head = valid_conv(wide(gated), filt_taps) + skip_bias[None, :] * own_gated
+    query_feat_head = jnp.concatenate([query_head, query_body[: full_reach - feat_reach]], 0)
+    product_head = (query_feat_head * mixed_head).astype(jnp.bfloat16)
+    product = jnp.concatenate([product_head, product_tail], 0)
     return line_reduce_scatter(product, out_weight, "tp")
 
 

time: 233 us -> 227 us (0.974)
  the two profiles are of different devices: /device:TPU:126 before, /device:TPU:414 now
where the time goes in v5:
time: 227 us; the launch traced here: 225 us
  waiting for transfers between devices  80 us (35%)
  starting transfers between devices  79.8 us (35%)
  matrix products  41.9 us (18%)
  other arithmetic  18.4 us (8%)
  local copies, waits for them, and re-layouts  3.77 us (2%)
    ppermute x15, starting transfers between devices, line_reduce_scatter(): from_right[chain] = lax.ppermute(send_left, axis, leftward)  63.2 us
    ppermute x15, waiting for transfers between devices, line_reduce_scatter(): from_right[chain] = lax.ppermute(send_left, axis, leftward)  50.8 us
    dot_general x31, matrix products, block(): term = jnp.dot(product, columns, preferred_element_type=jnp.float32)  41.9 us
    ppermute x1, waiting for transfers between devices, shifted(): return lax.ppermute(block, axis, route)  23 us
    ppermute x15, starting transfers between devices, line_reduce_scatter(): from_left[chain] = lax.ppermute(send_right, axis, rightward)  14.7 us
    convert_element_type x1, other arithmetic, shards(): product_head = (query_feat_head * mixed_head).astype(jnp.bfloat16)  7.07 us
    convert_element_type x1, other arithmetic, shards(): product_tail = (query_body[filt_reach:] * mixed_tail).astype(jnp.bfloat16)  6.91 us
    ppermute x15, waiting for transfers between devices, line_reduce_scatter(): from_left[chain] = lax.ppermute(send_right, axis, rightward)  6.23 us
  transfers between devices with their start and end apart: 31, of which 14 were waited for; matrix products, arithmetic and copies ran while one was open for 22% of the time, Pallas kernels for 0%

profile of v5, /device:TPU:414, one launch (start us, length us, event | category | flops | bytes accessed | tf_op | source)
XLA Modules:
  0.0 224.8 jit_solution(10175191715367501013)
XLA Ops:
  5.7 1.9 collective-permute-start
  9.2 6.9 %fusion.213 = bf16[123,512]{1,0:T(8,128)(2,1)S(1)} fusion(f32[250,512]{1,0:T(8,128)S(1)} %get-tuple-element.5, f32[512]{0:T(512)S(1)} %bitcast.211, f32[512]{0:T(512)S(1)} %bitcast.213, f32[512]{0:T(512)S(1)} %bitcast.217, f32[512]{0:T(512)S(1)} %bitcast.219, f32[512]{0:T(512)S(1)} %bitcast.221, f32[512]{0:T(512)S(1)} %bitcast.223, f32[512]{0:T(512)S(1)} %bitcast.225, ...), kind=kLoop, calls=%fused_computation.426 | loop fusion | flops 16373760 | bytes 33011712 | tf_op jit(solution)/shard_map/convert_element_type | solution.py:70
  16.2 23.0 %collective-permute-done = bf16[145,512]{1,0:T(8,128)(2,1)S(1)} collective-permute-done((bf16[145,512]{1,0:T(8,128)(2,1)S(1)}, bf16[145,512]{1,0:T(8,128)(2,1)S(1)}, u32[]{:S(2)}, u32[]{:S(2)}) %collective-permute-start) | collective-permute-done | bytes 148512 | tf_op jit(solution)/shard_map/ppermute | solution.py:10
  39.4 7.1 %fusion.83 = bf16[133,512]{1,0:T(8,128)(2,1)S(1)} fusion(f32[260,512]{1,0:T(8,128)S(1)} %maximum_convert_fusion, bf16[127,512]{1,0:T(8,128)(2,1)S(1)} %get-tuple-element.12, bf16[6,512]{1,0:T(8,128)(2,1)S(1)} %fusion.342, f32[512]{0:T(512)S(1)} %copy-done.2, f32[512]{0:T(512)S(1)} %bitcast.212, f32[512]{0:T(512)S(1)} %bitcast.214, f32[512]{0:T(512)S(1)} %bitcast.218, ...), kind=kLoop, calls=%fused_computation.165 | loop fusion | flops 17977344 | bytes 35674112 | tf_op jit(solution)/shard_map/convert_element_type | solution.py:83
  59.4 23.0 %collective-permute-done.18 = bf16[256,512]{1,0:T(8,128)(2,1)S(1)} collective-permute-done((bf16[256,512]{1,0:T(8,128)(2,1)S(1)}, bf16[256,512]{1,0:T(8,128)(2,1)S(1)}, u32[]{:S(2)}, u32[]{:S(2)}) %collective-permute-start.18) | collective-permute-done | bytes 262176 | tf_op jit(solution)/shard_map/ppermute | solution.py:48
  88.0 4.9 %collective-permute-done.19 = bf16[256,512]{1,0:T(8,128)(2,1)S(1)} collective-permute-done((bf16[256,512]{1,0:T(8,128)(2,1)S(1)}, bf16[256,512]{1,0:T(8,128)(2,1)S(1)}, u32[]{:S(2)}, u32[]{:S(2)}) %collective-permute-start.19) | collective-permute-done | bytes 262176 | tf_op jit(solution)/shard_map/ppermute | solution.py:48
  94.3 3.4 %collective-permute-start.20 = (bf16[256,512]{1,0:T(8,128)(2,1)S(1)}, bf16[256,512]{1,0:T(8,128)(2,1)S(1)}, u32[]{:S(2)}, u32[]{:S(2)}) collective-permute-start(bf16[256,512]{1,0:T(8,128)(2,1)S(1)} %add_convert_fusion.11), channel_id=1, source_target_pairs={{11,10},{12,11},{13,12},{14,13},{15,14},{27,26},{28,27},{29,28},{3... | collective-permute-start | bytes 786440 | tf_op jit(solution)/shard_map/ppermute | solution.py:48
  99.8 2.8 %collective-permute-done.20 = bf16[256,512]{1,0:T(8,128)(2,1)S(1)} collective-permute-done((bf16[256,512]{1,0:T(8,128)(2,1)S(1)}, bf16[256,512]{1,0:T(8,128)(2,1)S(1)}, u32[]{:S(2)}, u32[]{:S(2)}) %collective-permute-start.20) | collective-permute-done | bytes 262176 | tf_op jit(solution)/shard_map/ppermute | solution.py:48
  103.9 4.8 %collective-permute-start.21 = (bf16[256,512]{1,0:T(8,128)(2,1)S(1)}, bf16[256,512]{1,0:T(8,128)(2,1)S(1)}, u32[]{:S(2)}, u32[]{:S(2)}) collective-permute-start(bf16[256,512]{1,0:T(8,128)(2,1)S(1)} %add_convert_fusion.10), channel_id=1, source_target_pairs={{10,9},{11,10},{12,11},{13,12},{14,13},{15,14},{26,25},{27,26},{28... | collective-permute-start | bytes 786440 | tf_op jit(solution)/shard_map/ppermute | solution.py:48
  114.0 5.6 %collective-permute-start.22 = (bf16[256,512]{1,0:T(8,128)(2,1)S(1)}, bf16[256,512]{1,0:T(8,128)(2,1)S(1)}, u32[]{:S(2)}, u32[]{:S(2)}) collective-permute-start(bf16[256,512]{1,0:T(8,128)(2,1)S(1)} %add_convert_fusion.9), channel_id=1, source_target_pairs={{9,8},{10,9},{11,10},{12,11},{13,12},{14,13},{15,14},{25,24},{26,2... | collective-permute-start | bytes 786440 | tf_op jit(solution)/shard_map/ppermute | solution.py:48
  124.8 5.6 %collective-permute-start.23 = (bf16[256,512]{1,0:T(8,128)(2,1)S(1)}, bf16[256,512]{1,0:T(8,128)(2,1)S(1)}, u32[]{:S(2)}, u32[]{:S(2)}) collective-permute-start(bf16[256,512]{1,0:T(8,128)(2,1)S(1)} %add_convert_fusion.8), channel_id=1, source_target_pairs={{8,7},{9,8},{10,9},{11,10},{12,11},{13,12},{14,13},{15,14},{24,23}... | collective-permute-start | bytes 786440 | tf_op jit(solution)/shard_map/ppermute | solution.py:48
  135.6 5.6 %collective-permute-start.24 = (bf16[256,512]{1,0:T(8,128)(2,1)S(1)}, bf16[256,512]{1,0:T(8,128)(2,1)S(1)}, u32[]{:S(2)}, u32[]{:S(2)}) collective-permute-start(bf16[256,512]{1,0:T(8,128)(2,1)S(1)} %add_convert_fusion.7), channel_id=1, source_target_pairs={{7,6},{8,7},{9,8},{10,9},{11,10},{12,11},{13,12},{14,13},{15,14},{... | collective-permute-start | bytes 786440 | tf_op jit(solution)/shard_map/ppermute | solution.py:48
  146.4 5.6 %collective-permute-start.25 = (bf16[256,512]{1,0:T(8,128)(2,1)S(1)}, bf16[256,512]{1,0:T(8,128)(2,1)S(1)}, u32[]{:S(2)}, u32[]{:S(2)}) collective-permute-start(bf16[256,512]{1,0:T(8,128)(2,1)S(1)} %add_convert_fusion.6), channel_id=1, source_target_pairs={{6,5},{7,6},{8,7},{9,8},{10,9},{11,10},{12,11},{13,12},{14,13},{15... | collective-permute-start | bytes 786440 | tf_op jit(solution)/shard_map/ppermute | solution.py:48
  154.2 2.9 %collective-permute-done.25 = bf16[256,512]{1,0:T(8,128)(2,1)S(1)} collective-permute-done((bf16[256,512]{1,0:T(8,128)(2,1)S(1)}, bf16[256,512]{1,0:T(8,128)(2,1)S(1)}, u32[]{:S(2)}, u32[]{:S(2)}) %collective-permute-start.25) | collective-permute-done | bytes 262176 | tf_op jit(solution)/shard_map/ppermute | solution.py:48
  158.4 5.6 %collective-permute-start.26 = (bf16[256,512]{1,0:T(8,128)(2,1)S(1)}, bf16[256,512]{1,0:T(8,128)(2,1)S(1)}, u32[]{:S(2)}, u32[]{:S(2)}) collective-permute-start(bf16[256,512]{1,0:T(8,128)(2,1)S(1)} %add_convert_fusion.5), channel_id=1, source_target_pairs={{5,4},{6,5},{7,6},{8,7},{9,8},{10,9},{11,10},{12,11},{13,12},{14,1... | collective-permute-start | bytes 786440 | tf_op jit(solution)/shard_map/ppermute | solution.py:48
  166.1 4.1 %collective-permute-done.26 = bf16[256,512]{1,0:T(8,128)(2,1)S(1)} collective-permute-done((bf16[256,512]{1,0:T(8,128)(2,1)S(1)}, bf16[256,512]{1,0:T(8,128)(2,1)S(1)}, u32[]{:S(2)}, u32[]{:S(2)}) %collective-permute-start.26) | collective-permute-done | bytes 262176 | tf_op jit(solution)/shard_map/ppermute | solution.py:48
  171.6 5.6 %collective-permute-start.27 = (bf16[256,512]{1,0:T(8,128)(2,1)S(1)}, bf16[256,512]{1,0:T(8,128)(2,1)S(1)}, u32[]{:S(2)}, u32[]{:S(2)}) collective-permute-start(bf16[256,512]{1,0:T(8,128)(2,1)S(1)} %add_convert_fusion.4), channel_id=1, source_target_pairs={{4,3},{5,4},{6,5},{7,6},{8,7},{9,8},{10,9},{11,10},{12,11},{13,12}... | collective-permute-start | bytes 786440 | tf_op jit(solution)/shard_map/ppermute | solution.py:48
  179.9 3.3 %collective-permute-done.27 = bf16[256,512]{1,0:T(8,128)(2,1)S(1)} collective-permute-done((bf16[256,512]{1,0:T(8,128)(2,1)S(1)}, bf16[256,512]{1,0:T(8,128)(2,1)S(1)}, u32[]{:S(2)}, u32[]{:S(2)}) %collective-permute-start.27) | collective-permute-done | bytes 262176 | tf_op jit(solution)/shard_map/ppermute | solution.py:48
  184.5 5.6 %collective-permute-start.28 = (bf16[256,512]{1,0:T(8,128)(2,1)S(1)}, bf16[256,512]{1,0:T(8,128)(2,1)S(1)}, u32[]{:S(2)}, u32[]{:S(2)}) collective-permute-start(bf16[256,512]{1,0:T(8,128)(2,1)S(1)} %add_convert_fusion.3), channel_id=1, source_target_pairs={{3,2},{4,3},{5,4},{6,5},{7,6},{8,7},{9,8},{10,9},{11,10},{12,11},{... | collective-permute-start | bytes 786440 | tf_op jit(solution)/shard_map/ppermute | solution.py:48
  196.7 5.6 %collective-permute-start.29 = (bf16[256,512]{1,0:T(8,128)(2,1)S(1)}, bf16[256,512]{1,0:T(8,128)(2,1)S(1)}, u32[]{:S(2)}, u32[]{:S(2)}) collective-permute-start(bf16[256,512]{1,0:T(8,128)(2,1)S(1)} %add_convert_fusion.2), channel_id=1, source_target_pairs={{2,1},{3,2},{4,3},{5,4},{6,5},{7,6},{8,7},{9,8},{10,9},{11,10},{12... | collective-permute-start | bytes 786440 | tf_op jit(solution)/shard_map/ppermute | solution.py:48
  203.7 1.9 collective-permute-start.14
  207.5 5.6 %collective-permute-start.30 = (bf16[256,512]{1,0:T(8,128)(2,1)S(1)}, bf16[256,512]{1,0:T(8,128)(2,1)S(1)}, u32[]{:S(2)}, u32[]{:S(2)}) collective-permute-start(bf16[256,512]{1,0:T(8,128)(2,1)S(1)} %add_convert_fusion.1), channel_id=1, source_target_pairs={{1,0},{2,1},{3,2},{4,3},{5,4},{6,5},{7,6},{8,7},{9,8},{10,9},{11,1... | collective-permute-start | bytes 786440 | tf_op jit(solution)/shard_map/ppermute | solution.py:48
  214.5 1.9 collective-permute-start.15
  217.8 6.2 %collective-permute-done.15 = bf16[256,512]{1,0:T(8,128)(2,1)S(1)} collective-permute-done((bf16[256,512]{1,0:T(8,128)(2,1)S(1)}, bf16[256,512]{1,0:T(8,128)(2,1)S(1)}, u32[]{:S(2)}, u32[]{:S(2)}) %collective-permute-start.15) | collective-permute-done | bytes 262176 | tf_op jit(solution)/shard_map/ppermute | solution.py:47
  (105 shorter events, 75.2 us)
Async XLA Ops:
  5.7 33.4 %collective-permute-start = (bf16[145,512]{1,0:T(8,128)(2,1)S(1)}, bf16[145,512]{1,0:T(8,128)(2,1)S(1)}, u32[]{:S(2)}, u32[]{:S(2)}) collective-permute-start(bf16[145,512]{1,0:T(8,128)(2,1)S(1)} %pad_maximum_fusion.2), channel_id=1, source_target_pairs={{0,16},{16,32},{32,48},{48,64},{64,80},{80,96},{96,112},{112,128},... | collective-permute-start | bytes 445448 | tf_op jit(solution)/shard_map/ppermute | solution.py:10
  56.1 26.4 %collective-permute-start.18 = (bf16[256,512]{1,0:T(8,128)(2,1)S(1)}, bf16[256,512]{1,0:T(8,128)(2,1)S(1)}, u32[]{:S(2)}, u32[]{:S(2)}) collective-permute-start(bf16[256,512]{1,0:T(8,128)(2,1)S(1)} %add_convert_fusion.13), channel_id=1, source_target_pairs={{13,12},{14,13},{15,14},{29,28},{30,29},{31,30},{45,44},{46,45},{4... | collective-permute-start | bytes 786440 | tf_op jit(solution)/shard_map/ppermute | solution.py:48
  58.7 27.0 %collective-permute-start.3 = (bf16[256,512]{1,0:T(8,128)(2,1)S(1)}, bf16[256,512]{1,0:T(8,128)(2,1)S(1)}, u32[]{:S(2)}, u32[]{:S(2)}) collective-permute-start(bf16[256,512]{1,0:T(8,128)(2,1)S(1)} %add_convert_fusion.27), channel_id=1, source_target_pairs={{0,1},{1,2},{2,3},{16,17},{17,18},{18,19},{32,33},{33,34},{34,35},... | collective-permute-start | bytes 786440 | tf_op jit(solution)/shard_map/ppermute | solution.py:47
  87.1 10.6 %collective-permute-start.4 = (bf16[256,512]{1,0:T(8,128)(2,1)S(1)}, bf16[256,512]{1,0:T(8,128)(2,1)S(1)}, u32[]{:S(2)}, u32[]{:S(2)}) collective-permute-start(bf16[256,512]{1,0:T(8,128)(2,1)S(1)} %add_convert_fusion.26), channel_id=1, source_target_pairs={{0,1},{1,2},{2,3},{3,4},{16,17},{17,18},{18,19},{19,20},{32,33},{3... | collective-permute-start | bytes 786440 | tf_op jit(solution)/shard_map/ppermute | solution.py:47
  99.1 9.7 %collective-permute-start.5 = (bf16[256,512]{1,0:T(8,128)(2,1)S(1)}, bf16[256,512]{1,0:T(8,128)(2,1)S(1)}, u32[]{:S(2)}, u32[]{:S(2)}) collective-permute-start(bf16[256,512]{1,0:T(8,128)(2,1)S(1)} %add_convert_fusion.25), channel_id=1, source_target_pairs={{0,1},{1,2},{2,3},{3,4},{4,5},{16,17},{17,18},{18,19},{19,20},{20,... | collective-permute-start | bytes 786440 | tf_op jit(solution)/shard_map/ppermute | solution.py:47
  110.1 9.5 %collective-permute-start.6 = (bf16[256,512]{1,0:T(8,128)(2,1)S(1)}, bf16[256,512]{1,0:T(8,128)(2,1)S(1)}, u32[]{:S(2)}, u32[]{:S(2)}) collective-permute-start(bf16[256,512]{1,0:T(8,128)(2,1)S(1)} %add_convert_fusion.24), channel_id=1, source_target_pairs={{0,1},{1,2},{2,3},{3,4},{4,5},{5,6},{16,17},{17,18},{18,19},{19,20... | collective-permute-start | bytes 786440 | tf_op jit(solution)/shard_map/ppermute | solution.py:47
  114.0 9.5 %collective-permute-start.22 = (bf16[256,512]{1,0:T(8,128)(2,1)S(1)}, bf16[256,512]{1,0:T(8,128)(2,1)S(1)}, u32[]{:S(2)}, u32[]{:S(2)}) collective-permute-start(bf16[256,512]{1,0:T(8,128)(2,1)S(1)} %add_convert_fusion.9), channel_id=1, source_target_pairs={{9,8},{10,9},{11,10},{12,11},{13,12},{14,13},{15,14},{25,24},{26,2... | collective-permute-start | bytes 786440 | tf_op jit(solution)/shard_map/ppermute | solution.py:48
  120.9 9.5 %collective-permute-start.7 = (bf16[256,512]{1,0:T(8,128)(2,1)S(1)}, bf16[256,512]{1,0:T(8,128)(2,1)S(1)}, u32[]{:S(2)}, u32[]{:S(2)}) collective-permute-start(bf16[256,512]{1,0:T(8,128)(2,1)S(1)} %add_convert_fusion.23), channel_id=1, source_target_pairs={{0,1},{1,2},{2,3},{3,4},{4,5},{5,6},{6,7},{16,17},{17,18},{18,19},... | collective-permute-start | bytes 786440 | tf_op jit(solution)/shard_map/ppermute | solution.py:47
  124.8 9.5 %collective-permute-start.23 = (bf16[256,512]{1,0:T(8,128)(2,1)S(1)}, bf16[256,512]{1,0:T(8,128)(2,1)S(1)}, u32[]{:S(2)}, u32[]{:S(2)}) collective-permute-start(bf16[256,512]{1,0:T(8,128)(2,1)S(1)} %add_convert_fusion.8), channel_id=1, source_target_pairs={{8,7},{9,8},{10,9},{11,10},{12,11},{13,12},{14,13},{15,14},{24,23}... | collective-permute-start | bytes 786440 | tf_op jit(solution)/shard_map/ppermute | solution.py:48
  131.8 9.5 %collective-permute-start.8 = (bf16[256,512]{1,0:T(8,128)(2,1)S(1)}, bf16[256,512]{1,0:T(8,128)(2,1)S(1)}, u32[]{:S(2)}, u32[]{:S(2)}) collective-permute-start(bf16[256,512]{1,0:T(8,128)(2,1)S(1)} %add_convert_fusion.22), channel_id=1, source_target_pairs={{0,1},{1,2},{2,3},{3,4},{4,5},{5,6},{6,7},{7,8},{16,17},{17,18},{1... | collective-permute-start | bytes 786440 | tf_op jit(solution)/shard_map/ppermute | solution.py:47
  135.6 9.5 %collective-permute-start.24 = (bf16[256,512]{1,0:T(8,128)(2,1)S(1)}, bf16[256,512]{1,0:T(8,128)(2,1)S(1)}, u32[]{:S(2)}, u32[]{:S(2)}) collective-permute-start(bf16[256,512]{1,0:T(8,128)(2,1)S(1)} %add_convert_fusion.7), channel_id=1, source_target_pairs={{7,6},{8,7},{9,8},{10,9},{11,10},{12,11},{13,12},{14,13},{15,14},{... | collective-permute-start | bytes 786440 | tf_op jit(solution)/shard_map/ppermute | solution.py:48
  142.6 9.5 %collective-permute-start.9 = (bf16[256,512]{1,0:T(8,128)(2,1)S(1)}, bf16[256,512]{1,0:T(8,128)(2,1)S(1)}, u32[]{:S(2)}, u32[]{:S(2)}) collective-permute-start(bf16[256,512]{1,0:T(8,128)(2,1)S(1)} %add_convert_fusion.21), channel_id=1, source_target_pairs={{0,1},{1,2},{2,3},{3,4},{4,5},{5,6},{6,7},{7,8},{8,9},{16,17},{17,... | collective-permute-start | bytes 786440 | tf_op jit(solution)/shard_map/ppermute | solution.py:47
  146.4 10.6 %collective-permute-start.25 = (bf16[256,512]{1,0:T(8,128)(2,1)S(1)}, bf16[256,512]{1,0:T(8,128)(2,1)S(1)}, u32[]{:S(2)}, u32[]{:S(2)}) collective-permute-start(bf16[256,512]{1,0:T(8,128)(2,1)S(1)} %add_convert_fusion.6), channel_id=1, source_target_pairs={{6,5},{7,6},{8,7},{9,8},{10,9},{11,10},{12,11},{13,12},{14,13},{15... | collective-permute-start | bytes 786440 | tf_op jit(solution)/shard_map/ppermute | solution.py:48
  153.5 10.6 %collective-permute-start.10 = (bf16[256,512]{1,0:T(8,128)(2,1)S(1)}, bf16[256,512]{1,0:T(8,128)(2,1)S(1)}, u32[]{:S(2)}, u32[]{:S(2)}) collective-permute-start(bf16[256,512]{1,0:T(8,128)(2,1)S(1)} %add_convert_fusion.20), channel_id=1, source_target_pairs={{0,1},{1,2},{2,3},{3,4},{4,5},{5,6},{6,7},{7,8},{8,9},{9,10},{16,1... | collective-permute-start | bytes 786440 | tf_op jit(solution)/shard_map/ppermute | solution.py:47
  158.4 11.8 %collective-permute-start.26 = (bf16[256,512]{1,0:T(8,128)(2,1)S(1)}, bf16[256,512]{1,0:T(8,128)(2,1)S(1)}, u32[]{:S(2)}, u32[]{:S(2)}) collective-permute-start(bf16[256,512]{1,0:T(8,128)(2,1)S(1)} %add_convert_fusion.5), channel_id=1, source_target_pairs={{5,4},{6,5},{7,6},{8,7},{9,8},{10,9},{11,10},{12,11},{13,12},{14,1... | collective-permute-start | bytes 786440 | tf_op jit(solution)/shard_map/ppermute | solution.py:48
  165.4 11.8 %collective-permute-start.11 = (bf16[256,512]{1,0:T(8,128)(2,1)S(1)}, bf16[256,512]{1,0:T(8,128)(2,1)S(1)}, u32[]{:S(2)}, u32[]{:S(2)}) collective-permute-start(bf16[256,512]{1,0:T(8,128)(2,1)S(1)} %add_convert_fusion.19), channel_id=1, source_target_pairs={{0,1},{1,2},{2,3},{3,4},{4,5},{5,6},{6,7},{7,8},{8,9},{9,10},{10,1... | collective-permute-start | bytes 786440 | tf_op jit(solution)/shard_map/ppermute | solution.py:47
  171.6 11.6 %collective-permute-start.27 = (bf16[256,512]{1,0:T(8,128)(2,1)S(1)}, bf16[256,512]{1,0:T(8,128)(2,1)S(1)}, u32[]{:S(2)}, u32[]{:S(2)}) collective-permute-start(bf16[256,512]{1,0:T(8,128)(2,1)S(1)} %add_convert_fusion.4), channel_id=1, source_target_pairs={{4,3},{5,4},{6,5},{7,6},{8,7},{9,8},{10,9},{11,10},{12,11},{13,12}... | collective-permute-start | bytes 786440 | tf_op jit(solution)/shard_map/ppermute | solution.py:48
  178.5 11.6 %collective-permute-start.12 = (bf16[256,512]{1,0:T(8,128)(2,1)S(1)}, bf16[256,512]{1,0:T(8,128)(2,1)S(1)}, u32[]{:S(2)}, u32[]{:S(2)}) collective-permute-start(bf16[256,512]{1,0:T(8,128)(2,1)S(1)} %add_convert_fusion.18), channel_id=1, source_target_pairs={{0,1},{1,2},{2,3},{3,4},{4,5},{5,6},{6,7},{7,8},{8,9},{9,10},{10,1... | collective-permute-start | bytes 786440 | tf_op jit(solution)/shard_map/ppermute | solution.py:47
  184.5 10.8 %collective-permute-start.28 = (bf16[256,512]{1,0:T(8,128)(2,1)S(1)}, bf16[256,512]{1,0:T(8,128)(2,1)S(1)}, u32[]{:S(2)}, u32[]{:S(2)}) collective-permute-start(bf16[256,512]{1,0:T(8,128)(2,1)S(1)} %add_convert_fusion.3), channel_id=1, source_target_pairs={{3,2},{4,3},{5,4},{6,5},{7,6},{8,7},{9,8},{10,9},{11,10},{12,11},{... | collective-permute-start | bytes 786440 | tf_op jit(solution)/shard_map/ppermute | solution.py:48
  191.5 10.8 %collective-permute-start.13 = (bf16[256,512]{1,0:T(8,128)(2,1)S(1)}, bf16[256,512]{1,0:T(8,128)(2,1)S(1)}, u32[]{:S(2)}, u32[]{:S(2)}) collective-permute-start(bf16[256,512]{1,0:T(8,128)(2,1)S(1)} %add_convert_fusion.17), channel_id=1, source_target_pairs={{0,1},{1,2},{2,3},{3,4},{4,5},{5,6},{6,7},{7,8},{8,9},{9,10},{10,1... | collective-permute-start | bytes 786440 | tf_op jit(solution)/shard_map/ppermute | solution.py:47
  196.7 9.5 %collective-permute-start.29 = (bf16[256,512]{1,0:T(8,128)(2,1)S(1)}, bf16[256,512]{1,0:T(8,128)(2,1)S(1)}, u32[]{:S(2)}, u32[]{:S(2)}) collective-permute-start(bf16[256,512]{1,0:T(8,128)(2,1)S(1)} %add_convert_fusion.2), channel_id=1, source_target_pairs={{2,1},{3,2},{4,3},{5,4},{6,5},{7,6},{8,7},{9,8},{10,9},{11,10},{12... | collective-permute-start | bytes 786440 | tf_op jit(solution)/shard_map/ppermute | solution.py:48
  203.7 9.5 %collective-permute-start.14 = (bf16[256,512]{1,0:T(8,128)(2,1)S(1)}, bf16[256,512]{1,0:T(8,128)(2,1)S(1)}, u32[]{:S(2)}, u32[]{:S(2)}) collective-permute-start(bf16[256,512]{1,0:T(8,128)(2,1)S(1)} %add_convert_fusion.16), channel_id=1, source_target_pairs={{0,1},{1,2},{2,3},{3,4},{4,5},{5,6},{6,7},{7,8},{8,9},{9,10},{10,1... | collective-permute-start | bytes 786440 | tf_op jit(solution)/shard_map/ppermute | solution.py:47
  207.5 10.3 %collective-permute-start.30 = (bf16[256,512]{1,0:T(8,128)(2,1)S(1)}, bf16[256,512]{1,0:T(8,128)(2,1)S(1)}, u32[]{:S(2)}, u32[]{:S(2)}) collective-permute-start(bf16[256,512]{1,0:T(8,128)(2,1)S(1)} %add_convert_fusion.1), channel_id=1, source_target_pairs={{1,0},{2,1},{3,2},{4,3},{5,4},{6,5},{7,6},{8,7},{9,8},{10,9},{11,1... | collective-permute-start | bytes 786440 | tf_op jit(solution)/shard_map/ppermute | solution.py:48
  214.5 9.5 %collective-permute-start.15 = (bf16[256,512]{1,0:T(8,128)(2,1)S(1)}, bf16[256,512]{1,0:T(8,128)(2,1)S(1)}, u32[]{:S(2)}, u32[]{:S(2)}) collective-permute-start(bf16[256,512]{1,0:T(8,128)(2,1)S(1)} %add_convert_fusion.15), channel_id=1, source_target_pairs={{0,1},{1,2},{2,3},{3,4},{4,5},{5,6},{6,7},{7,8},{8,9},{9,10},{10,1... | collective-permute-start | bytes 786440 | tf_op jit(solution)/shard_map/ppermute | solution.py:47
  (10 other events, 59.5 us)

commit v6 on v5

--- a/solution.py
+++ b/solution.py
@@ -32,8 +32,8 @@
     def block(j, chain):
         j = jnp.clip(j, 0, n - 1)
         columns = lax.dynamic_slice_in_dim(out_weight, j * width + chain * piece, piece, 1)
-        term = jnp.dot(product, columns, preferred_element_type=jnp.float32)
-        return term.astype(jnp.bfloat16).astype(jnp.float32)
+        term = jnp.dot(product, columns, preferred_element_type=jnp.float32).astype(jnp.bfloat16)
+        return lax.optimization_barrier(term).astype(jnp.float32)
 
     zeros = jnp.zeros((product.shape[0], piece), jnp.bfloat16)
     from_left = [zeros] * chains

time: 227 us -> 212 us (0.934)
  the two profiles are of different devices: /device:TPU:414 before, /device:TPU:376 now
where the time goes in v6:
time: 212 us; the launch traced here: 210 us
  waiting for transfers between devices  119 us (56%)
  starting transfers between devices  55.3 us (26%)
  other arithmetic  20.3 us (10%)
  matrix products  10.9 us (5%)
  local copies, waits for them, and re-layouts  3.78 us (2%)
    ppermute x15, waiting for transfers between devices, line_reduce_scatter(): from_right[chain] = lax.ppermute(send_left, axis, leftward)  102 us
    ppermute x15, starting transfers between devices, line_reduce_scatter(): from_left[chain] = lax.ppermute(send_right, axis, rightward)  29 us
    ppermute x15, starting transfers between devices, line_reduce_scatter(): from_right[chain] = lax.ppermute(send_left, axis, leftward)  24.4 us
    ppermute x1, waiting for transfers between devices, shifted(): return lax.ppermute(block, axis, route)  17.3 us
    dot_general x31, matrix products, block(): jnp.dot(product, columns, preferred_element_type=jnp.float32)  10.9 us
    convert_element_type x1, other arithmetic, shards(): product_head = (query_feat_head * mixed_head).astype(jnp.bfloat16)  7.08 us
    convert_element_type x1, other arithmetic, shards(): product_tail = (query_body[filt_reach:] * mixed_tail).astype(jnp.bfloat16)  6.92 us
  transfers between devices with their start and end apart: 31, of which 13 were waited for; matrix products, arithmetic and copies ran while one was open for 10% of the time, Pallas kernels for 0%

profile of v6, /device:TPU:376, one launch (start us, length us, event | category | flops | bytes accessed | tf_op | source)
XLA Modules:
  0.0 210.3 jit_solution(299097787111141585)
XLA Ops:
  5.7 1.9 collective-permute-start
  9.2 6.9 %fusion.184 = bf16[123,512]{1,0:T(8,128)(2,1)S(1)} fusion(f32[250,512]{1,0:T(8,128)S(1)} %get-tuple-element.5, f32[512]{0:T(512)S(1)} %bitcast.439, f32[512]{0:T(512)S(1)} %bitcast.441, f32[512]{0:T(512)S(1)} %bitcast.265, f32[512]{0:T(512)S(1)} %bitcast.267, f32[512]{0:T(512)S(1)} %bitcast.269, f32[512]{0:T(512)S(1)} %bitcast.271, f32[512]{0:T(512)S(1)} %bitcast.273, ...), kind=kLoop, calls=%fused_computation.397 | loop fusion | flops 16373760 | bytes 33011712 | tf_op jit(solution)/shard_map/convert_element_type | solution.py:70
  16.3 17.3 %collective-permute-done = bf16[145,512]{1,0:T(8,128)(2,1)S(1)} collective-permute-done((bf16[145,512]{1,0:T(8,128)(2,1)S(1)}, bf16[145,512]{1,0:T(8,128)(2,1)S(1)}, u32[]{:S(2)}, u32[]{:S(2)}) %collective-permute-start) | collective-permute-done | bytes 148512 | tf_op jit(solution)/shard_map/ppermute | solution.py:10
  33.9 7.1 %fusion.54 = bf16[133,512]{1,0:T(8,128)(2,1)S(1)} fusion(f32[260,512]{1,0:T(8,128)S(1)} %maximum_convert_fusion, bf16[127,512]{1,0:T(8,128)(2,1)S(1)} %get-tuple-element.12, bf16[6,512]{1,0:T(8,128)(2,1)S(1)} %fusion.313, f32[512]{0:T(512)S(1)} %copy-done.2, f32[512]{0:T(512)S(1)} %bitcast.440, f32[512]{0:T(512)S(1)} %bitcast.442, f32[512]{0:T(512)S(1)} %bitcast.266, ...), kind=kLoop, calls=%fused_computation.136 | loop fusion | flops 17977344 | bytes 35674112 | tf_op jit(solution)/shard_map/convert_element_type | solution.py:83
  55.0 42.2 %collective-permute-done.19 = bf16[256,512]{1,0:T(8,128)(2,1)S(1)} collective-permute-done((bf16[256,512]{1,0:T(8,128)(2,1)S(1)}, bf16[256,512]{1,0:T(8,128)(2,1)S(1)}, u32[]{:S(2)}, u32[]{:S(2)}) %collective-permute-start.19) | collective-permute-done | bytes 262176 | tf_op jit(solution)/shard_map/ppermute | solution.py:48
  97.3 1.9 collective-permute-start.20
  100.3 7.6 %collective-permute-done.20 = bf16[256,512]{1,0:T(8,128)(2,1)S(1)} collective-permute-done((bf16[256,512]{1,0:T(8,128)(2,1)S(1)}, bf16[256,512]{1,0:T(8,128)(2,1)S(1)}, u32[]{:S(2)}, u32[]{:S(2)}) %collective-permute-start.20) | collective-permute-done | bytes 262176 | tf_op jit(solution)/shard_map/ppermute | solution.py:48
  108.0 1.9 collective-permute-start.21
  111.0 6.7 %collective-permute-done.21 = bf16[256,512]{1,0:T(8,128)(2,1)S(1)} collective-permute-done((bf16[256,512]{1,0:T(8,128)(2,1)S(1)}, bf16[256,512]{1,0:T(8,128)(2,1)S(1)}, u32[]{:S(2)}, u32[]{:S(2)}) %collective-permute-start.21) | collective-permute-done | bytes 262176 | tf_op jit(solution)/shard_map/ppermute | solution.py:48
  117.8 1.9 collective-permute-start.22
  120.8 6.5 %collective-permute-done.22 = bf16[256,512]{1,0:T(8,128)(2,1)S(1)} collective-permute-done((bf16[256,512]{1,0:T(8,128)(2,1)S(1)}, bf16[256,512]{1,0:T(8,128)(2,1)S(1)}, u32[]{:S(2)}, u32[]{:S(2)}) %collective-permute-start.22) | collective-permute-done | bytes 262176 | tf_op jit(solution)/shard_map/ppermute | solution.py:48
  130.4 6.5 %collective-permute-done.23 = bf16[256,512]{1,0:T(8,128)(2,1)S(1)} collective-permute-done((bf16[256,512]{1,0:T(8,128)(2,1)S(1)}, bf16[256,512]{1,0:T(8,128)(2,1)S(1)}, u32[]{:S(2)}, u32[]{:S(2)}) %collective-permute-start.23) | collective-permute-done | bytes 262176 | tf_op jit(solution)/shard_map/ppermute | solution.py:48
  139.9 6.6 %collective-permute-done.24 = bf16[256,512]{1,0:T(8,128)(2,1)S(1)} collective-permute-done((bf16[256,512]{1,0:T(8,128)(2,1)S(1)}, bf16[256,512]{1,0:T(8,128)(2,1)S(1)}, u32[]{:S(2)}, u32[]{:S(2)}) %collective-permute-start.24) | collective-permute-done | bytes 262176 | tf_op jit(solution)/shard_map/ppermute | solution.py:48
  150.2 7.1 %collective-permute-done.25 = bf16[256,512]{1,0:T(8,128)(2,1)S(1)} collective-permute-done((bf16[256,512]{1,0:T(8,128)(2,1)S(1)}, bf16[256,512]{1,0:T(8,128)(2,1)S(1)}, u32[]{:S(2)}, u32[]{:S(2)}) %collective-permute-start.25) | collective-permute-done | bytes 262176 | tf_op jit(solution)/shard_map/ppermute | solution.py:48
  159.7 5.1 %collective-permute-start.12 = (bf16[256,512]{1,0:T(8,128)(2,1)S(1)}, bf16[256,512]{1,0:T(8,128)(2,1)S(1)}, u32[]{:S(2)}, u32[]{:S(2)}) collective-permute-start(bf16[256,512]{1,0:T(8,128)(2,1)S(1)} %add_convert_fusion.18), channel_id=1, source_target_pairs={{0,1},{1,2},{2,3},{3,4},{4,5},{5,6},{6,7},{7,8},{8,9},{9,10},{10,1... | collective-permute-start | bytes 786440 | tf_op jit(solution)/shard_map/ppermute | solution.py:47
  164.8 4.5 %collective-permute-done.26 = bf16[256,512]{1,0:T(8,128)(2,1)S(1)} collective-permute-done((bf16[256,512]{1,0:T(8,128)(2,1)S(1)}, bf16[256,512]{1,0:T(8,128)(2,1)S(1)}, u32[]{:S(2)}, u32[]{:S(2)}) %collective-permute-start.26) | collective-permute-done | bytes 262176 | tf_op jit(solution)/shard_map/ppermute | solution.py:48
  171.7 5.3 %collective-permute-start.13 = (bf16[256,512]{1,0:T(8,128)(2,1)S(1)}, bf16[256,512]{1,0:T(8,128)(2,1)S(1)}, u32[]{:S(2)}, u32[]{:S(2)}) collective-permute-start(bf16[256,512]{1,0:T(8,128)(2,1)S(1)} %add_convert_fusion.17), channel_id=1, source_target_pairs={{0,1},{1,2},{2,3},{3,4},{4,5},{5,6},{6,7},{7,8},{8,9},{9,10},{10,1... | collective-permute-start | bytes 786440 | tf_op jit(solution)/shard_map/ppermute | solution.py:47
  177.0 3.8 %collective-permute-done.27 = bf16[256,512]{1,0:T(8,128)(2,1)S(1)} collective-permute-done((bf16[256,512]{1,0:T(8,128)(2,1)S(1)}, bf16[256,512]{1,0:T(8,128)(2,1)S(1)}, u32[]{:S(2)}, u32[]{:S(2)}) %collective-permute-start.27) | collective-permute-done | bytes 262176 | tf_op jit(solution)/shard_map/ppermute | solution.py:48
  183.2 5.1 %collective-permute-start.14 = (bf16[256,512]{1,0:T(8,128)(2,1)S(1)}, bf16[256,512]{1,0:T(8,128)(2,1)S(1)}, u32[]{:S(2)}, u32[]{:S(2)}) collective-permute-start(bf16[256,512]{1,0:T(8,128)(2,1)S(1)} %add_convert_fusion.16), channel_id=1, source_target_pairs={{0,1},{1,2},{2,3},{3,4},{4,5},{5,6},{6,7},{7,8},{8,9},{9,10},{10,1... | collective-permute-start | bytes 786440 | tf_op jit(solution)/shard_map/ppermute | solution.py:47
  188.4 2.0 collective-permute-done.28
  192.8 5.1 %collective-permute-start.15 = (bf16[256,512]{1,0:T(8,128)(2,1)S(1)}, bf16[256,512]{1,0:T(8,128)(2,1)S(1)}, u32[]{:S(2)}, u32[]{:S(2)}) collective-permute-start(bf16[256,512]{1,0:T(8,128)(2,1)S(1)} %add_convert_fusion.15), channel_id=1, source_target_pairs={{0,1},{1,2},{2,3},{3,4},{4,5},{5,6},{6,7},{7,8},{8,9},{9,10},{10,1... | collective-permute-start | bytes 786440 | tf_op jit(solution)/shard_map/ppermute | solution.py:47
  197.9 2.0 collective-permute-done.29
  200.0 1.9 collective-permute-start.30
  203.3 6.2 %collective-permute-done.30 = bf16[256,512]{1,0:T(8,128)(2,1)S(1)} collective-permute-done((bf16[256,512]{1,0:T(8,128)(2,1)S(1)}, bf16[256,512]{1,0:T(8,128)(2,1)S(1)}, u32[]{:S(2)}, u32[]{:S(2)}) %collective-permute-start.30) | collective-permute-done | bytes 262176 | tf_op jit(solution)/shard_map/ppermute | solution.py:48
  (138 shorter events, 46.1 us)
Async XLA Ops:
  5.7 27.9 %collective-permute-start = (bf16[145,512]{1,0:T(8,128)(2,1)S(1)}, bf16[145,512]{1,0:T(8,128)(2,1)S(1)}, u32[]{:S(2)}, u32[]{:S(2)}) collective-permute-start(bf16[145,512]{1,0:T(8,128)(2,1)S(1)} %pad_maximum_fusion.2), channel_id=1, source_target_pairs={{0,16},{16,32},{32,48},{48,64},{64,80},{80,96},{96,112},{112,128},... | collective-permute-start | bytes 445448 | tf_op jit(solution)/shard_map/ppermute | solution.py:10
  52.6 44.6 %collective-permute-start.19 = (bf16[256,512]{1,0:T(8,128)(2,1)S(1)}, bf16[256,512]{1,0:T(8,128)(2,1)S(1)}, u32[]{:S(2)}, u32[]{:S(2)}) collective-permute-start(bf16[256,512]{1,0:T(8,128)(2,1)S(1)} %add_convert_fusion.12), channel_id=1, source_target_pairs={{12,11},{13,12},{14,13},{15,14},{28,27},{29,28},{30,29},{31,30},{4... | collective-permute-start | bytes 786440 | tf_op jit(solution)/shard_map/ppermute | solution.py:48
  54.4 45.2 %collective-permute-start.5 = (bf16[256,512]{1,0:T(8,128)(2,1)S(1)}, bf16[256,512]{1,0:T(8,128)(2,1)S(1)}, u32[]{:S(2)}, u32[]{:S(2)}) collective-permute-start(bf16[256,512]{1,0:T(8,128)(2,1)S(1)} %add_convert_fusion.25), channel_id=1, source_target_pairs={{0,1},{1,2},{2,3},{3,4},{4,5},{16,17},{17,18},{18,19},{19,20},{20,... | collective-permute-start | bytes 786440 | tf_op jit(solution)/shard_map/ppermute | solution.py:47
  97.3 10.6 %collective-permute-start.20 = (bf16[256,512]{1,0:T(8,128)(2,1)S(1)}, bf16[256,512]{1,0:T(8,128)(2,1)S(1)}, u32[]{:S(2)}, u32[]{:S(2)}) collective-permute-start(bf16[256,512]{1,0:T(8,128)(2,1)S(1)} %add_convert_fusion.11), channel_id=1, source_target_pairs={{11,10},{12,11},{13,12},{14,13},{15,14},{27,26},{28,27},{29,28},{3... | collective-permute-start | bytes 786440 | tf_op jit(solution)/shard_map/ppermute | solution.py:48
  99.7 10.6 %collective-permute-start.6 = (bf16[256,512]{1,0:T(8,128)(2,1)S(1)}, bf16[256,512]{1,0:T(8,128)(2,1)S(1)}, u32[]{:S(2)}, u32[]{:S(2)}) collective-permute-start(bf16[256,512]{1,0:T(8,128)(2,1)S(1)} %add_convert_fusion.24), channel_id=1, source_target_pairs={{0,1},{1,2},{2,3},{3,4},{4,5},{5,6},{16,17},{17,18},{18,19},{19,20... | collective-permute-start | bytes 786440 | tf_op jit(solution)/shard_map/ppermute | solution.py:47
  108.0 9.7 %collective-permute-start.21 = (bf16[256,512]{1,0:T(8,128)(2,1)S(1)}, bf16[256,512]{1,0:T(8,128)(2,1)S(1)}, u32[]{:S(2)}, u32[]{:S(2)}) collective-permute-start(bf16[256,512]{1,0:T(8,128)(2,1)S(1)} %add_convert_fusion.10), channel_id=1, source_target_pairs={{10,9},{11,10},{12,11},{13,12},{14,13},{15,14},{26,25},{27,26},{28... | collective-permute-start | bytes 786440 | tf_op jit(solution)/shard_map/ppermute | solution.py:48
  110.4 9.7 %collective-permute-start.7 = (bf16[256,512]{1,0:T(8,128)(2,1)S(1)}, bf16[256,512]{1,0:T(8,128)(2,1)S(1)}, u32[]{:S(2)}, u32[]{:S(2)}) collective-permute-start(bf16[256,512]{1,0:T(8,128)(2,1)S(1)} %add_convert_fusion.23), channel_id=1, source_target_pairs={{0,1},{1,2},{2,3},{3,4},{4,5},{5,6},{6,7},{16,17},{17,18},{18,19},... | collective-permute-start | bytes 786440 | tf_op jit(solution)/shard_map/ppermute | solution.py:47
  117.8 9.5 %collective-permute-start.22 = (bf16[256,512]{1,0:T(8,128)(2,1)S(1)}, bf16[256,512]{1,0:T(8,128)(2,1)S(1)}, u32[]{:S(2)}, u32[]{:S(2)}) collective-permute-start(bf16[256,512]{1,0:T(8,128)(2,1)S(1)} %add_convert_fusion.9), channel_id=1, source_target_pairs={{9,8},{10,9},{11,10},{12,11},{13,12},{14,13},{15,14},{25,24},{26,2... | collective-permute-start | bytes 786440 | tf_op jit(solution)/shard_map/ppermute | solution.py:48
  120.1 9.5 %collective-permute-start.8 = (bf16[256,512]{1,0:T(8,128)(2,1)S(1)}, bf16[256,512]{1,0:T(8,128)(2,1)S(1)}, u32[]{:S(2)}, u32[]{:S(2)}) collective-permute-start(bf16[256,512]{1,0:T(8,128)(2,1)S(1)} %add_convert_fusion.22), channel_id=1, source_target_pairs={{0,1},{1,2},{2,3},{3,4},{4,5},{5,6},{6,7},{7,8},{16,17},{17,18},{1... | collective-permute-start | bytes 786440 | tf_op jit(solution)/shard_map/ppermute | solution.py:47
  127.3 9.5 %collective-permute-start.23 = (bf16[256,512]{1,0:T(8,128)(2,1)S(1)}, bf16[256,512]{1,0:T(8,128)(2,1)S(1)}, u32[]{:S(2)}, u32[]{:S(2)}) collective-permute-start(bf16[256,512]{1,0:T(8,128)(2,1)S(1)} %add_convert_fusion.8), channel_id=1, source_target_pairs={{8,7},{9,8},{10,9},{11,10},{12,11},{13,12},{14,13},{15,14},{24,23}... | collective-permute-start | bytes 786440 | tf_op jit(solution)/shard_map/ppermute | solution.py:48
  129.7 9.5 %collective-permute-start.9 = (bf16[256,512]{1,0:T(8,128)(2,1)S(1)}, bf16[256,512]{1,0:T(8,128)(2,1)S(1)}, u32[]{:S(2)}, u32[]{:S(2)}) collective-permute-start(bf16[256,512]{1,0:T(8,128)(2,1)S(1)} %add_convert_fusion.21), channel_id=1, source_target_pairs={{0,1},{1,2},{2,3},{3,4},{4,5},{5,6},{6,7},{7,8},{8,9},{16,17},{17,... | collective-permute-start | bytes 786440 | tf_op jit(solution)/shard_map/ppermute | solution.py:47
  136.9 9.6 %collective-permute-start.24 = (bf16[256,512]{1,0:T(8,128)(2,1)S(1)}, bf16[256,512]{1,0:T(8,128)(2,1)S(1)}, u32[]{:S(2)}, u32[]{:S(2)}) collective-permute-start(bf16[256,512]{1,0:T(8,128)(2,1)S(1)} %add_convert_fusion.7), channel_id=1, source_target_pairs={{7,6},{8,7},{9,8},{10,9},{11,10},{12,11},{13,12},{14,13},{15,14},{... | collective-permute-start | bytes 786440 | tf_op jit(solution)/shard_map/ppermute | solution.py:48
  139.2 9.6 %collective-permute-start.10 = (bf16[256,512]{1,0:T(8,128)(2,1)S(1)}, bf16[256,512]{1,0:T(8,128)(2,1)S(1)}, u32[]{:S(2)}, u32[]{:S(2)}) collective-permute-start(bf16[256,512]{1,0:T(8,128)(2,1)S(1)} %add_convert_fusion.20), channel_id=1, source_target_pairs={{0,1},{1,2},{2,3},{3,4},{4,5},{5,6},{6,7},{7,8},{8,9},{9,10},{16,1... | collective-permute-start | bytes 786440 | tf_op jit(solution)/shard_map/ppermute | solution.py:47
  146.6 10.7 %collective-permute-start.25 = (bf16[256,512]{1,0:T(8,128)(2,1)S(1)}, bf16[256,512]{1,0:T(8,128)(2,1)S(1)}, u32[]{:S(2)}, u32[]{:S(2)}) collective-permute-start(bf16[256,512]{1,0:T(8,128)(2,1)S(1)} %add_convert_fusion.6), channel_id=1, source_target_pairs={{6,5},{7,6},{8,7},{9,8},{10,9},{11,10},{12,11},{13,12},{14,13},{15... | collective-permute-start | bytes 786440 | tf_op jit(solution)/shard_map/ppermute | solution.py:48
  148.9 10.7 %collective-permute-start.11 = (bf16[256,512]{1,0:T(8,128)(2,1)S(1)}, bf16[256,512]{1,0:T(8,128)(2,1)S(1)}, u32[]{:S(2)}, u32[]{:S(2)}) collective-permute-start(bf16[256,512]{1,0:T(8,128)(2,1)S(1)} %add_convert_fusion.19), channel_id=1, source_target_pairs={{0,1},{1,2},{2,3},{3,4},{4,5},{5,6},{6,7},{7,8},{8,9},{9,10},{10,1... | collective-permute-start | bytes 786440 | tf_op jit(solution)/shard_map/ppermute | solution.py:47
  157.4 11.9 %collective-permute-start.26 = (bf16[256,512]{1,0:T(8,128)(2,1)S(1)}, bf16[256,512]{1,0:T(8,128)(2,1)S(1)}, u32[]{:S(2)}, u32[]{:S(2)}) collective-permute-start(bf16[256,512]{1,0:T(8,128)(2,1)S(1)} %add_convert_fusion.5), channel_id=1, source_target_pairs={{5,4},{6,5},{7,6},{8,7},{9,8},{10,9},{11,10},{12,11},{13,12},{14,1... | collective-permute-start | bytes 786440 | tf_op jit(solution)/shard_map/ppermute | solution.py:48
  159.7 11.9 %collective-permute-start.12 = (bf16[256,512]{1,0:T(8,128)(2,1)S(1)}, bf16[256,512]{1,0:T(8,128)(2,1)S(1)}, u32[]{:S(2)}, u32[]{:S(2)}) collective-permute-start(bf16[256,512]{1,0:T(8,128)(2,1)S(1)} %add_convert_fusion.18), channel_id=1, source_target_pairs={{0,1},{1,2},{2,3},{3,4},{4,5},{5,6},{6,7},{7,8},{8,9},{9,10},{10,1... | collective-permute-start | bytes 786440 | tf_op jit(solution)/shard_map/ppermute | solution.py:47
  169.4 11.5 %collective-permute-start.27 = (bf16[256,512]{1,0:T(8,128)(2,1)S(1)}, bf16[256,512]{1,0:T(8,128)(2,1)S(1)}, u32[]{:S(2)}, u32[]{:S(2)}) collective-permute-start(bf16[256,512]{1,0:T(8,128)(2,1)S(1)} %add_convert_fusion.4), channel_id=1, source_target_pairs={{4,3},{5,4},{6,5},{7,6},{8,7},{9,8},{10,9},{11,10},{12,11},{13,12}... | collective-permute-start | bytes 786440 | tf_op jit(solution)/shard_map/ppermute | solution.py:48
  171.7 11.5 %collective-permute-start.13 = (bf16[256,512]{1,0:T(8,128)(2,1)S(1)}, bf16[256,512]{1,0:T(8,128)(2,1)S(1)}, u32[]{:S(2)}, u32[]{:S(2)}) collective-permute-start(bf16[256,512]{1,0:T(8,128)(2,1)S(1)} %add_convert_fusion.17), channel_id=1, source_target_pairs={{0,1},{1,2},{2,3},{3,4},{4,5},{5,6},{6,7},{7,8},{8,9},{9,10},{10,1... | collective-permute-start | bytes 786440 | tf_op jit(solution)/shard_map/ppermute | solution.py:47
  180.9 9.5 %collective-permute-start.28 = (bf16[256,512]{1,0:T(8,128)(2,1)S(1)}, bf16[256,512]{1,0:T(8,128)(2,1)S(1)}, u32[]{:S(2)}, u32[]{:S(2)}) collective-permute-start(bf16[256,512]{1,0:T(8,128)(2,1)S(1)} %add_convert_fusion.3), channel_id=1, source_target_pairs={{3,2},{4,3},{5,4},{6,5},{7,6},{8,7},{9,8},{10,9},{11,10},{12,11},{... | collective-permute-start | bytes 786440 | tf_op jit(solution)/shard_map/ppermute | solution.py:48
  183.2 9.5 %collective-permute-start.14 = (bf16[256,512]{1,0:T(8,128)(2,1)S(1)}, bf16[256,512]{1,0:T(8,128)(2,1)S(1)}, u32[]{:S(2)}, u32[]{:S(2)}) collective-permute-start(bf16[256,512]{1,0:T(8,128)(2,1)S(1)} %add_convert_fusion.16), channel_id=1, source_target_pairs={{0,1},{1,2},{2,3},{3,4},{4,5},{5,6},{6,7},{7,8},{8,9},{9,10},{10,1... | collective-permute-start | bytes 786440 | tf_op jit(solution)/shard_map/ppermute | solution.py:47
  190.5 9.5 %collective-permute-start.29 = (bf16[256,512]{1,0:T(8,128)(2,1)S(1)}, bf16[256,512]{1,0:T(8,128)(2,1)S(1)}, u32[]{:S(2)}, u32[]{:S(2)}) collective-permute-start(bf16[256,512]{1,0:T(8,128)(2,1)S(1)} %add_convert_fusion.2), channel_id=1, source_target_pairs={{2,1},{3,2},{4,3},{5,4},{6,5},{7,6},{8,7},{9,8},{10,9},{11,10},{12... | collective-permute-start | bytes 786440 | tf_op jit(solution)/shard_map/ppermute | solution.py:48
  192.8 10.5 %collective-permute-start.15 = (bf16[256,512]{1,0:T(8,128)(2,1)S(1)}, bf16[256,512]{1,0:T(8,128)(2,1)S(1)}, u32[]{:S(2)}, u32[]{:S(2)}) collective-permute-start(bf16[256,512]{1,0:T(8,128)(2,1)S(1)} %add_convert_fusion.15), channel_id=1, source_target_pairs={{0,1},{1,2},{2,3},{3,4},{4,5},{5,6},{6,7},{7,8},{8,9},{9,10},{10,1... | collective-permute-start | bytes 786440 | tf_op jit(solution)/shard_map/ppermute | solution.py:47
  200.0 9.5 %collective-permute-start.30 = (bf16[256,512]{1,0:T(8,128)(2,1)S(1)}, bf16[256,512]{1,0:T(8,128)(2,1)S(1)}, u32[]{:S(2)}, u32[]{:S(2)}) collective-permute-start(bf16[256,512]{1,0:T(8,128)(2,1)S(1)} %add_convert_fusion.1), channel_id=1, source_target_pairs={{1,0},{2,1},{3,2},{4,3},{5,4},{6,5},{7,6},{8,7},{9,8},{10,9},{11,1... | collective-permute-start | bytes 786440 | tf_op jit(solution)/shard_map/ppermute | solution.py:48
  (12 other events, 55.4 us)

commit v7 on v6

--- a/solution.py
+++ b/solution.py
@@ -46,6 +46,7 @@
             send_left = (from_right[chain].astype(jnp.float32) + block(step - (n - 1) + me, chain)).astype(jnp.bfloat16)
             from_left[chain] = lax.ppermute(send_right, axis, rightward)
             from_right[chain] = lax.ppermute(send_left, axis, leftward)
+            from_left[chain], from_right[chain] = lax.optimization_barrier((from_left[chain], from_right[chain]))
     pieces = [
         from_left[chain].astype(jnp.float32) + block(me, chain) + from_right[chain].astype(jnp.float32)
         for chain in range(chains)

time: 212 us -> 225 us (1.061)
  the two profiles are of different devices: /device:TPU:376 before, /device:TPU:272 now
where the time goes in v7:
time: 225 us; the launch traced here: 223 us
  waiting for transfers between devices  99.5 us (44%)
  starting transfers between devices  56.3 us (25%)
  matrix products  41.9 us (19%)
  other arithmetic  20.3 us (9%)
  local copies, waits for them, and re-layouts  3.77 us (2%)
    ppermute x15, waiting for transfers between devices, line_reduce_scatter(): from_right[chain] = lax.ppermute(send_left, axis, leftward)  48.4 us
    dot_general x31, matrix products, block(): jnp.dot(product, columns, preferred_element_type=jnp.float32)  41.9 us
    ppermute x15, starting transfers between devices, line_reduce_scatter(): from_left[chain] = lax.ppermute(send_right, axis, rightward)  33.6 us
    ppermute x15, waiting for transfers between devices, line_reduce_scatter(): from_left[chain] = lax.ppermute(send_right, axis, rightward)  27.6 us
    ppermute x1, waiting for transfers between devices, shifted(): return lax.ppermute(block, axis, route)  23.5 us
    ppermute x15, starting transfers between devices, line_reduce_scatter(): from_right[chain] = lax.ppermute(send_left, axis, leftward)  20.8 us
    convert_element_type x1, other arithmetic, shards(): product_head = (query_feat_head * mixed_head).astype(jnp.bfloat16)  7.08 us
    convert_element_type x1, other arithmetic, shards(): product_tail = (query_body[filt_reach:] * mixed_tail).astype(jnp.bfloat16)  6.92 us
  transfers between devices with their start and end apart: 31, of which 14 were waited for; matrix products, arithmetic and copies ran while one was open for 22% of the time, Pallas kernels for 0%

profile of v7, /device:TPU:272, one launch (start us, length us, event | category | flops | bytes accessed | tf_op | source)
XLA Modules:
  0.0 222.8 jit_solution(5999208347544726020)
XLA Ops:
  5.7 1.9 collective-permute-start
  9.2 6.9 %fusion.184 = bf16[123,512]{1,0:T(8,128)(2,1)S(1)} fusion(f32[250,512]{1,0:T(8,128)S(1)} %get-tuple-element.65, f32[512]{0:T(512)S(1)} %bitcast.439, f32[512]{0:T(512)S(1)} %bitcast.441, f32[512]{0:T(512)S(1)} %bitcast.265, f32[512]{0:T(512)S(1)} %bitcast.267, f32[512]{0:T(512)S(1)} %bitcast.269, f32[512]{0:T(512)S(1)} %bitcast.271, f32[512]{0:T(512)S(1)} %bitcast.273, ...), kind=kLoop, calls=%fused_computation.397 | loop fusion | flops 16373760 | bytes 33011712 | tf_op jit(solution)/shard_map/convert_element_type | solution.py:71
  16.2 23.5 %collective-permute-done = bf16[145,512]{1,0:T(8,128)(2,1)S(1)} collective-permute-done((bf16[145,512]{1,0:T(8,128)(2,1)S(1)}, bf16[145,512]{1,0:T(8,128)(2,1)S(1)}, u32[]{:S(2)}, u32[]{:S(2)}) %collective-permute-start) | collective-permute-done | bytes 148512 | tf_op jit(solution)/shard_map/ppermute | solution.py:10
  39.9 7.1 %fusion.54 = bf16[133,512]{1,0:T(8,128)(2,1)S(1)} fusion(f32[260,512]{1,0:T(8,128)S(1)} %maximum_convert_fusion, bf16[127,512]{1,0:T(8,128)(2,1)S(1)} %get-tuple-element.72, bf16[6,512]{1,0:T(8,128)(2,1)S(1)} %fusion.313, f32[512]{0:T(512)S(1)} %copy-done.2, f32[512]{0:T(512)S(1)} %bitcast.440, f32[512]{0:T(512)S(1)} %bitcast.442, f32[512]{0:T(512)S(1)} %bitcast.266, ...), kind=kLoop, calls=%fused_computation.136 | loop fusion | flops 17977344 | bytes 35674112 | tf_op jit(solution)/shard_map/convert_element_type | solution.py:84
  80.2 42.4 %collective-permute-done.14 = bf16[256,512]{1,0:T(8,128)(2,1)S(1)} collective-permute-done((bf16[256,512]{1,0:T(8,128)(2,1)S(1)}, bf16[256,512]{1,0:T(8,128)(2,1)S(1)}, u32[]{:S(2)}, u32[]{:S(2)}) %collective-permute-start.14) | collective-permute-done | bytes 262176 | tf_op jit(solution)/shard_map/ppermute | solution.py:48
  122.7 1.9 collective-permute-start.16
  128.7 3.4 %collective-permute-done.16 = bf16[256,512]{1,0:T(8,128)(2,1)S(1)} collective-permute-done((bf16[256,512]{1,0:T(8,128)(2,1)S(1)}, bf16[256,512]{1,0:T(8,128)(2,1)S(1)}, u32[]{:S(2)}, u32[]{:S(2)}) %collective-permute-start.16) | collective-permute-done | bytes 262176 | tf_op jit(solution)/shard_map/ppermute | solution.py:48
  132.1 2.5 %collective-permute-done.15 = bf16[256,512]{1,0:T(8,128)(2,1)S(1)} collective-permute-done((bf16[256,512]{1,0:T(8,128)(2,1)S(1)}, bf16[256,512]{1,0:T(8,128)(2,1)S(1)}, u32[]{:S(2)}, u32[]{:S(2)}) %collective-permute-start.15) | collective-permute-done | bytes 262176 | tf_op jit(solution)/shard_map/ppermute | solution.py:47
  134.6 1.9 collective-permute-start.18
  136.6 3.9 %collective-permute-start.17 = (bf16[256,512]{1,0:T(8,128)(2,1)S(1)}, bf16[256,512]{1,0:T(8,128)(2,1)S(1)}, u32[]{:S(2)}, u32[]{:S(2)}) collective-permute-start(bf16[256,512]{1,0:T(8,128)(2,1)S(1)} %add_convert_fusion.14), channel_id=1, source_target_pairs={{0,1},{1,2},{2,3},{3,4},{4,5},{5,6},{6,7},{7,8},{8,9},{16,17},{17,... | collective-permute-start | bytes 786440 | tf_op jit(solution)/shard_map/ppermute | solution.py:47
  143.3 2.8 %collective-permute-done.17 = bf16[256,512]{1,0:T(8,128)(2,1)S(1)} collective-permute-done((bf16[256,512]{1,0:T(8,128)(2,1)S(1)}, bf16[256,512]{1,0:T(8,128)(2,1)S(1)}, u32[]{:S(2)}, u32[]{:S(2)}) %collective-permute-start.17) | collective-permute-done | bytes 262176 | tf_op jit(solution)/shard_map/ppermute | solution.py:47
  146.2 2.0 collective-permute-start.20
  148.2 3.9 %collective-permute-start.19 = (bf16[256,512]{1,0:T(8,128)(2,1)S(1)}, bf16[256,512]{1,0:T(8,128)(2,1)S(1)}, u32[]{:S(2)}, u32[]{:S(2)}) collective-permute-start(bf16[256,512]{1,0:T(8,128)(2,1)S(1)} %add_convert_fusion.12), channel_id=1, source_target_pairs={{0,1},{1,2},{2,3},{3,4},{4,5},{5,6},{6,7},{7,8},{8,9},{9,10},{16,1... | collective-permute-start | bytes 786440 | tf_op jit(solution)/shard_map/ppermute | solution.py:47
  154.9 5.3 %collective-permute-done.19 = bf16[256,512]{1,0:T(8,128)(2,1)S(1)} collective-permute-done((bf16[256,512]{1,0:T(8,128)(2,1)S(1)}, bf16[256,512]{1,0:T(8,128)(2,1)S(1)}, u32[]{:S(2)}, u32[]{:S(2)}) %collective-permute-start.19) | collective-permute-done | bytes 262176 | tf_op jit(solution)/shard_map/ppermute | solution.py:47
  162.2 3.9 %collective-permute-start.21 = (bf16[256,512]{1,0:T(8,128)(2,1)S(1)}, bf16[256,512]{1,0:T(8,128)(2,1)S(1)}, u32[]{:S(2)}, u32[]{:S(2)}) collective-permute-start(bf16[256,512]{1,0:T(8,128)(2,1)S(1)} %add_convert_fusion.10), channel_id=1, source_target_pairs={{0,1},{1,2},{2,3},{3,4},{4,5},{5,6},{6,7},{7,8},{8,9},{9,10},{10,1... | collective-permute-start | bytes 786440 | tf_op jit(solution)/shard_map/ppermute | solution.py:47
  170.1 3.2 %collective-permute-done.21 = bf16[256,512]{1,0:T(8,128)(2,1)S(1)} collective-permute-done((bf16[256,512]{1,0:T(8,128)(2,1)S(1)}, bf16[256,512]{1,0:T(8,128)(2,1)S(1)}, u32[]{:S(2)}, u32[]{:S(2)}) %collective-permute-start.21) | collective-permute-done | bytes 262176 | tf_op jit(solution)/shard_map/ppermute | solution.py:47
  175.4 3.9 %collective-permute-start.23 = (bf16[256,512]{1,0:T(8,128)(2,1)S(1)}, bf16[256,512]{1,0:T(8,128)(2,1)S(1)}, u32[]{:S(2)}, u32[]{:S(2)}) collective-permute-start(bf16[256,512]{1,0:T(8,128)(2,1)S(1)} %add_convert_fusion.8), channel_id=1, source_target_pairs={{0,1},{1,2},{2,3},{3,4},{4,5},{5,6},{6,7},{7,8},{8,9},{9,10},{10,1... | collective-permute-start | bytes 786440 | tf_op jit(solution)/shard_map/ppermute | solution.py:47
  182.4 3.6 %collective-permute-done.23 = bf16[256,512]{1,0:T(8,128)(2,1)S(1)} collective-permute-done((bf16[256,512]{1,0:T(8,128)(2,1)S(1)}, bf16[256,512]{1,0:T(8,128)(2,1)S(1)}, u32[]{:S(2)}, u32[]{:S(2)}) %collective-permute-start.23) | collective-permute-done | bytes 262176 | tf_op jit(solution)/shard_map/ppermute | solution.py:47
  188.1 3.9 %collective-permute-start.25 = (bf16[256,512]{1,0:T(8,128)(2,1)S(1)}, bf16[256,512]{1,0:T(8,128)(2,1)S(1)}, u32[]{:S(2)}, u32[]{:S(2)}) collective-permute-start(bf16[256,512]{1,0:T(8,128)(2,1)S(1)} %add_convert_fusion.6), channel_id=1, source_target_pairs={{0,1},{1,2},{2,3},{3,4},{4,5},{5,6},{6,7},{7,8},{8,9},{9,10},{10,1... | collective-permute-start | bytes 786440 | tf_op jit(solution)/shard_map/ppermute | solution.py:47
  194.8 4.2 %collective-permute-done.25 = bf16[256,512]{1,0:T(8,128)(2,1)S(1)} collective-permute-done((bf16[256,512]{1,0:T(8,128)(2,1)S(1)}, bf16[256,512]{1,0:T(8,128)(2,1)S(1)}, u32[]{:S(2)}, u32[]{:S(2)}) %collective-permute-start.25) | collective-permute-done | bytes 262176 | tf_op jit(solution)/shard_map/ppermute | solution.py:47
  201.0 3.9 %collective-permute-start.27 = (bf16[256,512]{1,0:T(8,128)(2,1)S(1)}, bf16[256,512]{1,0:T(8,128)(2,1)S(1)}, u32[]{:S(2)}, u32[]{:S(2)}) collective-permute-start(bf16[256,512]{1,0:T(8,128)(2,1)S(1)} %add_convert_fusion.4), channel_id=1, source_target_pairs={{0,1},{1,2},{2,3},{3,4},{4,5},{5,6},{6,7},{7,8},{8,9},{9,10},{10,1... | collective-permute-start | bytes 786440 | tf_op jit(solution)/shard_map/ppermute | solution.py:47
  207.7 2.8 %collective-permute-done.27 = bf16[256,512]{1,0:T(8,128)(2,1)S(1)} collective-permute-done((bf16[256,512]{1,0:T(8,128)(2,1)S(1)}, bf16[256,512]{1,0:T(8,128)(2,1)S(1)}, u32[]{:S(2)}, u32[]{:S(2)}) %collective-permute-start.27) | collective-permute-done | bytes 262176 | tf_op jit(solution)/shard_map/ppermute | solution.py:47
  212.6 3.9 %collective-permute-start.29 = (bf16[256,512]{1,0:T(8,128)(2,1)S(1)}, bf16[256,512]{1,0:T(8,128)(2,1)S(1)}, u32[]{:S(2)}, u32[]{:S(2)}) collective-permute-start(bf16[256,512]{1,0:T(8,128)(2,1)S(1)} %add_convert_fusion.2), channel_id=1, source_target_pairs={{0,1},{1,2},{2,3},{3,4},{4,5},{5,6},{6,7},{7,8},{8,9},{9,10},{10,1... | collective-permute-start | bytes 786440 | tf_op jit(solution)/shard_map/ppermute | solution.py:47
  218.8 3.2 %collective-permute-done.29 = bf16[256,512]{1,0:T(8,128)(2,1)S(1)} collective-permute-done((bf16[256,512]{1,0:T(8,128)(2,1)S(1)}, bf16[256,512]{1,0:T(8,128)(2,1)S(1)}, u32[]{:S(2)}, u32[]{:S(2)}) %collective-permute-start.29) | collective-permute-done | bytes 262176 | tf_op jit(solution)/shard_map/ppermute | solution.py:47
  (133 shorter events, 75.7 us)
Async XLA Ops:
  5.7 34.0 %collective-permute-start = (bf16[145,512]{1,0:T(8,128)(2,1)S(1)}, bf16[145,512]{1,0:T(8,128)(2,1)S(1)}, u32[]{:S(2)}, u32[]{:S(2)}) collective-permute-start(bf16[145,512]{1,0:T(8,128)(2,1)S(1)} %pad_maximum_fusion.2), channel_id=1, source_target_pairs={{0,16},{16,32},{32,48},{48,64},{64,80},{80,96},{96,112},{112,128},... | collective-permute-start | bytes 445448 | tf_op jit(solution)/shard_map/ppermute | solution.py:10
  48.4 5.5 %collective-permute-start.1 = (bf16[256,512]{1,0:T(8,128)(2,1)S(1)}, bf16[256,512]{1,0:T(8,128)(2,1)S(1)}, u32[]{:S(2)}, u32[]{:S(2)}) collective-permute-start(bf16[256,512]{1,0:T(8,128)(2,1)S(1)} %convolution_convert_fusion.30), channel_id=1, source_target_pairs={{0,1},{16,17},{32,33},{48,49},{64,65},{80,81},{96,97},{112,113},{1... | collective-permute-start | bytes 786440 | tf_op jit(solution)/shard_map/ppermute | solution.py:47
  53.9 4.2 %collective-permute-start.4 = (bf16[256,512]{1,0:T(8,128)(2,1)S(1)}, bf16[256,512]{1,0:T(8,128)(2,1)S(1)}, u32[]{:S(2)}, u32[]{:S(2)}) collective-permute-start(bf16[256,512]{1,0:T(8,128)(2,1)S(1)} %add_convert_fusion.27), channel_id=1, source_target_pairs={{14,13},{15,14},{30,29},{31,30},{46,45},{47,46},{62,61},{63,62},{7... | collective-permute-start | bytes 786440 | tf_op jit(solution)/shard_map/ppermute | solution.py:48
  58.2 4.4 %collective-permute-start.6 = (bf16[256,512]{1,0:T(8,128)(2,1)S(1)}, bf16[256,512]{1,0:T(8,128)(2,1)S(1)}, u32[]{:S(2)}, u32[]{:S(2)}) collective-permute-start(bf16[256,512]{1,0:T(8,128)(2,1)S(1)} %add_convert_fusion.25), channel_id=1, source_target_pairs={{13,12},{14,13},{15,14},{29,28},{30,29},{31,30},{45,44},{46,45},{4... | collective-permute-start | bytes 786440 | tf_op jit(solution)/shard_map/ppermute | solution.py:48
  62.6 4.2 %collective-permute-start.8 = (bf16[256,512]{1,0:T(8,128)(2,1)S(1)}, bf16[256,512]{1,0:T(8,128)(2,1)S(1)}, u32[]{:S(2)}, u32[]{:S(2)}) collective-permute-start(bf16[256,512]{1,0:T(8,128)(2,1)S(1)} %add_convert_fusion.23), channel_id=1, source_target_pairs={{12,11},{13,12},{14,13},{15,14},{28,27},{29,28},{30,29},{31,30},{4... | collective-permute-start | bytes 786440 | tf_op jit(solution)/shard_map/ppermute | solution.py:48
  66.9 4.2 %collective-permute-start.10 = (bf16[256,512]{1,0:T(8,128)(2,1)S(1)}, bf16[256,512]{1,0:T(8,128)(2,1)S(1)}, u32[]{:S(2)}, u32[]{:S(2)}) collective-permute-start(bf16[256,512]{1,0:T(8,128)(2,1)S(1)} %add_convert_fusion.21), channel_id=1, source_target_pairs={{11,10},{12,11},{13,12},{14,13},{15,14},{27,26},{28,27},{29,28},{3... | collective-permute-start | bytes 786440 | tf_op jit(solution)/shard_map/ppermute | solution.py:48
  75.4 47.2 %collective-permute-start.14 = (bf16[256,512]{1,0:T(8,128)(2,1)S(1)}, bf16[256,512]{1,0:T(8,128)(2,1)S(1)}, u32[]{:S(2)}, u32[]{:S(2)}) collective-permute-start(bf16[256,512]{1,0:T(8,128)(2,1)S(1)} %add_convert_fusion.17), channel_id=1, source_target_pairs={{9,8},{10,9},{11,10},{12,11},{13,12},{14,13},{15,14},{25,24},{26,2... | collective-permute-start | bytes 786440 | tf_op jit(solution)/shard_map/ppermute | solution.py:48
  76.8 45.8 %collective-permute-start.13 = (bf16[256,512]{1,0:T(8,128)(2,1)S(1)}, bf16[256,512]{1,0:T(8,128)(2,1)S(1)}, u32[]{:S(2)}, u32[]{:S(2)}) collective-permute-start(bf16[256,512]{1,0:T(8,128)(2,1)S(1)} %add_convert_fusion.18), channel_id=1, source_target_pairs={{0,1},{1,2},{2,3},{3,4},{4,5},{5,6},{6,7},{16,17},{17,18},{18,19},... | collective-permute-start | bytes 786440 | tf_op jit(solution)/shard_map/ppermute | solution.py:47
  122.7 9.4 %collective-permute-start.16 = (bf16[256,512]{1,0:T(8,128)(2,1)S(1)}, bf16[256,512]{1,0:T(8,128)(2,1)S(1)}, u32[]{:S(2)}, u32[]{:S(2)}) collective-permute-start(bf16[256,512]{1,0:T(8,128)(2,1)S(1)} %add_convert_fusion.15), channel_id=1, source_target_pairs={{8,7},{9,8},{10,9},{11,10},{12,11},{13,12},{14,13},{15,14},{24,23}... | collective-permute-start | bytes 786440 | tf_op jit(solution)/shard_map/ppermute | solution.py:48
  124.7 9.9 %collective-permute-start.15 = (bf16[256,512]{1,0:T(8,128)(2,1)S(1)}, bf16[256,512]{1,0:T(8,128)(2,1)S(1)}, u32[]{:S(2)}, u32[]{:S(2)}) collective-permute-start(bf16[256,512]{1,0:T(8,128)(2,1)S(1)} %add_convert_fusion.16), channel_id=1, source_target_pairs={{0,1},{1,2},{2,3},{3,4},{4,5},{5,6},{6,7},{7,8},{16,17},{17,18},{1... | collective-permute-start | bytes 786440 | tf_op jit(solution)/shard_map/ppermute | solution.py:47
  134.6 8.7 %collective-permute-start.18 = (bf16[256,512]{1,0:T(8,128)(2,1)S(1)}, bf16[256,512]{1,0:T(8,128)(2,1)S(1)}, u32[]{:S(2)}, u32[]{:S(2)}) collective-permute-start(bf16[256,512]{1,0:T(8,128)(2,1)S(1)} %add_convert_fusion.13), channel_id=1, source_target_pairs={{7,6},{8,7},{9,8},{10,9},{11,10},{12,11},{13,12},{14,13},{15,14},{... | collective-permute-start | bytes 786440 | tf_op jit(solution)/shard_map/ppermute | solution.py:48
  136.6 9.5 %collective-permute-start.17 = (bf16[256,512]{1,0:T(8,128)(2,1)S(1)}, bf16[256,512]{1,0:T(8,128)(2,1)S(1)}, u32[]{:S(2)}, u32[]{:S(2)}) collective-permute-start(bf16[256,512]{1,0:T(8,128)(2,1)S(1)} %add_convert_fusion.14), channel_id=1, source_target_pairs={{0,1},{1,2},{2,3},{3,4},{4,5},{5,6},{6,7},{7,8},{8,9},{16,17},{17,... | collective-permute-start | bytes 786440 | tf_op jit(solution)/shard_map/ppermute | solution.py:47
  146.2 8.7 %collective-permute-start.20 = (bf16[256,512]{1,0:T(8,128)(2,1)S(1)}, bf16[256,512]{1,0:T(8,128)(2,1)S(1)}, u32[]{:S(2)}, u32[]{:S(2)}) collective-permute-start(bf16[256,512]{1,0:T(8,128)(2,1)S(1)} %add_convert_fusion.11), channel_id=1, source_target_pairs={{6,5},{7,6},{8,7},{9,8},{10,9},{11,10},{12,11},{13,12},{14,13},{15... | collective-permute-start | bytes 786440 | tf_op jit(solution)/shard_map/ppermute | solution.py:48
  148.2 11.9 %collective-permute-start.19 = (bf16[256,512]{1,0:T(8,128)(2,1)S(1)}, bf16[256,512]{1,0:T(8,128)(2,1)S(1)}, u32[]{:S(2)}, u32[]{:S(2)}) collective-permute-start(bf16[256,512]{1,0:T(8,128)(2,1)S(1)} %add_convert_fusion.12), channel_id=1, source_target_pairs={{0,1},{1,2},{2,3},{3,4},{4,5},{5,6},{6,7},{7,8},{8,9},{9,10},{16,1... | collective-permute-start | bytes 786440 | tf_op jit(solution)/shard_map/ppermute | solution.py:47
  160.2 9.9 %collective-permute-start.22 = (bf16[256,512]{1,0:T(8,128)(2,1)S(1)}, bf16[256,512]{1,0:T(8,128)(2,1)S(1)}, u32[]{:S(2)}, u32[]{:S(2)}) collective-permute-start(bf16[256,512]{1,0:T(8,128)(2,1)S(1)} %add_convert_fusion.9), channel_id=1, source_target_pairs={{5,4},{6,5},{7,6},{8,7},{9,8},{10,9},{11,10},{12,11},{13,12},{14,1... | collective-permute-start | bytes 786440 | tf_op jit(solution)/shard_map/ppermute | solution.py:48
  162.2 11.1 %collective-permute-start.21 = (bf16[256,512]{1,0:T(8,128)(2,1)S(1)}, bf16[256,512]{1,0:T(8,128)(2,1)S(1)}, u32[]{:S(2)}, u32[]{:S(2)}) collective-permute-start(bf16[256,512]{1,0:T(8,128)(2,1)S(1)} %add_convert_fusion.10), channel_id=1, source_target_pairs={{0,1},{1,2},{2,3},{3,4},{4,5},{5,6},{6,7},{7,8},{8,9},{9,10},{10,1... | collective-permute-start | bytes 786440 | tf_op jit(solution)/shard_map/ppermute | solution.py:47
  173.4 9.0 %collective-permute-start.24 = (bf16[256,512]{1,0:T(8,128)(2,1)S(1)}, bf16[256,512]{1,0:T(8,128)(2,1)S(1)}, u32[]{:S(2)}, u32[]{:S(2)}) collective-permute-start(bf16[256,512]{1,0:T(8,128)(2,1)S(1)} %add_convert_fusion.7), channel_id=1, source_target_pairs={{4,3},{5,4},{6,5},{7,6},{8,7},{9,8},{10,9},{11,10},{12,11},{13,12}... | collective-permute-start | bytes 786440 | tf_op jit(solution)/shard_map/ppermute | solution.py:48
  175.4 10.6 %collective-permute-start.23 = (bf16[256,512]{1,0:T(8,128)(2,1)S(1)}, bf16[256,512]{1,0:T(8,128)(2,1)S(1)}, u32[]{:S(2)}, u32[]{:S(2)}) collective-permute-start(bf16[256,512]{1,0:T(8,128)(2,1)S(1)} %add_convert_fusion.8), channel_id=1, source_target_pairs={{0,1},{1,2},{2,3},{3,4},{4,5},{5,6},{6,7},{7,8},{8,9},{9,10},{10,1... | collective-permute-start | bytes 786440 | tf_op jit(solution)/shard_map/ppermute | solution.py:47
  186.1 8.7 %collective-permute-start.26 = (bf16[256,512]{1,0:T(8,128)(2,1)S(1)}, bf16[256,512]{1,0:T(8,128)(2,1)S(1)}, u32[]{:S(2)}, u32[]{:S(2)}) collective-permute-start(bf16[256,512]{1,0:T(8,128)(2,1)S(1)} %add_convert_fusion.5), channel_id=1, source_target_pairs={{3,2},{4,3},{5,4},{6,5},{7,6},{8,7},{9,8},{10,9},{11,10},{12,11},{... | collective-permute-start | bytes 786440 | tf_op jit(solution)/shard_map/ppermute | solution.py:48
  188.1 10.8 %collective-permute-start.25 = (bf16[256,512]{1,0:T(8,128)(2,1)S(1)}, bf16[256,512]{1,0:T(8,128)(2,1)S(1)}, u32[]{:S(2)}, u32[]{:S(2)}) collective-permute-start(bf16[256,512]{1,0:T(8,128)(2,1)S(1)} %add_convert_fusion.6), channel_id=1, source_target_pairs={{0,1},{1,2},{2,3},{3,4},{4,5},{5,6},{6,7},{7,8},{8,9},{9,10},{10,1... | collective-permute-start | bytes 786440 | tf_op jit(solution)/shard_map/ppermute | solution.py:47
  199.0 8.7 %collective-permute-start.28 = (bf16[256,512]{1,0:T(8,128)(2,1)S(1)}, bf16[256,512]{1,0:T(8,128)(2,1)S(1)}, u32[]{:S(2)}, u32[]{:S(2)}) collective-permute-start(bf16[256,512]{1,0:T(8,128)(2,1)S(1)} %add_convert_fusion.3), channel_id=1, source_target_pairs={{2,1},{3,2},{4,3},{5,4},{6,5},{7,6},{8,7},{9,8},{10,9},{11,10},{12... | collective-permute-start | bytes 786440 | tf_op jit(solution)/shard_map/ppermute | solution.py:48
  201.0 9.5 %collective-permute-start.27 = (bf16[256,512]{1,0:T(8,128)(2,1)S(1)}, bf16[256,512]{1,0:T(8,128)(2,1)S(1)}, u32[]{:S(2)}, u32[]{:S(2)}) collective-permute-start(bf16[256,512]{1,0:T(8,128)(2,1)S(1)} %add_convert_fusion.4), channel_id=1, source_target_pairs={{0,1},{1,2},{2,3},{3,4},{4,5},{5,6},{6,7},{7,8},{8,9},{9,10},{10,1... | collective-permute-start | bytes 786440 | tf_op jit(solution)/shard_map/ppermute | solution.py:47
  210.6 8.3 %collective-permute-start.30 = (bf16[256,512]{1,0:T(8,128)(2,1)S(1)}, bf16[256,512]{1,0:T(8,128)(2,1)S(1)}, u32[]{:S(2)}, u32[]{:S(2)}) collective-permute-start(bf16[256,512]{1,0:T(8,128)(2,1)S(1)} %add_convert_fusion.1), channel_id=1, source_target_pairs={{1,0},{2,1},{3,2},{4,3},{5,4},{6,5},{7,6},{8,7},{9,8},{10,9},{11,1... | collective-permute-start | bytes 786440 | tf_op jit(solution)/shard_map/ppermute | solution.py:48
  212.6 9.5 %collective-permute-start.29 = (bf16[256,512]{1,0:T(8,128)(2,1)S(1)}, bf16[256,512]{1,0:T(8,128)(2,1)S(1)}, u32[]{:S(2)}, u32[]{:S(2)}) collective-permute-start(bf16[256,512]{1,0:T(8,128)(2,1)S(1)} %add_convert_fusion.2), channel_id=1, source_target_pairs={{0,1},{1,2},{2,3},{3,4},{4,5},{5,6},{6,7},{7,8},{8,9},{9,10},{10,1... | collective-permute-start | bytes 786440 | tf_op jit(solution)/shard_map/ppermute | solution.py:47
  (10 other events, 47.6 us)

commit v8 on v6

--- a/solution.py
+++ b/solution.py
@@ -8,6 +8,27 @@
     devices = range(lax.axis_size(axis))
     route = [(i - distance, i) for i in devices if i - distance in devices]
     return lax.ppermute(block, axis, route)
+
+
+def halo_shift(outgoing, axis, other):
+    n_ctx, n_tp = lax.axis_size(axis), lax.axis_size(other)
+    pairs = [(i - 1, i) for i in range(1, n_ctx)]
+    crossing = [i for i in range(1, n_ctx) if i % 2 == 0 and (i // 2) % 2 == 1]
+    split = outgoing.shape[0] // 2
+    moved_head = lax.ppermute(outgoing[:split], axis, pairs)
+    rest = outgoing[split:]
+    direct = lax.ppermute(rest, axis, [(a, b) for a, b in pairs if b not in crossing])
+    flat = lambda c, t: c * n_tp + t
+    first, second = [], []
+    for i in crossing:
+        for j in range(n_tp):
+            relay = flat(i, j + 1) if j + 1 < n_tp else flat(i - 1, 0)
+            first.append((flat(i - 1, j), relay))
+            second.append((relay, flat(i, j)))
+    relayed = lax.ppermute(lax.ppermute(rest, (axis, other), first), (axis, other), second)
+    me = lax.axis_index(axis)
+    moved_rest = jnp.where((me % 2 == 0) & ((me // 2) % 2 == 1), relayed, direct)
+    return jnp.concatenate([moved_head, moved_rest], 0)
 
 
 def valid_conv(extended, taps):
@@ -64,7 +85,7 @@
     outgoing = jnp.concatenate(
         [gated_body[-filt_reach:], key_stream[-feat_reach:], value_stream[-feat_reach:], query_stream[-feat_reach:]], 0
     )
-    incoming = shifted(outgoing, "ctx", 1)
+    incoming = halo_shift(outgoing, "ctx", "tp")
     query_body = valid_conv(wide(query_stream), feat_taps[0])
     mixed_tail = valid_conv(wide(gated_body), filt_taps) + skip_bias[None, :] * wide(gated_body[filt_reach:])
     product_tail = (query_body[filt_reach:] * mixed_tail).astype(jnp.bfloat16)

time: 212 us -> 230 us (1.085)
  the two profiles are of different devices: /device:TPU:376 before, /device:TPU:98 now
where the time goes in v8:
time: 230 us; the launch traced here: 229 us
  starting transfers between devices  107 us (47%)
  waiting for transfers between devices  85.2 us (37%)
  other arithmetic  20.4 us (9%)
  matrix products  10.9 us (5%)
  local copies, waits for them, and re-layouts  3.8 us (2%)
    ppermute x15, waiting for transfers between devices, line_reduce_scatter(): from_left[chain] = lax.ppermute(send_right, axis, rightward)  66 us
    ppermute x15, starting transfers between devices, line_reduce_scatter(): from_left[chain] = lax.ppermute(send_right, axis, rightward)  63.4 us
    ppermute x1, starting transfers between devices, halo_shift(): lax.ppermute(rest, axis, [(a, b) for a, b in pairs if b not in crossing])  26 us
    ppermute x15, starting transfers between devices, line_reduce_scatter(): from_right[chain] = lax.ppermute(send_left, axis, leftward)  14.5 us
    ppermute x1, waiting for transfers between devices, halo_shift(): moved_head = lax.ppermute(outgoing[:split], axis, pairs)  13.4 us
    dot_general x31, matrix products, block(): jnp.dot(product, columns, preferred_element_type=jnp.float32)  10.9 us
    convert_element_type x1, other arithmetic, shards(): product_head = (query_feat_head * mixed_head).astype(jnp.bfloat16)  7.12 us
    convert_element_type x1, other arithmetic, shards(): product_tail = (query_body[filt_reach:] * mixed_tail).astype(jnp.bfloat16)  6.97 us
  transfers between devices with their start and end apart: 34, of which 15 were waited for; matrix products, arithmetic and copies ran while one was open for 9% of the time, Pallas kernels for 0%

profile of v8, /device:TPU:98, one launch (start us, length us, event | category | flops | bytes accessed | tf_op | source)
XLA Modules:
  0.0 228.5 jit_solution(9437074154726014134)
XLA Ops:
  6.4 26.0 %collective-permute-start.2 = (bf16[73,512]{1,0:T(8,128)(2,1)S(1)}, bf16[73,512]{1,0:T(8,128)(2,1)S(1)}, u32[]{:S(2)}, u32[]{:S(2)}) collective-permute-start(bf16[73,512]{1,0:T(8,128)(2,1)S(1)} %pad_maximum_fusion.2), channel_id=1, source_target_pairs={{0,16},{32,48},{48,64},{64,80},{96,112},{112,128},{128,144},{160,1... | collective-permute-start | bytes 224264 | tf_op jit(solution)/shard_map/ppermute | solution.py:20
  36.6 7.0 %fusion.189 = bf16[123,512]{1,0:T(8,128)(2,1)S(1)} fusion(f32[250,512]{1,0:T(8,128)S(1)} %get-tuple-element.5, f32[512]{0:T(512)S(1)} %bitcast.439, f32[512]{0:T(512)S(1)} %bitcast.441, f32[512]{0:T(512)S(1)} %bitcast.265, f32[512]{0:T(512)S(1)} %bitcast.267, f32[512]{0:T(512)S(1)} %bitcast.269, f32[512]{0:T(512)S(1)} %bitcast.271, f32[512]{0:T(512)S(1)} %bitcast.273, ...), kind=kLoop, calls=%fused_computation.402 | loop fusion | flops 16373760 | bytes 33011712 | tf_op jit(solution)/shard_map/convert_element_type | solution.py:91
  44.0 13.4 %collective-permute-done.3 = bf16[72,512]{1,0:T(8,128)(2,1)S(1)} collective-permute-done((bf16[72,512]{1,0:T(8,128)(2,1)S(1)}, bf16[72,512]{1,0:T(8,128)(2,1)S(1)}, u32[]{:S(2)}, u32[]{:S(2)}) %collective-permute-start.3) | collective-permute-done | bytes 73760 | tf_op jit(solution)/shard_map/ppermute | solution.py:18
  57.4 7.1 %fusion.55 = bf16[133,512]{1,0:T(8,128)(2,1)S(1)} fusion(f32[260,512]{1,0:T(8,128)S(1)} %fusion.185, bf16[127,512]{1,0:T(8,128)(2,1)S(1)} %get-tuple-element.13, bf16[6,512]{1,0:T(8,128)(2,1)S(1)} %fusion.318, f32[512]{0:T(512)S(1)} %copy-done.2, f32[512]{0:T(512)S(1)} %bitcast.440, f32[512]{0:T(512)S(1)} %bitcast.442, f32[512]{0:T(512)S(1)} %bitcast.266, ...), kind=kLoop, calls=%fused_computation.138 | loop fusion | flops 17977344 | bytes 35674112 | tf_op jit(solution)/shard_map/convert_element_type | solution.py:104
  76.0 24.4 %collective-permute-done.6 = bf16[256,512]{1,0:T(8,128)(2,1)S(1)} collective-permute-done((bf16[256,512]{1,0:T(8,128)(2,1)S(1)}, bf16[256,512]{1,0:T(8,128)(2,1)S(1)}, u32[]{:S(2)}, u32[]{:S(2)}) %collective-permute-start.6) | collective-permute-done | bytes 262176 | tf_op jit(solution)/shard_map/ppermute | solution.py:68
  103.5 7.1 %collective-permute-done.7 = bf16[256,512]{1,0:T(8,128)(2,1)S(1)} collective-permute-done((bf16[256,512]{1,0:T(8,128)(2,1)S(1)}, bf16[256,512]{1,0:T(8,128)(2,1)S(1)}, u32[]{:S(2)}, u32[]{:S(2)}) %collective-permute-start.7) | collective-permute-done | bytes 262176 | tf_op jit(solution)/shard_map/ppermute | solution.py:68
  110.7 3.4 %collective-permute-start.8 = (bf16[256,512]{1,0:T(8,128)(2,1)S(1)}, bf16[256,512]{1,0:T(8,128)(2,1)S(1)}, u32[]{:S(2)}, u32[]{:S(2)}) collective-permute-start(bf16[256,512]{1,0:T(8,128)(2,1)S(1)} %add_convert_fusion.25), channel_id=1, source_target_pairs={{0,1},{1,2},{2,3},{3,4},{4,5},{16,17},{17,18},{18,19},{19,20},{20,... | collective-permute-start | bytes 786440 | tf_op jit(solution)/shard_map/ppermute | solution.py:68
  115.2 4.8 %collective-permute-done.8 = bf16[256,512]{1,0:T(8,128)(2,1)S(1)} collective-permute-done((bf16[256,512]{1,0:T(8,128)(2,1)S(1)}, bf16[256,512]{1,0:T(8,128)(2,1)S(1)}, u32[]{:S(2)}, u32[]{:S(2)}) %collective-permute-start.8) | collective-permute-done | bytes 262176 | tf_op jit(solution)/shard_map/ppermute | solution.py:68
  120.1 4.8 %collective-permute-start.9 = (bf16[256,512]{1,0:T(8,128)(2,1)S(1)}, bf16[256,512]{1,0:T(8,128)(2,1)S(1)}, u32[]{:S(2)}, u32[]{:S(2)}) collective-permute-start(bf16[256,512]{1,0:T(8,128)(2,1)S(1)} %add_convert_fusion.24), channel_id=1, source_target_pairs={{0,1},{1,2},{2,3},{3,4},{4,5},{5,6},{16,17},{17,18},{18,19},{19,20... | collective-permute-start | bytes 786440 | tf_op jit(solution)/shard_map/ppermute | solution.py:68
  126.0 3.2 %collective-permute-done.9 = bf16[256,512]{1,0:T(8,128)(2,1)S(1)} collective-permute-done((bf16[256,512]{1,0:T(8,128)(2,1)S(1)}, bf16[256,512]{1,0:T(8,128)(2,1)S(1)}, u32[]{:S(2)}, u32[]{:S(2)}) %collective-permute-start.9) | collective-permute-done | bytes 262176 | tf_op jit(solution)/shard_map/ppermute | solution.py:68
  129.3 5.6 %collective-permute-start.10 = (bf16[256,512]{1,0:T(8,128)(2,1)S(1)}, bf16[256,512]{1,0:T(8,128)(2,1)S(1)}, u32[]{:S(2)}, u32[]{:S(2)}) collective-permute-start(bf16[256,512]{1,0:T(8,128)(2,1)S(1)} %add_convert_fusion.23), channel_id=1, source_target_pairs={{0,1},{1,2},{2,3},{3,4},{4,5},{5,6},{6,7},{16,17},{17,18},{18,19},... | collective-permute-start | bytes 786440 | tf_op jit(solution)/shard_map/ppermute | solution.py:68
  138.8 5.6 %collective-permute-start.11 = (bf16[256,512]{1,0:T(8,128)(2,1)S(1)}, bf16[256,512]{1,0:T(8,128)(2,1)S(1)}, u32[]{:S(2)}, u32[]{:S(2)}) collective-permute-start(bf16[256,512]{1,0:T(8,128)(2,1)S(1)} %add_convert_fusion.22), channel_id=1, source_target_pairs={{0,1},{1,2},{2,3},{3,4},{4,5},{5,6},{6,7},{7,8},{16,17},{17,18},{1... | collective-permute-start | bytes 786440 | tf_op jit(solution)/shard_map/ppermute | solution.py:68
  148.4 5.6 %collective-permute-start.12 = (bf16[256,512]{1,0:T(8,128)(2,1)S(1)}, bf16[256,512]{1,0:T(8,128)(2,1)S(1)}, u32[]{:S(2)}, u32[]{:S(2)}) collective-permute-start(bf16[256,512]{1,0:T(8,128)(2,1)S(1)} %add_convert_fusion.21), channel_id=1, source_target_pairs={{0,1},{1,2},{2,3},{3,4},{4,5},{5,6},{6,7},{7,8},{8,9},{16,17},{17,... | collective-permute-start | bytes 786440 | tf_op jit(solution)/shard_map/ppermute | solution.py:68
  157.9 5.6 %collective-permute-start.13 = (bf16[256,512]{1,0:T(8,128)(2,1)S(1)}, bf16[256,512]{1,0:T(8,128)(2,1)S(1)}, u32[]{:S(2)}, u32[]{:S(2)}) collective-permute-start(bf16[256,512]{1,0:T(8,128)(2,1)S(1)} %add_convert_fusion.20), channel_id=1, source_target_pairs={{0,1},{1,2},{2,3},{3,4},{4,5},{5,6},{6,7},{7,8},{8,9},{9,10},{16,1... | collective-permute-start | bytes 786440 | tf_op jit(solution)/shard_map/ppermute | solution.py:68
  164.6 3.8 %collective-permute-done.13 = bf16[256,512]{1,0:T(8,128)(2,1)S(1)} collective-permute-done((bf16[256,512]{1,0:T(8,128)(2,1)S(1)}, bf16[256,512]{1,0:T(8,128)(2,1)S(1)}, u32[]{:S(2)}, u32[]{:S(2)}) %collective-permute-start.13) | collective-permute-done | bytes 262176 | tf_op jit(solution)/shard_map/ppermute | solution.py:68
  168.5 5.6 %collective-permute-start.14 = (bf16[256,512]{1,0:T(8,128)(2,1)S(1)}, bf16[256,512]{1,0:T(8,128)(2,1)S(1)}, u32[]{:S(2)}, u32[]{:S(2)}) collective-permute-start(bf16[256,512]{1,0:T(8,128)(2,1)S(1)} %add_convert_fusion.19), channel_id=1, source_target_pairs={{0,1},{1,2},{2,3},{3,4},{4,5},{5,6},{6,7},{7,8},{8,9},{9,10},{10,1... | collective-permute-start | bytes 786440 | tf_op jit(solution)/shard_map/ppermute | solution.py:68
  175.2 5.1 %collective-permute-done.14 = bf16[256,512]{1,0:T(8,128)(2,1)S(1)} collective-permute-done((bf16[256,512]{1,0:T(8,128)(2,1)S(1)}, bf16[256,512]{1,0:T(8,128)(2,1)S(1)}, u32[]{:S(2)}, u32[]{:S(2)}) %collective-permute-start.14) | collective-permute-done | bytes 262176 | tf_op jit(solution)/shard_map/ppermute | solution.py:68
  180.4 5.6 %collective-permute-start.15 = (bf16[256,512]{1,0:T(8,128)(2,1)S(1)}, bf16[256,512]{1,0:T(8,128)(2,1)S(1)}, u32[]{:S(2)}, u32[]{:S(2)}) collective-permute-start(bf16[256,512]{1,0:T(8,128)(2,1)S(1)} %add_convert_fusion.18), channel_id=1, source_target_pairs={{0,1},{1,2},{2,3},{3,4},{4,5},{5,6},{6,7},{7,8},{8,9},{9,10},{10,1... | collective-permute-start | bytes 786440 | tf_op jit(solution)/shard_map/ppermute | solution.py:68
  187.7 4.3 %collective-permute-done.15 = bf16[256,512]{1,0:T(8,128)(2,1)S(1)} collective-permute-done((bf16[256,512]{1,0:T(8,128)(2,1)S(1)}, bf16[256,512]{1,0:T(8,128)(2,1)S(1)}, u32[]{:S(2)}, u32[]{:S(2)}) %collective-permute-start.15) | collective-permute-done | bytes 262176 | tf_op jit(solution)/shard_map/ppermute | solution.py:68
  192.1 5.6 %collective-permute-start.16 = (bf16[256,512]{1,0:T(8,128)(2,1)S(1)}, bf16[256,512]{1,0:T(8,128)(2,1)S(1)}, u32[]{:S(2)}, u32[]{:S(2)}) collective-permute-start(bf16[256,512]{1,0:T(8,128)(2,1)S(1)} %add_convert_fusion.17), channel_id=1, source_target_pairs={{0,1},{1,2},{2,3},{3,4},{4,5},{5,6},{6,7},{7,8},{8,9},{9,10},{10,1... | collective-permute-start | bytes 786440 | tf_op jit(solution)/shard_map/ppermute | solution.py:68
  200.0 2.9 %collective-permute-done.16 = bf16[256,512]{1,0:T(8,128)(2,1)S(1)} collective-permute-done((bf16[256,512]{1,0:T(8,128)(2,1)S(1)}, bf16[256,512]{1,0:T(8,128)(2,1)S(1)}, u32[]{:S(2)}, u32[]{:S(2)}) %collective-permute-start.16) | collective-permute-done | bytes 262176 | tf_op jit(solution)/shard_map/ppermute | solution.py:68
  203.0 5.6 %collective-permute-start.17 = (bf16[256,512]{1,0:T(8,128)(2,1)S(1)}, bf16[256,512]{1,0:T(8,128)(2,1)S(1)}, u32[]{:S(2)}, u32[]{:S(2)}) collective-permute-start(bf16[256,512]{1,0:T(8,128)(2,1)S(1)} %add_convert_fusion.16), channel_id=1, source_target_pairs={{0,1},{1,2},{2,3},{3,4},{4,5},{5,6},{6,7},{7,8},{8,9},{9,10},{10,1... | collective-permute-start | bytes 786440 | tf_op jit(solution)/shard_map/ppermute | solution.py:68
  212.6 5.6 %collective-permute-start.18 = (bf16[256,512]{1,0:T(8,128)(2,1)S(1)}, bf16[256,512]{1,0:T(8,128)(2,1)S(1)}, u32[]{:S(2)}, u32[]{:S(2)}) collective-permute-start(bf16[256,512]{1,0:T(8,128)(2,1)S(1)} %add_convert_fusion.15), channel_id=1, source_target_pairs={{0,1},{1,2},{2,3},{3,4},{4,5},{5,6},{6,7},{7,8},{8,9},{9,10},{10,1... | collective-permute-start | bytes 786440 | tf_op jit(solution)/shard_map/ppermute | solution.py:68
  222.1 5.7 %collective-permute-done.33 = bf16[256,512]{1,0:T(8,128)(2,1)S(1)} collective-permute-done((bf16[256,512]{1,0:T(8,128)(2,1)S(1)}, bf16[256,512]{1,0:T(8,128)(2,1)S(1)}, u32[]{:S(2)}, u32[]{:S(2)}) %collective-permute-start.33) | collective-permute-done | bytes 262176 | tf_op jit(solution)/shard_map/ppermute | solution.py:69
  (145 shorter events, 53.9 us)
Async XLA Ops:
  5.7 30.2 %collective-permute-start = (bf16[73,512]{1,0:T(8,128)(2,1)S(1)}, bf16[73,512]{1,0:T(8,128)(2,1)S(1)}, u32[]{:S(2)}, u32[]{:S(2)}) collective-permute-start(bf16[73,512]{1,0:T(8,128)(2,1)S(1)} %pad_maximum_fusion.2), channel_id=1, source_target_pairs={{16,33},{17,34},{18,35},{19,36},{20,37},{21,38},{22,39},{23,40},{2... | collective-permute-start | bytes 224264 | tf_op jit(solution)/shard_map/ppermute | solution.py:28
  6.4 37.4 %collective-permute-start.2 = (bf16[73,512]{1,0:T(8,128)(2,1)S(1)}, bf16[73,512]{1,0:T(8,128)(2,1)S(1)}, u32[]{:S(2)}, u32[]{:S(2)}) collective-permute-start(bf16[73,512]{1,0:T(8,128)(2,1)S(1)} %pad_maximum_fusion.2), channel_id=1, source_target_pairs={{0,16},{32,48},{48,64},{64,80},{96,112},{112,128},{128,144},{160,1... | collective-permute-start | bytes 224264 | tf_op jit(solution)/shard_map/ppermute | solution.py:20
  32.4 24.9 %collective-permute-start.3 = (bf16[72,512]{1,0:T(8,128)(2,1)S(1)}, bf16[72,512]{1,0:T(8,128)(2,1)S(1)}, u32[]{:S(2)}, u32[]{:S(2)}) collective-permute-start(bf16[72,512]{1,0:T(8,128)(2,1)S(1)} %slice.2087), channel_id=1, source_target_pairs={{0,16},{16,32},{32,48},{48,64},{64,80},{80,96},{96,112},{112,128},... | collective-permute-start | bytes 221192 | tf_op jit(solution)/shard_map/ppermute | solution.py:18
  73.6 26.8 %collective-permute-start.6 = (bf16[256,512]{1,0:T(8,128)(2,1)S(1)}, bf16[256,512]{1,0:T(8,128)(2,1)S(1)}, u32[]{:S(2)}, u32[]{:S(2)}) collective-permute-start(bf16[256,512]{1,0:T(8,128)(2,1)S(1)} %add_convert_fusion.27), channel_id=1, source_target_pairs={{0,1},{1,2},{2,3},{16,17},{17,18},{18,19},{32,33},{33,34},{34,35},... | collective-permute-start | bytes 786440 | tf_op jit(solution)/shard_map/ppermute | solution.py:68
  75.0 27.4 %collective-permute-start.21 = (bf16[256,512]{1,0:T(8,128)(2,1)S(1)}, bf16[256,512]{1,0:T(8,128)(2,1)S(1)}, u32[]{:S(2)}, u32[]{:S(2)}) collective-permute-start(bf16[256,512]{1,0:T(8,128)(2,1)S(1)} %add_convert_fusion.13), channel_id=1, source_target_pairs={{13,12},{14,13},{15,14},{29,28},{30,29},{31,30},{45,44},{46,45},{4... | collective-permute-start | bytes 786440 | tf_op jit(solution)/shard_map/ppermute | solution.py:69
  100.5 10.2 %collective-permute-start.7 = (bf16[256,512]{1,0:T(8,128)(2,1)S(1)}, bf16[256,512]{1,0:T(8,128)(2,1)S(1)}, u32[]{:S(2)}, u32[]{:S(2)}) collective-permute-start(bf16[256,512]{1,0:T(8,128)(2,1)S(1)} %add_convert_fusion.26), channel_id=1, source_target_pairs={{0,1},{1,2},{2,3},{3,4},{16,17},{17,18},{18,19},{19,20},{32,33},{3... | collective-permute-start | bytes 786440 | tf_op jit(solution)/shard_map/ppermute | solution.py:68
  102.5 11.6 %collective-permute-start.22 = (bf16[256,512]{1,0:T(8,128)(2,1)S(1)}, bf16[256,512]{1,0:T(8,128)(2,1)S(1)}, u32[]{:S(2)}, u32[]{:S(2)}) collective-permute-start(bf16[256,512]{1,0:T(8,128)(2,1)S(1)} %add_convert_fusion.12), channel_id=1, source_target_pairs={{12,11},{13,12},{14,13},{15,14},{28,27},{29,28},{30,29},{31,30},{4... | collective-permute-start | bytes 786440 | tf_op jit(solution)/shard_map/ppermute | solution.py:69
  114.1 10.8 %collective-permute-start.23 = (bf16[256,512]{1,0:T(8,128)(2,1)S(1)}, bf16[256,512]{1,0:T(8,128)(2,1)S(1)}, u32[]{:S(2)}, u32[]{:S(2)}) collective-permute-start(bf16[256,512]{1,0:T(8,128)(2,1)S(1)} %add_convert_fusion.11), channel_id=1, source_target_pairs={{11,10},{12,11},{13,12},{14,13},{15,14},{27,26},{28,27},{29,28},{3... | collective-permute-start | bytes 786440 | tf_op jit(solution)/shard_map/ppermute | solution.py:69
  125.0 9.9 %collective-permute-start.24 = (bf16[256,512]{1,0:T(8,128)(2,1)S(1)}, bf16[256,512]{1,0:T(8,128)(2,1)S(1)}, u32[]{:S(2)}, u32[]{:S(2)}) collective-permute-start(bf16[256,512]{1,0:T(8,128)(2,1)S(1)} %add_convert_fusion.10), channel_id=1, source_target_pairs={{10,9},{11,10},{12,11},{13,12},{14,13},{15,14},{26,25},{27,26},{28... | collective-permute-start | bytes 786440 | tf_op jit(solution)/shard_map/ppermute | solution.py:69
  129.3 9.5 %collective-permute-start.10 = (bf16[256,512]{1,0:T(8,128)(2,1)S(1)}, bf16[256,512]{1,0:T(8,128)(2,1)S(1)}, u32[]{:S(2)}, u32[]{:S(2)}) collective-permute-start(bf16[256,512]{1,0:T(8,128)(2,1)S(1)} %add_convert_fusion.23), channel_id=1, source_target_pairs={{0,1},{1,2},{2,3},{3,4},{4,5},{5,6},{6,7},{16,17},{17,18},{18,19},... | collective-permute-start | bytes 786440 | tf_op jit(solution)/shard_map/ppermute | solution.py:68
  138.8 9.5 %collective-permute-start.11 = (bf16[256,512]{1,0:T(8,128)(2,1)S(1)}, bf16[256,512]{1,0:T(8,128)(2,1)S(1)}, u32[]{:S(2)}, u32[]{:S(2)}) collective-permute-start(bf16[256,512]{1,0:T(8,128)(2,1)S(1)} %add_convert_fusion.22), channel_id=1, source_target_pairs={{0,1},{1,2},{2,3},{3,4},{4,5},{5,6},{6,7},{7,8},{16,17},{17,18},{1... | collective-permute-start | bytes 786440 | tf_op jit(solution)/shard_map/ppermute | solution.py:68
  148.4 9.5 %collective-permute-start.12 = (bf16[256,512]{1,0:T(8,128)(2,1)S(1)}, bf16[256,512]{1,0:T(8,128)(2,1)S(1)}, u32[]{:S(2)}, u32[]{:S(2)}) collective-permute-start(bf16[256,512]{1,0:T(8,128)(2,1)S(1)} %add_convert_fusion.21), channel_id=1, source_target_pairs={{0,1},{1,2},{2,3},{3,4},{4,5},{5,6},{6,7},{7,8},{8,9},{16,17},{17,... | collective-permute-start | bytes 786440 | tf_op jit(solution)/shard_map/ppermute | solution.py:68
  157.9 10.6 %collective-permute-start.13 = (bf16[256,512]{1,0:T(8,128)(2,1)S(1)}, bf16[256,512]{1,0:T(8,128)(2,1)S(1)}, u32[]{:S(2)}, u32[]{:S(2)}) collective-permute-start(bf16[256,512]{1,0:T(8,128)(2,1)S(1)} %add_convert_fusion.20), channel_id=1, source_target_pairs={{0,1},{1,2},{2,3},{3,4},{4,5},{5,6},{6,7},{7,8},{8,9},{9,10},{16,1... | collective-permute-start | bytes 786440 | tf_op jit(solution)/shard_map/ppermute | solution.py:68
  163.6 10.5 %collective-permute-start.28 = (bf16[256,512]{1,0:T(8,128)(2,1)S(1)}, bf16[256,512]{1,0:T(8,128)(2,1)S(1)}, u32[]{:S(2)}, u32[]{:S(2)}) collective-permute-start(bf16[256,512]{1,0:T(8,128)(2,1)S(1)} %add_convert_fusion.6), channel_id=1, source_target_pairs={{6,5},{7,6},{8,7},{9,8},{10,9},{11,10},{12,11},{13,12},{14,13},{15... | collective-permute-start | bytes 786440 | tf_op jit(solution)/shard_map/ppermute | solution.py:69
  168.5 11.8 %collective-permute-start.14 = (bf16[256,512]{1,0:T(8,128)(2,1)S(1)}, bf16[256,512]{1,0:T(8,128)(2,1)S(1)}, u32[]{:S(2)}, u32[]{:S(2)}) collective-permute-start(bf16[256,512]{1,0:T(8,128)(2,1)S(1)} %add_convert_fusion.19), channel_id=1, source_target_pairs={{0,1},{1,2},{2,3},{3,4},{4,5},{5,6},{6,7},{7,8},{8,9},{9,10},{10,1... | collective-permute-start | bytes 786440 | tf_op jit(solution)/shard_map/ppermute | solution.py:68
  174.2 11.8 %collective-permute-start.29 = (bf16[256,512]{1,0:T(8,128)(2,1)S(1)}, bf16[256,512]{1,0:T(8,128)(2,1)S(1)}, u32[]{:S(2)}, u32[]{:S(2)}) collective-permute-start(bf16[256,512]{1,0:T(8,128)(2,1)S(1)} %add_convert_fusion.5), channel_id=1, source_target_pairs={{5,4},{6,5},{7,6},{8,7},{9,8},{10,9},{11,10},{12,11},{13,12},{14,1... | collective-permute-start | bytes 786440 | tf_op jit(solution)/shard_map/ppermute | solution.py:69
  180.4 11.7 %collective-permute-start.15 = (bf16[256,512]{1,0:T(8,128)(2,1)S(1)}, bf16[256,512]{1,0:T(8,128)(2,1)S(1)}, u32[]{:S(2)}, u32[]{:S(2)}) collective-permute-start(bf16[256,512]{1,0:T(8,128)(2,1)S(1)} %add_convert_fusion.18), channel_id=1, source_target_pairs={{0,1},{1,2},{2,3},{3,4},{4,5},{5,6},{6,7},{7,8},{8,9},{9,10},{10,1... | collective-permute-start | bytes 786440 | tf_op jit(solution)/shard_map/ppermute | solution.py:68
  186.1 11.6 %collective-permute-start.30 = (bf16[256,512]{1,0:T(8,128)(2,1)S(1)}, bf16[256,512]{1,0:T(8,128)(2,1)S(1)}, u32[]{:S(2)}, u32[]{:S(2)}) collective-permute-start(bf16[256,512]{1,0:T(8,128)(2,1)S(1)} %add_convert_fusion.4), channel_id=1, source_target_pairs={{4,3},{5,4},{6,5},{7,6},{8,7},{9,8},{10,9},{11,10},{12,11},{13,12}... | collective-permute-start | bytes 786440 | tf_op jit(solution)/shard_map/ppermute | solution.py:69
  192.1 10.9 %collective-permute-start.16 = (bf16[256,512]{1,0:T(8,128)(2,1)S(1)}, bf16[256,512]{1,0:T(8,128)(2,1)S(1)}, u32[]{:S(2)}, u32[]{:S(2)}) collective-permute-start(bf16[256,512]{1,0:T(8,128)(2,1)S(1)} %add_convert_fusion.17), channel_id=1, source_target_pairs={{0,1},{1,2},{2,3},{3,4},{4,5},{5,6},{6,7},{7,8},{8,9},{9,10},{10,1... | collective-permute-start | bytes 786440 | tf_op jit(solution)/shard_map/ppermute | solution.py:68
  197.8 10.8 %collective-permute-start.31 = (bf16[256,512]{1,0:T(8,128)(2,1)S(1)}, bf16[256,512]{1,0:T(8,128)(2,1)S(1)}, u32[]{:S(2)}, u32[]{:S(2)}) collective-permute-start(bf16[256,512]{1,0:T(8,128)(2,1)S(1)} %add_convert_fusion.3), channel_id=1, source_target_pairs={{3,2},{4,3},{5,4},{6,5},{7,6},{8,7},{9,8},{10,9},{11,10},{12,11},{... | collective-permute-start | bytes 786440 | tf_op jit(solution)/shard_map/ppermute | solution.py:69
  203.0 9.5 %collective-permute-start.17 = (bf16[256,512]{1,0:T(8,128)(2,1)S(1)}, bf16[256,512]{1,0:T(8,128)(2,1)S(1)}, u32[]{:S(2)}, u32[]{:S(2)}) collective-permute-start(bf16[256,512]{1,0:T(8,128)(2,1)S(1)} %add_convert_fusion.16), channel_id=1, source_target_pairs={{0,1},{1,2},{2,3},{3,4},{4,5},{5,6},{6,7},{7,8},{8,9},{9,10},{10,1... | collective-permute-start | bytes 786440 | tf_op jit(solution)/shard_map/ppermute | solution.py:68
  208.7 9.5 %collective-permute-start.32 = (bf16[256,512]{1,0:T(8,128)(2,1)S(1)}, bf16[256,512]{1,0:T(8,128)(2,1)S(1)}, u32[]{:S(2)}, u32[]{:S(2)}) collective-permute-start(bf16[256,512]{1,0:T(8,128)(2,1)S(1)} %add_convert_fusion.2), channel_id=1, source_target_pairs={{2,1},{3,2},{4,3},{5,4},{6,5},{7,6},{8,7},{9,8},{10,9},{11,10},{12... | collective-permute-start | bytes 786440 | tf_op jit(solution)/shard_map/ppermute | solution.py:69
  212.6 9.5 %collective-permute-start.18 = (bf16[256,512]{1,0:T(8,128)(2,1)S(1)}, bf16[256,512]{1,0:T(8,128)(2,1)S(1)}, u32[]{:S(2)}, u32[]{:S(2)}) collective-permute-start(bf16[256,512]{1,0:T(8,128)(2,1)S(1)} %add_convert_fusion.15), channel_id=1, source_target_pairs={{0,1},{1,2},{2,3},{3,4},{4,5},{5,6},{6,7},{7,8},{8,9},{9,10},{10,1... | collective-permute-start | bytes 786440 | tf_op jit(solution)/shard_map/ppermute | solution.py:68
  218.3 9.5 %collective-permute-start.33 = (bf16[256,512]{1,0:T(8,128)(2,1)S(1)}, bf16[256,512]{1,0:T(8,128)(2,1)S(1)}, u32[]{:S(2)}, u32[]{:S(2)}) collective-permute-start(bf16[256,512]{1,0:T(8,128)(2,1)S(1)} %add_convert_fusion.1), channel_id=1, source_target_pairs={{1,0},{2,1},{3,2},{4,3},{5,4},{6,5},{7,6},{8,7},{9,8},{10,9},{11,1... | collective-permute-start | bytes 786440 | tf_op jit(solution)/shard_map/ppermute | solution.py:69
  (15 other events, 172.3 us)

commit v9 on v6

--- a/solution.py
+++ b/solution.py
@@ -64,10 +64,11 @@
     outgoing = jnp.concatenate(
         [gated_body[-filt_reach:], key_stream[-feat_reach:], value_stream[-feat_reach:], query_stream[-feat_reach:]], 0
     )
-    incoming = shifted(outgoing, "ctx", 1)
     query_body = valid_conv(wide(query_stream), feat_taps[0])
     mixed_tail = valid_conv(wide(gated_body), filt_taps) + skip_bias[None, :] * wide(gated_body[filt_reach:])
     product_tail = (query_body[filt_reach:] * mixed_tail).astype(jnp.bfloat16)
+    outgoing, product_tail = lax.optimization_barrier((outgoing, product_tail))
+    incoming = shifted(outgoing, "ctx", 1)
     gated_halo = incoming[:filt_reach]
     key_halo = incoming[filt_reach : filt_reach + feat_reach]
     value_halo = incoming[filt_reach + feat_reach : filt_reach + 2 * feat_reach]

time: 212 us -> 229 us (1.080)
  local copies, waits for them, and re-layouts: 3.78 us -> 12 us
  waiting for transfers between devices: 119 us -> 127 us
    ppermute x1, waiting for transfers between devices: 17.3 us -> 25.8 us  [shifted(): return lax.ppermute(block, axis, route)]
    slice x7, local copies, waits for them, and re-layouts: 0.99 us -> 8.02 us  [valid_conv(): taps[offset][None, :]]
  transfers between devices with their start and end apart: 31 -> 31, of which waited for: 13 -> 13; matrix products, arithmetic and copies ran while one was open for 10% -> 6% of each run, Pallas kernels for 0% -> 0%
where the time goes in v9:
time: 229 us; the launch traced here: 228 us
  waiting for transfers between devices  127 us (55%)
  starting transfers between devices  55.4 us (24%)
  other arithmetic  21.3 us (9%)
  local copies, waits for them, and re-layouts  12 us (5%)
  matrix products  10.9 us (5%)
    ppermute x15, waiting for transfers between devices, line_reduce_scatter(): from_right[chain] = lax.ppermute(send_left, axis, leftward)  101 us
    ppermute x15, starting transfers between devices, line_reduce_scatter(): from_left[chain] = lax.ppermute(send_right, axis, rightward)  29 us
    ppermute x1, waiting for transfers between devices, shifted(): return lax.ppermute(block, axis, route)  25.8 us
    ppermute x15, starting transfers between devices, line_reduce_scatter(): from_right[chain] = lax.ppermute(send_left, axis, leftward)  24.4 us
    dot_general x31, matrix products, block(): jnp.dot(product, columns, preferred_element_type=jnp.float32)  10.9 us
    slice x7, local copies, waits for them, and re-layouts, valid_conv(): taps[offset][None, :]  8.02 us
    convert_element_type x1, other arithmetic, shards(): product_head = (query_feat_head * mixed_head).astype(jnp.bfloat16)  7.09 us
    convert_element_type x1, other arithmetic, shards(): product_tail = (query_body[filt_reach:] * mixed_tail).astype(jnp.bfloat16)  6.93 us
  transfers between devices with their start and end apart: 31, of which 13 were waited for; matrix products, arithmetic and copies ran while one was open for 6% of the time, Pallas kernels for 0%

profile of v9, /device:TPU:376, one launch (start us, length us, event | category | flops | bytes accessed | tf_op | source)
XLA Modules:
  0.0 227.9 jit_solution(13491183561212252185)
XLA Ops:
  16.3 6.9 %fusion.184 = bf16[123,512]{1,0:T(8,128)(2,1)S(1)} fusion(f32[250,512]{1,0:T(8,128)S(1)} %get-tuple-element.9, f32[512]{0:T(512)S(1)} %bitcast.429, f32[512]{0:T(512)S(1)} %bitcast.431, f32[512]{0:T(512)S(1)} %bitcast.227, f32[512]{0:T(512)S(1)} %bitcast.229, f32[512]{0:T(512)S(1)} %bitcast.231, f32[512]{0:T(512)S(1)} %bitcast.233, f32[512]{0:T(512)S(1)} %bitcast.235, ...), kind=kLoop, calls=%fused_computation.397 | loop fusion | flops 16373760 | bytes 33011712 | tf_op jit(solution)/shard_map/convert_element_type | solution.py:69
  23.3 1.9 collective-permute-start
  25.3 25.8 %collective-permute-done = bf16[145,512]{1,0:T(8,128)(2,1)S(1)} collective-permute-done((bf16[145,512]{1,0:T(8,128)(2,1)S(1)}, bf16[145,512]{1,0:T(8,128)(2,1)S(1)}, u32[]{:S(2)}, u32[]{:S(2)}) %collective-permute-start) | collective-permute-done | bytes 148512 | tf_op jit(solution)/shard_map/ppermute | solution.py:10
  51.4 7.1 %fusion.54 = bf16[133,512]{1,0:T(8,128)(2,1)S(1)} fusion(f32[260,512]{1,0:T(8,128)S(1)} %maximum_convert_fusion, bf16[127,512]{1,0:T(8,128)(2,1)S(1)} %get-tuple-element.17, bf16[6,512]{1,0:T(8,128)(2,1)S(1)} %fusion.313, f32[512]{0:T(512)S(1)} %copy-done, f32[512]{0:T(512)S(1)} %bitcast.430, f32[512]{0:T(512)S(1)} %bitcast.432, f32[512]{0:T(512)S(1)} %bitcast.228, ...), kind=kLoop, calls=%fused_computation.136 | loop fusion | flops 17977344 | bytes 35674112 | tf_op jit(solution)/shard_map/convert_element_type | solution.py:84
  72.6 42.2 %collective-permute-done.19 = bf16[256,512]{1,0:T(8,128)(2,1)S(1)} collective-permute-done((bf16[256,512]{1,0:T(8,128)(2,1)S(1)}, bf16[256,512]{1,0:T(8,128)(2,1)S(1)}, u32[]{:S(2)}, u32[]{:S(2)}) %collective-permute-start.19) | collective-permute-done | bytes 262176 | tf_op jit(solution)/shard_map/ppermute | solution.py:48
  114.9 1.9 collective-permute-start.20
  117.9 7.6 %collective-permute-done.20 = bf16[256,512]{1,0:T(8,128)(2,1)S(1)} collective-permute-done((bf16[256,512]{1,0:T(8,128)(2,1)S(1)}, bf16[256,512]{1,0:T(8,128)(2,1)S(1)}, u32[]{:S(2)}, u32[]{:S(2)}) %collective-permute-start.20) | collective-permute-done | bytes 262176 | tf_op jit(solution)/shard_map/ppermute | solution.py:48
  128.6 6.7 %collective-permute-done.21 = bf16[256,512]{1,0:T(8,128)(2,1)S(1)} collective-permute-done((bf16[256,512]{1,0:T(8,128)(2,1)S(1)}, bf16[256,512]{1,0:T(8,128)(2,1)S(1)}, u32[]{:S(2)}, u32[]{:S(2)}) %collective-permute-start.21) | collective-permute-done | bytes 262176 | tf_op jit(solution)/shard_map/ppermute | solution.py:48
  138.4 6.5 %collective-permute-done.22 = bf16[256,512]{1,0:T(8,128)(2,1)S(1)} collective-permute-done((bf16[256,512]{1,0:T(8,128)(2,1)S(1)}, bf16[256,512]{1,0:T(8,128)(2,1)S(1)}, u32[]{:S(2)}, u32[]{:S(2)}) %collective-permute-start.22) | collective-permute-done | bytes 262176 | tf_op jit(solution)/shard_map/ppermute | solution.py:48
  144.9 1.9 collective-permute-start.23
  147.9 6.5 %collective-permute-done.23 = bf16[256,512]{1,0:T(8,128)(2,1)S(1)} collective-permute-done((bf16[256,512]{1,0:T(8,128)(2,1)S(1)}, bf16[256,512]{1,0:T(8,128)(2,1)S(1)}, u32[]{:S(2)}, u32[]{:S(2)}) %collective-permute-start.23) | collective-permute-done | bytes 262176 | tf_op jit(solution)/shard_map/ppermute | solution.py:48
  154.5 1.9 collective-permute-start.24
  157.5 6.6 %collective-permute-done.24 = bf16[256,512]{1,0:T(8,128)(2,1)S(1)} collective-permute-done((bf16[256,512]{1,0:T(8,128)(2,1)S(1)}, bf16[256,512]{1,0:T(8,128)(2,1)S(1)}, u32[]{:S(2)}, u32[]{:S(2)}) %collective-permute-start.24) | collective-permute-done | bytes 262176 | tf_op jit(solution)/shard_map/ppermute | solution.py:48
  164.2 1.9 collective-permute-start.25
  167.8 7.1 %collective-permute-done.25 = bf16[256,512]{1,0:T(8,128)(2,1)S(1)} collective-permute-done((bf16[256,512]{1,0:T(8,128)(2,1)S(1)}, bf16[256,512]{1,0:T(8,128)(2,1)S(1)}, u32[]{:S(2)}, u32[]{:S(2)}) %collective-permute-start.25) | collective-permute-done | bytes 262176 | tf_op jit(solution)/shard_map/ppermute | solution.py:48
  177.3 5.1 %collective-permute-start.12 = (bf16[256,512]{1,0:T(8,128)(2,1)S(1)}, bf16[256,512]{1,0:T(8,128)(2,1)S(1)}, u32[]{:S(2)}, u32[]{:S(2)}) collective-permute-start(bf16[256,512]{1,0:T(8,128)(2,1)S(1)} %add_convert_fusion.18), channel_id=1, source_target_pairs={{0,1},{1,2},{2,3},{3,4},{4,5},{5,6},{6,7},{7,8},{8,9},{9,10},{10,1... | collective-permute-start | bytes 786440 | tf_op jit(solution)/shard_map/ppermute | solution.py:47
  182.4 4.4 %collective-permute-done.26 = bf16[256,512]{1,0:T(8,128)(2,1)S(1)} collective-permute-done((bf16[256,512]{1,0:T(8,128)(2,1)S(1)}, bf16[256,512]{1,0:T(8,128)(2,1)S(1)}, u32[]{:S(2)}, u32[]{:S(2)}) %collective-permute-start.26) | collective-permute-done | bytes 262176 | tf_op jit(solution)/shard_map/ppermute | solution.py:48
  189.3 5.3 %collective-permute-start.13 = (bf16[256,512]{1,0:T(8,128)(2,1)S(1)}, bf16[256,512]{1,0:T(8,128)(2,1)S(1)}, u32[]{:S(2)}, u32[]{:S(2)}) collective-permute-start(bf16[256,512]{1,0:T(8,128)(2,1)S(1)} %add_convert_fusion.17), channel_id=1, source_target_pairs={{0,1},{1,2},{2,3},{3,4},{4,5},{5,6},{6,7},{7,8},{8,9},{9,10},{10,1... | collective-permute-start | bytes 786440 | tf_op jit(solution)/shard_map/ppermute | solution.py:47
  194.6 3.8 %collective-permute-done.27 = bf16[256,512]{1,0:T(8,128)(2,1)S(1)} collective-permute-done((bf16[256,512]{1,0:T(8,128)(2,1)S(1)}, bf16[256,512]{1,0:T(8,128)(2,1)S(1)}, u32[]{:S(2)}, u32[]{:S(2)}) %collective-permute-start.27) | collective-permute-done | bytes 262176 | tf_op jit(solution)/shard_map/ppermute | solution.py:48
  200.8 5.1 %collective-permute-start.14 = (bf16[256,512]{1,0:T(8,128)(2,1)S(1)}, bf16[256,512]{1,0:T(8,128)(2,1)S(1)}, u32[]{:S(2)}, u32[]{:S(2)}) collective-permute-start(bf16[256,512]{1,0:T(8,128)(2,1)S(1)} %add_convert_fusion.16), channel_id=1, source_target_pairs={{0,1},{1,2},{2,3},{3,4},{4,5},{5,6},{6,7},{7,8},{8,9},{9,10},{10,1... | collective-permute-start | bytes 786440 | tf_op jit(solution)/shard_map/ppermute | solution.py:47
  206.0 2.0 collective-permute-done.28
  210.4 5.1 %collective-permute-start.15 = (bf16[256,512]{1,0:T(8,128)(2,1)S(1)}, bf16[256,512]{1,0:T(8,128)(2,1)S(1)}, u32[]{:S(2)}, u32[]{:S(2)}) collective-permute-start(bf16[256,512]{1,0:T(8,128)(2,1)S(1)} %add_convert_fusion.15), channel_id=1, source_target_pairs={{0,1},{1,2},{2,3},{3,4},{4,5},{5,6},{6,7},{7,8},{8,9},{9,10},{10,1... | collective-permute-start | bytes 786440 | tf_op jit(solution)/shard_map/ppermute | solution.py:47
  215.5 2.0 collective-permute-done.29
  220.9 6.2 %collective-permute-done.30 = bf16[256,512]{1,0:T(8,128)(2,1)S(1)} collective-permute-done((bf16[256,512]{1,0:T(8,128)(2,1)S(1)}, bf16[256,512]{1,0:T(8,128)(2,1)S(1)}, u32[]{:S(2)}, u32[]{:S(2)}) %collective-permute-start.30) | collective-permute-done | bytes 262176 | tf_op jit(solution)/shard_map/ppermute | solution.py:48
  (134 shorter events, 55.2 us)
Async XLA Ops:
  23.3 27.9 %collective-permute-start = (bf16[145,512]{1,0:T(8,128)(2,1)S(1)}, bf16[145,512]{1,0:T(8,128)(2,1)S(1)}, u32[]{:S(2)}, u32[]{:S(2)}) collective-permute-start(bf16[145,512]{1,0:T(8,128)(2,1)S(1)} %pad_maximum_fusion.2), channel_id=1, source_target_pairs={{0,16},{16,32},{32,48},{48,64},{64,80},{80,96},{96,112},{112,128},... | collective-permute-start | bytes 445448 | tf_op jit(solution)/shard_map/ppermute | solution.py:10
  70.2 44.6 %collective-permute-start.19 = (bf16[256,512]{1,0:T(8,128)(2,1)S(1)}, bf16[256,512]{1,0:T(8,128)(2,1)S(1)}, u32[]{:S(2)}, u32[]{:S(2)}) collective-permute-start(bf16[256,512]{1,0:T(8,128)(2,1)S(1)} %add_convert_fusion.12), channel_id=1, source_target_pairs={{12,11},{13,12},{14,13},{15,14},{28,27},{29,28},{30,29},{31,30},{4... | collective-permute-start | bytes 786440 | tf_op jit(solution)/shard_map/ppermute | solution.py:48
  72.0 45.2 %collective-permute-start.5 = (bf16[256,512]{1,0:T(8,128)(2,1)S(1)}, bf16[256,512]{1,0:T(8,128)(2,1)S(1)}, u32[]{:S(2)}, u32[]{:S(2)}) collective-permute-start(bf16[256,512]{1,0:T(8,128)(2,1)S(1)} %add_convert_fusion.25), channel_id=1, source_target_pairs={{0,1},{1,2},{2,3},{3,4},{4,5},{16,17},{17,18},{18,19},{19,20},{20,... | collective-permute-start | bytes 786440 | tf_op jit(solution)/shard_map/ppermute | solution.py:47
  114.9 10.6 %collective-permute-start.20 = (bf16[256,512]{1,0:T(8,128)(2,1)S(1)}, bf16[256,512]{1,0:T(8,128)(2,1)S(1)}, u32[]{:S(2)}, u32[]{:S(2)}) collective-permute-start(bf16[256,512]{1,0:T(8,128)(2,1)S(1)} %add_convert_fusion.11), channel_id=1, source_target_pairs={{11,10},{12,11},{13,12},{14,13},{15,14},{27,26},{28,27},{29,28},{3... | collective-permute-start | bytes 786440 | tf_op jit(solution)/shard_map/ppermute | solution.py:48
  117.2 10.6 %collective-permute-start.6 = (bf16[256,512]{1,0:T(8,128)(2,1)S(1)}, bf16[256,512]{1,0:T(8,128)(2,1)S(1)}, u32[]{:S(2)}, u32[]{:S(2)}) collective-permute-start(bf16[256,512]{1,0:T(8,128)(2,1)S(1)} %add_convert_fusion.24), channel_id=1, source_target_pairs={{0,1},{1,2},{2,3},{3,4},{4,5},{5,6},{16,17},{17,18},{18,19},{19,20... | collective-permute-start | bytes 786440 | tf_op jit(solution)/shard_map/ppermute | solution.py:47
  125.6 9.7 %collective-permute-start.21 = (bf16[256,512]{1,0:T(8,128)(2,1)S(1)}, bf16[256,512]{1,0:T(8,128)(2,1)S(1)}, u32[]{:S(2)}, u32[]{:S(2)}) collective-permute-start(bf16[256,512]{1,0:T(8,128)(2,1)S(1)} %add_convert_fusion.10), channel_id=1, source_target_pairs={{10,9},{11,10},{12,11},{13,12},{14,13},{15,14},{26,25},{27,26},{28... | collective-permute-start | bytes 786440 | tf_op jit(solution)/shard_map/ppermute | solution.py:48
  127.9 9.7 %collective-permute-start.7 = (bf16[256,512]{1,0:T(8,128)(2,1)S(1)}, bf16[256,512]{1,0:T(8,128)(2,1)S(1)}, u32[]{:S(2)}, u32[]{:S(2)}) collective-permute-start(bf16[256,512]{1,0:T(8,128)(2,1)S(1)} %add_convert_fusion.23), channel_id=1, source_target_pairs={{0,1},{1,2},{2,3},{3,4},{4,5},{5,6},{6,7},{16,17},{17,18},{18,19},... | collective-permute-start | bytes 786440 | tf_op jit(solution)/shard_map/ppermute | solution.py:47
  135.4 9.5 %collective-permute-start.22 = (bf16[256,512]{1,0:T(8,128)(2,1)S(1)}, bf16[256,512]{1,0:T(8,128)(2,1)S(1)}, u32[]{:S(2)}, u32[]{:S(2)}) collective-permute-start(bf16[256,512]{1,0:T(8,128)(2,1)S(1)} %add_convert_fusion.9), channel_id=1, source_target_pairs={{9,8},{10,9},{11,10},{12,11},{13,12},{14,13},{15,14},{25,24},{26,2... | collective-permute-start | bytes 786440 | tf_op jit(solution)/shard_map/ppermute | solution.py:48
  137.7 9.5 %collective-permute-start.8 = (bf16[256,512]{1,0:T(8,128)(2,1)S(1)}, bf16[256,512]{1,0:T(8,128)(2,1)S(1)}, u32[]{:S(2)}, u32[]{:S(2)}) collective-permute-start(bf16[256,512]{1,0:T(8,128)(2,1)S(1)} %add_convert_fusion.22), channel_id=1, source_target_pairs={{0,1},{1,2},{2,3},{3,4},{4,5},{5,6},{6,7},{7,8},{16,17},{17,18},{1... | collective-permute-start | bytes 786440 | tf_op jit(solution)/shard_map/ppermute | solution.py:47
  144.9 9.5 %collective-permute-start.23 = (bf16[256,512]{1,0:T(8,128)(2,1)S(1)}, bf16[256,512]{1,0:T(8,128)(2,1)S(1)}, u32[]{:S(2)}, u32[]{:S(2)}) collective-permute-start(bf16[256,512]{1,0:T(8,128)(2,1)S(1)} %add_convert_fusion.8), channel_id=1, source_target_pairs={{8,7},{9,8},{10,9},{11,10},{12,11},{13,12},{14,13},{15,14},{24,23}... | collective-permute-start | bytes 786440 | tf_op jit(solution)/shard_map/ppermute | solution.py:48
  147.3 9.5 %collective-permute-start.9 = (bf16[256,512]{1,0:T(8,128)(2,1)S(1)}, bf16[256,512]{1,0:T(8,128)(2,1)S(1)}, u32[]{:S(2)}, u32[]{:S(2)}) collective-permute-start(bf16[256,512]{1,0:T(8,128)(2,1)S(1)} %add_convert_fusion.21), channel_id=1, source_target_pairs={{0,1},{1,2},{2,3},{3,4},{4,5},{5,6},{6,7},{7,8},{8,9},{16,17},{17,... | collective-permute-start | bytes 786440 | tf_op jit(solution)/shard_map/ppermute | solution.py:47
  154.5 9.6 %collective-permute-start.24 = (bf16[256,512]{1,0:T(8,128)(2,1)S(1)}, bf16[256,512]{1,0:T(8,128)(2,1)S(1)}, u32[]{:S(2)}, u32[]{:S(2)}) collective-permute-start(bf16[256,512]{1,0:T(8,128)(2,1)S(1)} %add_convert_fusion.7), channel_id=1, source_target_pairs={{7,6},{8,7},{9,8},{10,9},{11,10},{12,11},{13,12},{14,13},{15,14},{... | collective-permute-start | bytes 786440 | tf_op jit(solution)/shard_map/ppermute | solution.py:48
  156.8 9.6 %collective-permute-start.10 = (bf16[256,512]{1,0:T(8,128)(2,1)S(1)}, bf16[256,512]{1,0:T(8,128)(2,1)S(1)}, u32[]{:S(2)}, u32[]{:S(2)}) collective-permute-start(bf16[256,512]{1,0:T(8,128)(2,1)S(1)} %add_convert_fusion.20), channel_id=1, source_target_pairs={{0,1},{1,2},{2,3},{3,4},{4,5},{5,6},{6,7},{7,8},{8,9},{9,10},{16,1... | collective-permute-start | bytes 786440 | tf_op jit(solution)/shard_map/ppermute | solution.py:47
  164.2 10.7 %collective-permute-start.25 = (bf16[256,512]{1,0:T(8,128)(2,1)S(1)}, bf16[256,512]{1,0:T(8,128)(2,1)S(1)}, u32[]{:S(2)}, u32[]{:S(2)}) collective-permute-start(bf16[256,512]{1,0:T(8,128)(2,1)S(1)} %add_convert_fusion.6), channel_id=1, source_target_pairs={{6,5},{7,6},{8,7},{9,8},{10,9},{11,10},{12,11},{13,12},{14,13},{15... | collective-permute-start | bytes 786440 | tf_op jit(solution)/shard_map/ppermute | solution.py:48
  166.5 10.7 %collective-permute-start.11 = (bf16[256,512]{1,0:T(8,128)(2,1)S(1)}, bf16[256,512]{1,0:T(8,128)(2,1)S(1)}, u32[]{:S(2)}, u32[]{:S(2)}) collective-permute-start(bf16[256,512]{1,0:T(8,128)(2,1)S(1)} %add_convert_fusion.19), channel_id=1, source_target_pairs={{0,1},{1,2},{2,3},{3,4},{4,5},{5,6},{6,7},{7,8},{8,9},{9,10},{10,1... | collective-permute-start | bytes 786440 | tf_op jit(solution)/shard_map/ppermute | solution.py:47
  174.9 11.9 %collective-permute-start.26 = (bf16[256,512]{1,0:T(8,128)(2,1)S(1)}, bf16[256,512]{1,0:T(8,128)(2,1)S(1)}, u32[]{:S(2)}, u32[]{:S(2)}) collective-permute-start(bf16[256,512]{1,0:T(8,128)(2,1)S(1)} %add_convert_fusion.5), channel_id=1, source_target_pairs={{5,4},{6,5},{7,6},{8,7},{9,8},{10,9},{11,10},{12,11},{13,12},{14,1... | collective-permute-start | bytes 786440 | tf_op jit(solution)/shard_map/ppermute | solution.py:48
  177.3 11.9 %collective-permute-start.12 = (bf16[256,512]{1,0:T(8,128)(2,1)S(1)}, bf16[256,512]{1,0:T(8,128)(2,1)S(1)}, u32[]{:S(2)}, u32[]{:S(2)}) collective-permute-start(bf16[256,512]{1,0:T(8,128)(2,1)S(1)} %add_convert_fusion.18), channel_id=1, source_target_pairs={{0,1},{1,2},{2,3},{3,4},{4,5},{5,6},{6,7},{7,8},{8,9},{9,10},{10,1... | collective-permute-start | bytes 786440 | tf_op jit(solution)/shard_map/ppermute | solution.py:47
  186.9 11.5 %collective-permute-start.27 = (bf16[256,512]{1,0:T(8,128)(2,1)S(1)}, bf16[256,512]{1,0:T(8,128)(2,1)S(1)}, u32[]{:S(2)}, u32[]{:S(2)}) collective-permute-start(bf16[256,512]{1,0:T(8,128)(2,1)S(1)} %add_convert_fusion.4), channel_id=1, source_target_pairs={{4,3},{5,4},{6,5},{7,6},{8,7},{9,8},{10,9},{11,10},{12,11},{13,12}... | collective-permute-start | bytes 786440 | tf_op jit(solution)/shard_map/ppermute | solution.py:48
  189.3 11.5 %collective-permute-start.13 = (bf16[256,512]{1,0:T(8,128)(2,1)S(1)}, bf16[256,512]{1,0:T(8,128)(2,1)S(1)}, u32[]{:S(2)}, u32[]{:S(2)}) collective-permute-start(bf16[256,512]{1,0:T(8,128)(2,1)S(1)} %add_convert_fusion.17), channel_id=1, source_target_pairs={{0,1},{1,2},{2,3},{3,4},{4,5},{5,6},{6,7},{7,8},{8,9},{9,10},{10,1... | collective-permute-start | bytes 786440 | tf_op jit(solution)/shard_map/ppermute | solution.py:47
  198.5 9.5 %collective-permute-start.28 = (bf16[256,512]{1,0:T(8,128)(2,1)S(1)}, bf16[256,512]{1,0:T(8,128)(2,1)S(1)}, u32[]{:S(2)}, u32[]{:S(2)}) collective-permute-start(bf16[256,512]{1,0:T(8,128)(2,1)S(1)} %add_convert_fusion.3), channel_id=1, source_target_pairs={{3,2},{4,3},{5,4},{6,5},{7,6},{8,7},{9,8},{10,9},{11,10},{12,11},{... | collective-permute-start | bytes 786440 | tf_op jit(solution)/shard_map/ppermute | solution.py:48
  200.8 9.5 %collective-permute-start.14 = (bf16[256,512]{1,0:T(8,128)(2,1)S(1)}, bf16[256,512]{1,0:T(8,128)(2,1)S(1)}, u32[]{:S(2)}, u32[]{:S(2)}) collective-permute-start(bf16[256,512]{1,0:T(8,128)(2,1)S(1)} %add_convert_fusion.16), channel_id=1, source_target_pairs={{0,1},{1,2},{2,3},{3,4},{4,5},{5,6},{6,7},{7,8},{8,9},{9,10},{10,1... | collective-permute-start | bytes 786440 | tf_op jit(solution)/shard_map/ppermute | solution.py:47
  208.0 9.5 %collective-permute-start.29 = (bf16[256,512]{1,0:T(8,128)(2,1)S(1)}, bf16[256,512]{1,0:T(8,128)(2,1)S(1)}, u32[]{:S(2)}, u32[]{:S(2)}) collective-permute-start(bf16[256,512]{1,0:T(8,128)(2,1)S(1)} %add_convert_fusion.2), channel_id=1, source_target_pairs={{2,1},{3,2},{4,3},{5,4},{6,5},{7,6},{8,7},{9,8},{10,9},{11,10},{12... | collective-permute-start | bytes 786440 | tf_op jit(solution)/shard_map/ppermute | solution.py:48
  210.4 10.5 %collective-permute-start.15 = (bf16[256,512]{1,0:T(8,128)(2,1)S(1)}, bf16[256,512]{1,0:T(8,128)(2,1)S(1)}, u32[]{:S(2)}, u32[]{:S(2)}) collective-permute-start(bf16[256,512]{1,0:T(8,128)(2,1)S(1)} %add_convert_fusion.15), channel_id=1, source_target_pairs={{0,1},{1,2},{2,3},{3,4},{4,5},{5,6},{6,7},{7,8},{8,9},{9,10},{10,1... | collective-permute-start | bytes 786440 | tf_op jit(solution)/shard_map/ppermute | solution.py:47
  217.6 9.5 %collective-permute-start.30 = (bf16[256,512]{1,0:T(8,128)(2,1)S(1)}, bf16[256,512]{1,0:T(8,128)(2,1)S(1)}, u32[]{:S(2)}, u32[]{:S(2)}) collective-permute-start(bf16[256,512]{1,0:T(8,128)(2,1)S(1)} %add_convert_fusion.1), channel_id=1, source_target_pairs={{1,0},{2,1},{3,2},{4,3},{5,4},{6,5},{7,6},{8,7},{9,8},{10,9},{11,1... | collective-permute-start | bytes 786440 | tf_op jit(solution)/shard_map/ppermute | solution.py:48
  (10 other events, 47.9 us)

commit v10 on v6

--- a/solution.py
+++ b/solution.py
@@ -61,8 +61,11 @@
     key_body = valid_conv(wide(key_stream), feat_taps[1])
     value_body = valid_conv(wide(value_stream), feat_taps[2])
     gated_body = (key_body * value_body).astype(jnp.bfloat16)
+    key_last = valid_conv(wide(key_stream[-full_reach:]), feat_taps[1])
+    value_last = valid_conv(wide(value_stream[-full_reach:]), feat_taps[2])
+    gated_last = (key_last * value_last).astype(jnp.bfloat16)
     outgoing = jnp.concatenate(
-        [gated_body[-filt_reach:], key_stream[-feat_reach:], value_stream[-feat_reach:], query_stream[-feat_reach:]], 0
+        [gated_last, key_stream[-feat_reach:], value_stream[-feat_reach:], query_stream[-feat_reach:]], 0
     )
     incoming = shifted(outgoing, "ctx", 1)
     query_body = valid_conv(wide(query_stream), feat_taps[0])

time: 212 us -> 208 us (0.981)
  waiting for transfers between devices: 119 us -> 104 us
  local copies, waits for them, and re-layouts: 3.78 us -> 11.9 us
  other arithmetic: 20.3 us -> 22.6 us
    ppermute x1, waiting for transfers between devices: 17.3 us -> 5.34 us  [shifted(): return lax.ppermute(block, axis, route)]
    slice x7, local copies, waits for them, and re-layouts: 0.99 us -> 8.03 us  [valid_conv(): taps[offset][None, :]]
    ppermute x15, waiting for transfers between devices: 102 us -> 98.2 us  [line_reduce_scatter(): from_right[chain] = lax.ppermute(send_left, axis, leftward)]
    convert_element_type x8 -> x9, other arithmetic: 3.09 us -> 5.03 us  [shards(): wide = lambda x: x.astype(jnp.float32)]
  transfers between devices with their start and end apart: 31 -> 31, of which waited for: 13 -> 14; matrix products, arithmetic and copies ran while one was open for 10% -> 16% of each run, Pallas kernels for 0% -> 0%
where the time goes in v10:
time: 208 us; the launch traced here: 206 us
  waiting for transfers between devices  104 us (50%)
  starting transfers between devices  55.9 us (27%)
  other arithmetic  22.6 us (11%)
  local copies, waits for them, and re-layouts  11.9 us (6%)
  matrix products  10.9 us (5%)
    ppermute x15, waiting for transfers between devices, line_reduce_scatter(): from_right[chain] = lax.ppermute(send_left, axis, leftward)  98.2 us
    ppermute x15, starting transfers between devices, line_reduce_scatter(): from_left[chain] = lax.ppermute(send_right, axis, rightward)  29.5 us
    ppermute x15, starting transfers between devices, line_reduce_scatter(): from_right[chain] = lax.ppermute(send_left, axis, leftward)  24.4 us
    dot_general x31, matrix products, block(): jnp.dot(product, columns, preferred_element_type=jnp.float32)  10.9 us
    slice x7, local copies, waits for them, and re-layouts, valid_conv(): taps[offset][None, :]  8.03 us
    convert_element_type x1, other arithmetic, shards(): product_head = (query_feat_head * mixed_head).astype(jnp.bfloat16)  7.06 us
    convert_element_type x1, other arithmetic, shards(): product_tail = (query_body[filt_reach:] * mixed_tail).astype(jnp.bfloat16)  6.91 us
    ppermute x1, waiting for transfers between devices, shifted(): return lax.ppermute(block, axis, route)  5.34 us
  transfers between devices with their start and end apart: 31, of which 14 were waited for; matrix products, arithmetic and copies ran while one was open for 16% of the time, Pallas kernels for 0%

profile of v10, /device:TPU:376, one launch (start us, length us, event | category | flops | bytes accessed | tf_op | source)
XLA Modules:
  0.0 206.1 jit_solution(7163147540421036712)
XLA Ops:
  4.2 1.9 collective-permute-start
  19.7 6.9 %fusion.184 = bf16[123,512]{1,0:T(8,128)(2,1)S(1)} fusion(f32[250,512]{1,0:T(8,128)S(1)} %get-tuple-element.5, f32[512]{0:T(512)S(1)} %bitcast.453, f32[512]{0:T(512)S(1)} %bitcast.455, f32[512]{0:T(512)S(1)} %bitcast.279, f32[512]{0:T(512)S(1)} %bitcast.281, f32[512]{0:T(512)S(1)} %bitcast.283, f32[512]{0:T(512)S(1)} %bitcast.285, f32[512]{0:T(512)S(1)} %bitcast.287, ...), kind=kLoop, calls=%fused_computation.397 | loop fusion | flops 16373760 | bytes 33011712 | tf_op jit(solution)/shard_map/convert_element_type | solution.py:73
  26.8 5.3 %collective-permute-done = bf16[145,512]{1,0:T(8,128)(2,1)S(1)} collective-permute-done((bf16[145,512]{1,0:T(8,128)(2,1)S(1)}, bf16[145,512]{1,0:T(8,128)(2,1)S(1)}, u32[]{:S(2)}, u32[]{:S(2)}) %collective-permute-start) | collective-permute-done | bytes 148512 | tf_op jit(solution)/shard_map/ppermute | solution.py:10
  32.4 7.1 %fusion.54 = bf16[133,512]{1,0:T(8,128)(2,1)S(1)} fusion(f32[260,512]{1,0:T(8,128)S(1)} %maximum_convert_fusion, bf16[127,512]{1,0:T(8,128)(2,1)S(1)} %slice.2184, bf16[6,512]{1,0:T(8,128)(2,1)S(1)} %fusion.327, f32[512]{0:T(512)S(1)} %copy-done, f32[512]{0:T(512)S(1)} %bitcast.454, f32[512]{0:T(512)S(1)} %bitcast.456, f32[512]{0:T(512)S(1)} %bitcast.280, ...), kind=kLoop, calls=%fused_computation.136 | loop fusion | flops 17977344 | bytes 35674112 | tf_op jit(solution)/shard_map/convert_element_type | solution.py:86
  53.5 36.8 %collective-permute-done.19 = bf16[256,512]{1,0:T(8,128)(2,1)S(1)} collective-permute-done((bf16[256,512]{1,0:T(8,128)(2,1)S(1)}, bf16[256,512]{1,0:T(8,128)(2,1)S(1)}, u32[]{:S(2)}, u32[]{:S(2)}) %collective-permute-start.19) | collective-permute-done | bytes 262176 | tf_op jit(solution)/shard_map/ppermute | solution.py:48
  90.4 1.9 collective-permute-start.20
  93.4 9.2 %collective-permute-done.20 = bf16[256,512]{1,0:T(8,128)(2,1)S(1)} collective-permute-done((bf16[256,512]{1,0:T(8,128)(2,1)S(1)}, bf16[256,512]{1,0:T(8,128)(2,1)S(1)}, u32[]{:S(2)}, u32[]{:S(2)}) %collective-permute-start.20) | collective-permute-done | bytes 262176 | tf_op jit(solution)/shard_map/ppermute | solution.py:48
  105.8 8.4 %collective-permute-done.21 = bf16[256,512]{1,0:T(8,128)(2,1)S(1)} collective-permute-done((bf16[256,512]{1,0:T(8,128)(2,1)S(1)}, bf16[256,512]{1,0:T(8,128)(2,1)S(1)}, u32[]{:S(2)}, u32[]{:S(2)}) %collective-permute-start.21) | collective-permute-done | bytes 262176 | tf_op jit(solution)/shard_map/ppermute | solution.py:48
  114.2 1.9 collective-permute-start.22
  117.2 7.6 %collective-permute-done.22 = bf16[256,512]{1,0:T(8,128)(2,1)S(1)} collective-permute-done((bf16[256,512]{1,0:T(8,128)(2,1)S(1)}, bf16[256,512]{1,0:T(8,128)(2,1)S(1)}, u32[]{:S(2)}, u32[]{:S(2)}) %collective-permute-start.22) | collective-permute-done | bytes 262176 | tf_op jit(solution)/shard_map/ppermute | solution.py:48
  127.9 6.7 %collective-permute-done.23 = bf16[256,512]{1,0:T(8,128)(2,1)S(1)} collective-permute-done((bf16[256,512]{1,0:T(8,128)(2,1)S(1)}, bf16[256,512]{1,0:T(8,128)(2,1)S(1)}, u32[]{:S(2)}, u32[]{:S(2)}) %collective-permute-start.23) | collective-permute-done | bytes 262176 | tf_op jit(solution)/shard_map/ppermute | solution.py:48
  137.7 6.5 %collective-permute-done.24 = bf16[256,512]{1,0:T(8,128)(2,1)S(1)} collective-permute-done((bf16[256,512]{1,0:T(8,128)(2,1)S(1)}, bf16[256,512]{1,0:T(8,128)(2,1)S(1)}, u32[]{:S(2)}, u32[]{:S(2)}) %collective-permute-start.24) | collective-permute-done | bytes 262176 | tf_op jit(solution)/shard_map/ppermute | solution.py:48
  144.2 1.9 collective-permute-start.25
  147.8 5.8 %collective-permute-done.25 = bf16[256,512]{1,0:T(8,128)(2,1)S(1)} collective-permute-done((bf16[256,512]{1,0:T(8,128)(2,1)S(1)}, bf16[256,512]{1,0:T(8,128)(2,1)S(1)}, u32[]{:S(2)}, u32[]{:S(2)}) %collective-permute-start.25) | collective-permute-done | bytes 262176 | tf_op jit(solution)/shard_map/ppermute | solution.py:48
  153.7 1.9 collective-permute-start.26
  156.1 5.1 %collective-permute-start.12 = (bf16[256,512]{1,0:T(8,128)(2,1)S(1)}, bf16[256,512]{1,0:T(8,128)(2,1)S(1)}, u32[]{:S(2)}, u32[]{:S(2)}) collective-permute-start(bf16[256,512]{1,0:T(8,128)(2,1)S(1)} %add_convert_fusion.18), channel_id=1, source_target_pairs={{0,1},{1,2},{2,3},{3,4},{4,5},{5,6},{6,7},{7,8},{8,9},{9,10},{10,1... | collective-permute-start | bytes 786440 | tf_op jit(solution)/shard_map/ppermute | solution.py:47
  161.2 2.2 %collective-permute-done.26 = bf16[256,512]{1,0:T(8,128)(2,1)S(1)} collective-permute-done((bf16[256,512]{1,0:T(8,128)(2,1)S(1)}, bf16[256,512]{1,0:T(8,128)(2,1)S(1)}, u32[]{:S(2)}, u32[]{:S(2)}) %collective-permute-start.26) | collective-permute-done | bytes 262176 | tf_op jit(solution)/shard_map/ppermute | solution.py:48
  165.8 5.4 %collective-permute-start.13 = (bf16[256,512]{1,0:T(8,128)(2,1)S(1)}, bf16[256,512]{1,0:T(8,128)(2,1)S(1)}, u32[]{:S(2)}, u32[]{:S(2)}) collective-permute-start(bf16[256,512]{1,0:T(8,128)(2,1)S(1)} %add_convert_fusion.17), channel_id=1, source_target_pairs={{0,1},{1,2},{2,3},{3,4},{4,5},{5,6},{6,7},{7,8},{8,9},{9,10},{10,1... | collective-permute-start | bytes 786440 | tf_op jit(solution)/shard_map/ppermute | solution.py:47
  171.2 3.0 %collective-permute-done.27 = bf16[256,512]{1,0:T(8,128)(2,1)S(1)} collective-permute-done((bf16[256,512]{1,0:T(8,128)(2,1)S(1)}, bf16[256,512]{1,0:T(8,128)(2,1)S(1)}, u32[]{:S(2)}, u32[]{:S(2)}) %collective-permute-start.27) | collective-permute-done | bytes 262176 | tf_op jit(solution)/shard_map/ppermute | solution.py:48
  176.7 5.6 %collective-permute-start.14 = (bf16[256,512]{1,0:T(8,128)(2,1)S(1)}, bf16[256,512]{1,0:T(8,128)(2,1)S(1)}, u32[]{:S(2)}, u32[]{:S(2)}) collective-permute-start(bf16[256,512]{1,0:T(8,128)(2,1)S(1)} %add_convert_fusion.16), channel_id=1, source_target_pairs={{0,1},{1,2},{2,3},{3,4},{4,5},{5,6},{6,7},{7,8},{8,9},{9,10},{10,1... | collective-permute-start | bytes 786440 | tf_op jit(solution)/shard_map/ppermute | solution.py:47
  182.3 3.9 %collective-permute-done.28 = bf16[256,512]{1,0:T(8,128)(2,1)S(1)} collective-permute-done((bf16[256,512]{1,0:T(8,128)(2,1)S(1)}, bf16[256,512]{1,0:T(8,128)(2,1)S(1)}, u32[]{:S(2)}, u32[]{:S(2)}) %collective-permute-start.28) | collective-permute-done | bytes 262176 | tf_op jit(solution)/shard_map/ppermute | solution.py:48
  188.6 5.1 %collective-permute-start.15 = (bf16[256,512]{1,0:T(8,128)(2,1)S(1)}, bf16[256,512]{1,0:T(8,128)(2,1)S(1)}, u32[]{:S(2)}, u32[]{:S(2)}) collective-permute-start(bf16[256,512]{1,0:T(8,128)(2,1)S(1)} %add_convert_fusion.15), channel_id=1, source_target_pairs={{0,1},{1,2},{2,3},{3,4},{4,5},{5,6},{6,7},{7,8},{8,9},{9,10},{10,1... | collective-permute-start | bytes 786440 | tf_op jit(solution)/shard_map/ppermute | solution.py:47
  193.8 2.0 collective-permute-done.29
  199.1 6.2 %collective-permute-done.30 = bf16[256,512]{1,0:T(8,128)(2,1)S(1)} collective-permute-done((bf16[256,512]{1,0:T(8,128)(2,1)S(1)}, bf16[256,512]{1,0:T(8,128)(2,1)S(1)}, u32[]{:S(2)}, u32[]{:S(2)}) %collective-permute-start.30) | collective-permute-done | bytes 262176 | tf_op jit(solution)/shard_map/ppermute | solution.py:48
  (136 shorter events, 56.7 us)
Async XLA Ops:
  4.2 27.9 %collective-permute-start = (bf16[145,512]{1,0:T(8,128)(2,1)S(1)}, bf16[145,512]{1,0:T(8,128)(2,1)S(1)}, u32[]{:S(2)}, u32[]{:S(2)}) collective-permute-start(bf16[145,512]{1,0:T(8,128)(2,1)S(1)} %pad_maximum_fusion.2), channel_id=1, source_target_pairs={{0,16},{16,32},{32,48},{48,64},{64,80},{80,96},{96,112},{112,128},... | collective-permute-start | bytes 445448 | tf_op jit(solution)/shard_map/ppermute | solution.py:10
  51.1 39.2 %collective-permute-start.19 = (bf16[256,512]{1,0:T(8,128)(2,1)S(1)}, bf16[256,512]{1,0:T(8,128)(2,1)S(1)}, u32[]{:S(2)}, u32[]{:S(2)}) collective-permute-start(bf16[256,512]{1,0:T(8,128)(2,1)S(1)} %add_convert_fusion.12), channel_id=1, source_target_pairs={{12,11},{13,12},{14,13},{15,14},{28,27},{29,28},{30,29},{31,30},{4... | collective-permute-start | bytes 786440 | tf_op jit(solution)/shard_map/ppermute | solution.py:48
  52.9 39.8 %collective-permute-start.5 = (bf16[256,512]{1,0:T(8,128)(2,1)S(1)}, bf16[256,512]{1,0:T(8,128)(2,1)S(1)}, u32[]{:S(2)}, u32[]{:S(2)}) collective-permute-start(bf16[256,512]{1,0:T(8,128)(2,1)S(1)} %add_convert_fusion.25), channel_id=1, source_target_pairs={{0,1},{1,2},{2,3},{3,4},{4,5},{16,17},{17,18},{18,19},{19,20},{20,... | collective-permute-start | bytes 786440 | tf_op jit(solution)/shard_map/ppermute | solution.py:47
  90.4 12.2 %collective-permute-start.20 = (bf16[256,512]{1,0:T(8,128)(2,1)S(1)}, bf16[256,512]{1,0:T(8,128)(2,1)S(1)}, u32[]{:S(2)}, u32[]{:S(2)}) collective-permute-start(bf16[256,512]{1,0:T(8,128)(2,1)S(1)} %add_convert_fusion.11), channel_id=1, source_target_pairs={{11,10},{12,11},{13,12},{14,13},{15,14},{27,26},{28,27},{29,28},{3... | collective-permute-start | bytes 786440 | tf_op jit(solution)/shard_map/ppermute | solution.py:48
  92.7 12.2 %collective-permute-start.6 = (bf16[256,512]{1,0:T(8,128)(2,1)S(1)}, bf16[256,512]{1,0:T(8,128)(2,1)S(1)}, u32[]{:S(2)}, u32[]{:S(2)}) collective-permute-start(bf16[256,512]{1,0:T(8,128)(2,1)S(1)} %add_convert_fusion.24), channel_id=1, source_target_pairs={{0,1},{1,2},{2,3},{3,4},{4,5},{5,6},{16,17},{17,18},{18,19},{19,20... | collective-permute-start | bytes 786440 | tf_op jit(solution)/shard_map/ppermute | solution.py:47
  102.7 11.4 %collective-permute-start.21 = (bf16[256,512]{1,0:T(8,128)(2,1)S(1)}, bf16[256,512]{1,0:T(8,128)(2,1)S(1)}, u32[]{:S(2)}, u32[]{:S(2)}) collective-permute-start(bf16[256,512]{1,0:T(8,128)(2,1)S(1)} %add_convert_fusion.10), channel_id=1, source_target_pairs={{10,9},{11,10},{12,11},{13,12},{14,13},{15,14},{26,25},{27,26},{28... | collective-permute-start | bytes 786440 | tf_op jit(solution)/shard_map/ppermute | solution.py:48
  105.1 11.4 %collective-permute-start.7 = (bf16[256,512]{1,0:T(8,128)(2,1)S(1)}, bf16[256,512]{1,0:T(8,128)(2,1)S(1)}, u32[]{:S(2)}, u32[]{:S(2)}) collective-permute-start(bf16[256,512]{1,0:T(8,128)(2,1)S(1)} %add_convert_fusion.23), channel_id=1, source_target_pairs={{0,1},{1,2},{2,3},{3,4},{4,5},{5,6},{6,7},{16,17},{17,18},{18,19},... | collective-permute-start | bytes 786440 | tf_op jit(solution)/shard_map/ppermute | solution.py:47
  114.2 10.6 %collective-permute-start.22 = (bf16[256,512]{1,0:T(8,128)(2,1)S(1)}, bf16[256,512]{1,0:T(8,128)(2,1)S(1)}, u32[]{:S(2)}, u32[]{:S(2)}) collective-permute-start(bf16[256,512]{1,0:T(8,128)(2,1)S(1)} %add_convert_fusion.9), channel_id=1, source_target_pairs={{9,8},{10,9},{11,10},{12,11},{13,12},{14,13},{15,14},{25,24},{26,2... | collective-permute-start | bytes 786440 | tf_op jit(solution)/shard_map/ppermute | solution.py:48
  116.6 10.6 %collective-permute-start.8 = (bf16[256,512]{1,0:T(8,128)(2,1)S(1)}, bf16[256,512]{1,0:T(8,128)(2,1)S(1)}, u32[]{:S(2)}, u32[]{:S(2)}) collective-permute-start(bf16[256,512]{1,0:T(8,128)(2,1)S(1)} %add_convert_fusion.22), channel_id=1, source_target_pairs={{0,1},{1,2},{2,3},{3,4},{4,5},{5,6},{6,7},{7,8},{16,17},{17,18},{1... | collective-permute-start | bytes 786440 | tf_op jit(solution)/shard_map/ppermute | solution.py:47
  124.9 9.7 %collective-permute-start.23 = (bf16[256,512]{1,0:T(8,128)(2,1)S(1)}, bf16[256,512]{1,0:T(8,128)(2,1)S(1)}, u32[]{:S(2)}, u32[]{:S(2)}) collective-permute-start(bf16[256,512]{1,0:T(8,128)(2,1)S(1)} %add_convert_fusion.8), channel_id=1, source_target_pairs={{8,7},{9,8},{10,9},{11,10},{12,11},{13,12},{14,13},{15,14},{24,23}... | collective-permute-start | bytes 786440 | tf_op jit(solution)/shard_map/ppermute | solution.py:48
  127.2 9.7 %collective-permute-start.9 = (bf16[256,512]{1,0:T(8,128)(2,1)S(1)}, bf16[256,512]{1,0:T(8,128)(2,1)S(1)}, u32[]{:S(2)}, u32[]{:S(2)}) collective-permute-start(bf16[256,512]{1,0:T(8,128)(2,1)S(1)} %add_convert_fusion.21), channel_id=1, source_target_pairs={{0,1},{1,2},{2,3},{3,4},{4,5},{5,6},{6,7},{7,8},{8,9},{16,17},{17,... | collective-permute-start | bytes 786440 | tf_op jit(solution)/shard_map/ppermute | solution.py:47
  134.6 9.5 %collective-permute-start.24 = (bf16[256,512]{1,0:T(8,128)(2,1)S(1)}, bf16[256,512]{1,0:T(8,128)(2,1)S(1)}, u32[]{:S(2)}, u32[]{:S(2)}) collective-permute-start(bf16[256,512]{1,0:T(8,128)(2,1)S(1)} %add_convert_fusion.7), channel_id=1, source_target_pairs={{7,6},{8,7},{9,8},{10,9},{11,10},{12,11},{13,12},{14,13},{15,14},{... | collective-permute-start | bytes 786440 | tf_op jit(solution)/shard_map/ppermute | solution.py:48
  137.0 9.5 %collective-permute-start.10 = (bf16[256,512]{1,0:T(8,128)(2,1)S(1)}, bf16[256,512]{1,0:T(8,128)(2,1)S(1)}, u32[]{:S(2)}, u32[]{:S(2)}) collective-permute-start(bf16[256,512]{1,0:T(8,128)(2,1)S(1)} %add_convert_fusion.20), channel_id=1, source_target_pairs={{0,1},{1,2},{2,3},{3,4},{4,5},{5,6},{6,7},{7,8},{8,9},{9,10},{16,1... | collective-permute-start | bytes 786440 | tf_op jit(solution)/shard_map/ppermute | solution.py:47
  144.2 9.5 %collective-permute-start.25 = (bf16[256,512]{1,0:T(8,128)(2,1)S(1)}, bf16[256,512]{1,0:T(8,128)(2,1)S(1)}, u32[]{:S(2)}, u32[]{:S(2)}) collective-permute-start(bf16[256,512]{1,0:T(8,128)(2,1)S(1)} %add_convert_fusion.6), channel_id=1, source_target_pairs={{6,5},{7,6},{8,7},{9,8},{10,9},{11,10},{12,11},{13,12},{14,13},{15... | collective-permute-start | bytes 786440 | tf_op jit(solution)/shard_map/ppermute | solution.py:48
  146.5 9.5 %collective-permute-start.11 = (bf16[256,512]{1,0:T(8,128)(2,1)S(1)}, bf16[256,512]{1,0:T(8,128)(2,1)S(1)}, u32[]{:S(2)}, u32[]{:S(2)}) collective-permute-start(bf16[256,512]{1,0:T(8,128)(2,1)S(1)} %add_convert_fusion.19), channel_id=1, source_target_pairs={{0,1},{1,2},{2,3},{3,4},{4,5},{5,6},{6,7},{7,8},{8,9},{9,10},{10,1... | collective-permute-start | bytes 786440 | tf_op jit(solution)/shard_map/ppermute | solution.py:47
  153.7 9.7 %collective-permute-start.26 = (bf16[256,512]{1,0:T(8,128)(2,1)S(1)}, bf16[256,512]{1,0:T(8,128)(2,1)S(1)}, u32[]{:S(2)}, u32[]{:S(2)}) collective-permute-start(bf16[256,512]{1,0:T(8,128)(2,1)S(1)} %add_convert_fusion.5), channel_id=1, source_target_pairs={{5,4},{6,5},{7,6},{8,7},{9,8},{10,9},{11,10},{12,11},{13,12},{14,1... | collective-permute-start | bytes 786440 | tf_op jit(solution)/shard_map/ppermute | solution.py:48
  156.1 9.6 %collective-permute-start.12 = (bf16[256,512]{1,0:T(8,128)(2,1)S(1)}, bf16[256,512]{1,0:T(8,128)(2,1)S(1)}, u32[]{:S(2)}, u32[]{:S(2)}) collective-permute-start(bf16[256,512]{1,0:T(8,128)(2,1)S(1)} %add_convert_fusion.18), channel_id=1, source_target_pairs={{0,1},{1,2},{2,3},{3,4},{4,5},{5,6},{6,7},{7,8},{8,9},{9,10},{10,1... | collective-permute-start | bytes 786440 | tf_op jit(solution)/shard_map/ppermute | solution.py:47
  163.5 10.7 %collective-permute-start.27 = (bf16[256,512]{1,0:T(8,128)(2,1)S(1)}, bf16[256,512]{1,0:T(8,128)(2,1)S(1)}, u32[]{:S(2)}, u32[]{:S(2)}) collective-permute-start(bf16[256,512]{1,0:T(8,128)(2,1)S(1)} %add_convert_fusion.4), channel_id=1, source_target_pairs={{4,3},{5,4},{6,5},{7,6},{8,7},{9,8},{10,9},{11,10},{12,11},{13,12}... | collective-permute-start | bytes 786440 | tf_op jit(solution)/shard_map/ppermute | solution.py:48
  165.8 10.9 %collective-permute-start.13 = (bf16[256,512]{1,0:T(8,128)(2,1)S(1)}, bf16[256,512]{1,0:T(8,128)(2,1)S(1)}, u32[]{:S(2)}, u32[]{:S(2)}) collective-permute-start(bf16[256,512]{1,0:T(8,128)(2,1)S(1)} %add_convert_fusion.17), channel_id=1, source_target_pairs={{0,1},{1,2},{2,3},{3,4},{4,5},{5,6},{6,7},{7,8},{8,9},{9,10},{10,1... | collective-permute-start | bytes 786440 | tf_op jit(solution)/shard_map/ppermute | solution.py:47
  174.3 12.0 %collective-permute-start.28 = (bf16[256,512]{1,0:T(8,128)(2,1)S(1)}, bf16[256,512]{1,0:T(8,128)(2,1)S(1)}, u32[]{:S(2)}, u32[]{:S(2)}) collective-permute-start(bf16[256,512]{1,0:T(8,128)(2,1)S(1)} %add_convert_fusion.3), channel_id=1, source_target_pairs={{3,2},{4,3},{5,4},{6,5},{7,6},{8,7},{9,8},{10,9},{11,10},{12,11},{... | collective-permute-start | bytes 786440 | tf_op jit(solution)/shard_map/ppermute | solution.py:48
  176.7 11.8 %collective-permute-start.14 = (bf16[256,512]{1,0:T(8,128)(2,1)S(1)}, bf16[256,512]{1,0:T(8,128)(2,1)S(1)}, u32[]{:S(2)}, u32[]{:S(2)}) collective-permute-start(bf16[256,512]{1,0:T(8,128)(2,1)S(1)} %add_convert_fusion.16), channel_id=1, source_target_pairs={{0,1},{1,2},{2,3},{3,4},{4,5},{5,6},{6,7},{7,8},{8,9},{9,10},{10,1... | collective-permute-start | bytes 786440 | tf_op jit(solution)/shard_map/ppermute | solution.py:47
  186.3 9.5 %collective-permute-start.29 = (bf16[256,512]{1,0:T(8,128)(2,1)S(1)}, bf16[256,512]{1,0:T(8,128)(2,1)S(1)}, u32[]{:S(2)}, u32[]{:S(2)}) collective-permute-start(bf16[256,512]{1,0:T(8,128)(2,1)S(1)} %add_convert_fusion.2), channel_id=1, source_target_pairs={{2,1},{3,2},{4,3},{5,4},{6,5},{7,6},{8,7},{9,8},{10,9},{11,10},{12... | collective-permute-start | bytes 786440 | tf_op jit(solution)/shard_map/ppermute | solution.py:48
  188.6 10.5 %collective-permute-start.15 = (bf16[256,512]{1,0:T(8,128)(2,1)S(1)}, bf16[256,512]{1,0:T(8,128)(2,1)S(1)}, u32[]{:S(2)}, u32[]{:S(2)}) collective-permute-start(bf16[256,512]{1,0:T(8,128)(2,1)S(1)} %add_convert_fusion.15), channel_id=1, source_target_pairs={{0,1},{1,2},{2,3},{3,4},{4,5},{5,6},{6,7},{7,8},{8,9},{9,10},{10,1... | collective-permute-start | bytes 786440 | tf_op jit(solution)/shard_map/ppermute | solution.py:47
  195.8 9.5 %collective-permute-start.30 = (bf16[256,512]{1,0:T(8,128)(2,1)S(1)}, bf16[256,512]{1,0:T(8,128)(2,1)S(1)}, u32[]{:S(2)}, u32[]{:S(2)}) collective-permute-start(bf16[256,512]{1,0:T(8,128)(2,1)S(1)} %add_convert_fusion.1), channel_id=1, source_target_pairs={{1,0},{2,1},{3,2},{4,3},{5,4},{6,5},{7,6},{8,7},{9,8},{10,9},{11,1... | collective-permute-start | bytes 786440 | tf_op jit(solution)/shard_map/ppermute | solution.py:48
  (10 other events, 48.2 us)

commit v11 on v10

--- a/solution.py
+++ b/solution.py
@@ -23,7 +23,7 @@
     return running
 
 
-def line_reduce_scatter(product, out_weight, axis, chains=1):
+def line_reduce_scatter(product, out_weight, axis, chains=2):
     n = lax.axis_size(axis)
     me = lax.axis_index(axis)
     width = out_weight.shape[1] // n
@@ -38,14 +38,17 @@
     zeros = jnp.zeros((product.shape[0], piece), jnp.bfloat16)
     from_left = [zeros] * chains
     from_right = [zeros] * chains
+    all_right = [(k, k + 1) for k in range(n - 1)]
+    all_left = [(k, k - 1) for k in range(1, n)]
     for step in range(n - 1):
         rightward = [(k, k + 1) for k in range(n - 1) if k <= step]
         leftward = [(k, k - 1) for k in range(1, n) if k >= n - 1 - step]
         for chain in range(chains):
             send_right = (from_left[chain].astype(jnp.float32) + block(n - 1 + me - step, chain)).astype(jnp.bfloat16)
             send_left = (from_right[chain].astype(jnp.float32) + block(step - (n - 1) + me, chain)).astype(jnp.bfloat16)
-            from_left[chain] = lax.ppermute(send_right, axis, rightward)
-            from_right[chain] = lax.ppermute(send_left, axis, leftward)
+            every = chain % 2 == 1
+            from_left[chain] = lax.ppermute(send_right, axis, all_right if every else rightward)
+            from_right[chain] = lax.ppermute(send_left, axis, all_left if every else leftward)
     pieces = [
         from_left[chain].astype(jnp.float32) + block(me, chain) + from_right[chain].astype(jnp.float32)
         for chain in range(chains)

time: 208 us -> 247 us (1.19)
  the two profiles are of different devices: /device:TPU:376 before, /device:TPU:280 now
where the time goes in v11:
time: 247 us; the launch traced here: 244 us
  starting transfers between devices  174 us (70%)
  other arithmetic  23 us (9%)
  waiting for transfers between devices  17.6 us (7%)
  matrix products  15.4 us (6%)
  local copies, waits for them, and re-layouts  11.9 us (5%)
    ppermute x30, starting transfers between devices, line_reduce_scatter(): lax.ppermute(send_left, axis, all_left if every else leftward)  107 us
    ppermute x30, starting transfers between devices, line_reduce_scatter(): lax.ppermute(send_right, axis, all_right if every else rightward)  65 us
    dot_general x62, matrix products, block(): jnp.dot(product, columns, preferred_element_type=jnp.float32)  15.4 us
    ppermute x1, waiting for transfers between devices, shifted(): return lax.ppermute(block, axis, route)  11.4 us
    slice x7, local copies, waits for them, and re-layouts, valid_conv(): taps[offset][None, :]  8.03 us
    convert_element_type x1, other arithmetic, shards(): product_tail = (query_body[filt_reach:] * mixed_tail).astype(jnp.bfloat16)  7.13 us
    convert_element_type x1, other arithmetic, shards(): product_head = (query_feat_head * mixed_head).astype(jnp.bfloat16)  7.11 us
    ppermute x30, waiting for transfers between devices, line_reduce_scatter(): lax.ppermute(send_right, axis, all_right if every else rightward)  5.7 us
  transfers between devices with their start and end apart: 61, of which 3 were waited for; matrix products, arithmetic and copies ran while one was open for 14% of the time, Pallas kernels for 0%

profile of v11, /device:TPU:280, one launch (start us, length us, event | category | flops | bytes accessed | tf_op | source)
XLA Modules:
  0.0 244.1 jit_solution(7652715833763909039)
XLA Ops:
  19.7 7.1 %fusion.153 = bf16[123,512]{1,0:T(8,128)(2,1)S(1)} fusion(f32[250,512]{1,0:T(8,128)S(1)} %get-tuple-element.5, f32[512]{0:T(512)S(1)} %bitcast.225, f32[512]{0:T(512)S(1)} %bitcast.227, f32[512]{0:T(512)S(1)} %bitcast.231, f32[512]{0:T(512)S(1)} %bitcast.233, f32[512]{0:T(512)S(1)} %bitcast.235, f32[512]{0:T(512)S(1)} %bitcast.237, f32[512]{0:T(512)S(1)} %bitcast.239, ...), kind=kLoop, calls=%fused_computation.368 | loop fusion | flops 16373760 | bytes 33011712 | tf_op jit(solution)/shard_map/convert_element_type | solution.py:76
  27.1 11.4 %collective-permute-done = bf16[145,512]{1,0:T(8,128)(2,1)S(1)} collective-permute-done((bf16[145,512]{1,0:T(8,128)(2,1)S(1)}, bf16[145,512]{1,0:T(8,128)(2,1)S(1)}, u32[]{:S(2)}, u32[]{:S(2)}) %collective-permute-start) | collective-permute-done | bytes 148512 | tf_op jit(solution)/shard_map/ppermute | solution.py:10
  38.7 7.1 %fusion.23 = bf16[133,512]{1,0:T(8,128)(2,1)S(1)} fusion(f32[260,512]{1,0:T(8,128)S(1)} %maximum_convert_fusion, bf16[127,512]{1,0:T(8,128)(2,1)S(1)} %slice.2184, bf16[6,512]{1,0:T(8,128)(2,1)S(1)} %fusion.358, f32[512]{0:T(512)S(1)} %copy-done, f32[512]{0:T(512)S(1)} %bitcast.226, f32[512]{0:T(512)S(1)} %bitcast.228, f32[512]{0:T(512)S(1)} %bitcast.232, ...), kind=kLoop, calls=%fused_computation.107 | loop fusion | flops 17977344 | bytes 35674112 | tf_op jit(solution)/shard_map/convert_element_type | solution.py:89
  56.0 3.9 %collective-permute-start.31 = (bf16[256,256]{1,0:T(8,128)(2,1)S(1)}, bf16[256,256]{1,0:T(8,128)(2,1)S(1)}, u32[]{:S(2)}, u32[]{:S(2)}) collective-permute-start(bf16[256,256]{1,0:T(8,128)(2,1)S(1)} %convolution_convert_fusion.30), channel_id=1, source_target_pairs={{0,1},{1,2},{2,3},{3,4},{4,5},{5,6},{6,7},{7,8},{8,9},{9,10},{10,1... | collective-permute-start | bytes 393224 | tf_op jit(solution)/shard_map/ppermute | solution.py:50
  77.0 3.9 %collective-permute-start.48 = (bf16[256,256]{1,0:T(8,128)(2,1)S(1)}, bf16[256,256]{1,0:T(8,128)(2,1)S(1)}, u32[]{:S(2)}, u32[]{:S(2)}) collective-permute-start(bf16[256,256]{1,0:T(8,128)(2,1)S(1)} %add_convert_fusion.13), channel_id=1, source_target_pairs={{1,0},{2,1},{3,2},{4,3},{5,4},{6,5},{7,6},{8,7},{9,8},{10,9},{11,1... | collective-permute-start | bytes 393224 | tf_op jit(solution)/shard_map/ppermute | solution.py:51
  84.4 5.1 %collective-permute-start.49 = (bf16[256,256]{1,0:T(8,128)(2,1)S(1)}, bf16[256,256]{1,0:T(8,128)(2,1)S(1)}, u32[]{:S(2)}, u32[]{:S(2)}) collective-permute-start(bf16[256,256]{1,0:T(8,128)(2,1)S(1)} %add_convert_fusion.12), channel_id=1, source_target_pairs={{1,0},{2,1},{3,2},{4,3},{5,4},{6,5},{7,6},{8,7},{9,8},{10,9},{11,1... | collective-permute-start | bytes 393224 | tf_op jit(solution)/shard_map/ppermute | solution.py:51
  93.5 4.6 %collective-permute-start.50 = (bf16[256,256]{1,0:T(8,128)(2,1)S(1)}, bf16[256,256]{1,0:T(8,128)(2,1)S(1)}, u32[]{:S(2)}, u32[]{:S(2)}) collective-permute-start(bf16[256,256]{1,0:T(8,128)(2,1)S(1)} %add_convert_fusion.11), channel_id=1, source_target_pairs={{1,0},{2,1},{3,2},{4,3},{5,4},{6,5},{7,6},{8,7},{9,8},{10,9},{11,1... | collective-permute-start | bytes 393224 | tf_op jit(solution)/shard_map/ppermute | solution.py:51
  115.4 5.4 %collective-permute-start.37 = (bf16[256,256]{1,0:T(8,128)(2,1)S(1)}, bf16[256,256]{1,0:T(8,128)(2,1)S(1)}, u32[]{:S(2)}, u32[]{:S(2)}) collective-permute-start(bf16[256,256]{1,0:T(8,128)(2,1)S(1)} %add_convert_fusion.23), channel_id=1, source_target_pairs={{0,1},{1,2},{2,3},{3,4},{4,5},{5,6},{6,7},{7,8},{8,9},{9,10},{10,1... | collective-permute-start | bytes 393224 | tf_op jit(solution)/shard_map/ppermute | solution.py:50
  124.9 7.6 %collective-permute-start.38 = (bf16[256,256]{1,0:T(8,128)(2,1)S(1)}, bf16[256,256]{1,0:T(8,128)(2,1)S(1)}, u32[]{:S(2)}, u32[]{:S(2)}) collective-permute-start(bf16[256,256]{1,0:T(8,128)(2,1)S(1)} %add_convert_fusion.22), channel_id=1, source_target_pairs={{0,1},{1,2},{2,3},{3,4},{4,5},{5,6},{6,7},{7,8},{8,9},{9,10},{10,1... | collective-permute-start | bytes 393224 | tf_op jit(solution)/shard_map/ppermute | solution.py:50
  135.9 5.8 %collective-permute-start.54 = (bf16[256,256]{1,0:T(8,128)(2,1)S(1)}, bf16[256,256]{1,0:T(8,128)(2,1)S(1)}, u32[]{:S(2)}, u32[]{:S(2)}) collective-permute-start(bf16[256,256]{1,0:T(8,128)(2,1)S(1)} %add_convert_fusion.7), channel_id=1, source_target_pairs={{1,0},{2,1},{3,2},{4,3},{5,4},{6,5},{7,6},{8,7},{9,8},{10,9},{11,1... | collective-permute-start | bytes 393224 | tf_op jit(solution)/shard_map/ppermute | solution.py:51
  143.7 5.1 %collective-permute-start.24 = (bf16[256,256]{1,0:T(8,128)(2,1)S(1)}, bf16[256,256]{1,0:T(8,128)(2,1)S(1)}, u32[]{:S(2)}, u32[]{:S(2)}) collective-permute-start(bf16[256,256]{1,0:T(8,128)(2,1)S(1)} %add_convert_fusion.36), channel_id=1, source_target_pairs={{7,6},{8,7},{9,8},{10,9},{11,10},{12,11},{13,12},{14,13},{15,14},{... | collective-permute-start | bytes 393224 | tf_op jit(solution)/shard_map/ppermute | solution.py:51
  150.9 5.1 %collective-permute-start.55 = (bf16[256,256]{1,0:T(8,128)(2,1)S(1)}, bf16[256,256]{1,0:T(8,128)(2,1)S(1)}, u32[]{:S(2)}, u32[]{:S(2)}) collective-permute-start(bf16[256,256]{1,0:T(8,128)(2,1)S(1)} %add_convert_fusion.6), channel_id=1, source_target_pairs={{1,0},{2,1},{3,2},{4,3},{5,4},{6,5},{7,6},{8,7},{9,8},{10,9},{11,1... | collective-permute-start | bytes 393224 | tf_op jit(solution)/shard_map/ppermute | solution.py:51
  158.3 5.1 %collective-permute-start.25 = (bf16[256,256]{1,0:T(8,128)(2,1)S(1)}, bf16[256,256]{1,0:T(8,128)(2,1)S(1)}, u32[]{:S(2)}, u32[]{:S(2)}) collective-permute-start(bf16[256,256]{1,0:T(8,128)(2,1)S(1)} %add_convert_fusion.35), channel_id=1, source_target_pairs={{6,5},{7,6},{8,7},{9,8},{10,9},{11,10},{12,11},{13,12},{14,13},{15... | collective-permute-start | bytes 393224 | tf_op jit(solution)/shard_map/ppermute | solution.py:51
  165.5 5.1 %collective-permute-start.56 = (bf16[256,256]{1,0:T(8,128)(2,1)S(1)}, bf16[256,256]{1,0:T(8,128)(2,1)S(1)}, u32[]{:S(2)}, u32[]{:S(2)}) collective-permute-start(bf16[256,256]{1,0:T(8,128)(2,1)S(1)} %add_convert_fusion.5), channel_id=1, source_target_pairs={{1,0},{2,1},{3,2},{4,3},{5,4},{6,5},{7,6},{8,7},{9,8},{10,9},{11,1... | collective-permute-start | bytes 393224 | tf_op jit(solution)/shard_map/ppermute | solution.py:51
  172.7 5.1 %collective-permute-start.26 = (bf16[256,256]{1,0:T(8,128)(2,1)S(1)}, bf16[256,256]{1,0:T(8,128)(2,1)S(1)}, u32[]{:S(2)}, u32[]{:S(2)}) collective-permute-start(bf16[256,256]{1,0:T(8,128)(2,1)S(1)} %add_convert_fusion.34), channel_id=1, source_target_pairs={{5,4},{6,5},{7,6},{8,7},{9,8},{10,9},{11,10},{12,11},{13,12},{14,1... | collective-permute-start | bytes 393224 | tf_op jit(solution)/shard_map/ppermute | solution.py:51
  179.9 5.1 %collective-permute-start.57 = (bf16[256,256]{1,0:T(8,128)(2,1)S(1)}, bf16[256,256]{1,0:T(8,128)(2,1)S(1)}, u32[]{:S(2)}, u32[]{:S(2)}) collective-permute-start(bf16[256,256]{1,0:T(8,128)(2,1)S(1)} %add_convert_fusion.4), channel_id=1, source_target_pairs={{1,0},{2,1},{3,2},{4,3},{5,4},{6,5},{7,6},{8,7},{9,8},{10,9},{11,1... | collective-permute-start | bytes 393224 | tf_op jit(solution)/shard_map/ppermute | solution.py:51
  187.0 5.1 %collective-permute-start.27 = (bf16[256,256]{1,0:T(8,128)(2,1)S(1)}, bf16[256,256]{1,0:T(8,128)(2,1)S(1)}, u32[]{:S(2)}, u32[]{:S(2)}) collective-permute-start(bf16[256,256]{1,0:T(8,128)(2,1)S(1)} %add_convert_fusion.33), channel_id=1, source_target_pairs={{4,3},{5,4},{6,5},{7,6},{8,7},{9,8},{10,9},{11,10},{12,11},{13,12}... | collective-permute-start | bytes 393224 | tf_op jit(solution)/shard_map/ppermute | solution.py:51
  194.2 5.1 %collective-permute-start.58 = (bf16[256,256]{1,0:T(8,128)(2,1)S(1)}, bf16[256,256]{1,0:T(8,128)(2,1)S(1)}, u32[]{:S(2)}, u32[]{:S(2)}) collective-permute-start(bf16[256,256]{1,0:T(8,128)(2,1)S(1)} %add_convert_fusion.3), channel_id=1, source_target_pairs={{1,0},{2,1},{3,2},{4,3},{5,4},{6,5},{7,6},{8,7},{9,8},{10,9},{11,1... | collective-permute-start | bytes 393224 | tf_op jit(solution)/shard_map/ppermute | solution.py:51
  201.4 5.1 %collective-permute-start.28 = (bf16[256,256]{1,0:T(8,128)(2,1)S(1)}, bf16[256,256]{1,0:T(8,128)(2,1)S(1)}, u32[]{:S(2)}, u32[]{:S(2)}) collective-permute-start(bf16[256,256]{1,0:T(8,128)(2,1)S(1)} %add_convert_fusion.32), channel_id=1, source_target_pairs={{3,2},{4,3},{5,4},{6,5},{7,6},{8,7},{9,8},{10,9},{11,10},{12,11},{... | collective-permute-start | bytes 393224 | tf_op jit(solution)/shard_map/ppermute | solution.py:51
  208.6 5.1 %collective-permute-start.59 = (bf16[256,256]{1,0:T(8,128)(2,1)S(1)}, bf16[256,256]{1,0:T(8,128)(2,1)S(1)}, u32[]{:S(2)}, u32[]{:S(2)}) collective-permute-start(bf16[256,256]{1,0:T(8,128)(2,1)S(1)} %add_convert_fusion.2), channel_id=1, source_target_pairs={{1,0},{2,1},{3,2},{4,3},{5,4},{6,5},{7,6},{8,7},{9,8},{10,9},{11,1... | collective-permute-start | bytes 393224 | tf_op jit(solution)/shard_map/ppermute | solution.py:51
  215.7 5.1 %collective-permute-start.29 = (bf16[256,256]{1,0:T(8,128)(2,1)S(1)}, bf16[256,256]{1,0:T(8,128)(2,1)S(1)}, u32[]{:S(2)}, u32[]{:S(2)}) collective-permute-start(bf16[256,256]{1,0:T(8,128)(2,1)S(1)} %add_convert_fusion.31), channel_id=1, source_target_pairs={{2,1},{3,2},{4,3},{5,4},{6,5},{7,6},{8,7},{9,8},{10,9},{11,10},{12... | collective-permute-start | bytes 393224 | tf_op jit(solution)/shard_map/ppermute | solution.py:51
  222.9 5.1 %collective-permute-start.60 = (bf16[256,256]{1,0:T(8,128)(2,1)S(1)}, bf16[256,256]{1,0:T(8,128)(2,1)S(1)}, u32[]{:S(2)}, u32[]{:S(2)}) collective-permute-start(bf16[256,256]{1,0:T(8,128)(2,1)S(1)} %add_convert_fusion.1), channel_id=1, source_target_pairs={{1,0},{2,1},{3,2},{4,3},{5,4},{6,5},{7,6},{8,7},{9,8},{10,9},{11,1... | collective-permute-start | bytes 393224 | tf_op jit(solution)/shard_map/ppermute | solution.py:51
  230.1 5.1 %collective-permute-start.30 = (bf16[256,256]{1,0:T(8,128)(2,1)S(1)}, bf16[256,256]{1,0:T(8,128)(2,1)S(1)}, u32[]{:S(2)}, u32[]{:S(2)}) collective-permute-start(bf16[256,256]{1,0:T(8,128)(2,1)S(1)} %add_convert_fusion.30), channel_id=1, source_target_pairs={{1,0},{2,1},{3,2},{4,3},{5,4},{6,5},{7,6},{8,7},{9,8},{10,9},{11,1... | collective-permute-start | bytes 393224 | tf_op jit(solution)/shard_map/ppermute | solution.py:51
  237.7 5.6 %collective-permute-done.15 = bf16[256,256]{1,0:T(8,128)(2,1)S(1)} collective-permute-done((bf16[256,256]{1,0:T(8,128)(2,1)S(1)}, bf16[256,256]{1,0:T(8,128)(2,1)S(1)}, u32[]{:S(2)}, u32[]{:S(2)}) %collective-permute-start.15) | collective-permute-done | bytes 131104 | tf_op jit(solution)/shard_map/ppermute | solution.py:50
  (257 shorter events, 107.9 us)
Async XLA Ops:
  4.2 34.2 %collective-permute-start = (bf16[145,512]{1,0:T(8,128)(2,1)S(1)}, bf16[145,512]{1,0:T(8,128)(2,1)S(1)}, u32[]{:S(2)}, u32[]{:S(2)}) collective-permute-start(bf16[145,512]{1,0:T(8,128)(2,1)S(1)} %pad_maximum_fusion.3), channel_id=1, source_target_pairs={{0,16},{16,32},{32,48},{48,64},{64,80},{80,96},{96,112},{112,128},... | collective-permute-start | bytes 445448 | tf_op jit(solution)/shard_map/ppermute | solution.py:10
  49.7 19.3 %collective-permute-start.46 = (bf16[256,256]{1,0:T(8,128)(2,1)S(1)}, bf16[256,256]{1,0:T(8,128)(2,1)S(1)}, u32[]{:S(2)}, u32[]{:S(2)}) collective-permute-start(bf16[256,256]{1,0:T(8,128)(2,1)S(1)} %convolution_convert_fusion.14), channel_id=1, source_target_pairs={{1,0},{2,1},{3,2},{4,3},{5,4},{6,5},{7,6},{8,7},{9,8},{10,9},{11,1... | collective-permute-start | bytes 393224 | tf_op jit(solution)/shard_map/ppermute | solution.py:51
  56.0 16.2 %collective-permute-start.31 = (bf16[256,256]{1,0:T(8,128)(2,1)S(1)}, bf16[256,256]{1,0:T(8,128)(2,1)S(1)}, u32[]{:S(2)}, u32[]{:S(2)}) collective-permute-start(bf16[256,256]{1,0:T(8,128)(2,1)S(1)} %convolution_convert_fusion.30), channel_id=1, source_target_pairs={{0,1},{1,2},{2,3},{3,4},{4,5},{5,6},{6,7},{7,8},{8,9},{9,10},{10,1... | collective-permute-start | bytes 393224 | tf_op jit(solution)/shard_map/ppermute | solution.py:50
  124.9 16.8 %collective-permute-start.38 = (bf16[256,256]{1,0:T(8,128)(2,1)S(1)}, bf16[256,256]{1,0:T(8,128)(2,1)S(1)}, u32[]{:S(2)}, u32[]{:S(2)}) collective-permute-start(bf16[256,256]{1,0:T(8,128)(2,1)S(1)} %add_convert_fusion.22), channel_id=1, source_target_pairs={{0,1},{1,2},{2,3},{3,4},{4,5},{5,6},{6,7},{7,8},{8,9},{9,10},{10,1... | collective-permute-start | bytes 393224 | tf_op jit(solution)/shard_map/ppermute | solution.py:50
  134.6 14.3 %collective-permute-start.8 = (bf16[256,256]{1,0:T(8,128)(2,1)S(1)}, bf16[256,256]{1,0:T(8,128)(2,1)S(1)}, u32[]{:S(2)}, u32[]{:S(2)}) collective-permute-start(bf16[256,256]{1,0:T(8,128)(2,1)S(1)} %add_convert_fusion.51), channel_id=1, source_target_pairs={{0,1},{1,2},{2,3},{3,4},{4,5},{5,6},{6,7},{7,8},{16,17},{17,18},{1... | collective-permute-start | bytes 393224 | tf_op jit(solution)/shard_map/ppermute | solution.py:50
  135.9 14.9 %collective-permute-start.54 = (bf16[256,256]{1,0:T(8,128)(2,1)S(1)}, bf16[256,256]{1,0:T(8,128)(2,1)S(1)}, u32[]{:S(2)}, u32[]{:S(2)}) collective-permute-start(bf16[256,256]{1,0:T(8,128)(2,1)S(1)} %add_convert_fusion.7), channel_id=1, source_target_pairs={{1,0},{2,1},{3,2},{4,3},{5,4},{6,5},{7,6},{8,7},{9,8},{10,9},{11,1... | collective-permute-start | bytes 393224 | tf_op jit(solution)/shard_map/ppermute | solution.py:51
  141.8 14.3 %collective-permute-start.39 = (bf16[256,256]{1,0:T(8,128)(2,1)S(1)}, bf16[256,256]{1,0:T(8,128)(2,1)S(1)}, u32[]{:S(2)}, u32[]{:S(2)}) collective-permute-start(bf16[256,256]{1,0:T(8,128)(2,1)S(1)} %add_convert_fusion.21), channel_id=1, source_target_pairs={{0,1},{1,2},{2,3},{3,4},{4,5},{5,6},{6,7},{7,8},{8,9},{9,10},{10,1... | collective-permute-start | bytes 393224 | tf_op jit(solution)/shard_map/ppermute | solution.py:50
  143.7 14.6 %collective-permute-start.24 = (bf16[256,256]{1,0:T(8,128)(2,1)S(1)}, bf16[256,256]{1,0:T(8,128)(2,1)S(1)}, u32[]{:S(2)}, u32[]{:S(2)}) collective-permute-start(bf16[256,256]{1,0:T(8,128)(2,1)S(1)} %add_convert_fusion.36), channel_id=1, source_target_pairs={{7,6},{8,7},{9,8},{10,9},{11,10},{12,11},{13,12},{14,13},{15,14},{... | collective-permute-start | bytes 393224 | tf_op jit(solution)/shard_map/ppermute | solution.py:51
  148.9 14.6 %collective-permute-start.9 = (bf16[256,256]{1,0:T(8,128)(2,1)S(1)}, bf16[256,256]{1,0:T(8,128)(2,1)S(1)}, u32[]{:S(2)}, u32[]{:S(2)}) collective-permute-start(bf16[256,256]{1,0:T(8,128)(2,1)S(1)} %add_convert_fusion.50), channel_id=1, source_target_pairs={{0,1},{1,2},{2,3},{3,4},{4,5},{5,6},{6,7},{7,8},{8,9},{16,17},{17,... | collective-permute-start | bytes 393224 | tf_op jit(solution)/shard_map/ppermute | solution.py:50
  150.9 14.6 %collective-permute-start.55 = (bf16[256,256]{1,0:T(8,128)(2,1)S(1)}, bf16[256,256]{1,0:T(8,128)(2,1)S(1)}, u32[]{:S(2)}, u32[]{:S(2)}) collective-permute-start(bf16[256,256]{1,0:T(8,128)(2,1)S(1)} %add_convert_fusion.6), channel_id=1, source_target_pairs={{1,0},{2,1},{3,2},{4,3},{5,4},{6,5},{7,6},{8,7},{9,8},{10,9},{11,1... | collective-permute-start | bytes 393224 | tf_op jit(solution)/shard_map/ppermute | solution.py:51
  156.1 14.6 %collective-permute-start.40 = (bf16[256,256]{1,0:T(8,128)(2,1)S(1)}, bf16[256,256]{1,0:T(8,128)(2,1)S(1)}, u32[]{:S(2)}, u32[]{:S(2)}) collective-permute-start(bf16[256,256]{1,0:T(8,128)(2,1)S(1)} %add_convert_fusion.20), channel_id=1, source_target_pairs={{0,1},{1,2},{2,3},{3,4},{4,5},{5,6},{6,7},{7,8},{8,9},{9,10},{10,1... | collective-permute-start | bytes 393224 | tf_op jit(solution)/shard_map/ppermute | solution.py:50
  158.3 14.3 %collective-permute-start.25 = (bf16[256,256]{1,0:T(8,128)(2,1)S(1)}, bf16[256,256]{1,0:T(8,128)(2,1)S(1)}, u32[]{:S(2)}, u32[]{:S(2)}) collective-permute-start(bf16[256,256]{1,0:T(8,128)(2,1)S(1)} %add_convert_fusion.35), channel_id=1, source_target_pairs={{6,5},{7,6},{8,7},{9,8},{10,9},{11,10},{12,11},{13,12},{14,13},{15... | collective-permute-start | bytes 393224 | tf_op jit(solution)/shard_map/ppermute | solution.py:51
  163.5 14.3 %collective-permute-start.10 = (bf16[256,256]{1,0:T(8,128)(2,1)S(1)}, bf16[256,256]{1,0:T(8,128)(2,1)S(1)}, u32[]{:S(2)}, u32[]{:S(2)}) collective-permute-start(bf16[256,256]{1,0:T(8,128)(2,1)S(1)} %add_convert_fusion.49), channel_id=1, source_target_pairs={{0,1},{1,2},{2,3},{3,4},{4,5},{5,6},{6,7},{7,8},{8,9},{9,10},{16,1... | collective-permute-start | bytes 393224 | tf_op jit(solution)/shard_map/ppermute | solution.py:50
  165.5 14.3 %collective-permute-start.56 = (bf16[256,256]{1,0:T(8,128)(2,1)S(1)}, bf16[256,256]{1,0:T(8,128)(2,1)S(1)}, u32[]{:S(2)}, u32[]{:S(2)}) collective-permute-start(bf16[256,256]{1,0:T(8,128)(2,1)S(1)} %add_convert_fusion.5), channel_id=1, source_target_pairs={{1,0},{2,1},{3,2},{4,3},{5,4},{6,5},{7,6},{8,7},{9,8},{10,9},{11,1... | collective-permute-start | bytes 393224 | tf_op jit(solution)/shard_map/ppermute | solution.py:51
  170.7 14.3 %collective-permute-start.41 = (bf16[256,256]{1,0:T(8,128)(2,1)S(1)}, bf16[256,256]{1,0:T(8,128)(2,1)S(1)}, u32[]{:S(2)}, u32[]{:S(2)}) collective-permute-start(bf16[256,256]{1,0:T(8,128)(2,1)S(1)} %add_convert_fusion.19), channel_id=1, source_target_pairs={{0,1},{1,2},{2,3},{3,4},{4,5},{5,6},{6,7},{7,8},{8,9},{9,10},{10,1... | collective-permute-start | bytes 393224 | tf_op jit(solution)/shard_map/ppermute | solution.py:50
  172.7 14.3 %collective-permute-start.26 = (bf16[256,256]{1,0:T(8,128)(2,1)S(1)}, bf16[256,256]{1,0:T(8,128)(2,1)S(1)}, u32[]{:S(2)}, u32[]{:S(2)}) collective-permute-start(bf16[256,256]{1,0:T(8,128)(2,1)S(1)} %add_convert_fusion.34), channel_id=1, source_target_pairs={{5,4},{6,5},{7,6},{8,7},{9,8},{10,9},{11,10},{12,11},{13,12},{14,1... | collective-permute-start | bytes 393224 | tf_op jit(solution)/shard_map/ppermute | solution.py:51
  177.9 14.3 %collective-permute-start.11 = (bf16[256,256]{1,0:T(8,128)(2,1)S(1)}, bf16[256,256]{1,0:T(8,128)(2,1)S(1)}, u32[]{:S(2)}, u32[]{:S(2)}) collective-permute-start(bf16[256,256]{1,0:T(8,128)(2,1)S(1)} %add_convert_fusion.48), channel_id=1, source_target_pairs={{0,1},{1,2},{2,3},{3,4},{4,5},{5,6},{6,7},{7,8},{8,9},{9,10},{10,1... | collective-permute-start | bytes 393224 | tf_op jit(solution)/shard_map/ppermute | solution.py:50
  179.9 14.3 %collective-permute-start.57 = (bf16[256,256]{1,0:T(8,128)(2,1)S(1)}, bf16[256,256]{1,0:T(8,128)(2,1)S(1)}, u32[]{:S(2)}, u32[]{:S(2)}) collective-permute-start(bf16[256,256]{1,0:T(8,128)(2,1)S(1)} %add_convert_fusion.4), channel_id=1, source_target_pairs={{1,0},{2,1},{3,2},{4,3},{5,4},{6,5},{7,6},{8,7},{9,8},{10,9},{11,1... | collective-permute-start | bytes 393224 | tf_op jit(solution)/shard_map/ppermute | solution.py:51
  185.1 14.3 %collective-permute-start.42 = (bf16[256,256]{1,0:T(8,128)(2,1)S(1)}, bf16[256,256]{1,0:T(8,128)(2,1)S(1)}, u32[]{:S(2)}, u32[]{:S(2)}) collective-permute-start(bf16[256,256]{1,0:T(8,128)(2,1)S(1)} %add_convert_fusion.18), channel_id=1, source_target_pairs={{0,1},{1,2},{2,3},{3,4},{4,5},{5,6},{6,7},{7,8},{8,9},{9,10},{10,1... | collective-permute-start | bytes 393224 | tf_op jit(solution)/shard_map/ppermute | solution.py:50
  187.0 14.3 %collective-permute-start.27 = (bf16[256,256]{1,0:T(8,128)(2,1)S(1)}, bf16[256,256]{1,0:T(8,128)(2,1)S(1)}, u32[]{:S(2)}, u32[]{:S(2)}) collective-permute-start(bf16[256,256]{1,0:T(8,128)(2,1)S(1)} %add_convert_fusion.33), channel_id=1, source_target_pairs={{4,3},{5,4},{6,5},{7,6},{8,7},{9,8},{10,9},{11,10},{12,11},{13,12}... | collective-permute-start | bytes 393224 | tf_op jit(solution)/shard_map/ppermute | solution.py:51
  192.2 14.3 %collective-permute-start.12 = (bf16[256,256]{1,0:T(8,128)(2,1)S(1)}, bf16[256,256]{1,0:T(8,128)(2,1)S(1)}, u32[]{:S(2)}, u32[]{:S(2)}) collective-permute-start(bf16[256,256]{1,0:T(8,128)(2,1)S(1)} %add_convert_fusion.47), channel_id=1, source_target_pairs={{0,1},{1,2},{2,3},{3,4},{4,5},{5,6},{6,7},{7,8},{8,9},{9,10},{10,1... | collective-permute-start | bytes 393224 | tf_op jit(solution)/shard_map/ppermute | solution.py:50
  194.2 14.3 %collective-permute-start.58 = (bf16[256,256]{1,0:T(8,128)(2,1)S(1)}, bf16[256,256]{1,0:T(8,128)(2,1)S(1)}, u32[]{:S(2)}, u32[]{:S(2)}) collective-permute-start(bf16[256,256]{1,0:T(8,128)(2,1)S(1)} %add_convert_fusion.3), channel_id=1, source_target_pairs={{1,0},{2,1},{3,2},{4,3},{5,4},{6,5},{7,6},{8,7},{9,8},{10,9},{11,1... | collective-permute-start | bytes 393224 | tf_op jit(solution)/shard_map/ppermute | solution.py:51
  199.4 14.3 %collective-permute-start.43 = (bf16[256,256]{1,0:T(8,128)(2,1)S(1)}, bf16[256,256]{1,0:T(8,128)(2,1)S(1)}, u32[]{:S(2)}, u32[]{:S(2)}) collective-permute-start(bf16[256,256]{1,0:T(8,128)(2,1)S(1)} %add_convert_fusion.17), channel_id=1, source_target_pairs={{0,1},{1,2},{2,3},{3,4},{4,5},{5,6},{6,7},{7,8},{8,9},{9,10},{10,1... | collective-permute-start | bytes 393224 | tf_op jit(solution)/shard_map/ppermute | solution.py:50
  215.7 14.3 %collective-permute-start.29 = (bf16[256,256]{1,0:T(8,128)(2,1)S(1)}, bf16[256,256]{1,0:T(8,128)(2,1)S(1)}, u32[]{:S(2)}, u32[]{:S(2)}) collective-permute-start(bf16[256,256]{1,0:T(8,128)(2,1)S(1)} %add_convert_fusion.31), channel_id=1, source_target_pairs={{2,1},{3,2},{4,3},{5,4},{6,5},{7,6},{8,7},{9,8},{10,9},{11,10},{12... | collective-permute-start | bytes 393224 | tf_op jit(solution)/shard_map/ppermute | solution.py:51
  (40 other events, 405.0 us)

commit v12 on v10

--- a/solution.py
+++ b/solution.py
@@ -44,8 +44,12 @@
         for chain in range(chains):
             send_right = (from_left[chain].astype(jnp.float32) + block(n - 1 + me - step, chain)).astype(jnp.bfloat16)
             send_left = (from_right[chain].astype(jnp.float32) + block(step - (n - 1) + me, chain)).astype(jnp.bfloat16)
-            from_left[chain] = lax.ppermute(send_right, axis, rightward)
-            from_right[chain] = lax.ppermute(send_left, axis, leftward)
+            if step + 1 < n - 2 - step:
+                both = lax.ppermute(jnp.where(me <= step, send_right, send_left), axis, rightward + leftward)
+                from_left[chain], from_right[chain] = both, both
+            else:
+                from_left[chain] = lax.ppermute(send_right, axis, rightward)
+                from_right[chain] = lax.ppermute(send_left, axis, leftward)
     pieces = [
         from_left[chain].astype(jnp.float32) + block(me, chain) + from_right[chain].astype(jnp.float32)
         for chain in range(chains)

time: 208 us -> 211 us (1.014)
  the two profiles are of different devices: /device:TPU:376 before, /device:TPU:240 now
where the time goes in v12:
time: 211 us; the launch traced here: 209 us
  starting transfers between devices  85.4 us (40%)
  waiting for transfers between devices  60.3 us (29%)
  matrix products  27.8 us (13%)
  other arithmetic  22.5 us (11%)
  local copies, waits for them, and re-layouts  11.9 us (6%)
    ppermute x8, starting transfers between devices, line_reduce_scatter(): from_left[chain] = lax.ppermute(send_right, axis, rightward)  63.2 us
    ppermute x7, waiting for transfers between devices, line_reduce_scatter(): lax.ppermute(jnp.where(me <= step, send_right, send_left), axis, rightwar...  29.4 us
    dot_general x31, matrix products, block(): jnp.dot(product, columns, preferred_element_type=jnp.float32)  27.8 us
    ppermute x8, waiting for transfers between devices, line_reduce_scatter(): from_left[chain] = lax.ppermute(send_right, axis, rightward)  14.8 us
    ppermute x8, starting transfers between devices, line_reduce_scatter(): from_right[chain] = lax.ppermute(send_left, axis, leftward)  14.7 us
    ppermute x8, waiting for transfers between devices, line_reduce_scatter(): from_right[chain] = lax.ppermute(send_left, axis, leftward)  10.5 us
    slice x7, local copies, waits for them, and re-layouts, valid_conv(): taps[offset][None, :]  8.03 us
    convert_element_type x1, other arithmetic, shards(): product_head = (query_feat_head * mixed_head).astype(jnp.bfloat16)  7.06 us
  transfers between devices with their start and end apart: 24, of which 18 were waited for; matrix products, arithmetic and copies ran while one was open for 22% of the time, Pallas kernels for 0%

profile of v12, /device:TPU:240, one launch (start us, length us, event | category | flops | bytes accessed | tf_op | source)
XLA Modules:
  0.0 208.9 jit_solution(13518221769360864724)
XLA Ops:
  4.2 1.9 collective-permute-start
  19.7 6.9 %fusion.204 = bf16[123,512]{1,0:T(8,128)(2,1)S(1)} fusion(f32[250,512]{1,0:T(8,128)S(1)} %get-tuple-element.5, f32[512]{0:T(512)S(1)} %bitcast.453, f32[512]{0:T(512)S(1)} %bitcast.455, f32[512]{0:T(512)S(1)} %bitcast.279, f32[512]{0:T(512)S(1)} %bitcast.281, f32[512]{0:T(512)S(1)} %bitcast.283, f32[512]{0:T(512)S(1)} %bitcast.285, f32[512]{0:T(512)S(1)} %bitcast.287, ...), kind=kLoop, calls=%fused_computation.417 | loop fusion | flops 16373760 | bytes 33011712 | tf_op jit(solution)/shard_map/convert_element_type | solution.py:77
  26.7 5.6 %collective-permute-done = bf16[145,512]{1,0:T(8,128)(2,1)S(1)} collective-permute-done((bf16[145,512]{1,0:T(8,128)(2,1)S(1)}, bf16[145,512]{1,0:T(8,128)(2,1)S(1)}, u32[]{:S(2)}, u32[]{:S(2)}) %collective-permute-start) | collective-permute-done | bytes 148512 | tf_op jit(solution)/shard_map/ppermute | solution.py:10
  32.6 7.1 %fusion.68 = bf16[133,512]{1,0:T(8,128)(2,1)S(1)} fusion(f32[260,512]{1,0:T(8,128)S(1)} %maximum_convert_fusion, bf16[127,512]{1,0:T(8,128)(2,1)S(1)} %slice.2184, bf16[6,512]{1,0:T(8,128)(2,1)S(1)} %fusion.347, f32[512]{0:T(512)S(1)} %copy-done, f32[512]{0:T(512)S(1)} %bitcast.454, f32[512]{0:T(512)S(1)} %bitcast.456, f32[512]{0:T(512)S(1)} %bitcast.280, ...), kind=kLoop, calls=%fused_computation.150 | loop fusion | flops 17977344 | bytes 35674112 | tf_op jit(solution)/shard_map/convert_element_type | solution.py:90
  69.9 29.4 %collective-permute-done.7 = bf16[256,512]{1,0:T(8,128)(2,1)S(1)} collective-permute-done((bf16[256,512]{1,0:T(8,128)(2,1)S(1)}, bf16[256,512]{1,0:T(8,128)(2,1)S(1)}, u32[]{:S(2)}, u32[]{:S(2)}) %collective-permute-start.7) | collective-permute-done | bytes 262176 | tf_op jit(solution)/shard_map/ppermute | solution.py:48
  99.4 24.0 %collective-permute-start.8 = (bf16[256,512]{1,0:T(8,128)(2,1)S(1)}, bf16[256,512]{1,0:T(8,128)(2,1)S(1)}, u32[]{:S(2)}, u32[]{:S(2)}) collective-permute-start(bf16[256,512]{1,0:T(8,128)(2,1)S(1)} %get-tuple-element.7), channel_id=1, source_target_pairs={{0,1},{1,2},{2,3},{3,4},{4,5},{5,6},{6,7},{7,8},{16,17},{17,18},{1... | collective-permute-start | bytes 786440 | tf_op jit(solution)/shard_map/ppermute | solution.py:51
  125.8 2.2 %collective-permute-done.8 = bf16[256,512]{1,0:T(8,128)(2,1)S(1)} collective-permute-done((bf16[256,512]{1,0:T(8,128)(2,1)S(1)}, bf16[256,512]{1,0:T(8,128)(2,1)S(1)}, u32[]{:S(2)}, u32[]{:S(2)}) %collective-permute-start.8) | collective-permute-done | bytes 262176 | tf_op jit(solution)/shard_map/ppermute | solution.py:51
  128.1 5.6 %collective-permute-start.9 = (bf16[256,512]{1,0:T(8,128)(2,1)S(1)}, bf16[256,512]{1,0:T(8,128)(2,1)S(1)}, u32[]{:S(2)}, u32[]{:S(2)}) collective-permute-start(bf16[256,512]{1,0:T(8,128)(2,1)S(1)} %add_convert_fusion.14), channel_id=1, source_target_pairs={{0,1},{1,2},{2,3},{3,4},{4,5},{5,6},{6,7},{7,8},{8,9},{16,17},{17,... | collective-permute-start | bytes 786440 | tf_op jit(solution)/shard_map/ppermute | solution.py:51
  134.6 1.9 collective-permute-start.17
  136.9 2.5 %collective-permute-done.9 = bf16[256,512]{1,0:T(8,128)(2,1)S(1)} collective-permute-done((bf16[256,512]{1,0:T(8,128)(2,1)S(1)}, bf16[256,512]{1,0:T(8,128)(2,1)S(1)}, u32[]{:S(2)}, u32[]{:S(2)}) %collective-permute-start.9) | collective-permute-done | bytes 262176 | tf_op jit(solution)/shard_map/ppermute | solution.py:51
  139.4 5.6 %collective-permute-start.10 = (bf16[256,512]{1,0:T(8,128)(2,1)S(1)}, bf16[256,512]{1,0:T(8,128)(2,1)S(1)}, u32[]{:S(2)}, u32[]{:S(2)}) collective-permute-start(bf16[256,512]{1,0:T(8,128)(2,1)S(1)} %add_convert_fusion.13), channel_id=1, source_target_pairs={{0,1},{1,2},{2,3},{3,4},{4,5},{5,6},{6,7},{7,8},{8,9},{9,10},{16,1... | collective-permute-start | bytes 786440 | tf_op jit(solution)/shard_map/ppermute | solution.py:51
  146.3 1.9 collective-permute-start.18
  148.5 3.0 %collective-permute-done.10 = bf16[256,512]{1,0:T(8,128)(2,1)S(1)} collective-permute-done((bf16[256,512]{1,0:T(8,128)(2,1)S(1)}, bf16[256,512]{1,0:T(8,128)(2,1)S(1)}, u32[]{:S(2)}, u32[]{:S(2)}) %collective-permute-start.10) | collective-permute-done | bytes 262176 | tf_op jit(solution)/shard_map/ppermute | solution.py:51
  151.6 5.6 %collective-permute-start.11 = (bf16[256,512]{1,0:T(8,128)(2,1)S(1)}, bf16[256,512]{1,0:T(8,128)(2,1)S(1)}, u32[]{:S(2)}, u32[]{:S(2)}) collective-permute-start(bf16[256,512]{1,0:T(8,128)(2,1)S(1)} %add_convert_fusion.12), channel_id=1, source_target_pairs={{0,1},{1,2},{2,3},{3,4},{4,5},{5,6},{6,7},{7,8},{8,9},{9,10},{10,1... | collective-permute-start | bytes 786440 | tf_op jit(solution)/shard_map/ppermute | solution.py:51
  158.2 1.9 collective-permute-start.19
  160.4 2.5 %collective-permute-done.11 = bf16[256,512]{1,0:T(8,128)(2,1)S(1)} collective-permute-done((bf16[256,512]{1,0:T(8,128)(2,1)S(1)}, bf16[256,512]{1,0:T(8,128)(2,1)S(1)}, u32[]{:S(2)}, u32[]{:S(2)}) %collective-permute-start.11) | collective-permute-done | bytes 262176 | tf_op jit(solution)/shard_map/ppermute | solution.py:51
  163.0 5.6 %collective-permute-start.12 = (bf16[256,512]{1,0:T(8,128)(2,1)S(1)}, bf16[256,512]{1,0:T(8,128)(2,1)S(1)}, u32[]{:S(2)}, u32[]{:S(2)}) collective-permute-start(bf16[256,512]{1,0:T(8,128)(2,1)S(1)} %add_convert_fusion.11), channel_id=1, source_target_pairs={{0,1},{1,2},{2,3},{3,4},{4,5},{5,6},{6,7},{7,8},{8,9},{9,10},{10,1... | collective-permute-start | bytes 786440 | tf_op jit(solution)/shard_map/ppermute | solution.py:51
  169.3 1.9 collective-permute-start.20
  173.5 5.6 %collective-permute-start.13 = (bf16[256,512]{1,0:T(8,128)(2,1)S(1)}, bf16[256,512]{1,0:T(8,128)(2,1)S(1)}, u32[]{:S(2)}, u32[]{:S(2)}) collective-permute-start(bf16[256,512]{1,0:T(8,128)(2,1)S(1)} %add_convert_fusion.10), channel_id=1, source_target_pairs={{0,1},{1,2},{2,3},{3,4},{4,5},{5,6},{6,7},{7,8},{8,9},{9,10},{10,1... | collective-permute-start | bytes 786440 | tf_op jit(solution)/shard_map/ppermute | solution.py:51
  179.5 1.9 collective-permute-start.21
  183.1 5.6 %collective-permute-start.14 = (bf16[256,512]{1,0:T(8,128)(2,1)S(1)}, bf16[256,512]{1,0:T(8,128)(2,1)S(1)}, u32[]{:S(2)}, u32[]{:S(2)}) collective-permute-start(bf16[256,512]{1,0:T(8,128)(2,1)S(1)} %add_convert_fusion.9), channel_id=1, source_target_pairs={{0,1},{1,2},{2,3},{3,4},{4,5},{5,6},{6,7},{7,8},{8,9},{9,10},{10,1... | collective-permute-start | bytes 786440 | tf_op jit(solution)/shard_map/ppermute | solution.py:51
  192.6 5.6 %collective-permute-start.15 = (bf16[256,512]{1,0:T(8,128)(2,1)S(1)}, bf16[256,512]{1,0:T(8,128)(2,1)S(1)}, u32[]{:S(2)}, u32[]{:S(2)}) collective-permute-start(bf16[256,512]{1,0:T(8,128)(2,1)S(1)} %add_convert_fusion.8), channel_id=1, source_target_pairs={{0,1},{1,2},{2,3},{3,4},{4,5},{5,6},{6,7},{7,8},{8,9},{9,10},{10,1... | collective-permute-start | bytes 786440 | tf_op jit(solution)/shard_map/ppermute | solution.py:51
  198.6 1.9 collective-permute-start.23
  202.1 6.0 %collective-permute-done.23 = bf16[256,512]{1,0:T(8,128)(2,1)S(1)} collective-permute-done((bf16[256,512]{1,0:T(8,128)(2,1)S(1)}, bf16[256,512]{1,0:T(8,128)(2,1)S(1)}, u32[]{:S(2)}, u32[]{:S(2)}) %collective-permute-start.23) | collective-permute-done | bytes 262176 | tf_op jit(solution)/shard_map/ppermute | solution.py:52
  (116 shorter events, 66.0 us)
Async XLA Ops:
  4.2 28.1 %collective-permute-start = (bf16[145,512]{1,0:T(8,128)(2,1)S(1)}, bf16[145,512]{1,0:T(8,128)(2,1)S(1)}, u32[]{:S(2)}, u32[]{:S(2)}) collective-permute-start(bf16[145,512]{1,0:T(8,128)(2,1)S(1)} %pad_maximum_fusion.2), channel_id=1, source_target_pairs={{0,16},{16,32},{32,48},{48,64},{64,80},{80,96},{96,112},{112,128},... | collective-permute-start | bytes 445448 | tf_op jit(solution)/shard_map/ppermute | solution.py:10
  42.4 3.4 %collective-permute-start.1 = (bf16[256,512]{1,0:T(8,128)(2,1)S(1)}, bf16[256,512]{1,0:T(8,128)(2,1)S(1)}, u32[]{:S(2)}, u32[]{:S(2)}) collective-permute-start(bf16[256,512]{1,0:T(8,128)(2,1)S(1)} %broadcast_select_fusion), channel_id=1, source_target_pairs={{0,1},{15,14},{16,17},{31,30},{32,33},{47,46},{48,49},{63,62},{64,... | collective-permute-start | bytes 786440 | tf_op jit(solution)/shard_map/ppermute | solution.py:48
  45.9 3.8 %collective-permute-start.2 = (bf16[256,512]{1,0:T(8,128)(2,1)S(1)}, bf16[256,512]{1,0:T(8,128)(2,1)S(1)}, u32[]{:S(2)}, u32[]{:S(2)}) collective-permute-start(bf16[256,512]{1,0:T(8,128)(2,1)S(1)} %fusion.200), channel_id=1, source_target_pairs={{0,1},{1,2},{14,13},{15,14},{16,17},{17,18},{30,29},{31,30},{32,33... | collective-permute-start | bytes 786440 | tf_op jit(solution)/shard_map/ppermute | solution.py:48
  49.9 4.8 %collective-permute-start.3 = (bf16[256,512]{1,0:T(8,128)(2,1)S(1)}, bf16[256,512]{1,0:T(8,128)(2,1)S(1)}, u32[]{:S(2)}, u32[]{:S(2)}) collective-permute-start(bf16[256,512]{1,0:T(8,128)(2,1)S(1)} %fusion.199), channel_id=1, source_target_pairs={{0,1},{1,2},{2,3},{13,12},{14,13},{15,14},{16,17},{17,18},{18,19},... | collective-permute-start | bytes 786440 | tf_op jit(solution)/shard_map/ppermute | solution.py:48
  54.8 4.9 %collective-permute-start.4 = (bf16[256,512]{1,0:T(8,128)(2,1)S(1)}, bf16[256,512]{1,0:T(8,128)(2,1)S(1)}, u32[]{:S(2)}, u32[]{:S(2)}) collective-permute-start(bf16[256,512]{1,0:T(8,128)(2,1)S(1)} %fusion.198), channel_id=1, source_target_pairs={{0,1},{1,2},{2,3},{3,4},{12,11},{13,12},{14,13},{15,14},{16,17},{1... | collective-permute-start | bytes 786440 | tf_op jit(solution)/shard_map/ppermute | solution.py:48
  59.9 4.8 %collective-permute-start.5 = (bf16[256,512]{1,0:T(8,128)(2,1)S(1)}, bf16[256,512]{1,0:T(8,128)(2,1)S(1)}, u32[]{:S(2)}, u32[]{:S(2)}) collective-permute-start(bf16[256,512]{1,0:T(8,128)(2,1)S(1)} %fusion.197), channel_id=1, source_target_pairs={{0,1},{1,2},{2,3},{3,4},{4,5},{11,10},{12,11},{13,12},{14,13},{15,... | collective-permute-start | bytes 786440 | tf_op jit(solution)/shard_map/ppermute | solution.py:48
  64.8 2.7 %collective-permute-start.6 = (bf16[256,512]{1,0:T(8,128)(2,1)S(1)}, bf16[256,512]{1,0:T(8,128)(2,1)S(1)}, u32[]{:S(2)}, u32[]{:S(2)}) collective-permute-start(bf16[256,512]{1,0:T(8,128)(2,1)S(1)} %fusion.196), channel_id=1, source_target_pairs={{0,1},{1,2},{2,3},{3,4},{4,5},{5,6},{10,9},{11,10},{12,11},{13,12}... | collective-permute-start | bytes 786440 | tf_op jit(solution)/shard_map/ppermute | solution.py:48
  67.6 31.7 %collective-permute-start.7 = (bf16[256,512]{1,0:T(8,128)(2,1)S(1)}, bf16[256,512]{1,0:T(8,128)(2,1)S(1)}, u32[]{:S(2)}, u32[]{:S(2)}) collective-permute-start(bf16[256,512]{1,0:T(8,128)(2,1)S(1)} %fusion.195), channel_id=1, source_target_pairs={{0,1},{1,2},{2,3},{3,4},{4,5},{5,6},{6,7},{9,8},{10,9},{11,10},{12... | collective-permute-start | bytes 786440 | tf_op jit(solution)/shard_map/ppermute | solution.py:48
  99.4 28.6 %collective-permute-start.8 = (bf16[256,512]{1,0:T(8,128)(2,1)S(1)}, bf16[256,512]{1,0:T(8,128)(2,1)S(1)}, u32[]{:S(2)}, u32[]{:S(2)}) collective-permute-start(bf16[256,512]{1,0:T(8,128)(2,1)S(1)} %get-tuple-element.7), channel_id=1, source_target_pairs={{0,1},{1,2},{2,3},{3,4},{4,5},{5,6},{6,7},{7,8},{16,17},{17,18},{1... | collective-permute-start | bytes 786440 | tf_op jit(solution)/shard_map/ppermute | solution.py:51
  124.1 10.4 %collective-permute-start.16 = (bf16[256,512]{1,0:T(8,128)(2,1)S(1)}, bf16[256,512]{1,0:T(8,128)(2,1)S(1)}, u32[]{:S(2)}, u32[]{:S(2)}) collective-permute-start(bf16[256,512]{1,0:T(8,128)(2,1)S(1)} %get-tuple-element.8), channel_id=1, source_target_pairs={{8,7},{9,8},{10,9},{11,10},{12,11},{13,12},{14,13},{15,14},{24,23}... | collective-permute-start | bytes 786440 | tf_op jit(solution)/shard_map/ppermute | solution.py:52
  128.1 11.3 %collective-permute-start.9 = (bf16[256,512]{1,0:T(8,128)(2,1)S(1)}, bf16[256,512]{1,0:T(8,128)(2,1)S(1)}, u32[]{:S(2)}, u32[]{:S(2)}) collective-permute-start(bf16[256,512]{1,0:T(8,128)(2,1)S(1)} %add_convert_fusion.14), channel_id=1, source_target_pairs={{0,1},{1,2},{2,3},{3,4},{4,5},{5,6},{6,7},{7,8},{8,9},{16,17},{17,... | collective-permute-start | bytes 786440 | tf_op jit(solution)/shard_map/ppermute | solution.py:51
  134.6 11.6 %collective-permute-start.17 = (bf16[256,512]{1,0:T(8,128)(2,1)S(1)}, bf16[256,512]{1,0:T(8,128)(2,1)S(1)}, u32[]{:S(2)}, u32[]{:S(2)}) collective-permute-start(bf16[256,512]{1,0:T(8,128)(2,1)S(1)} %add_convert_fusion.7), channel_id=1, source_target_pairs={{7,6},{8,7},{9,8},{10,9},{11,10},{12,11},{13,12},{14,13},{15,14},{... | collective-permute-start | bytes 786440 | tf_op jit(solution)/shard_map/ppermute | solution.py:52
  139.4 12.1 %collective-permute-start.10 = (bf16[256,512]{1,0:T(8,128)(2,1)S(1)}, bf16[256,512]{1,0:T(8,128)(2,1)S(1)}, u32[]{:S(2)}, u32[]{:S(2)}) collective-permute-start(bf16[256,512]{1,0:T(8,128)(2,1)S(1)} %add_convert_fusion.13), channel_id=1, source_target_pairs={{0,1},{1,2},{2,3},{3,4},{4,5},{5,6},{6,7},{7,8},{8,9},{9,10},{16,1... | collective-permute-start | bytes 786440 | tf_op jit(solution)/shard_map/ppermute | solution.py:51
  146.3 11.8 %collective-permute-start.18 = (bf16[256,512]{1,0:T(8,128)(2,1)S(1)}, bf16[256,512]{1,0:T(8,128)(2,1)S(1)}, u32[]{:S(2)}, u32[]{:S(2)}) collective-permute-start(bf16[256,512]{1,0:T(8,128)(2,1)S(1)} %add_convert_fusion.6), channel_id=1, source_target_pairs={{6,5},{7,6},{8,7},{9,8},{10,9},{11,10},{12,11},{13,12},{14,13},{15... | collective-permute-start | bytes 786440 | tf_op jit(solution)/shard_map/ppermute | solution.py:52
  151.6 11.3 %collective-permute-start.11 = (bf16[256,512]{1,0:T(8,128)(2,1)S(1)}, bf16[256,512]{1,0:T(8,128)(2,1)S(1)}, u32[]{:S(2)}, u32[]{:S(2)}) collective-permute-start(bf16[256,512]{1,0:T(8,128)(2,1)S(1)} %add_convert_fusion.12), channel_id=1, source_target_pairs={{0,1},{1,2},{2,3},{3,4},{4,5},{5,6},{6,7},{7,8},{8,9},{9,10},{10,1... | collective-permute-start | bytes 786440 | tf_op jit(solution)/shard_map/ppermute | solution.py:51
  158.2 11.0 %collective-permute-start.19 = (bf16[256,512]{1,0:T(8,128)(2,1)S(1)}, bf16[256,512]{1,0:T(8,128)(2,1)S(1)}, u32[]{:S(2)}, u32[]{:S(2)}) collective-permute-start(bf16[256,512]{1,0:T(8,128)(2,1)S(1)} %add_convert_fusion.5), channel_id=1, source_target_pairs={{5,4},{6,5},{7,6},{8,7},{9,8},{10,9},{11,10},{12,11},{13,12},{14,1... | collective-permute-start | bytes 786440 | tf_op jit(solution)/shard_map/ppermute | solution.py:52
  163.0 10.4 %collective-permute-start.12 = (bf16[256,512]{1,0:T(8,128)(2,1)S(1)}, bf16[256,512]{1,0:T(8,128)(2,1)S(1)}, u32[]{:S(2)}, u32[]{:S(2)}) collective-permute-start(bf16[256,512]{1,0:T(8,128)(2,1)S(1)} %add_convert_fusion.11), channel_id=1, source_target_pairs={{0,1},{1,2},{2,3},{3,4},{4,5},{5,6},{6,7},{7,8},{8,9},{9,10},{10,1... | collective-permute-start | bytes 786440 | tf_op jit(solution)/shard_map/ppermute | solution.py:51
  169.3 10.2 %collective-permute-start.20 = (bf16[256,512]{1,0:T(8,128)(2,1)S(1)}, bf16[256,512]{1,0:T(8,128)(2,1)S(1)}, u32[]{:S(2)}, u32[]{:S(2)}) collective-permute-start(bf16[256,512]{1,0:T(8,128)(2,1)S(1)} %add_convert_fusion.4), channel_id=1, source_target_pairs={{4,3},{5,4},{6,5},{7,6},{8,7},{9,8},{10,9},{11,10},{12,11},{13,12}... | collective-permute-start | bytes 786440 | tf_op jit(solution)/shard_map/ppermute | solution.py:52
  173.5 9.5 %collective-permute-start.13 = (bf16[256,512]{1,0:T(8,128)(2,1)S(1)}, bf16[256,512]{1,0:T(8,128)(2,1)S(1)}, u32[]{:S(2)}, u32[]{:S(2)}) collective-permute-start(bf16[256,512]{1,0:T(8,128)(2,1)S(1)} %add_convert_fusion.10), channel_id=1, source_target_pairs={{0,1},{1,2},{2,3},{3,4},{4,5},{5,6},{6,7},{7,8},{8,9},{9,10},{10,1... | collective-permute-start | bytes 786440 | tf_op jit(solution)/shard_map/ppermute | solution.py:51
  179.5 9.5 %collective-permute-start.21 = (bf16[256,512]{1,0:T(8,128)(2,1)S(1)}, bf16[256,512]{1,0:T(8,128)(2,1)S(1)}, u32[]{:S(2)}, u32[]{:S(2)}) collective-permute-start(bf16[256,512]{1,0:T(8,128)(2,1)S(1)} %add_convert_fusion.3), channel_id=1, source_target_pairs={{3,2},{4,3},{5,4},{6,5},{7,6},{8,7},{9,8},{10,9},{11,10},{12,11},{... | collective-permute-start | bytes 786440 | tf_op jit(solution)/shard_map/ppermute | solution.py:52
  183.1 9.5 %collective-permute-start.14 = (bf16[256,512]{1,0:T(8,128)(2,1)S(1)}, bf16[256,512]{1,0:T(8,128)(2,1)S(1)}, u32[]{:S(2)}, u32[]{:S(2)}) collective-permute-start(bf16[256,512]{1,0:T(8,128)(2,1)S(1)} %add_convert_fusion.9), channel_id=1, source_target_pairs={{0,1},{1,2},{2,3},{3,4},{4,5},{5,6},{6,7},{7,8},{8,9},{9,10},{10,1... | collective-permute-start | bytes 786440 | tf_op jit(solution)/shard_map/ppermute | solution.py:51
  189.1 9.5 %collective-permute-start.22 = (bf16[256,512]{1,0:T(8,128)(2,1)S(1)}, bf16[256,512]{1,0:T(8,128)(2,1)S(1)}, u32[]{:S(2)}, u32[]{:S(2)}) collective-permute-start(bf16[256,512]{1,0:T(8,128)(2,1)S(1)} %add_convert_fusion.2), channel_id=1, source_target_pairs={{2,1},{3,2},{4,3},{5,4},{6,5},{7,6},{8,7},{9,8},{10,9},{11,10},{12... | collective-permute-start | bytes 786440 | tf_op jit(solution)/shard_map/ppermute | solution.py:52
  192.6 9.5 %collective-permute-start.15 = (bf16[256,512]{1,0:T(8,128)(2,1)S(1)}, bf16[256,512]{1,0:T(8,128)(2,1)S(1)}, u32[]{:S(2)}, u32[]{:S(2)}) collective-permute-start(bf16[256,512]{1,0:T(8,128)(2,1)S(1)} %add_convert_fusion.8), channel_id=1, source_target_pairs={{0,1},{1,2},{2,3},{3,4},{4,5},{5,6},{6,7},{7,8},{8,9},{9,10},{10,1... | collective-permute-start | bytes 786440 | tf_op jit(solution)/shard_map/ppermute | solution.py:51
  198.6 9.5 %collective-permute-start.23 = (bf16[256,512]{1,0:T(8,128)(2,1)S(1)}, bf16[256,512]{1,0:T(8,128)(2,1)S(1)}, u32[]{:S(2)}, u32[]{:S(2)}) collective-permute-start(bf16[256,512]{1,0:T(8,128)(2,1)S(1)} %add_convert_fusion.1), channel_id=1, source_target_pairs={{1,0},{2,1},{3,2},{4,3},{5,4},{6,5},{7,6},{8,7},{9,8},{10,9},{11,1... | collective-permute-start | bytes 786440 | tf_op jit(solution)/shard_map/ppermute | solution.py:52
  (3 other events, 44.1 us)

commit v13 on v10

--- a/solution.py
+++ b/solution.py
@@ -13,13 +13,10 @@
 def valid_conv(extended, taps):
     tap_count = taps.shape[0]
     out_rows = extended.shape[0] - tap_count + 1
-    running = taps[0][None, :] * extended[tap_count - 1 : tap_count - 1 + out_rows]
+    rows = lambda start: extended[start : start + out_rows].astype(jnp.float32)
+    running = taps[0][None, :] * rows(tap_count - 1)
     for offset in range(1, tap_count):
-        running = (
-            running
-            + taps[offset][None, :]
-            * extended[tap_count - 1 - offset : tap_count - 1 - offset + out_rows]
-        )
+        running = running + taps[offset][None, :] * rows(tap_count - 1 - offset)
     return running
 
 
@@ -58,17 +55,17 @@
     feat_reach = feat_taps.shape[1] - 1
     full_reach = filt_reach + feat_reach
     wide = lambda x: x.astype(jnp.float32)
-    key_body = valid_conv(wide(key_stream), feat_taps[1])
-    value_body = valid_conv(wide(value_stream), feat_taps[2])
+    key_body = valid_conv(key_stream, feat_taps[1])
+    value_body = valid_conv(value_stream, feat_taps[2])
     gated_body = (key_body * value_body).astype(jnp.bfloat16)
-    key_last = valid_conv(wide(key_stream[-full_reach:]), feat_taps[1])
-    value_last = valid_conv(wide(value_stream[-full_reach:]), feat_taps[2])
+    key_last = valid_conv(key_stream[-full_reach:], feat_taps[1])
+    value_last = valid_conv(value_stream[-full_reach:], feat_taps[2])
     gated_last = (key_last * value_last).astype(jnp.bfloat16)
     outgoing = jnp.concatenate(
         [gated_last, key_stream[-feat_reach:], value_stream[-feat_reach:], query_stream[-feat_reach:]], 0
     )
     incoming = shifted(outgoing, "ctx", 1)
-    query_body = valid_conv(wide(query_stream), feat_taps[0])
+    query_body = valid_conv(query_stream, feat_taps[0])
     mixed_tail = valid_conv(wide(gated_body), filt_taps) + skip_bias[None, :] * wide(gated_body[filt_reach:])
     product_tail = (query_body[filt_reach:] * mixed_tail).astype(jnp.bfloat16)
     gated_halo = incoming[:filt_reach]

time: 208 us -> 210 us (level)
    convert_element_type x9 -> x5, other arithmetic: 5.03 us -> 3.83 us  [shards(): wide = lambda x: x.astype(jnp.float32)]
where the time goes in v13:
time: 210 us; the launch traced here: 208 us
  waiting for transfers between devices  105 us (50%)
  starting transfers between devices  55.9 us (27%)
  other arithmetic  23.5 us (11%)
  local copies, waits for them, and re-layouts  11.9 us (6%)
  matrix products  10.9 us (5%)
    ppermute x15, waiting for transfers between devices, line_reduce_scatter(): from_right[chain] = lax.ppermute(send_left, axis, leftward)  99.1 us
    ppermute x15, starting transfers between devices, line_reduce_scatter(): from_left[chain] = lax.ppermute(send_right, axis, rightward)  29.5 us
    ppermute x15, starting transfers between devices, line_reduce_scatter(): from_right[chain] = lax.ppermute(send_left, axis, leftward)  24.4 us
    dot_general x31, matrix products, block(): jnp.dot(product, columns, preferred_element_type=jnp.float32)  10.9 us
    slice x7, local copies, waits for them, and re-layouts, valid_conv(): running = running + taps[offset][None, :] * rows(tap_count - 1 - offset)  8.02 us
    convert_element_type x1, other arithmetic, shards(): product_head = (query_feat_head * mixed_head).astype(jnp.bfloat16)  7.06 us
    convert_element_type x1, other arithmetic, shards(): product_tail = (query_body[filt_reach:] * mixed_tail).astype(jnp.bfloat16)  6.91 us
    ppermute x1, waiting for transfers between devices, shifted(): return lax.ppermute(block, axis, route)  5.5 us
  transfers between devices with their start and end apart: 31, of which 14 were waited for; matrix products, arithmetic and copies ran while one was open for 16% of the time, Pallas kernels for 0%

profile of v13, /device:TPU:376, one launch (start us, length us, event | category | flops | bytes accessed | tf_op | source)
XLA Modules:
  0.0 208.0 jit_solution(3199419051011870200)
XLA Ops:
  2.7 2.5 %multiply_convert_fusion.1 = bf16[127,512]{1,0:T(8,128)(2,1)S(1)} fusion(bf16[256,512]{1,0:T(8,128)(2,1)} %param.9, f32[512]{0:T(512)S(1)} %bitcast.152, f32[512]{0:T(512)S(1)} %bitcast.155, f32[512]{0:T(512)S(1)} %bitcast.158, f32[512]{0:T(512)S(1)} %bitcast.161, f32[512]{0:T(512)S(1)} %bitcast.164, f32[512]{0:T(512)S(1)} %bitcast.167, ...), kind=kLoop, calls=%fused_computation.614 | loop fusion | flops 2731008 | bytes 1979392 | tf_op jit(solution)/shard_map/convert_element_type | solution.py:63
  5.2 1.9 collective-permute-start
  7.1 3.7 %fusion.342 = (f32[250,512]{1,0:T(8,128)S(1)}, bf16[250,512]{1,0:T(8,128)(2,1)S(1)}) fusion(bf16[256,512]{1,0:T(8,128)(2,1)} %param.9, f32[512]{0:T(512)S(1)} %bitcast.153, f32[512]{0:T(512)S(1)} %bitcast.156, f32[512]{0:T(512)S(1)} %bitcast.159, f32[512]{0:T(512)S(1)} %bitcast.162, f32[512]{0:T(512)S(1)} %bitcast.165, f32[512]{0:T(512)S(1)} %bitcast.168, ...), kind=kLoop, calls=%fused_computation.691 | loop fusion | flops 5504000 | bytes 4380672 | tf_op jit(solution)/shard_map/convert_element_type | solution.py:57
  20.5 6.9 %fusion.164 = bf16[123,512]{1,0:T(8,128)(2,1)S(1)} fusion(f32[250,512]{1,0:T(8,128)S(1)} %get-tuple-element.5, f32[512]{0:T(512)S(1)} %bitcast.443, f32[512]{0:T(512)S(1)} %bitcast.445, f32[512]{0:T(512)S(1)} %bitcast.269, f32[512]{0:T(512)S(1)} %bitcast.271, f32[512]{0:T(512)S(1)} %bitcast.273, f32[512]{0:T(512)S(1)} %bitcast.275, f32[512]{0:T(512)S(1)} %bitcast.277, ...), kind=kLoop, calls=%fused_computation.358 | loop fusion | flops 16373760 | bytes 33011712 | tf_op jit(solution)/shard_map/convert_element_type | solution.py:70
  27.6 5.5 %collective-permute-done = bf16[145,512]{1,0:T(8,128)(2,1)S(1)} collective-permute-done((bf16[145,512]{1,0:T(8,128)(2,1)S(1)}, bf16[145,512]{1,0:T(8,128)(2,1)S(1)}, u32[]{:S(2)}, u32[]{:S(2)}) %collective-permute-start) | collective-permute-done | bytes 148512 | tf_op jit(solution)/shard_map/ppermute | solution.py:10
  33.3 7.1 %fusion.34 = bf16[133,512]{1,0:T(8,128)(2,1)S(1)} fusion(f32[260,512]{1,0:T(8,128)S(1)} %maximum_convert_fusion, bf16[127,512]{1,0:T(8,128)(2,1)S(1)} %slice.2157, bf16[6,512]{1,0:T(8,128)(2,1)S(1)} %fusion.293, f32[512]{0:T(512)S(1)} %copy-done.1, f32[512]{0:T(512)S(1)} %bitcast.444, f32[512]{0:T(512)S(1)} %bitcast.446, f32[512]{0:T(512)S(1)} %bitcast.270, ...), kind=kLoop, calls=%fused_computation.97 | loop fusion | flops 17977344 | bytes 35674112 | tf_op jit(solution)/shard_map/convert_element_type | solution.py:83
  54.5 37.7 %collective-permute-done.19 = bf16[256,512]{1,0:T(8,128)(2,1)S(1)} collective-permute-done((bf16[256,512]{1,0:T(8,128)(2,1)S(1)}, bf16[256,512]{1,0:T(8,128)(2,1)S(1)}, u32[]{:S(2)}, u32[]{:S(2)}) %collective-permute-start.19) | collective-permute-done | bytes 262176 | tf_op jit(solution)/shard_map/ppermute | solution.py:45
  95.2 8.9 %collective-permute-done.20 = bf16[256,512]{1,0:T(8,128)(2,1)S(1)} collective-permute-done((bf16[256,512]{1,0:T(8,128)(2,1)S(1)}, bf16[256,512]{1,0:T(8,128)(2,1)S(1)}, u32[]{:S(2)}, u32[]{:S(2)}) %collective-permute-start.20) | collective-permute-done | bytes 262176 | tf_op jit(solution)/shard_map/ppermute | solution.py:45
  107.2 8.1 %collective-permute-done.21 = bf16[256,512]{1,0:T(8,128)(2,1)S(1)} collective-permute-done((bf16[256,512]{1,0:T(8,128)(2,1)S(1)}, bf16[256,512]{1,0:T(8,128)(2,1)S(1)}, u32[]{:S(2)}, u32[]{:S(2)}) %collective-permute-start.21) | collective-permute-done | bytes 262176 | tf_op jit(solution)/shard_map/ppermute | solution.py:45
  118.4 7.2 %collective-permute-done.22 = bf16[256,512]{1,0:T(8,128)(2,1)S(1)} collective-permute-done((bf16[256,512]{1,0:T(8,128)(2,1)S(1)}, bf16[256,512]{1,0:T(8,128)(2,1)S(1)}, u32[]{:S(2)}, u32[]{:S(2)}) %collective-permute-start.22) | collective-permute-done | bytes 262176 | tf_op jit(solution)/shard_map/ppermute | solution.py:45
  128.7 6.5 %collective-permute-done.23 = bf16[256,512]{1,0:T(8,128)(2,1)S(1)} collective-permute-done((bf16[256,512]{1,0:T(8,128)(2,1)S(1)}, bf16[256,512]{1,0:T(8,128)(2,1)S(1)}, u32[]{:S(2)}, u32[]{:S(2)}) %collective-permute-start.23) | collective-permute-done | bytes 262176 | tf_op jit(solution)/shard_map/ppermute | solution.py:45
  138.2 6.5 %collective-permute-done.24 = bf16[256,512]{1,0:T(8,128)(2,1)S(1)} collective-permute-done((bf16[256,512]{1,0:T(8,128)(2,1)S(1)}, bf16[256,512]{1,0:T(8,128)(2,1)S(1)}, u32[]{:S(2)}, u32[]{:S(2)}) %collective-permute-start.24) | collective-permute-done | bytes 262176 | tf_op jit(solution)/shard_map/ppermute | solution.py:45
  148.4 5.8 %collective-permute-done.25 = bf16[256,512]{1,0:T(8,128)(2,1)S(1)} collective-permute-done((bf16[256,512]{1,0:T(8,128)(2,1)S(1)}, bf16[256,512]{1,0:T(8,128)(2,1)S(1)}, u32[]{:S(2)}, u32[]{:S(2)}) %collective-permute-start.25) | collective-permute-done | bytes 262176 | tf_op jit(solution)/shard_map/ppermute | solution.py:45
  156.6 5.1 %collective-permute-start.12 = (bf16[256,512]{1,0:T(8,128)(2,1)S(1)}, bf16[256,512]{1,0:T(8,128)(2,1)S(1)}, u32[]{:S(2)}, u32[]{:S(2)}) collective-permute-start(bf16[256,512]{1,0:T(8,128)(2,1)S(1)} %add_convert_fusion.18), channel_id=1, source_target_pairs={{0,1},{1,2},{2,3},{3,4},{4,5},{5,6},{6,7},{7,8},{8,9},{9,10},{10,1... | collective-permute-start | bytes 786440 | tf_op jit(solution)/shard_map/ppermute | solution.py:44
  161.8 2.8 %collective-permute-done.26 = bf16[256,512]{1,0:T(8,128)(2,1)S(1)} collective-permute-done((bf16[256,512]{1,0:T(8,128)(2,1)S(1)}, bf16[256,512]{1,0:T(8,128)(2,1)S(1)}, u32[]{:S(2)}, u32[]{:S(2)}) %collective-permute-start.26) | collective-permute-done | bytes 262176 | tf_op jit(solution)/shard_map/ppermute | solution.py:45
  167.0 5.4 %collective-permute-start.13 = (bf16[256,512]{1,0:T(8,128)(2,1)S(1)}, bf16[256,512]{1,0:T(8,128)(2,1)S(1)}, u32[]{:S(2)}, u32[]{:S(2)}) collective-permute-start(bf16[256,512]{1,0:T(8,128)(2,1)S(1)} %add_convert_fusion.17), channel_id=1, source_target_pairs={{0,1},{1,2},{2,3},{3,4},{4,5},{5,6},{6,7},{7,8},{8,9},{9,10},{10,1... | collective-permute-start | bytes 786440 | tf_op jit(solution)/shard_map/ppermute | solution.py:44
  172.4 3.7 %collective-permute-done.27 = bf16[256,512]{1,0:T(8,128)(2,1)S(1)} collective-permute-done((bf16[256,512]{1,0:T(8,128)(2,1)S(1)}, bf16[256,512]{1,0:T(8,128)(2,1)S(1)}, u32[]{:S(2)}, u32[]{:S(2)}) %collective-permute-start.27) | collective-permute-done | bytes 262176 | tf_op jit(solution)/shard_map/ppermute | solution.py:45
  176.1 1.9 collective-permute-start.28
  178.6 5.6 %collective-permute-start.14 = (bf16[256,512]{1,0:T(8,128)(2,1)S(1)}, bf16[256,512]{1,0:T(8,128)(2,1)S(1)}, u32[]{:S(2)}, u32[]{:S(2)}) collective-permute-start(bf16[256,512]{1,0:T(8,128)(2,1)S(1)} %add_convert_fusion.16), channel_id=1, source_target_pairs={{0,1},{1,2},{2,3},{3,4},{4,5},{5,6},{6,7},{7,8},{8,9},{9,10},{10,1... | collective-permute-start | bytes 786440 | tf_op jit(solution)/shard_map/ppermute | solution.py:44
  184.2 3.9 %collective-permute-done.28 = bf16[256,512]{1,0:T(8,128)(2,1)S(1)} collective-permute-done((bf16[256,512]{1,0:T(8,128)(2,1)S(1)}, bf16[256,512]{1,0:T(8,128)(2,1)S(1)}, u32[]{:S(2)}, u32[]{:S(2)}) %collective-permute-start.28) | collective-permute-done | bytes 262176 | tf_op jit(solution)/shard_map/ppermute | solution.py:45
  190.5 5.1 %collective-permute-start.15 = (bf16[256,512]{1,0:T(8,128)(2,1)S(1)}, bf16[256,512]{1,0:T(8,128)(2,1)S(1)}, u32[]{:S(2)}, u32[]{:S(2)}) collective-permute-start(bf16[256,512]{1,0:T(8,128)(2,1)S(1)} %add_convert_fusion.15), channel_id=1, source_target_pairs={{0,1},{1,2},{2,3},{3,4},{4,5},{5,6},{6,7},{7,8},{8,9},{9,10},{10,1... | collective-permute-start | bytes 786440 | tf_op jit(solution)/shard_map/ppermute | solution.py:44
  195.7 2.0 collective-permute-done.29
  197.7 1.9 collective-permute-start.30
  201.0 6.2 %collective-permute-done.30 = bf16[256,512]{1,0:T(8,128)(2,1)S(1)} collective-permute-done((bf16[256,512]{1,0:T(8,128)(2,1)S(1)}, bf16[256,512]{1,0:T(8,128)(2,1)S(1)}, u32[]{:S(2)}, u32[]{:S(2)}) %collective-permute-start.30) | collective-permute-done | bytes 262176 | tf_op jit(solution)/shard_map/ppermute | solution.py:45
  (134 shorter events, 55.2 us)
Async XLA Ops:
  5.2 27.9 %collective-permute-start = (bf16[145,512]{1,0:T(8,128)(2,1)S(1)}, bf16[145,512]{1,0:T(8,128)(2,1)S(1)}, u32[]{:S(2)}, u32[]{:S(2)}) collective-permute-start(bf16[145,512]{1,0:T(8,128)(2,1)S(1)} %pad_maximum_fusion.2), channel_id=1, source_target_pairs={{0,16},{16,32},{32,48},{48,64},{64,80},{80,96},{96,112},{112,128},... | collective-permute-start | bytes 445448 | tf_op jit(solution)/shard_map/ppermute | solution.py:10
  52.1 40.0 %collective-permute-start.19 = (bf16[256,512]{1,0:T(8,128)(2,1)S(1)}, bf16[256,512]{1,0:T(8,128)(2,1)S(1)}, u32[]{:S(2)}, u32[]{:S(2)}) collective-permute-start(bf16[256,512]{1,0:T(8,128)(2,1)S(1)} %add_convert_fusion.12), channel_id=1, source_target_pairs={{12,11},{13,12},{14,13},{15,14},{28,27},{29,28},{30,29},{31,30},{4... | collective-permute-start | bytes 786440 | tf_op jit(solution)/shard_map/ppermute | solution.py:45
  53.8 40.7 %collective-permute-start.5 = (bf16[256,512]{1,0:T(8,128)(2,1)S(1)}, bf16[256,512]{1,0:T(8,128)(2,1)S(1)}, u32[]{:S(2)}, u32[]{:S(2)}) collective-permute-start(bf16[256,512]{1,0:T(8,128)(2,1)S(1)} %add_convert_fusion.25), channel_id=1, source_target_pairs={{0,1},{1,2},{2,3},{3,4},{4,5},{16,17},{17,18},{18,19},{19,20},{20,... | collective-permute-start | bytes 786440 | tf_op jit(solution)/shard_map/ppermute | solution.py:44
  92.2 11.9 %collective-permute-start.20 = (bf16[256,512]{1,0:T(8,128)(2,1)S(1)}, bf16[256,512]{1,0:T(8,128)(2,1)S(1)}, u32[]{:S(2)}, u32[]{:S(2)}) collective-permute-start(bf16[256,512]{1,0:T(8,128)(2,1)S(1)} %add_convert_fusion.11), channel_id=1, source_target_pairs={{11,10},{12,11},{13,12},{14,13},{15,14},{27,26},{28,27},{29,28},{3... | collective-permute-start | bytes 786440 | tf_op jit(solution)/shard_map/ppermute | solution.py:45
  94.5 11.9 %collective-permute-start.6 = (bf16[256,512]{1,0:T(8,128)(2,1)S(1)}, bf16[256,512]{1,0:T(8,128)(2,1)S(1)}, u32[]{:S(2)}, u32[]{:S(2)}) collective-permute-start(bf16[256,512]{1,0:T(8,128)(2,1)S(1)} %add_convert_fusion.24), channel_id=1, source_target_pairs={{0,1},{1,2},{2,3},{3,4},{4,5},{5,6},{16,17},{17,18},{18,19},{19,20... | collective-permute-start | bytes 786440 | tf_op jit(solution)/shard_map/ppermute | solution.py:44
  104.2 11.1 %collective-permute-start.21 = (bf16[256,512]{1,0:T(8,128)(2,1)S(1)}, bf16[256,512]{1,0:T(8,128)(2,1)S(1)}, u32[]{:S(2)}, u32[]{:S(2)}) collective-permute-start(bf16[256,512]{1,0:T(8,128)(2,1)S(1)} %add_convert_fusion.10), channel_id=1, source_target_pairs={{10,9},{11,10},{12,11},{13,12},{14,13},{15,14},{26,25},{27,26},{28... | collective-permute-start | bytes 786440 | tf_op jit(solution)/shard_map/ppermute | solution.py:45
  106.6 11.1 %collective-permute-start.7 = (bf16[256,512]{1,0:T(8,128)(2,1)S(1)}, bf16[256,512]{1,0:T(8,128)(2,1)S(1)}, u32[]{:S(2)}, u32[]{:S(2)}) collective-permute-start(bf16[256,512]{1,0:T(8,128)(2,1)S(1)} %add_convert_fusion.23), channel_id=1, source_target_pairs={{0,1},{1,2},{2,3},{3,4},{4,5},{5,6},{6,7},{16,17},{17,18},{18,19},... | collective-permute-start | bytes 786440 | tf_op jit(solution)/shard_map/ppermute | solution.py:44
  115.4 10.2 %collective-permute-start.22 = (bf16[256,512]{1,0:T(8,128)(2,1)S(1)}, bf16[256,512]{1,0:T(8,128)(2,1)S(1)}, u32[]{:S(2)}, u32[]{:S(2)}) collective-permute-start(bf16[256,512]{1,0:T(8,128)(2,1)S(1)} %add_convert_fusion.9), channel_id=1, source_target_pairs={{9,8},{10,9},{11,10},{12,11},{13,12},{14,13},{15,14},{25,24},{26,2... | collective-permute-start | bytes 786440 | tf_op jit(solution)/shard_map/ppermute | solution.py:45
  117.7 10.2 %collective-permute-start.8 = (bf16[256,512]{1,0:T(8,128)(2,1)S(1)}, bf16[256,512]{1,0:T(8,128)(2,1)S(1)}, u32[]{:S(2)}, u32[]{:S(2)}) collective-permute-start(bf16[256,512]{1,0:T(8,128)(2,1)S(1)} %add_convert_fusion.22), channel_id=1, source_target_pairs={{0,1},{1,2},{2,3},{3,4},{4,5},{5,6},{6,7},{7,8},{16,17},{17,18},{1... | collective-permute-start | bytes 786440 | tf_op jit(solution)/shard_map/ppermute | solution.py:44
  125.7 9.5 %collective-permute-start.23 = (bf16[256,512]{1,0:T(8,128)(2,1)S(1)}, bf16[256,512]{1,0:T(8,128)(2,1)S(1)}, u32[]{:S(2)}, u32[]{:S(2)}) collective-permute-start(bf16[256,512]{1,0:T(8,128)(2,1)S(1)} %add_convert_fusion.8), channel_id=1, source_target_pairs={{8,7},{9,8},{10,9},{11,10},{12,11},{13,12},{14,13},{15,14},{24,23}... | collective-permute-start | bytes 786440 | tf_op jit(solution)/shard_map/ppermute | solution.py:45
  128.0 9.5 %collective-permute-start.9 = (bf16[256,512]{1,0:T(8,128)(2,1)S(1)}, bf16[256,512]{1,0:T(8,128)(2,1)S(1)}, u32[]{:S(2)}, u32[]{:S(2)}) collective-permute-start(bf16[256,512]{1,0:T(8,128)(2,1)S(1)} %add_convert_fusion.21), channel_id=1, source_target_pairs={{0,1},{1,2},{2,3},{3,4},{4,5},{5,6},{6,7},{7,8},{8,9},{16,17},{17,... | collective-permute-start | bytes 786440 | tf_op jit(solution)/shard_map/ppermute | solution.py:44
  135.2 9.5 %collective-permute-start.24 = (bf16[256,512]{1,0:T(8,128)(2,1)S(1)}, bf16[256,512]{1,0:T(8,128)(2,1)S(1)}, u32[]{:S(2)}, u32[]{:S(2)}) collective-permute-start(bf16[256,512]{1,0:T(8,128)(2,1)S(1)} %add_convert_fusion.7), channel_id=1, source_target_pairs={{7,6},{8,7},{9,8},{10,9},{11,10},{12,11},{13,12},{14,13},{15,14},{... | collective-permute-start | bytes 786440 | tf_op jit(solution)/shard_map/ppermute | solution.py:45
  137.5 9.5 %collective-permute-start.10 = (bf16[256,512]{1,0:T(8,128)(2,1)S(1)}, bf16[256,512]{1,0:T(8,128)(2,1)S(1)}, u32[]{:S(2)}, u32[]{:S(2)}) collective-permute-start(bf16[256,512]{1,0:T(8,128)(2,1)S(1)} %add_convert_fusion.20), channel_id=1, source_target_pairs={{0,1},{1,2},{2,3},{3,4},{4,5},{5,6},{6,7},{7,8},{8,9},{9,10},{16,1... | collective-permute-start | bytes 786440 | tf_op jit(solution)/shard_map/ppermute | solution.py:44
  144.8 9.5 %collective-permute-start.25 = (bf16[256,512]{1,0:T(8,128)(2,1)S(1)}, bf16[256,512]{1,0:T(8,128)(2,1)S(1)}, u32[]{:S(2)}, u32[]{:S(2)}) collective-permute-start(bf16[256,512]{1,0:T(8,128)(2,1)S(1)} %add_convert_fusion.6), channel_id=1, source_target_pairs={{6,5},{7,6},{8,7},{9,8},{10,9},{11,10},{12,11},{13,12},{14,13},{15... | collective-permute-start | bytes 786440 | tf_op jit(solution)/shard_map/ppermute | solution.py:45
  147.1 9.5 %collective-permute-start.11 = (bf16[256,512]{1,0:T(8,128)(2,1)S(1)}, bf16[256,512]{1,0:T(8,128)(2,1)S(1)}, u32[]{:S(2)}, u32[]{:S(2)}) collective-permute-start(bf16[256,512]{1,0:T(8,128)(2,1)S(1)} %add_convert_fusion.19), channel_id=1, source_target_pairs={{0,1},{1,2},{2,3},{3,4},{4,5},{5,6},{6,7},{7,8},{8,9},{9,10},{10,1... | collective-permute-start | bytes 786440 | tf_op jit(solution)/shard_map/ppermute | solution.py:44
  154.3 10.3 %collective-permute-start.26 = (bf16[256,512]{1,0:T(8,128)(2,1)S(1)}, bf16[256,512]{1,0:T(8,128)(2,1)S(1)}, u32[]{:S(2)}, u32[]{:S(2)}) collective-permute-start(bf16[256,512]{1,0:T(8,128)(2,1)S(1)} %add_convert_fusion.5), channel_id=1, source_target_pairs={{5,4},{6,5},{7,6},{8,7},{9,8},{10,9},{11,10},{12,11},{13,12},{14,1... | collective-permute-start | bytes 786440 | tf_op jit(solution)/shard_map/ppermute | solution.py:45
  156.6 10.3 %collective-permute-start.12 = (bf16[256,512]{1,0:T(8,128)(2,1)S(1)}, bf16[256,512]{1,0:T(8,128)(2,1)S(1)}, u32[]{:S(2)}, u32[]{:S(2)}) collective-permute-start(bf16[256,512]{1,0:T(8,128)(2,1)S(1)} %add_convert_fusion.18), channel_id=1, source_target_pairs={{0,1},{1,2},{2,3},{3,4},{4,5},{5,6},{6,7},{7,8},{8,9},{9,10},{10,1... | collective-permute-start | bytes 786440 | tf_op jit(solution)/shard_map/ppermute | solution.py:44
  164.6 11.4 %collective-permute-start.27 = (bf16[256,512]{1,0:T(8,128)(2,1)S(1)}, bf16[256,512]{1,0:T(8,128)(2,1)S(1)}, u32[]{:S(2)}, u32[]{:S(2)}) collective-permute-start(bf16[256,512]{1,0:T(8,128)(2,1)S(1)} %add_convert_fusion.4), channel_id=1, source_target_pairs={{4,3},{5,4},{6,5},{7,6},{8,7},{9,8},{10,9},{11,10},{12,11},{13,12}... | collective-permute-start | bytes 786440 | tf_op jit(solution)/shard_map/ppermute | solution.py:45
  167.0 11.6 %collective-permute-start.13 = (bf16[256,512]{1,0:T(8,128)(2,1)S(1)}, bf16[256,512]{1,0:T(8,128)(2,1)S(1)}, u32[]{:S(2)}, u32[]{:S(2)}) collective-permute-start(bf16[256,512]{1,0:T(8,128)(2,1)S(1)} %add_convert_fusion.17), channel_id=1, source_target_pairs={{0,1},{1,2},{2,3},{3,4},{4,5},{5,6},{6,7},{7,8},{8,9},{9,10},{10,1... | collective-permute-start | bytes 786440 | tf_op jit(solution)/shard_map/ppermute | solution.py:44
  176.1 12.0 %collective-permute-start.28 = (bf16[256,512]{1,0:T(8,128)(2,1)S(1)}, bf16[256,512]{1,0:T(8,128)(2,1)S(1)}, u32[]{:S(2)}, u32[]{:S(2)}) collective-permute-start(bf16[256,512]{1,0:T(8,128)(2,1)S(1)} %add_convert_fusion.3), channel_id=1, source_target_pairs={{3,2},{4,3},{5,4},{6,5},{7,6},{8,7},{9,8},{10,9},{11,10},{12,11},{... | collective-permute-start | bytes 786440 | tf_op jit(solution)/shard_map/ppermute | solution.py:45
  178.6 11.9 %collective-permute-start.14 = (bf16[256,512]{1,0:T(8,128)(2,1)S(1)}, bf16[256,512]{1,0:T(8,128)(2,1)S(1)}, u32[]{:S(2)}, u32[]{:S(2)}) collective-permute-start(bf16[256,512]{1,0:T(8,128)(2,1)S(1)} %add_convert_fusion.16), channel_id=1, source_target_pairs={{0,1},{1,2},{2,3},{3,4},{4,5},{5,6},{6,7},{7,8},{8,9},{9,10},{10,1... | collective-permute-start | bytes 786440 | tf_op jit(solution)/shard_map/ppermute | solution.py:44
  188.2 9.5 %collective-permute-start.29 = (bf16[256,512]{1,0:T(8,128)(2,1)S(1)}, bf16[256,512]{1,0:T(8,128)(2,1)S(1)}, u32[]{:S(2)}, u32[]{:S(2)}) collective-permute-start(bf16[256,512]{1,0:T(8,128)(2,1)S(1)} %add_convert_fusion.2), channel_id=1, source_target_pairs={{2,1},{3,2},{4,3},{5,4},{6,5},{7,6},{8,7},{9,8},{10,9},{11,10},{12... | collective-permute-start | bytes 786440 | tf_op jit(solution)/shard_map/ppermute | solution.py:45
  190.5 10.5 %collective-permute-start.15 = (bf16[256,512]{1,0:T(8,128)(2,1)S(1)}, bf16[256,512]{1,0:T(8,128)(2,1)S(1)}, u32[]{:S(2)}, u32[]{:S(2)}) collective-permute-start(bf16[256,512]{1,0:T(8,128)(2,1)S(1)} %add_convert_fusion.15), channel_id=1, source_target_pairs={{0,1},{1,2},{2,3},{3,4},{4,5},{5,6},{6,7},{7,8},{8,9},{9,10},{10,1... | collective-permute-start | bytes 786440 | tf_op jit(solution)/shard_map/ppermute | solution.py:44
  197.7 9.5 %collective-permute-start.30 = (bf16[256,512]{1,0:T(8,128)(2,1)S(1)}, bf16[256,512]{1,0:T(8,128)(2,1)S(1)}, u32[]{:S(2)}, u32[]{:S(2)}) collective-permute-start(bf16[256,512]{1,0:T(8,128)(2,1)S(1)} %add_convert_fusion.1), channel_id=1, source_target_pairs={{1,0},{2,1},{3,2},{4,3},{5,4},{6,5},{7,6},{8,7},{9,8},{10,9},{11,1... | collective-permute-start | bytes 786440 | tf_op jit(solution)/shard_map/ppermute | solution.py:45
  (11 other events, 73.3 us)
